TPU v7x, 32 devices: a whole 2x2x4 slice. The times are simulated.
32 devices in a mesh: pw: 8 (over z, y), band: 4 (over x, core).
Axes of the slice: x: 2, y: 2, z: 4, core: 2. Of those that a mesh axis runs over, the one named last changes fastest.
Arguments:
- psi_block: float32 [2, 8, 256, 128], P(None, 'band', 'pw'), may hold values from -6 to 6
- psi_all: bfloat16 [2, 1024, 256, 128], P(None, 'band', 'pw'), may hold values from -0.0234375 to 0.0234375
- potential: float32 [128, 128, 128], P('pw'), may hold values from -8 to 8
- stick_col: int32 [256], replicated, may hold values from 0 to 16383, as said below
Outputs:
- intersection: float32 [2, 8, 1024], P(None, 'pw', 'band')
- hpsi: float32 [2, 8, 256, 128], P(None, 'band', 'pw')
Inputs may be any that keep to these rules, and one draw needn't show every extreme that they name: `stick_col`: distinct columns of the 128 x 128 plane; column 0 and column 16383 are always among them.
All inputs are finite; a program needn't handle non-finite values.
Results may differ from a plain program's by a relative error of at most 0.0029.
Values may be sent and summed in bfloat16 or wider, within the bound.
No kernel may reach another device: no remote copies, remote signals or barrier semaphores. Data moves between devices by JAX's collectives and lax.ppermute only.
A program may use at most 64 MiB of HBM per device.

v0:
```python
import math

import jax
import jax.numpy as jnp
from jax import lax
from jax.sharding import PartitionSpec as P


def frequency(index, size):
    return jnp.where(index < size // 2, index, index - size)


def kinetic_table(columns, grid_size):
    col_x = frequency(columns // grid_size, grid_size).astype(jnp.float32)
    col_y = frequency(columns % grid_size, grid_size).astype(jnp.float32)
    along = frequency(jnp.arange(grid_size, dtype=jnp.int32), grid_size).astype(jnp.float32)
    plane = col_x * col_x + col_y * col_y
    return 4.0 * (plane[:, None] + along[None, :] * along[None, :]) / float(grid_size * grid_size)


def dft_table(grid_size, sign):
    indices = jnp.arange(grid_size, dtype=jnp.int32)
    products = indices[:, None] * indices[None, :] % grid_size
    angles = 2.0 * math.pi / grid_size * products.astype(jnp.float32)
    cosine = jnp.cos(angles)
    sine = sign * jnp.sin(angles)
    return jnp.stack([jnp.stack([cosine, -sine]), jnp.stack([sine, cosine])])


def per_device(psi_block, psi_all, potential, stick_col):
    local_bands = psi_block.shape[1]
    sticks_dev = psi_block.shape[2]
    grid_size = psi_block.shape[3]
    highest = lax.Precision.HIGHEST
    rank = lax.axis_index("pw")
    pw_count = lax.axis_size("pw")
    band_count = lax.axis_size("band")
    my_columns = lax.dynamic_slice_in_dim(stick_col, rank * sticks_dev, sticks_dev)
    kinetic = kinetic_table(my_columns, grid_size)
    inverse = dft_table(grid_size, 1.0)
    forward = dft_table(grid_size, -1.0)
    cosine = inverse[0, 0]
    sine = inverse[1, 0]
    grid_iota = jnp.arange(grid_size, dtype=jnp.int32)
    col_x = stick_col // grid_size
    col_y = stick_col % grid_size
    phase_angles = (
        2.0
        * math.pi
        / grid_size
        * (grid_iota[:, None] * col_y[None, :] % grid_size).astype(jnp.float32)
    )
    phase_cos = jnp.cos(phase_angles)
    phase_sin = jnp.sin(phase_angles)
    place_rows = (col_x[:, None] == grid_iota[None, :]).astype(jnp.float32)
    pick_rows = (grid_iota[:, None] == col_x[None, :]).astype(jnp.float32)
    turned_pot = (jnp.transpose(potential, (0, 2, 1)) / float(grid_size**3))[None]

    def mult(left, right):
        return jnp.dot(left, right, precision=highest, preferred_element_type=jnp.float32)

    all_re = psi_all[0].reshape(psi_all.shape[1], -1)
    all_im = psi_all[1].reshape(psi_all.shape[1], -1)
    dims = (((1,), (1,)), ((), ()))
    group_count = local_bands // 2
    z_lines = jnp.einsum("dcvu,cbsu->bvds", inverse, psi_block, precision=highest)
    planes_in = lax.all_to_all(z_lines, "pw", split_axis=1, concat_axis=3, tiled=True)
    val_re = planes_in[:, :, 0, None, :]
    val_im = planes_in[:, :, 1, None, :]
    spread_re = val_re * phase_cos - val_im * phase_sin
    spread_im = val_re * phase_sin + val_im * phase_cos
    rows_re = mult(spread_re, place_rows)
    rows_im = mult(spread_im, place_rows)
    wave_re = (mult(rows_re, cosine) - mult(rows_im, sine)) * turned_pot
    wave_im = (mult(rows_re, sine) + mult(rows_im, cosine)) * turned_pot
    back_re = mult(wave_re, cosine) + mult(wave_im, sine)
    back_im = mult(wave_im, cosine) - mult(wave_re, sine)
    sel_re = mult(back_re, pick_rows)
    sel_im = mult(back_im, pick_rows)
    picked_re = jnp.sum(sel_re * phase_cos + sel_im * phase_sin, axis=2)
    picked_im = jnp.sum(sel_im * phase_cos - sel_re * phase_sin, axis=2)
    picked = jnp.stack([picked_re, picked_im], axis=2)
    sticks_back = lax.all_to_all(picked, "pw", split_axis=3, concat_axis=1, tiled=True)
    vpsi = jnp.einsum("dcvu,bucs->dbsv", forward, sticks_back, precision=highest)
    applied = kinetic[None, None] * psi_block + vpsi
    lowered = applied.astype(jnp.bfloat16)
    gathered = lax.all_gather(lowered, "band", axis=1, tiled=True)
    h_re = gathered[0].reshape(gathered.shape[1], -1)
    h_im = gathered[1].reshape(gathered.shape[1], -1)
    real_part = lax.dot_general(
        h_re, all_re, dims, preferred_element_type=jnp.float32
    ) + lax.dot_general(h_im, all_im, dims, preferred_element_type=jnp.float32)
    imag_part = lax.dot_general(
        h_re, all_im, dims, preferred_element_type=jnp.float32
    ) - lax.dot_general(h_im, all_re, dims, preferred_element_type=jnp.float32)
    partials = [jnp.stack([real_part, imag_part])]
    stacked = jnp.stack(partials, axis=1)
    stacked = stacked.reshape(2, group_count, band_count, 2, stacked.shape[-1])
    partial_value = jnp.transpose(stacked, (0, 2, 1, 3, 4)).reshape(
        2, band_count * local_bands, stacked.shape[-1]
    )
    summed = lax.psum(partial_value, "pw")
    cols_dev = partial_value.shape[1] // pw_count
    intersection = lax.dynamic_slice_in_dim(summed, rank * cols_dev, cols_dev, 1)
    return (intersection, applied)


def solution(mesh):
    return jax.shard_map(
        per_device,
        mesh=mesh,
        in_specs=(
            P(None, "band", "pw", None),
            P(None, "band", "pw", None),
            P("pw", None, None),
            P(),
        ),
        out_specs=(P(None, "pw", "band"), P(None, "band", "pw", None)),
        check_vma=False,
    )
```

profile of v0, /device:TPU:0, one launch (start us, length us, event | category | flops | bytes accessed | tf_op | source)
XLA Modules:
  0.0 115.9 jit_solution(15763958665738720233)
XLA Ops:
  0.6 0.0 copy-start.6
  0.6 0.0 copy-start.2
  0.6 0.3 fusion.76
  0.9 0.3 fusion.74
  1.2 0.3 broadcast_multiply_fusion
  1.5 0.7 fusion.40
  2.2 1.2 %convolution_bitcast_fusion = f32[2,128,2,32]{1,3,0,2:T(8,128)S(1)} fusion(f32[1,2,128,128]{3,2,1,0:T(8,128)S(1)} %get-tuple-element.20, f32[1,2,128,128]{3,2,1,0:T(8,128)S(1)} %get-tuple-element.21, f32[2,2,32,128]{3,2,1,0:T(8,128)} %param.4), kind=kOutput, calls=%fused_computation.30 | convolution fusion | flops 50397184 | bytes 393216 | tf_op jit(solution)/shard_map/dcvu,cbsu->bvds/dot_general | solution.py:66
  3.4 0.2 copy.63
  3.6 0.9 reshape.230
  4.5 7.3 %all-to-all-start = ((f32[8,1,2048]{2,1,0:T(1,128)}), f32[8,1,2048]{2,1,0:T(1,128)}, u32[]{:S(2)}, u32[]{:S(2)}) async-start(f32[8,1,2048]{2,1,0:T(1,128)} %reshape.230), calls=%async_computation | async-start | bytes 131072 | tf_op jit(solution)/shard_map/all_to_all | solution.py:67
  11.8 0.0 copy-done.6
  11.8 1.2 %fusion.62 = (f32[128,256]{1,0:T(8,128)S(1)}, f32[128,256]{1,0:T(8,128)}) fusion(s32[256]{0:T(256)S(1)} %get-tuple-element.25), kind=kLoop, calls=%fused_computation.86 | loop fusion | flops 458752 | bytes 263168 | tf_op jit(solution)/shard_map/cos | solution.py:53
  13.0 0.0 copy-done.2
  13.0 1.1 multiply_bitcast_fusion
  14.1 4.3 %fusion.86 = (bf16[1,256,32,128]{3,2,1,0:T(8,128)(2,1)S(1)}, bf16[1,256,32,128]{3,2,1,0:T(8,128)(2,1)}) fusion(bf16[2,256,32,128]{3,2,1,0:T(8,128)(2,1)} %param.5), kind=kLoop, calls=%fused_computation.131 | loop fusion | bytes 8388608 | tf_op jit(solution)/shard_map/slice | solution.py:62
  18.4 1.6 %copy.66 = f32[16,128,128]{2,1,0:T(8,128)S(1)} copy(f32[16,128,128]{1,2,0:T(8,128)} %multiply_bitcast_fusion) | data formatting | bytes 2097152 | tf_op jit(solution)/shard_map/div | solution.py:57
  20.0 0.1 fusion.79
  20.1 0.0 all-to-all-done
  20.1 0.5 broadcast.384
  20.6 2.3 %reduce = f32[8,2048]{1,0:T(8,128)} reduce(f32[8,1,2048]{2,1,0:T(1,128)} %all-to-all-done, f32[]{:T(128)} %broadcast.384), dimensions={1}, to_apply=%all_to_all.26.reduce_sub_computation | reduce | bytes 131076 | tf_op jit(solution)/shard_map/all_to_all | solution.py:67
  22.8 1.8 %reshape.231 = f32[128,2,2,32]{3,2,1,0:T(2,128)} reshape(f32[8,2048]{1,0:T(8,128)} %reduce) | data formatting | bytes 131072
  24.6 1.0 copy.64
  25.6 0.8 copy.65
  26.4 1.7 %all_to_all.29 = f32[2,16,2,256]{3,1,2,0:T(8,128)} reshape(f32[2,16,2,8,32]{4,3,1,2,0:T(8,128)} %copy.65) | data formatting | bytes 131072 | tf_op jit(solution)/shard_map/all_to_all | solution.py:67
  28.1 0.0 copy-start.1
  28.1 0.8 slice_bitcast_fusion.11
  28.9 3.3 %fusion = f32[2,16,128,128]{3,2,1,0:T(8,128)S(1)} fusion(f32[128,256]{1,0:T(8,128)} %get-tuple-element.27, f32[2,16,256]{2,1,0:T(8,128)S(1)} %get-tuple-element.23, f32[128,256]{1,0:T(8,128)S(1)} %get-tuple-element.26, f32[2,16,256]{2,1,0:T(8,128)S(1)} %get-tuple-element.22, s32[256]{0:T(256)S(1)} %get-tuple-element.24), kind=kOutput, calls=%fused_computation.2 | convolution fusion | flops 1613791232 | bytes 2425856 | tf_op jit(solution)/shard_map/dot_general | solution.py:60
  32.3 0.0 copy-done.1
  32.3 2.5 %fusion.4 = f32[2,16,128,128]{3,2,1,0:T(8,128)S(1)} fusion(f32[128,256]{1,0:T(8,128)S(1)} %copy-done.1, f32[2,16,256]{2,1,0:T(8,128)S(1)} %get-tuple-element.23, f32[128,256]{1,0:T(8,128)S(1)} %get-tuple-element.26, f32[2,16,256]{2,1,0:T(8,128)S(1)} %get-tuple-element.22, s32[256]{0:T(256)S(1)} %get-tuple-element.24), kind=kOutput, calls=%fused_computation.6 | convolution fusion | flops 1613791232 | bytes 2425856 | tf_op jit(solution)/shard_map/dot_general | solution.py:60
  34.7 1.9 %fusion.72 = f32[2,16,128,128]{3,2,1,0:T(8,128)S(1)} fusion(f32[2,16,128,128]{3,2,1,0:T(8,128)S(1)} %fusion.4, f32[1,2,128,128]{3,2,1,0:T(8,128)S(1)} %get-tuple-element.20), kind=kOutput, calls=%fused_computation.96 | convolution fusion | flops 805306368 | bytes 4259840 | tf_op jit(solution)/shard_map/dot_general | solution.py:60
  36.6 1.8 %fusion.69 = f32[2,16,128,128]{3,2,1,0:T(8,128)S(1)} fusion(f32[2,16,128,128]{3,2,1,0:T(8,128)S(1)} %fusion.4, f32[1,2,128,128]{3,2,1,0:T(8,128)S(1)} %get-tuple-element.21), kind=kOutput, calls=%fused_computation.93 | convolution fusion | flops 805306368 | bytes 4259840 | tf_op jit(solution)/shard_map/dot_general | solution.py:60
  38.4 2.0 %subtract_multiply_fusion = f32[2,16,128,128]{3,2,1,0:T(8,128)S(1)} fusion(f32[2,16,128,128]{3,2,1,0:T(8,128)S(1)} %fusion.69, f32[2,16,128,128]{3,2,1,0:T(8,128)S(1)} %fusion, f32[16,128,128]{2,1,0:T(8,128)S(1)} %copy.66, f32[1,2,128,128]{3,2,1,0:T(8,128)S(1)} %get-tuple-element.20), kind=kOutput, calls=%fused_computation.17 | convolution fusion | flops 806354944 | bytes 7405568 | tf_op jit(solution)/shard_map/dot_general | solution.py:60
  40.4 1.8 %fusion.70 = f32[2,16,128,128]{3,2,1,0:T(8,128)S(1)} fusion(f32[2,16,128,128]{3,2,1,0:T(8,128)S(1)} %subtract_multiply_fusion, f32[1,2,128,128]{3,2,1,0:T(8,128)S(1)} %get-tuple-element.20), kind=kOutput, calls=%fused_computation.94 | convolution fusion | flops 805306368 | bytes 4259840 | tf_op jit(solution)/shard_map/dot_general | solution.py:60
  42.2 1.8 %fusion.68 = f32[2,16,128,128]{3,2,1,0:T(8,128)S(1)} fusion(f32[2,16,128,128]{3,2,1,0:T(8,128)S(1)} %subtract_multiply_fusion, f32[1,2,128,128]{3,2,1,0:T(8,128)S(1)} %get-tuple-element.21), kind=kOutput, calls=%fused_computation.92 | convolution fusion | flops 805306368 | bytes 4259840 | tf_op jit(solution)/shard_map/dot_general | solution.py:60
  44.0 1.9 %add_multiply_fusion = f32[2,16,128,128]{3,2,1,0:T(8,128)S(1)} fusion(f32[2,16,128,128]{3,2,1,0:T(8,128)S(1)} %fusion.72, f32[2,16,128,128]{3,2,1,0:T(8,128)S(1)} %fusion, f32[16,128,128]{2,1,0:T(8,128)S(1)} %copy.66, f32[1,2,128,128]{3,2,1,0:T(8,128)S(1)} %get-tuple-element.21), kind=kOutput, calls=%fused_computation.16 | convolution fusion | flops 806354944 | bytes 7405568 | tf_op jit(solution)/shard_map/dot_general | solution.py:60
  46.0 1.8 %fusion.67 = f32[2,16,128,128]{3,2,1,0:T(8,128)S(1)} fusion(f32[2,16,128,128]{3,2,1,0:T(8,128)S(1)} %add_multiply_fusion, f32[1,2,128,128]{3,2,1,0:T(8,128)S(1)} %get-tuple-element.21), kind=kOutput, calls=%fused_computation.91 | convolution fusion | flops 805306368 | bytes 4259840 | tf_op jit(solution)/shard_map/dot_general | solution.py:60
  47.7 1.8 %fusion.71 = f32[2,16,128,128]{3,2,1,0:T(8,128)S(1)} fusion(f32[2,16,128,128]{3,2,1,0:T(8,128)S(1)} %add_multiply_fusion, f32[1,2,128,128]{3,2,1,0:T(8,128)S(1)} %get-tuple-element.20), kind=kOutput, calls=%fused_computation.95 | convolution fusion | flops 805306368 | bytes 4259840 | tf_op jit(solution)/shard_map/dot_general | solution.py:60
  49.6 1.8 %fusion.10 = f32[2,16,128,256]{3,2,1,0:T(8,128)S(1)} fusion(f32[2,16,128,128]{3,2,1,0:T(8,128)S(1)} %fusion.68, f32[2,16,128,128]{3,2,1,0:T(8,128)S(1)} %fusion.71, s32[256]{0:T(256)S(1)} %get-tuple-element.24), kind=kOutput, calls=%fused_computation.14 | convolution fusion | flops 1611169792 | bytes 8389632 | tf_op jit(solution)/shard_map/dot_general | solution.py:60
  51.4 2.8 %add_reduce_fusion = (f32[2,16,256]{2,1,0:T(8,128)S(1)}, f32[2,16,256]{2,1,0:T(8,128)S(1)}) fusion(f32[2,16,128,256]{3,2,1,0:T(8,128)S(1)} %fusion.10, f32[128,256]{1,0:T(8,128)S(1)} %copy-done.1, f32[128,256]{1,0:T(8,128)S(1)} %get-tuple-element.26, s32[256]{0:T(256)S(1)} %get-tuple-element.24, f32[2,16,128,128]{3,2,1,0:T(8,128)S(1)} %fusion.67, ...), kind=kOutput, calls=%fused_computation.1 | convolution fusion | flops 1619542016 | bytes 8717312 | tf_op jit(solution)/shard_map/dot_general | solution.py:60
  54.2 0.0 copy-start.3
  54.2 0.0 copy-start.4
  54.2 0.0 copy-start.5
  54.2 0.3 copy.67
  54.5 1.4 %reshape.232 = f32[8,1,2048]{2,1,0:T(1,128)} reshape(f32[256,2,2,16]{3,2,1,0:T(2,128)S(1)} %bitcast.156) | data formatting | bytes 131072
  55.9 6.0 %all-to-all-start.1 = ((f32[8,1,2048]{2,1,0:T(1,128)}), f32[8,1,2048]{2,1,0:T(1,128)S(1)}, u32[]{:S(2)}, u32[]{:S(2)}) async-start(f32[8,1,2048]{2,1,0:T(1,128)} %reshape.232), calls=%async_computation.1 | async-start | bytes 131072 | tf_op jit(solution)/shard_map/all_to_all | solution.py:83
  61.9 0.1 add_multiply_fusion.1
  62.0 6.8 %all-to-all-done.1 = f32[8,1,2048]{2,1,0:T(1,128)S(1)} async-done(((f32[8,1,2048]{2,1,0:T(1,128)}), f32[8,1,2048]{2,1,0:T(1,128)S(1)}, u32[]{:S(2)}, u32[]{:S(2)}) %all-to-all-start.1) | async-done | bytes 65568 | tf_op jit(solution)/shard_map/all_to_all | solution.py:83
  68.8 0.8 reduce.1
  69.6 0.7 reshape.233
  70.3 0.3 copy.85
  70.6 0.0 copy-start
  70.6 0.0 copy-done.3
  70.7 0.0 copy-done.4
  70.7 0.0 copy-done.5
  70.7 0.6 fusion.88
  71.2 0.6 copy.75
  71.9 5.4 %all_gather.3 = bf16[2,8,32,128]{3,2,0,1:T(8,128)(2,1)S(1)} all-gather(bf16[2,2,32,128]{3,2,0,1:T(8,128)(2,1)S(1)} %get-tuple-element.28), channel_id=1, replica_groups=mesh['pw'=8,'band'=4] {'band'}, dimensions={1}, use_global_device_ids=true | all-gather | bytes 163840 | tf_op jit(solution)/shard_map/all_gather | solution.py:87
  77.3 2.3 %fusion.26 = f32[8,256]{1,0:T(8,128)S(1)} fusion(bf16[1,256,32,128]{3,2,1,0:T(8,128)(2,1)} %get-tuple-element.15, bf16[1,8,32,128]{3,2,0,1:T(8,128)(2,1)S(1)} %get-tuple-element.17), kind=kOutput, calls=%fused_computation.34 | convolution fusion | flops 16777216 | bytes 2170880 | tf_op jit(solution)/shard_map/dot_general | solution.py:93
  79.6 0.0 copy-done
  79.6 0.7 fusion.25
  80.3 0.7 fusion.30
  81.0 0.7 fusion.32
  81.7 33.7 %psum.7 = f32[2,8,256]{2,1,0:T(8,128)S(1)} all-reduce(f32[2,8,256]{2,1,0:T(8,128)S(1)} %pad_maximum_fusion.5), channel_id=1, replica_groups=mesh['pw'=8,'band'=4] {'pw'}, use_global_device_ids=true, to_apply=%region_2.3 | all-reduce | flops 4096 | bytes 32768 | tf_op jit(solution)/shard_map/psum | solution.py:102
  115.3 0.6 constant_dynamic-slice_fusion
  (5 shorter events, 0.0 us)
Async XLA Ops:
  0.6 11.2 %copy-start.6 = (s32[256]{0:T(256)S(1)}, s32[256]{0:T(256)}, u32[]{:S(2)}) copy-start(s32[256]{0:T(256)} %param.7) | copy-start | bytes 3076
  0.6 12.4 %copy-start.2 = (f32[16,128,128]{2,1,0:T(8,128)S(1)}, f32[16,128,128]{2,1,0:T(8,128)}, u32[]{:S(2)}) copy-start(f32[16,128,128]{2,1,0:T(8,128)} %param.6) | copy-start | bytes 3145732
  4.5 15.5 %all-to-all-start = ((f32[8,1,2048]{2,1,0:T(1,128)}), f32[8,1,2048]{2,1,0:T(1,128)}, u32[]{:S(2)}, u32[]{:S(2)}) async-start(f32[8,1,2048]{2,1,0:T(1,128)} %reshape.230), calls=%async_computation | async-start | bytes 131072 | tf_op jit(solution)/shard_map/all_to_all | solution.py:67
  28.1 4.2 %copy-start.1 = (f32[128,256]{1,0:T(8,128)S(1)}, f32[128,256]{1,0:T(8,128)}, u32[]{:S(2)}) copy-start(f32[128,256]{1,0:T(8,128)} %get-tuple-element.27) | copy-start | bytes 393220
  54.2 16.5 %copy-start.3 = (f32[1,2,128,128]{3,2,1,0:T(8,128)S(1)}, f32[1,2,128,128]{3,2,1,0:T(8,128)}, u32[]{:S(2)}) copy-start(f32[1,2,128,128]{3,2,1,0:T(8,128)} %get-tuple-element.18) | copy-start | bytes 393220
  54.2 16.5 %copy-start.4 = (f32[1,2,128,128]{3,2,1,0:T(8,128)S(1)}, f32[1,2,128,128]{3,2,1,0:T(8,128)}, u32[]{:S(2)}) copy-start(f32[1,2,128,128]{3,2,1,0:T(8,128)} %get-tuple-element.19) | copy-start | bytes 393220
  54.2 16.5 %copy-start.5 = (f32[2,2,32,128]{3,2,1,0:T(8,128)S(1)}, f32[2,2,32,128]{3,2,1,0:T(8,128)}, u32[]{:S(2)}) copy-start(f32[2,2,32,128]{3,2,1,0:T(8,128)} %param.4) | copy-start | bytes 196612
  55.9 12.9 %all-to-all-start.1 = ((f32[8,1,2048]{2,1,0:T(1,128)}), f32[8,1,2048]{2,1,0:T(1,128)S(1)}, u32[]{:S(2)}, u32[]{:S(2)}) async-start(f32[8,1,2048]{2,1,0:T(1,128)} %reshape.232), calls=%async_computation.1 | async-start | bytes 131072 | tf_op jit(solution)/shard_map/all_to_all | solution.py:83
  70.6 9.0 %copy-start = (bf16[1,256,32,128]{3,2,1,0:T(8,128)(2,1)S(1)}, bf16[1,256,32,128]{3,2,1,0:T(8,128)(2,1)}, u32[]{:S(2)}) copy-start(bf16[1,256,32,128]{3,2,1,0:T(8,128)(2,1)} %get-tuple-element.15) | copy-start | bytes 6291460
where the time goes:
time: 117 us; the launch traced here: 116 us
  blocking collectives  39.1 us (33%)
  matrix products  31.3 us (27%)
  local copies, waits for them, and re-layouts  17.5 us (15%)
  starting transfers between devices  13.3 us (11%)
  other arithmetic  7.07 us (6%)
  waiting for transfers between devices  6.84 us (6%)
    psum x1, blocking collectives, per_device(): summed = lax.psum(partial_value, 'pw')  33.7 us
    dot_general x12, matrix products, mult(): jnp.dot(left, right, precision=highest, preferred_element_type=jnp.float32)  25.2 us
    all_to_all x1, starting transfers between devices, per_device(): lax.all_to_all(z_lines, 'pw', split_axis=1, concat_axis=3, tiled=True)  7.28 us
    all_to_all x1, waiting for transfers between devices, per_device(): lax.all_to_all(picked, 'pw', split_axis=3, concat_axis=1, tiled=True)  6.83 us
    all_to_all x1, starting transfers between devices, per_device(): lax.all_to_all(picked, 'pw', split_axis=3, concat_axis=1, tiled=True)  5.99 us
    unnamed x19, local copies, waits for them, and re-layouts  5.42 us
    all_gather x1, blocking collectives, per_device(): gathered = lax.all_gather(lowered, 'band', axis=1, tiled=True)  5.41 us
    slice x1, local copies, waits for them, and re-layouts, per_device(): all_re = psi_all[0].reshape(psi_all.shape[1], -1)  4.29 us
  transfers between devices with their start and end apart: 2, of which 1 were waited for; matrix products, arithmetic and copies ran while one was open for 7% of the time, Pallas kernels for 0%

commit v1 on v0

--- a/solution.py
+++ b/solution.py
@@ -31,10 +31,9 @@
     local_bands = psi_block.shape[1]
     sticks_dev = psi_block.shape[2]
     grid_size = psi_block.shape[3]
-    highest = lax.Precision.HIGHEST
+    fast = lax.Precision.HIGH
     rank = lax.axis_index("pw")
     pw_count = lax.axis_size("pw")
-    band_count = lax.axis_size("band")
     my_columns = lax.dynamic_slice_in_dim(stick_col, rank * sticks_dev, sticks_dev)
     kinetic = kinetic_table(my_columns, grid_size)
     inverse = dft_table(grid_size, 1.0)
@@ -57,13 +56,9 @@
     turned_pot = (jnp.transpose(potential, (0, 2, 1)) / float(grid_size**3))[None]
 
     def mult(left, right):
-        return jnp.dot(left, right, precision=highest, preferred_element_type=jnp.float32)
+        return jnp.dot(left, right, precision=fast, preferred_element_type=jnp.float32)
 
-    all_re = psi_all[0].reshape(psi_all.shape[1], -1)
-    all_im = psi_all[1].reshape(psi_all.shape[1], -1)
-    dims = (((1,), (1,)), ((), ()))
-    group_count = local_bands // 2
-    z_lines = jnp.einsum("dcvu,cbsu->bvds", inverse, psi_block, precision=highest)
+    z_lines = jnp.einsum("dcvu,cbsu->bvds", inverse, psi_block, precision=fast)
     planes_in = lax.all_to_all(z_lines, "pw", split_axis=1, concat_axis=3, tiled=True)
     val_re = planes_in[:, :, 0, None, :]
     val_im = planes_in[:, :, 1, None, :]
@@ -81,27 +76,22 @@
     picked_im = jnp.sum(sel_im * phase_cos - sel_re * phase_sin, axis=2)
     picked = jnp.stack([picked_re, picked_im], axis=2)
     sticks_back = lax.all_to_all(picked, "pw", split_axis=3, concat_axis=1, tiled=True)
-    vpsi = jnp.einsum("dcvu,bucs->dbsv", forward, sticks_back, precision=highest)
+    vpsi = jnp.einsum("dcvu,bucs->dbsv", forward, sticks_back, precision=fast)
     applied = kinetic[None, None] * psi_block + vpsi
     lowered = applied.astype(jnp.bfloat16)
     gathered = lax.all_gather(lowered, "band", axis=1, tiled=True)
-    h_re = gathered[0].reshape(gathered.shape[1], -1)
-    h_im = gathered[1].reshape(gathered.shape[1], -1)
-    real_part = lax.dot_general(
-        h_re, all_re, dims, preferred_element_type=jnp.float32
-    ) + lax.dot_general(h_im, all_im, dims, preferred_element_type=jnp.float32)
-    imag_part = lax.dot_general(
-        h_re, all_im, dims, preferred_element_type=jnp.float32
-    ) - lax.dot_general(h_im, all_re, dims, preferred_element_type=jnp.float32)
-    partials = [jnp.stack([real_part, imag_part])]
-    stacked = jnp.stack(partials, axis=1)
-    stacked = stacked.reshape(2, group_count, band_count, 2, stacked.shape[-1])
-    partial_value = jnp.transpose(stacked, (0, 2, 1, 3, 4)).reshape(
-        2, band_count * local_bands, stacked.shape[-1]
-    )
-    summed = lax.psum(partial_value, "pw")
-    cols_dev = partial_value.shape[1] // pw_count
-    intersection = lax.dynamic_slice_in_dim(summed, rank * cols_dev, cols_dev, 1)
+    dims = (((1, 2), (1, 2)), ((), ()))
+
+    def inner(left, right):
+        return lax.dot_general(left, right, dims, preferred_element_type=jnp.float32)
+
+    real_part = inner(gathered[0], psi_all[0]) + inner(gathered[1], psi_all[1])
+    imag_part = inner(gathered[0], psi_all[1]) - inner(gathered[1], psi_all[0])
+    partial_value = jnp.stack([real_part, imag_part])
+    rows_dev = partial_value.shape[1] // pw_count
+    pieces = partial_value.reshape(2, pw_count, rows_dev, partial_value.shape[-1])
+    pieces = lax.all_to_all(pieces, "pw", split_axis=1, concat_axis=1, tiled=True)
+    intersection = jnp.sum(pieces, axis=1)
     return (intersection, applied)
 
 

time: 117 us -> 82.4 us (0.70)
  blocking collectives: 39.1 us -> 5.56 us
  matrix products: 31.3 us -> 20.8 us
  waiting for transfers between devices: 6.84 us -> 12.7 us
  starting transfers between devices: 13.3 us -> 16.6 us
    psum x1 -> x0, blocking collectives: 33.7 us -> none  [per_device(): summed = lax.psum(partial_value, 'pw')]
    dot_general x18, matrix products: 31.3 us -> 20.8 us  [the longest x12 15 us: mult(): jnp.dot(left, right, precision=fast, preferred_element_type=jnp.float32)]
    all_to_all x0 -> x1, waiting for transfers between devices: none -> 5.88 us  [per_device(): lax.all_to_all(pieces, 'pw', split_axis=1, concat_axis=1, tiled=True)]
    all_to_all x0 -> x1, starting transfers between devices: none -> 3.34 us  [per_device(): lax.all_to_all(pieces, 'pw', split_axis=1, concat_axis=1, tiled=True)]
  transfers between devices with their start and end apart: 2 -> 3, of which waited for: 1 -> 2; matrix products, arithmetic and copies ran while one was open for 7% -> 11% of each run, Pallas kernels for 0% -> 0%
where the time goes in v1:
time: 82.4 us; the launch traced here: 81.7 us
  matrix products  20.8 us (25%)
  local copies, waits for them, and re-layouts  18.1 us (22%)
  starting transfers between devices  16.6 us (20%)
  waiting for transfers between devices  12.7 us (15%)
  other arithmetic  7.07 us (9%)
  blocking collectives  5.56 us (7%)
  between operations  0.92 us (1%)
    dot_general x12, matrix products, mult(): jnp.dot(left, right, precision=fast, preferred_element_type=jnp.float32)  15 us
    all_to_all x1, starting transfers between devices, per_device(): lax.all_to_all(z_lines, 'pw', split_axis=1, concat_axis=3, tiled=True)  7.28 us
    all_to_all x1, waiting for transfers between devices, per_device(): lax.all_to_all(picked, 'pw', split_axis=3, concat_axis=1, tiled=True)  6.83 us
    all_to_all x1, starting transfers between devices, per_device(): lax.all_to_all(picked, 'pw', split_axis=3, concat_axis=1, tiled=True)  5.97 us
    all_to_all x1, waiting for transfers between devices, per_device(): lax.all_to_all(pieces, 'pw', split_axis=1, concat_axis=1, tiled=True)  5.88 us
    all_gather x1, blocking collectives, per_device(): gathered = lax.all_gather(lowered, 'band', axis=1, tiled=True)  5.56 us
    unnamed x19, local copies, waits for them, and re-layouts  5.43 us
    dot_general x4, matrix products, inner(): lax.dot_general(left, right, dims, preferred_element_type=jnp.float32)  4.35 us
  transfers between devices with their start and end apart: 3, of which 2 were waited for; matrix products, arithmetic and copies ran while one was open for 11% of the time, Pallas kernels for 0%

profile of v1, /device:TPU:0, one launch (start us, length us, event | category | flops | bytes accessed | tf_op | source)
XLA Modules:
  0.0 81.7 jit_solution(18443998476115046364)
XLA Ops:
  0.6 0.0 copy-start.6
  0.6 0.0 copy-start.2
  0.6 0.3 fusion.76
  0.9 0.3 fusion.74
  1.2 0.3 broadcast_multiply_fusion
  1.5 0.7 fusion.40
  2.2 1.1 %convolution_bitcast_fusion = f32[2,128,2,32]{1,3,0,2:T(8,128)S(1)} fusion(f32[1,2,128,128]{3,2,1,0:T(8,128)S(1)} %get-tuple-element.20, f32[1,2,128,128]{3,2,1,0:T(8,128)S(1)} %get-tuple-element.21, f32[2,2,32,128]{3,2,1,0:T(8,128)} %param.4), kind=kOutput, calls=%fused_computation.30 | convolution fusion | flops 25231360 | bytes 393216 | tf_op jit(solution)/shard_map/dcvu,cbsu->bvds/dot_general | solution.py:61
  3.3 0.2 copy.65
  3.5 0.9 %reshape.215 = f32[8,1,2048]{2,1,0:T(1,128)} reshape(f32[128,2,2,32]{3,2,1,0:T(2,128)S(1)} %bitcast.160) | data formatting | bytes 131072
  4.4 7.3 %all-to-all-start = ((f32[8,1,2048]{2,1,0:T(1,128)}), f32[8,1,2048]{2,1,0:T(1,128)}, u32[]{:S(2)}, u32[]{:S(2)}) async-start(f32[8,1,2048]{2,1,0:T(1,128)} %reshape.215), calls=%async_computation | async-start | bytes 131072 | tf_op jit(solution)/shard_map/all_to_all | solution.py:62
  11.7 0.0 copy-done.6
  11.7 1.2 %fusion.62 = (f32[128,256]{1,0:T(8,128)S(1)}, f32[128,256]{1,0:T(8,128)}) fusion(s32[256]{0:T(256)S(1)} %get-tuple-element.25), kind=kLoop, calls=%fused_computation.86 | loop fusion | flops 458752 | bytes 263168 | tf_op jit(solution)/shard_map/cos | solution.py:52
  12.9 0.0 copy-done.2
  12.9 1.1 %multiply_bitcast_fusion = f32[16,128,128]{1,2,0:T(8,128)} fusion(f32[16,128,128]{2,1,0:T(8,128)S(1)} %copy-done.2), kind=kLoop, calls=%fused_computation.41 | loop fusion | flops 262144 | bytes 2097152 | tf_op jit(solution)/shard_map/div | solution.py:56
  14.0 4.3 %fusion.86 = (bf16[1,256,32,128]{3,2,1,0:T(8,128)(2,1)S(1)}, bf16[1,256,32,128]{3,2,1,0:T(8,128)(2,1)}) fusion(bf16[2,256,32,128]{3,2,1,0:T(8,128)(2,1)} %param.5), kind=kLoop, calls=%fused_computation.130 | loop fusion | bytes 8388608 | tf_op jit(solution)/shard_map/slice | solution.py:88
  18.3 1.6 %copy.68 = f32[16,128,128]{2,1,0:T(8,128)S(1)} copy(f32[16,128,128]{1,2,0:T(8,128)} %multiply_bitcast_fusion) | data formatting | bytes 2097152 | tf_op jit(solution)/shard_map/div | solution.py:56
  19.8 0.1 fusion.79
  19.9 0.0 all-to-all-done
  19.9 0.5 broadcast.384
  20.5 2.3 %reduce.1 = f32[8,2048]{1,0:T(8,128)} reduce(f32[8,1,2048]{2,1,0:T(1,128)} %all-to-all-done, f32[]{:T(128)} %broadcast.384), dimensions={1}, to_apply=%all_to_all.29.reduce_sub_computation | reduce | bytes 131076 | tf_op jit(solution)/shard_map/all_to_all | solution.py:62
  22.7 1.8 %reshape.216 = f32[128,2,2,32]{3,2,1,0:T(2,128)} reshape(f32[8,2048]{1,0:T(8,128)} %reduce.1) | data formatting | bytes 131072
  24.5 1.0 %copy.66 = f32[2,128,2,32]{3,1,2,0:T(8,128)S(1)} copy(f32[2,128,2,32]{3,0,2,1:T(2,128)} %bitcast.161) | data formatting | bytes 131072 | tf_op jit(solution)/shard_map/all_to_all | solution.py:62
  25.5 0.8 copy.67
  26.3 1.7 %all_to_all.32 = f32[2,16,2,256]{3,1,2,0:T(8,128)} reshape(f32[2,16,2,8,32]{4,3,1,2,0:T(8,128)} %copy.67) | data formatting | bytes 131072 | tf_op jit(solution)/shard_map/all_to_all | solution.py:62
  28.0 0.8 slice_bitcast_fusion.11
  28.8 2.2 %fusion = f32[2,16,128,128]{3,2,1,0:T(8,128)S(1)} fusion(f32[128,256]{1,0:T(8,128)} %get-tuple-element.27, f32[2,16,256]{2,1,0:T(8,128)S(1)} %get-tuple-element.23, f32[128,256]{1,0:T(8,128)S(1)} %get-tuple-element.26, f32[2,16,256]{2,1,0:T(8,128)S(1)} %get-tuple-element.22, s32[256]{0:T(256)S(1)} %get-tuple-element.24), kind=kOutput, calls=%fused_computation.2 | convolution fusion | flops 808484864 | bytes 2425856 | tf_op jit(solution)/shard_map/dot_general | solution.py:59
  31.0 0.0 copy-done.1
  31.0 1.3 %fusion.4 = f32[2,16,128,128]{3,2,1,0:T(8,128)S(1)} fusion(f32[128,256]{1,0:T(8,128)S(1)} %copy-done.1, f32[2,16,256]{2,1,0:T(8,128)S(1)} %get-tuple-element.23, f32[128,256]{1,0:T(8,128)S(1)} %get-tuple-element.26, f32[2,16,256]{2,1,0:T(8,128)S(1)} %get-tuple-element.22, s32[256]{0:T(256)S(1)} %get-tuple-element.24), kind=kOutput, calls=%fused_computation.6 | convolution fusion | flops 808484864 | bytes 2425856 | tf_op jit(solution)/shard_map/dot_general | solution.py:59
  32.4 1.0 %fusion.72 = f32[2,16,128,128]{3,2,1,0:T(8,128)S(1)} fusion(f32[2,16,128,128]{3,2,1,0:T(8,128)S(1)} %fusion.4, f32[1,2,128,128]{3,2,1,0:T(8,128)S(1)} %get-tuple-element.20), kind=kOutput, calls=%fused_computation.96 | convolution fusion | flops 402653184 | bytes 4259840 | tf_op jit(solution)/shard_map/dot_general | solution.py:59
  33.4 1.0 %fusion.69 = f32[2,16,128,128]{3,2,1,0:T(8,128)S(1)} fusion(f32[2,16,128,128]{3,2,1,0:T(8,128)S(1)} %fusion.4, f32[1,2,128,128]{3,2,1,0:T(8,128)S(1)} %get-tuple-element.21), kind=kOutput, calls=%fused_computation.93 | convolution fusion | flops 402653184 | bytes 4259840 | tf_op jit(solution)/shard_map/dot_general | solution.py:59
  34.4 1.0 %subtract_multiply_fusion = f32[2,16,128,128]{3,2,1,0:T(8,128)S(1)} fusion(f32[2,16,128,128]{3,2,1,0:T(8,128)S(1)} %fusion.69, f32[2,16,128,128]{3,2,1,0:T(8,128)S(1)} %fusion, f32[16,128,128]{2,1,0:T(8,128)S(1)} %copy.68, f32[1,2,128,128]{3,2,1,0:T(8,128)S(1)} %get-tuple-element.20), kind=kOutput, calls=%fused_computation.17 | convolution fusion | flops 403701760 | bytes 7405568 | tf_op jit(solution)/shard_map/dot_general | solution.py:59
  35.4 1.0 %fusion.70 = f32[2,16,128,128]{3,2,1,0:T(8,128)S(1)} fusion(f32[2,16,128,128]{3,2,1,0:T(8,128)S(1)} %subtract_multiply_fusion, f32[1,2,128,128]{3,2,1,0:T(8,128)S(1)} %get-tuple-element.20), kind=kOutput, calls=%fused_computation.94 | convolution fusion | flops 402653184 | bytes 4259840 | tf_op jit(solution)/shard_map/dot_general | solution.py:59
  36.4 1.0 %fusion.68 = f32[2,16,128,128]{3,2,1,0:T(8,128)S(1)} fusion(f32[2,16,128,128]{3,2,1,0:T(8,128)S(1)} %subtract_multiply_fusion, f32[1,2,128,128]{3,2,1,0:T(8,128)S(1)} %get-tuple-element.21), kind=kOutput, calls=%fused_computation.92 | convolution fusion | flops 402653184 | bytes 4259840 | tf_op jit(solution)/shard_map/dot_general | solution.py:59
  37.4 1.1 %add_multiply_fusion = f32[2,16,128,128]{3,2,1,0:T(8,128)S(1)} fusion(f32[2,16,128,128]{3,2,1,0:T(8,128)S(1)} %fusion.72, f32[2,16,128,128]{3,2,1,0:T(8,128)S(1)} %fusion, f32[16,128,128]{2,1,0:T(8,128)S(1)} %copy.68, f32[1,2,128,128]{3,2,1,0:T(8,128)S(1)} %get-tuple-element.21), kind=kOutput, calls=%fused_computation.16 | convolution fusion | flops 403701760 | bytes 7405568 | tf_op jit(solution)/shard_map/dot_general | solution.py:59
  38.5 1.0 %fusion.67 = f32[2,16,128,128]{3,2,1,0:T(8,128)S(1)} fusion(f32[2,16,128,128]{3,2,1,0:T(8,128)S(1)} %add_multiply_fusion, f32[1,2,128,128]{3,2,1,0:T(8,128)S(1)} %get-tuple-element.21), kind=kOutput, calls=%fused_computation.91 | convolution fusion | flops 402653184 | bytes 4259840 | tf_op jit(solution)/shard_map/dot_general | solution.py:59
  39.5 1.2 %fusion.71 = f32[2,16,128,128]{3,2,1,0:T(8,128)S(1)} fusion(f32[2,16,128,128]{3,2,1,0:T(8,128)S(1)} %add_multiply_fusion, f32[1,2,128,128]{3,2,1,0:T(8,128)S(1)} %get-tuple-element.20), kind=kOutput, calls=%fused_computation.95 | convolution fusion | flops 402653184 | bytes 4259840 | tf_op jit(solution)/shard_map/dot_general | solution.py:59
  40.7 1.3 %fusion.10 = f32[2,16,128,256]{3,2,1,0:T(8,128)S(1)} fusion(f32[2,16,128,128]{3,2,1,0:T(8,128)S(1)} %fusion.68, f32[2,16,128,128]{3,2,1,0:T(8,128)S(1)} %fusion.71, s32[256]{0:T(256)S(1)} %get-tuple-element.24), kind=kOutput, calls=%fused_computation.14 | convolution fusion | flops 805863424 | bytes 8389632 | tf_op jit(solution)/shard_map/dot_general | solution.py:59
  41.9 1.9 %add_reduce_fusion = (f32[2,16,256]{2,1,0:T(8,128)S(1)}, f32[2,16,256]{2,1,0:T(8,128)S(1)}) fusion(f32[2,16,128,256]{3,2,1,0:T(8,128)S(1)} %fusion.10, f32[128,256]{1,0:T(8,128)S(1)} %copy-done.1, f32[128,256]{1,0:T(8,128)S(1)} %get-tuple-element.26, s32[256]{0:T(256)S(1)} %get-tuple-element.24, f32[2,16,128,128]{3,2,1,0:T(8,128)S(1)} %fusion.67, ...), kind=kOutput, calls=%fused_computation.1 | convolution fusion | flops 814235648 | bytes 8717312 | tf_op jit(solution)/shard_map/dot_general | solution.py:59
  43.9 0.0 copy-start.3
  43.9 0.0 copy-start.4
  43.9 0.0 copy-start.5
  43.9 0.3 copy.69
  44.2 1.4 %reshape.217 = f32[8,1,2048]{2,1,0:T(1,128)} reshape(f32[256,2,2,16]{3,2,1,0:T(2,128)S(1)} %bitcast.158) | data formatting | bytes 131072
  45.6 6.0 %all-to-all-start.1 = ((f32[8,1,2048]{2,1,0:T(1,128)}), f32[8,1,2048]{2,1,0:T(1,128)S(1)}, u32[]{:S(2)}, u32[]{:S(2)}) async-start(f32[8,1,2048]{2,1,0:T(1,128)} %reshape.217), calls=%async_computation.1 | async-start | bytes 131072 | tf_op jit(solution)/shard_map/all_to_all | solution.py:78
  51.6 0.1 add_multiply_fusion.1
  51.7 6.8 %all-to-all-done.1 = f32[8,1,2048]{2,1,0:T(1,128)S(1)} async-done(((f32[8,1,2048]{2,1,0:T(1,128)}), f32[8,1,2048]{2,1,0:T(1,128)S(1)}, u32[]{:S(2)}, u32[]{:S(2)}) %all-to-all-start.1) | async-done | bytes 65568 | tf_op jit(solution)/shard_map/all_to_all | solution.py:78
  58.5 0.8 reduce.2
  59.3 0.7 reshape.218
  60.0 0.3 copy.88
  60.3 0.0 copy-start
  60.3 0.0 copy-done.3
  60.3 0.0 copy-done.4
  60.3 0.0 copy-done.5
  60.4 0.4 fusion.88
  60.7 5.6 %all_gather.3 = bf16[2,8,32,128]{3,2,0,1:T(8,128)(2,1)S(1)} all-gather(bf16[2,2,32,128]{3,2,0,1:T(8,128)(2,1)S(1)} %get-tuple-element.28), channel_id=1, replica_groups=mesh['pw'=8,'band'=4] {'band'}, dimensions={1}, use_global_device_ids=true | all-gather | bytes 163840 | tf_op jit(solution)/shard_map/all_gather | solution.py:82
  66.3 2.3 %fusion.26 = f32[8,256]{1,0:T(8,128)S(1)} fusion(bf16[1,256,32,128]{3,2,1,0:T(8,128)(2,1)} %get-tuple-element.15, bf16[1,8,32,128]{3,2,0,1:T(8,128)(2,1)S(1)} %get-tuple-element.17), kind=kOutput, calls=%fused_computation.34 | convolution fusion | flops 16777216 | bytes 2170880 | tf_op jit(solution)/shard_map/dot_general | solution.py:86
  68.6 0.7 fusion.25
  69.3 0.7 fusion.30
  70.0 0.7 fusion.32
  70.7 0.6 copy.77
  71.3 3.3 %all-to-all-start.2 = ((f32[2,8,1,256]{3,0,2,1:T(2,128)}), f32[2,8,1,256]{3,0,2,1:T(2,128)S(1)}, u32[]{:S(2)}, u32[]{:S(2)}) async-start(f32[2,8,1,256]{3,0,2,1:T(2,128)} %copy.77), calls=%async_computation.2 | async-start | bytes 32768 | tf_op jit(solution)/shard_map/all_to_all | solution.py:93
  74.6 0.6 copy.78
  75.3 5.9 %all-to-all-done.2 = f32[2,8,1,256]{3,0,2,1:T(2,128)S(1)} async-done(((f32[2,8,1,256]{3,0,2,1:T(2,128)}), f32[2,8,1,256]{3,0,2,1:T(2,128)S(1)}, u32[]{:S(2)}, u32[]{:S(2)}) %all-to-all-start.2) | async-done | bytes 16416 | tf_op jit(solution)/shard_map/all_to_all | solution.py:93
  81.2 0.6 reduce_sum.32
  (8 shorter events, 0.1 us)
Async XLA Ops:
  0.6 11.1 %copy-start.6 = (s32[256]{0:T(256)S(1)}, s32[256]{0:T(256)}, u32[]{:S(2)}) copy-start(s32[256]{0:T(256)} %param.7) | copy-start | bytes 3076
  0.6 12.3 %copy-start.2 = (f32[16,128,128]{2,1,0:T(8,128)S(1)}, f32[16,128,128]{2,1,0:T(8,128)}, u32[]{:S(2)}) copy-start(f32[16,128,128]{2,1,0:T(8,128)} %param.6) | copy-start | bytes 3145732
  4.4 15.5 %all-to-all-start = ((f32[8,1,2048]{2,1,0:T(1,128)}), f32[8,1,2048]{2,1,0:T(1,128)}, u32[]{:S(2)}, u32[]{:S(2)}) async-start(f32[8,1,2048]{2,1,0:T(1,128)} %reshape.215), calls=%async_computation | async-start | bytes 131072 | tf_op jit(solution)/shard_map/all_to_all | solution.py:62
  28.0 3.1 %copy-start.1 = (f32[128,256]{1,0:T(8,128)S(1)}, f32[128,256]{1,0:T(8,128)}, u32[]{:S(2)}) copy-start(f32[128,256]{1,0:T(8,128)} %get-tuple-element.27) | copy-start | bytes 393220
  43.9 16.5 %copy-start.3 = (f32[1,2,128,128]{3,2,1,0:T(8,128)S(1)}, f32[1,2,128,128]{3,2,1,0:T(8,128)}, u32[]{:S(2)}) copy-start(f32[1,2,128,128]{3,2,1,0:T(8,128)} %get-tuple-element.18) | copy-start | bytes 393220
  43.9 16.5 %copy-start.4 = (f32[1,2,128,128]{3,2,1,0:T(8,128)S(1)}, f32[1,2,128,128]{3,2,1,0:T(8,128)}, u32[]{:S(2)}) copy-start(f32[1,2,128,128]{3,2,1,0:T(8,128)} %get-tuple-element.19) | copy-start | bytes 393220
  43.9 16.5 %copy-start.5 = (f32[2,2,32,128]{3,2,1,0:T(8,128)S(1)}, f32[2,2,32,128]{3,2,1,0:T(8,128)}, u32[]{:S(2)}) copy-start(f32[2,2,32,128]{3,2,1,0:T(8,128)} %param.4) | copy-start | bytes 196612
  45.6 12.9 %all-to-all-start.1 = ((f32[8,1,2048]{2,1,0:T(1,128)}), f32[8,1,2048]{2,1,0:T(1,128)S(1)}, u32[]{:S(2)}, u32[]{:S(2)}) async-start(f32[8,1,2048]{2,1,0:T(1,128)} %reshape.217), calls=%async_computation.1 | async-start | bytes 131072 | tf_op jit(solution)/shard_map/all_to_all | solution.py:78
  60.3 8.3 %copy-start = (bf16[1,256,32,128]{3,2,1,0:T(8,128)(2,1)S(1)}, bf16[1,256,32,128]{3,2,1,0:T(8,128)(2,1)}, u32[]{:S(2)}) copy-start(bf16[1,256,32,128]{3,2,1,0:T(8,128)(2,1)} %get-tuple-element.15) | copy-start | bytes 6291460
  71.3 9.9 %all-to-all-start.2 = ((f32[2,8,1,256]{3,0,2,1:T(2,128)}), f32[2,8,1,256]{3,0,2,1:T(2,128)S(1)}, u32[]{:S(2)}, u32[]{:S(2)}) async-start(f32[2,8,1,256]{3,0,2,1:T(2,128)} %copy.77), calls=%async_computation.2 | async-start | bytes 32768 | tf_op jit(solution)/shard_map/all_to_all | solution.py:93

commit v2 on v1

v2 whole, which is shorter than its diff:
```python
import math

import jax
import jax.numpy as jnp
from jax import lax
from jax.sharding import PartitionSpec as P


def frequency(index, size):
    return jnp.where(index < size // 2, index, index - size)


def kinetic_table(columns, grid_size):
    col_x = frequency(columns // grid_size, grid_size).astype(jnp.float32)
    col_y = frequency(columns % grid_size, grid_size).astype(jnp.float32)
    along = frequency(jnp.arange(grid_size, dtype=jnp.int32), grid_size).astype(jnp.float32)
    plane = col_x * col_x + col_y * col_y
    return 4.0 * (plane[:, None] + along[None, :] * along[None, :]) / float(grid_size * grid_size)


def dft_table(grid_size, sign):
    indices = jnp.arange(grid_size, dtype=jnp.int32)
    products = indices[:, None] * indices[None, :] % grid_size
    angles = 2.0 * math.pi / grid_size * products.astype(jnp.float32)
    cosine = jnp.cos(angles)
    sine = sign * jnp.sin(angles)
    return jnp.stack([jnp.stack([cosine, -sine]), jnp.stack([sine, cosine])])


def per_device(psi_block, psi_all, potential, stick_col):
    sticks_dev = psi_block.shape[2]
    grid_size = psi_block.shape[3]
    fast = lax.Precision.HIGH
    rank = lax.axis_index("pw")
    pw_count = lax.axis_size("pw")
    planes = potential.shape[0]
    my_columns = lax.dynamic_slice_in_dim(stick_col, rank * sticks_dev, sticks_dev)
    kinetic = kinetic_table(my_columns, grid_size)
    inverse = dft_table(grid_size, 1.0)
    forward = dft_table(grid_size, -1.0)
    cosine = inverse[0, 0]
    sine = inverse[1, 0]
    grid_iota = jnp.arange(grid_size, dtype=jnp.int32)
    col_x = stick_col // grid_size
    col_y = stick_col % grid_size
    phase_angles = (
        2.0
        * math.pi
        / grid_size
        * (grid_iota[:, None] * col_x[None, :] % grid_size).astype(jnp.float32)
    )
    phase_cos = jnp.cos(phase_angles)
    phase_sin = jnp.sin(phase_angles)
    place_cols = (col_y[:, None] == grid_iota[None, :]).astype(jnp.float32)
    pick_cols = (grid_iota[:, None] == col_y[None, :]).astype(jnp.float32)
    scaled_pot = (potential / float(grid_size**3))[None]

    def mult(left, right):
        return jnp.dot(left, right, precision=fast, preferred_element_type=jnp.float32)

    z_lines = jnp.einsum("dczk,cbsk->zdbs", inverse, psi_block, precision=fast)
    received = lax.all_to_all(z_lines, "pw", split_axis=0, concat_axis=0, tiled=True)
    lanes = received.shape[1:]
    received = received.reshape((pw_count, planes) + lanes)
    amp = jnp.transpose(received, (2, 3, 1, 0, 4)).reshape(
        lanes[0], lanes[1], planes, pw_count * sticks_dev
    )
    val_re = amp[0][:, :, None, :]
    val_im = amp[1][:, :, None, :]
    spread_re = val_re * phase_cos - val_im * phase_sin
    spread_im = val_re * phase_sin + val_im * phase_cos
    rows_re = mult(spread_re, place_cols)
    rows_im = mult(spread_im, place_cols)
    wave_re = (mult(rows_re, cosine) - mult(rows_im, sine)) * scaled_pot
    wave_im = (mult(rows_re, sine) + mult(rows_im, cosine)) * scaled_pot
    back_re = mult(wave_re, cosine) + mult(wave_im, sine)
    back_im = mult(wave_im, cosine) - mult(wave_re, sine)
    sel_re = mult(back_re, pick_cols)
    sel_im = mult(back_im, pick_cols)
    picked_re = jnp.sum(sel_re * phase_cos + sel_im * phase_sin, axis=2)
    picked_im = jnp.sum(sel_im * phase_cos - sel_re * phase_sin, axis=2)
    picked = jnp.stack([picked_re, picked_im])
    outgoing = picked.reshape(lanes[0], lanes[1], planes, pw_count, sticks_dev)
    outgoing = jnp.transpose(outgoing, (3, 2, 0, 1, 4)).reshape((pw_count * planes,) + lanes)
    sticks_back = lax.all_to_all(outgoing, "pw", split_axis=0, concat_axis=0, tiled=True)
    vpsi = jnp.einsum("dckz,zcbs->dbsk", forward, sticks_back, precision=fast)
    applied = kinetic[None, None] * psi_block + vpsi
    lowered = applied.astype(jnp.bfloat16)
    gathered = lax.all_gather(lowered, "band", axis=1, tiled=True)
    turned = jnp.stack([-gathered[1], gathered[0]])
    both = jnp.concatenate([gathered, turned], axis=1)
    dims = (((0, 2, 3), (0, 2, 3)), ((), ()))
    partial_value = lax.dot_general(both, psi_all, dims, preferred_element_type=jnp.float32)
    partial_value = partial_value.reshape(2, gathered.shape[1], partial_value.shape[-1])
    rows_dev = partial_value.shape[1] // pw_count
    pieces = partial_value.reshape(2, pw_count, rows_dev, partial_value.shape[-1])
    pieces = lax.all_to_all(pieces, "pw", split_axis=1, concat_axis=1, tiled=True)
    intersection = jnp.sum(pieces, axis=1)
    return (intersection, applied)


def solution(mesh):
    return jax.shard_map(
        per_device,
        mesh=mesh,
        in_specs=(
            P(None, "band", "pw", None),
            P(None, "band", "pw", None),
            P("pw", None, None),
            P(),
        ),
        out_specs=(P(None, "pw", "band"), P(None, "band", "pw", None)),
        check_vma=False,
    )
```

time: 82.4 us -> 68.8 us (0.83)
  local copies, waits for them, and re-layouts: 18.1 us -> 5.69 us
  waiting for transfers between devices: 12.7 us -> 18.8 us
  other arithmetic: 7.07 us -> 3.29 us
  starting transfers between devices: 16.6 us -> 13.9 us
    all_to_all x2, waiting for transfers between devices: 6.84 us -> 12.9 us  [the longest x1 6.77 us: per_device(): lax.all_to_all(outgoing, 'pw', split_axis=0, concat_axis=0, tiled=True)]
    slice x2 -> x3, local copies, waits for them, and re-layouts: 4.29 us -> 0.11 us  [the longest x2 0.06 us: per_device(): val_re = amp[0][:, :, None, :]]
    all_to_all x5 -> x3, local copies, waits for them, and re-layouts: 4.28 us -> 0.55 us  [the longest x2 0.53 us: per_device(): lax.all_to_all(z_lines, 'pw', split_axis=0, concat_axis=0, tiled=True)]
    all_to_all x2, starting transfers between devices: 13.3 us -> 10.6 us  [the longest x1 7.28 us: per_device(): lax.all_to_all(z_lines, 'pw', split_axis=0, concat_axis=0, tiled=True)]
    unnamed x19 -> x11, local copies, waits for them, and re-layouts: 5.43 us -> 2.94 us
    div x1 -> x0, local copies, waits for them, and re-layouts: 1.55 us -> none  [per_device(): jnp.transpose(potential, (0, 2, 1)) / float(grid_size ** 3)]
    all_to_all x2, other arithmetic: 3.06 us -> 1.6 us  [the longest x1 0.8 us: per_device(): lax.all_to_all(outgoing, 'pw', split_axis=0, concat_axis=0, tiled=True)]
    div x1, other arithmetic: 1.06 us -> 0.08 us  [per_device(): scaled_pot = (potential / float(grid_size ** 3))[None]]
  transfers between devices with their start and end apart: 3 -> 3, of which waited for: 2 -> 3; matrix products, arithmetic and copies ran while one was open for 11% -> 2% of each run, Pallas kernels for 0% -> 0%
where the time goes in v2:
time: 68.8 us; the launch traced here: 68.4 us
  matrix products  20.3 us (30%)
  waiting for transfers between devices  18.8 us (27%)
  starting transfers between devices  13.9 us (20%)
  local copies, waits for them, and re-layouts  5.69 us (8%)
  blocking collectives  5.43 us (8%)
  other arithmetic  3.29 us (5%)
  between operations  0.97 us (1%)
    dot_general x12, matrix products, mult(): jnp.dot(left, right, precision=fast, preferred_element_type=jnp.float32)  14.5 us
    all_to_all x1, starting transfers between devices, per_device(): lax.all_to_all(z_lines, 'pw', split_axis=0, concat_axis=0, tiled=True)  7.28 us
    all_to_all x1, waiting for transfers between devices, per_device(): lax.all_to_all(outgoing, 'pw', split_axis=0, concat_axis=0, tiled=True)  6.77 us
    all_to_all x1, waiting for transfers between devices, per_device(): lax.all_to_all(z_lines, 'pw', split_axis=0, concat_axis=0, tiled=True)  6.14 us
    all_to_all x1, waiting for transfers between devices, per_device(): lax.all_to_all(pieces, 'pw', split_axis=1, concat_axis=1, tiled=True)  5.88 us
    all_gather x1, blocking collectives, per_device(): gathered = lax.all_gather(lowered, 'band', axis=1, tiled=True)  5.43 us
    dot_general x1, matrix products, per_device(): lax.dot_general(both, psi_all, dims, preferred_element_type=jnp.float32)  4.32 us
    all_to_all x1, starting transfers between devices, per_device(): lax.all_to_all(outgoing, 'pw', split_axis=0, concat_axis=0, tiled=True)  3.35 us
  transfers between devices with their start and end apart: 3, of which 3 were waited for; matrix products, arithmetic and copies ran while one was open for 2% of the time, Pallas kernels for 0%

profile of v2, /device:TPU:0, one launch (start us, length us, event | category | flops | bytes accessed | tf_op | source)
XLA Modules:
  0.0 68.4 jit_solution(11531831070499861507)
XLA Ops:
  0.6 0.0 copy-start.2
  0.6 0.0 copy-start
  0.6 0.3 fusion.75
  0.9 0.3 fusion.73
  1.2 0.3 broadcast_multiply_fusion.1
  1.5 1.1 %convolution_bitcast_fusion = f32[128,2,2,32]{0,3,2,1:T(8,128)S(1)} fusion(f32[1,2,128,128]{3,2,1,0:T(8,128)S(1)} %get-tuple-element.17, f32[1,2,128,128]{3,2,1,0:T(8,128)S(1)} %get-tuple-element.14, f32[2,2,32,128]{3,2,1,0:T(8,128)} %param.4), kind=kOutput, calls=%fused_computation.26 | convolution fusion | flops 25231360 | bytes 393216 | tf_op jit(solution)/shard_map/dczk,cbsk->zdbs/dot_general | solution.py:61
  2.6 0.2 copy.23
  2.8 0.9 %reshape.228 = f32[8,1,2048]{2,1,0:T(1,128)} reshape(f32[128,2,2,32]{3,2,1,0:T(2,128)S(1)} %copy.23) | data formatting | bytes 131072
  3.7 7.3 %all-to-all-start = ((f32[8,1,2048]{2,1,0:T(1,128)}), f32[8,1,2048]{2,1,0:T(1,128)S(1)}, u32[]{:S(2)}, u32[]{:S(2)}) async-start(f32[8,1,2048]{2,1,0:T(1,128)} %reshape.228), calls=%async_computation | async-start | bytes 131072 | tf_op jit(solution)/shard_map/all_to_all | solution.py:62
  11.0 0.0 copy-done.2
  11.0 0.5 fusion.61
  11.6 0.0 copy-done
  11.6 0.1 broadcast_multiply_fusion
  11.7 0.1 fusion.78
  11.8 6.1 %all-to-all-done = f32[8,1,2048]{2,1,0:T(1,128)S(1)} async-done(((f32[8,1,2048]{2,1,0:T(1,128)}), f32[8,1,2048]{2,1,0:T(1,128)S(1)}, u32[]{:S(2)}, u32[]{:S(2)}) %all-to-all-start) | async-done | bytes 65568 | tf_op jit(solution)/shard_map/all_to_all | solution.py:62
  17.9 0.5 broadcast.382
  18.4 0.8 %reduce.1 = f32[8,2048]{1,0:T(8,128)S(1)} reduce(f32[8,1,2048]{2,1,0:T(1,128)S(1)} %all-to-all-done, f32[]{:T(128)} %broadcast.382), dimensions={1}, to_apply=%all_to_all.9.reduce_sub_computation | reduce | bytes 131076 | tf_op jit(solution)/shard_map/all_to_all | solution.py:62
  19.2 0.2 reshape.229
  19.6 0.1 mul.304
  19.7 0.1 mul.313
  19.8 1.3 %fusion.2 = f32[2,16,128,128]{3,2,1,0:T(8,128)S(1)} fusion(f32[128,256]{1,0:T(8,128)S(1)} %get-tuple-element.21, f32[2,16,256]{2,1,0:T(8,128)S(1)} %mul.313, f32[128,256]{1,0:T(8,128)S(1)} %get-tuple-element.20, f32[2,16,256]{2,1,0:T(8,128)S(1)} %mul.304, s32[256]{0:T(256)S(1)} %get-tuple-element.18), kind=kOutput, calls=%fused_computation.4 | convolution fusion | flops 808484864 | bytes 2425856 | tf_op jit(solution)/shard_map/dot_general | solution.py:59
  21.2 1.3 %fusion.6 = f32[2,16,128,128]{3,2,1,0:T(8,128)S(1)} fusion(f32[128,256]{1,0:T(8,128)S(1)} %get-tuple-element.21, f32[2,16,256]{2,1,0:T(8,128)S(1)} %mul.313, f32[128,256]{1,0:T(8,128)S(1)} %get-tuple-element.20, f32[2,16,256]{2,1,0:T(8,128)S(1)} %mul.304, s32[256]{0:T(256)S(1)} %get-tuple-element.18), kind=kOutput, calls=%fused_computation.8 | convolution fusion | flops 808484864 | bytes 2425856 | tf_op jit(solution)/shard_map/dot_general | solution.py:59
  22.5 1.0 %fusion.71 = f32[2,16,128,128]{3,2,1,0:T(8,128)S(1)} fusion(f32[2,16,128,128]{3,2,1,0:T(8,128)S(1)} %fusion.6, f32[1,2,128,128]{3,2,1,0:T(8,128)S(1)} %get-tuple-element.17), kind=kOutput, calls=%fused_computation.90 | convolution fusion | flops 402653184 | bytes 4259840 | tf_op jit(solution)/shard_map/dot_general | solution.py:59
  23.5 1.0 %fusion.68 = f32[2,16,128,128]{3,2,1,0:T(8,128)S(1)} fusion(f32[2,16,128,128]{3,2,1,0:T(8,128)S(1)} %fusion.6, f32[1,2,128,128]{3,2,1,0:T(8,128)S(1)} %get-tuple-element.14), kind=kOutput, calls=%fused_computation.87 | convolution fusion | flops 402653184 | bytes 4259840 | tf_op jit(solution)/shard_map/dot_general | solution.py:59
  24.5 1.1 %subtract_multiply_fusion = f32[2,16,128,128]{3,2,1,0:T(8,128)S(1)} fusion(f32[2,16,128,128]{3,2,1,0:T(8,128)S(1)} %fusion.68, f32[2,16,128,128]{3,2,1,0:T(8,128)S(1)} %fusion.2, f32[16,128,128]{2,1,0:T(8,128)S(1)} %broadcast_multiply_fusion, f32[1,2,128,128]{3,2,1,0:T(8,128)S(1)} %get-tuple-element.17), kind=kOutput, calls=%fused_computation.17 | convolution fusion | flops 403701760 | bytes 7405568 | tf_op jit(solution)/shard_map/dot_general | solution.py:59
  25.7 1.0 %fusion.69 = f32[2,16,128,128]{3,2,1,0:T(8,128)S(1)} fusion(f32[2,16,128,128]{3,2,1,0:T(8,128)S(1)} %subtract_multiply_fusion, f32[1,2,128,128]{3,2,1,0:T(8,128)S(1)} %get-tuple-element.17), kind=kOutput, calls=%fused_computation.88 | convolution fusion | flops 402653184 | bytes 4259840 | tf_op jit(solution)/shard_map/dot_general | solution.py:59
  26.7 1.0 %fusion.67 = f32[2,16,128,128]{3,2,1,0:T(8,128)S(1)} fusion(f32[2,16,128,128]{3,2,1,0:T(8,128)S(1)} %subtract_multiply_fusion, f32[1,2,128,128]{3,2,1,0:T(8,128)S(1)} %get-tuple-element.14), kind=kOutput, calls=%fused_computation.86 | convolution fusion | flops 402653184 | bytes 4259840 | tf_op jit(solution)/shard_map/dot_general | solution.py:59
  27.7 1.1 %add_multiply_fusion = f32[2,16,128,128]{3,2,1,0:T(8,128)S(1)} fusion(f32[2,16,128,128]{3,2,1,0:T(8,128)S(1)} %fusion.71, f32[2,16,128,128]{3,2,1,0:T(8,128)S(1)} %fusion.2, f32[16,128,128]{2,1,0:T(8,128)S(1)} %broadcast_multiply_fusion, f32[1,2,128,128]{3,2,1,0:T(8,128)S(1)} %get-tuple-element.14), kind=kOutput, calls=%fused_computation.16 | convolution fusion | flops 403701760 | bytes 7405568 | tf_op jit(solution)/shard_map/dot_general | solution.py:59
  28.8 1.0 %fusion.66 = f32[2,16,128,128]{3,2,1,0:T(8,128)S(1)} fusion(f32[2,16,128,128]{3,2,1,0:T(8,128)S(1)} %add_multiply_fusion, f32[1,2,128,128]{3,2,1,0:T(8,128)S(1)} %get-tuple-element.14), kind=kOutput, calls=%fused_computation.85 | convolution fusion | flops 402653184 | bytes 4259840 | tf_op jit(solution)/shard_map/dot_general | solution.py:59
  29.8 1.0 %fusion.70 = f32[2,16,128,128]{3,2,1,0:T(8,128)S(1)} fusion(f32[2,16,128,128]{3,2,1,0:T(8,128)S(1)} %add_multiply_fusion, f32[1,2,128,128]{3,2,1,0:T(8,128)S(1)} %get-tuple-element.17), kind=kOutput, calls=%fused_computation.89 | convolution fusion | flops 402653184 | bytes 4259840 | tf_op jit(solution)/shard_map/dot_general | solution.py:59
  30.8 1.5 %fusion.12 = f32[2,16,128,256]{3,2,1,0:T(8,128)S(1)} fusion(f32[2,16,128,128]{3,2,1,0:T(8,128)S(1)} %fusion.67, f32[2,16,128,128]{3,2,1,0:T(8,128)S(1)} %fusion.70, s32[256]{0:T(256)S(1)} %get-tuple-element.18), kind=kOutput, calls=%fused_computation.14 | convolution fusion | flops 805863424 | bytes 8389632 | tf_op jit(solution)/shard_map/dot_general | solution.py:59
  32.3 2.2 %add_reduce_fusion = (f32[2,16,256]{2,1,0:T(8,128)S(1)}, f32[2,16,256]{2,1,0:T(8,128)S(1)}) fusion(f32[2,16,128,256]{3,2,1,0:T(8,128)S(1)} %fusion.12, f32[128,256]{1,0:T(8,128)S(1)} %get-tuple-element.21, f32[128,256]{1,0:T(8,128)S(1)} %get-tuple-element.20, s32[256]{0:T(256)S(1)} %get-tuple-element.18, f32[2,16,128,128]{3,2,1,0:T(8,128)S(1)} %fusion.66, ...), kind=kOutput, calls=%fused_computation.3 | convolution fusion | flops 814235648 | bytes 8717312 | tf_op jit(solution)/shard_map/dot_general | solution.py:59
  34.4 0.0 copy-start.1
  34.4 0.1 stack.56
  34.5 0.1 stack.57
  34.7 0.2 copy.61
  34.9 0.9 %reshape.230 = f32[8,1,2048]{2,1,0:T(1,128)} reshape(f32[128,2,2,32]{3,2,1,0:T(2,128)S(1)} %bitcast.98) | data formatting | bytes 131072
  35.8 3.4 %all-to-all-start.1 = ((f32[8,1,2048]{2,1,0:T(1,128)}), f32[8,1,2048]{2,1,0:T(1,128)S(1)}, u32[]{:S(2)}, u32[]{:S(2)}) async-start(f32[8,1,2048]{2,1,0:T(1,128)} %reshape.230), calls=%async_computation.1 | async-start | bytes 131072 | tf_op jit(solution)/shard_map/all_to_all | solution.py:85
  39.2 0.1 add_multiply_fusion.1
  39.3 6.8 %all-to-all-done.1 = f32[8,1,2048]{2,1,0:T(1,128)S(1)} async-done(((f32[8,1,2048]{2,1,0:T(1,128)}), f32[8,1,2048]{2,1,0:T(1,128)S(1)}, u32[]{:S(2)}, u32[]{:S(2)}) %all-to-all-start.1) | async-done | bytes 65568 | tf_op jit(solution)/shard_map/all_to_all | solution.py:85
  46.0 0.8 %reduce.2 = f32[8,2048]{1,0:T(8,128)S(1)} reduce(f32[8,1,2048]{2,1,0:T(1,128)S(1)} %all-to-all-done.1, f32[]{:T(128)} %broadcast.382), dimensions={1}, to_apply=%all_to_all.10.reduce_sub_computation | reduce | bytes 131076 | tf_op jit(solution)/shard_map/all_to_all | solution.py:85
  46.8 0.2 reshape.231
  47.1 0.0 copy-done.1
  47.1 0.4 fusion.87
  47.5 5.4 %all_gather.3 = bf16[2,8,32,128]{3,2,0,1:T(8,128)(2,1)S(1)} all-gather(bf16[2,2,32,128]{3,2,0,1:T(8,128)(2,1)S(1)} %get-tuple-element.22), channel_id=1, replica_groups=mesh['pw'=8,'band'=4] {'band'}, dimensions={1}, use_global_device_ids=true | all-gather | bytes 163840 | tf_op jit(solution)/shard_map/all_gather | solution.py:89
  52.9 0.1 copy.32
  53.0 4.3 %fusion.23 = f32[2,8,1,256]{3,1,0,2:T(8,128)S(1)} fusion(bf16[2,256,32,128]{3,2,1,0:T(8,128)(2,1)} %param.5, bf16[1,8,32,128]{3,1,2,0:T(8,128)(2,1)S(1)} %get-tuple-element.13, bf16[1,8,32,128]{3,1,2,0:T(8,128)(2,1)S(1)} %get-tuple-element.12, bf16[2,8,32,128]{3,1,2,0:T(8,128)(2,1)S(1)} %copy.32), kind=kOutput, calls=%fused_computation.29 | convolution fusion | flops 67895296 | bytes 4472832 | tf_op jit(solution)/shard_map/dot_general | solution.py:93
  57.4 0.6 copy.34
  58.0 3.3 %all-to-all-start.2 = ((f32[2,8,1,256]{3,0,2,1:T(2,128)}), f32[2,8,1,256]{3,0,2,1:T(2,128)S(1)}, u32[]{:S(2)}, u32[]{:S(2)}) async-start(f32[2,8,1,256]{3,0,2,1:T(2,128)} %copy.34), calls=%async_computation.2 | async-start | bytes 32768 | tf_op jit(solution)/shard_map/all_to_all | solution.py:97
  61.3 0.6 copy.35
  61.9 5.9 %all-to-all-done.2 = f32[2,8,1,256]{3,0,2,1:T(2,128)S(1)} async-done(((f32[2,8,1,256]{3,0,2,1:T(2,128)}), f32[2,8,1,256]{3,0,2,1:T(2,128)S(1)}, u32[]{:S(2)}, u32[]{:S(2)}) %all-to-all-start.2) | async-done | bytes 16416 | tf_op jit(solution)/shard_map/all_to_all | solution.py:97
  67.8 0.6 reduce_sum.32
  (12 shorter events, 0.3 us)
Async XLA Ops:
  0.6 10.4 %copy-start.2 = (s32[256]{0:T(256)S(1)}, s32[256]{0:T(256)}, u32[]{:S(2)}) copy-start(s32[256]{0:T(256)} %param.7) | copy-start | bytes 3076
  0.6 10.9 %copy-start = (f32[16,128,128]{2,1,0:T(8,128)S(1)}, f32[16,128,128]{2,1,0:T(8,128)}, u32[]{:S(2)}) copy-start(f32[16,128,128]{2,1,0:T(8,128)} %param.6) | copy-start | bytes 3145732
  3.7 14.2 %all-to-all-start = ((f32[8,1,2048]{2,1,0:T(1,128)}), f32[8,1,2048]{2,1,0:T(1,128)S(1)}, u32[]{:S(2)}, u32[]{:S(2)}) async-start(f32[8,1,2048]{2,1,0:T(1,128)} %reshape.228), calls=%async_computation | async-start | bytes 131072 | tf_op jit(solution)/shard_map/all_to_all | solution.py:62
  34.4 12.7 %copy-start.1 = (f32[2,2,32,128]{3,2,1,0:T(8,128)S(1)}, f32[2,2,32,128]{3,2,1,0:T(8,128)}, u32[]{:S(2)}) copy-start(f32[2,2,32,128]{3,2,1,0:T(8,128)} %param.4) | copy-start | bytes 196612
  35.8 10.2 %all-to-all-start.1 = ((f32[8,1,2048]{2,1,0:T(1,128)}), f32[8,1,2048]{2,1,0:T(1,128)S(1)}, u32[]{:S(2)}, u32[]{:S(2)}) async-start(f32[8,1,2048]{2,1,0:T(1,128)} %reshape.230), calls=%async_computation.1 | async-start | bytes 131072 | tf_op jit(solution)/shard_map/all_to_all | solution.py:85
  58.0 9.8 %all-to-all-start.2 = ((f32[2,8,1,256]{3,0,2,1:T(2,128)}), f32[2,8,1,256]{3,0,2,1:T(2,128)S(1)}, u32[]{:S(2)}, u32[]{:S(2)}) async-start(f32[2,8,1,256]{3,0,2,1:T(2,128)} %copy.34), calls=%async_computation.2 | async-start | bytes 32768 | tf_op jit(solution)/shard_map/all_to_all | solution.py:97

commit v3 on v2

v3 whole, which is shorter than its diff:
```python
import math

import jax
import jax.numpy as jnp
from jax import lax
from jax.sharding import PartitionSpec as P


def frequency(index, size):
    return jnp.where(index < size // 2, index, index - size)


def kinetic_table(columns, grid_size):
    col_x = frequency(columns // grid_size, grid_size).astype(jnp.float32)
    col_y = frequency(columns % grid_size, grid_size).astype(jnp.float32)
    along = frequency(jnp.arange(grid_size, dtype=jnp.int32), grid_size).astype(jnp.float32)
    plane = col_x * col_x + col_y * col_y
    return 4.0 * (plane[:, None] + along[None, :] * along[None, :]) / float(grid_size * grid_size)


def dft_table(grid_size, sign):
    indices = jnp.arange(grid_size, dtype=jnp.int32)
    products = indices[:, None] * indices[None, :] % grid_size
    angles = 2.0 * math.pi / grid_size * products.astype(jnp.float32)
    cosine = jnp.cos(angles)
    sine = sign * jnp.sin(angles)
    return jnp.stack([jnp.stack([cosine, -sine]), jnp.stack([sine, cosine])])


def plane_tables(stick_col, grid_size):
    grid_iota = jnp.arange(grid_size, dtype=jnp.int32)
    col_x = stick_col // grid_size
    col_y = stick_col % grid_size
    phase_angles = (
        2.0
        * math.pi
        / grid_size
        * (grid_iota[:, None] * col_x[None, :] % grid_size).astype(jnp.float32)
    )
    place_cols = (col_y[:, None] == grid_iota[None, :]).astype(jnp.float32)
    pick_cols = (grid_iota[:, None] == col_y[None, :]).astype(jnp.float32)
    return jnp.cos(phase_angles), jnp.sin(phase_angles), place_cols, pick_cols


def mult(left, right):
    return jnp.dot(left, right, precision=lax.Precision.HIGH, preferred_element_type=jnp.float32)


def plane_phase(amp, pot, tables, grid_size):
    phase_cos, phase_sin, place_cols, pick_cols = tables
    inverse = dft_table(grid_size, 1.0)
    cosine = inverse[0, 0]
    sine = inverse[1, 0]
    scaled_pot = (pot / float(grid_size**3))[None]
    val_re = amp[0][:, :, None, :]
    val_im = amp[1][:, :, None, :]
    spread_re = val_re * phase_cos - val_im * phase_sin
    spread_im = val_re * phase_sin + val_im * phase_cos
    rows_re = mult(spread_re, place_cols)
    rows_im = mult(spread_im, place_cols)
    wave_re = (mult(rows_re, cosine) - mult(rows_im, sine)) * scaled_pot
    wave_im = (mult(rows_re, sine) + mult(rows_im, cosine)) * scaled_pot
    back_re = mult(wave_re, cosine) + mult(wave_im, sine)
    back_im = mult(wave_im, cosine) - mult(wave_re, sine)
    sel_re = mult(back_re, pick_cols)
    sel_im = mult(back_im, pick_cols)
    picked_re = jnp.sum(sel_re * phase_cos + sel_im * phase_sin, axis=2)
    picked_im = jnp.sum(sel_im * phase_cos - sel_re * phase_sin, axis=2)
    return jnp.stack([picked_re, picked_im])


def intersect(lowered, psi_all, pw_count):
    turned = jnp.stack([-lowered[1], lowered[0]])
    both = jnp.concatenate([lowered, turned], axis=1)
    dims = (((0, 2, 3), (0, 2, 3)), ((), ()))
    partial_value = lax.dot_general(both, psi_all, dims, preferred_element_type=jnp.float32)
    partial_value = partial_value.reshape(2, lowered.shape[1], partial_value.shape[-1])
    rows_dev = partial_value.shape[1] // pw_count
    pieces = partial_value.reshape(2, pw_count, rows_dev, partial_value.shape[-1])
    pieces = lax.all_to_all(pieces, "pw", split_axis=1, concat_axis=1, tiled=True)
    return jnp.sum(pieces, axis=1)


def per_device_spread(psi_block, psi_all, potential, stick_col):
    local_bands = psi_block.shape[1]
    sticks_dev = psi_block.shape[2]
    grid_size = psi_block.shape[3]
    fast = lax.Precision.HIGH
    rank = lax.axis_index("pw")
    band_rank = lax.axis_index("band")
    pw_count = lax.axis_size("pw")
    band_count = lax.axis_size("band")
    planes = potential.shape[0] // band_count
    all_bands = local_bands * band_count
    groups = pw_count * band_count
    my_columns = lax.dynamic_slice_in_dim(stick_col, rank * sticks_dev, sticks_dev)
    kinetic = kinetic_table(my_columns, grid_size)
    inverse = dft_table(grid_size, 1.0)
    forward = dft_table(grid_size, -1.0)
    tables = plane_tables(stick_col, grid_size)
    kin_part = kinetic[None, None] * psi_block / float(grid_size)
    sources = jnp.concatenate([psi_block, kin_part], axis=1)
    z_lines = jnp.einsum("dczk,cbsk->zdbs", inverse, sources, precision=fast)
    z_lines = z_lines.reshape((groups, planes) + z_lines.shape[1:])
    received = lax.all_to_all(z_lines, ("pw", "band"), split_axis=0, concat_axis=0, tiled=True)
    received = received.reshape(pw_count, band_count, planes, 2, 2, local_bands, sticks_dev)
    received = jnp.transpose(received, (4, 3, 1, 5, 2, 0, 6)).reshape(
        2, 2, all_bands, planes, pw_count * sticks_dev
    )
    pot = lax.dynamic_slice_in_dim(potential, band_rank * planes, planes)
    picked = plane_phase(received[0], pot, tables, grid_size) + received[1]
    outgoing = picked.reshape(2, all_bands, planes, pw_count, sticks_dev)
    outgoing = jnp.transpose(outgoing, (3, 2, 0, 1, 4))
    outgoing = jnp.broadcast_to(
        outgoing[:, None], (pw_count, band_count) + outgoing.shape[1:]
    ).reshape((groups,) + outgoing.shape[1:])
    gathered = lax.all_to_all(outgoing, ("pw", "band"), split_axis=0, concat_axis=0, tiled=True)
    gathered = gathered.reshape((groups * planes,) + gathered.shape[2:])
    hpsi = jnp.einsum("dckz,zcbs->dbsk", forward, gathered, precision=fast)
    applied = lax.dynamic_slice_in_dim(hpsi, band_rank * local_bands, local_bands, 1)
    intersection = intersect(hpsi.astype(jnp.bfloat16), psi_all, pw_count)
    return (intersection, applied)


def per_device_rows(psi_block, psi_all, potential, stick_col):
    sticks_dev = psi_block.shape[2]
    grid_size = psi_block.shape[3]
    fast = lax.Precision.HIGH
    rank = lax.axis_index("pw")
    pw_count = lax.axis_size("pw")
    planes = potential.shape[0]
    my_columns = lax.dynamic_slice_in_dim(stick_col, rank * sticks_dev, sticks_dev)
    kinetic = kinetic_table(my_columns, grid_size)
    inverse = dft_table(grid_size, 1.0)
    forward = dft_table(grid_size, -1.0)
    tables = plane_tables(stick_col, grid_size)
    z_lines = jnp.einsum("dczk,cbsk->zdbs", inverse, psi_block, precision=fast)
    received = lax.all_to_all(z_lines, "pw", split_axis=0, concat_axis=0, tiled=True)
    lanes = received.shape[1:]
    received = received.reshape((pw_count, planes) + lanes)
    amp = jnp.transpose(received, (2, 3, 1, 0, 4)).reshape(
        lanes[0], lanes[1], planes, pw_count * sticks_dev
    )
    picked = plane_phase(amp, potential, tables, grid_size)
    outgoing = picked.reshape(lanes[0], lanes[1], planes, pw_count, sticks_dev)
    outgoing = jnp.transpose(outgoing, (3, 2, 0, 1, 4)).reshape((pw_count * planes,) + lanes)
    sticks_back = lax.all_to_all(outgoing, "pw", split_axis=0, concat_axis=0, tiled=True)
    vpsi = jnp.einsum("dckz,zcbs->dbsk", forward, sticks_back, precision=fast)
    applied = kinetic[None, None] * psi_block + vpsi
    lowered = applied.astype(jnp.bfloat16)
    gathered = lax.all_gather(lowered, "band", axis=1, tiled=True)
    intersection = intersect(gathered, psi_all, pw_count)
    return (intersection, applied)


def per_device(psi_block, psi_all, potential, stick_col):
    band_count = lax.axis_size("band")
    if potential.shape[0] % band_count == 0:
        return per_device_spread(psi_block, psi_all, potential, stick_col)
    return per_device_rows(psi_block, psi_all, potential, stick_col)


def solution(mesh):
    return jax.shard_map(
        per_device,
        mesh=mesh,
        in_specs=(
            P(None, "band", "pw", None),
            P(None, "band", "pw", None),
            P("pw", None, None),
            P(),
        ),
        out_specs=(P(None, "pw", "band"), P(None, "band", "pw", None)),
        check_vma=False,
    )
```

time: 68.8 us -> 70.5 us (1.025)
  blocking collectives: 5.43 us -> 0 us
  waiting for transfers between devices: 18.8 us -> 23.1 us
  other arithmetic: 3.29 us -> 6.39 us
    all_gather x1 -> x0, blocking collectives: 5.43 us -> none  [per_device(): gathered = lax.all_gather(lowered, 'band', axis=1, tiled=True)]
    all_to_all x3, waiting for transfers between devices: 18.8 us -> 23.1 us  [the longest x1 10.6 us: per_device_spread(): lax.all_to_all(outgoing, ('pw', 'band'), split_axis=0, concat_axis=0, til...]
    div x1, other arithmetic: 0.08 us -> 0.97 us  [plane_phase(): scaled_pot = (pot / float(grid_size ** 3))[None]]
    unnamed x0 -> x1, other arithmetic: none -> 0.86 us
    all_to_all x3, starting transfers between devices: 13.9 us -> 13.2 us  [the longest x1 7.3 us: per_device_spread(): lax.all_to_all(z_lines, ('pw', 'band'), split_axis=0, concat_axis=0, tile...]
    unnamed x11 -> x7, local copies, waits for them, and re-layouts: 2.94 us -> 3.37 us
  transfers between devices with their start and end apart: 3 -> 3, of which waited for: 3 -> 3; matrix products, arithmetic and copies ran while one was open for 2% -> 3% of each run, Pallas kernels for 0% -> 0%
where the time goes in v3:
time: 70.5 us; the launch traced here: 70 us
  waiting for transfers between devices  23.1 us (33%)
  matrix products  19.9 us (28%)
  starting transfers between devices  13.2 us (19%)
  other arithmetic  6.39 us (9%)
  local copies, waits for them, and re-layouts  6.36 us (9%)
  between operations  1 us (1%)
    dot_general x12, matrix products, mult(): jnp.dot(left, right, precision=lax.Precision.HIGH, preferred_element_type...  14.1 us
    all_to_all x1, waiting for transfers between devices, per_device_spread(): lax.all_to_all(outgoing, ('pw', 'band'), split_axis=0, concat_axis=0, til...  10.6 us
    all_to_all x1, starting transfers between devices, per_device_spread(): lax.all_to_all(z_lines, ('pw', 'band'), split_axis=0, concat_axis=0, tile...  7.3 us
    all_to_all x1, waiting for transfers between devices, per_device_spread(): lax.all_to_all(z_lines, ('pw', 'band'), split_axis=0, concat_axis=0, tile...  6.69 us
    all_to_all x1, waiting for transfers between devices, intersect(): lax.all_to_all(pieces, 'pw', split_axis=1, concat_axis=1, tiled=True)  5.86 us
    dot_general x1, matrix products, intersect(): lax.dot_general(both, psi_all, dims, preferred_element_type=jnp.float32)  4.49 us
    unnamed x7, local copies, waits for them, and re-layouts  3.37 us
    all_to_all x1, starting transfers between devices, intersect(): lax.all_to_all(pieces, 'pw', split_axis=1, concat_axis=1, tiled=True)  3.31 us
  transfers between devices with their start and end apart: 3, of which 3 were waited for; matrix products, arithmetic and copies ran while one was open for 3% of the time, Pallas kernels for 0%

profile of v3, /device:TPU:0, one launch (start us, length us, event | category | flops | bytes accessed | tf_op | source)
XLA Modules:
  0.0 70.0 jit_solution(8260442667252844463)
XLA Ops:
  0.6 0.3 fusion.71
  0.9 0.3 fusion.69
  1.2 0.3 broadcast_multiply_fusion
  1.5 0.8 %fusion.74 = f32[32]{0:T(128)S(1)} fusion(s32[256]{0:T(256)} %param.7, s32[]{:T(128)S(6)} %select_n.106), kind=kLoop, calls=%fused_computation.113 | loop fusion | flops 960 | bytes 260 | tf_op jit(solution)/shard_map/add | solution.py:17
  2.2 0.1 add_multiply_fusion.1
  2.3 0.0 copy-start
  2.3 0.9 %fusion.82 = (f32[2,2,32,128]{3,2,0,1:T(8,128)S(1)}, f32[2,2,32,128]{3,2,0,1:T(8,128)S(1)}) fusion(f32[2,2,32,128]{3,2,1,0:T(8,128)} %param.4, f32[32,128]{1,0:T(8,128)S(1)} %add_multiply_fusion.1), kind=kLoop, calls=%fused_computation.123 | loop fusion | flops 32768 | bytes 212992 | tf_op args[0]
  3.2 0.3 convolution_bitcast_fusion.1
  3.5 0.2 copy.53
  3.7 0.1 copy.97
  3.9 1.0 %reshape.244 = f32[32,1,1024]{2,1,0:T(1,128)} reshape(f32[32,2,4,4,32]{4,3,2,1,0:T(4,128)S(1)} %bitcast.106) | data formatting | bytes 262144
  4.9 7.3 %all-to-all-start = ((f32[32,1,1024]{2,1,0:T(1,128)}), f32[32,1,1024]{2,1,0:T(1,128)S(1)}, u32[]{:S(2)}, u32[]{:S(2)}) async-start(f32[32,1,1024]{2,1,0:T(1,128)} %reshape.244), calls=%async_computation | async-start | bytes 262144 | tf_op jit(solution)/shard_map/all_to_all | solution.py:105
  12.2 0.0 copy-done
  12.2 1.0 %dynamic-slice_multiply_fusion = f32[4,128,128]{2,1,0:T(8,128)S(1)} fusion(f32[16,128,128]{2,1,0:T(8,128)} %param.6, s32[]{:T(128)S(6)} %select_n.116), kind=kLoop, calls=%fused_computation.40 | loop fusion | flops 65536 | bytes 524292 | tf_op jit(solution)/shard_map/div | solution.py:54
  13.2 0.5 fusion.58
  13.7 6.7 %all-to-all-done = f32[32,1,1024]{2,1,0:T(1,128)S(1)} async-done(((f32[32,1,1024]{2,1,0:T(1,128)}), f32[32,1,1024]{2,1,0:T(1,128)S(1)}, u32[]{:S(2)}, u32[]{:S(2)}) %all-to-all-start) | async-done | bytes 131104 | tf_op jit(solution)/shard_map/all_to_all | solution.py:105
  20.4 0.5 broadcast.385
  20.9 0.9 %reduce.1 = f32[32,1024]{1,0:T(8,128)S(1)} reduce(f32[32,1,1024]{2,1,0:T(1,128)S(1)} %all-to-all-done, f32[]{:T(128)} %broadcast.385), dimensions={1}, to_apply=%all_to_all.9.reduce_sub_computation | reduce | bytes 262148 | tf_op jit(solution)/shard_map/all_to_all | solution.py:105
  21.9 0.3 reshape.245
  22.1 0.3 copy.55
  22.5 0.1 reshape.242
  22.7 0.1 reshape.243
  22.8 1.3 %fusion.2 = f32[8,4,128,128]{3,2,1,0:T(8,128)S(1)} fusion(f32[128,256]{1,0:T(8,128)S(1)} %get-tuple-element.27, f32[8,4,256]{2,1,0:T(4,128)S(1)} %reshape.243, f32[128,256]{1,0:T(8,128)S(1)} %get-tuple-element.26, f32[8,4,256]{2,1,0:T(4,128)S(1)} %reshape.242, s32[256]{0:T(256)S(1)} %get-tuple-element.24), kind=kOutput, calls=%fused_computation.4 | convolution fusion | flops 808484864 | bytes 2425856 | tf_op jit(solution)/shard_map/dot_general | solution.py:46
  24.1 1.3 %fusion.6 = f32[8,4,128,128]{3,2,1,0:T(8,128)S(1)} fusion(f32[128,256]{1,0:T(8,128)S(1)} %get-tuple-element.27, f32[8,4,256]{2,1,0:T(4,128)S(1)} %reshape.243, f32[128,256]{1,0:T(8,128)S(1)} %get-tuple-element.26, f32[8,4,256]{2,1,0:T(4,128)S(1)} %reshape.242, s32[256]{0:T(256)S(1)} %get-tuple-element.24), kind=kOutput, calls=%fused_computation.8 | convolution fusion | flops 808484864 | bytes 2425856 | tf_op jit(solution)/shard_map/dot_general | solution.py:46
  25.4 1.0 %fusion.67 = f32[8,4,128,128]{3,2,1,0:T(8,128)S(1)} fusion(f32[8,4,128,128]{3,2,1,0:T(8,128)S(1)} %fusion.6, f32[1,2,128,128]{3,2,1,0:T(8,128)S(1)} %get-tuple-element.20), kind=kOutput, calls=%fused_computation.91 | convolution fusion | flops 402653184 | bytes 4259840 | tf_op jit(solution)/shard_map/dot_general | solution.py:46
  26.4 1.0 %fusion.64 = f32[8,4,128,128]{3,2,1,0:T(8,128)S(1)} fusion(f32[8,4,128,128]{3,2,1,0:T(8,128)S(1)} %fusion.6, f32[1,2,128,128]{3,2,1,0:T(8,128)S(1)} %get-tuple-element.21), kind=kOutput, calls=%fused_computation.88 | convolution fusion | flops 402653184 | bytes 4259840 | tf_op jit(solution)/shard_map/dot_general | solution.py:46
  27.4 1.0 %subtract_multiply_fusion = f32[8,4,128,128]{3,2,1,0:T(8,128)S(1)} fusion(f32[8,4,128,128]{3,2,1,0:T(8,128)S(1)} %fusion.64, f32[8,4,128,128]{3,2,1,0:T(8,128)S(1)} %fusion.2, f32[4,128,128]{2,1,0:T(8,128)S(1)} %dynamic-slice_multiply_fusion, f32[1,2,128,128]{3,2,1,0:T(8,128)S(1)} %get-tuple-element.20), kind=kOutput, calls=%fused_computation.17 | convolution fusion | flops 403701760 | bytes 6619136 | tf_op jit(solution)/shard_map/dot_general | solution.py:46
  28.5 1.0 %fusion.65 = f32[8,4,128,128]{3,2,1,0:T(8,128)S(1)} fusion(f32[8,4,128,128]{3,2,1,0:T(8,128)S(1)} %subtract_multiply_fusion, f32[1,2,128,128]{3,2,1,0:T(8,128)S(1)} %get-tuple-element.20), kind=kOutput, calls=%fused_computation.89 | convolution fusion | flops 402653184 | bytes 4259840 | tf_op jit(solution)/shard_map/dot_general | solution.py:46
  29.5 1.0 %fusion.63 = f32[8,4,128,128]{3,2,1,0:T(8,128)S(1)} fusion(f32[8,4,128,128]{3,2,1,0:T(8,128)S(1)} %subtract_multiply_fusion, f32[1,2,128,128]{3,2,1,0:T(8,128)S(1)} %get-tuple-element.21), kind=kOutput, calls=%fused_computation.87 | convolution fusion | flops 402653184 | bytes 4259840 | tf_op jit(solution)/shard_map/dot_general | solution.py:46
  30.5 1.0 %add_multiply_fusion = f32[8,4,128,128]{3,2,1,0:T(8,128)S(1)} fusion(f32[8,4,128,128]{3,2,1,0:T(8,128)S(1)} %fusion.67, f32[8,4,128,128]{3,2,1,0:T(8,128)S(1)} %fusion.2, f32[4,128,128]{2,1,0:T(8,128)S(1)} %dynamic-slice_multiply_fusion, f32[1,2,128,128]{3,2,1,0:T(8,128)S(1)} %get-tuple-element.21), kind=kOutput, calls=%fused_computation.16 | convolution fusion | flops 403701760 | bytes 6619136 | tf_op jit(solution)/shard_map/dot_general | solution.py:46
  31.5 1.0 %fusion.62 = f32[8,4,128,128]{3,2,1,0:T(8,128)S(1)} fusion(f32[8,4,128,128]{3,2,1,0:T(8,128)S(1)} %add_multiply_fusion, f32[1,2,128,128]{3,2,1,0:T(8,128)S(1)} %get-tuple-element.21), kind=kOutput, calls=%fused_computation.86 | convolution fusion | flops 402653184 | bytes 4259840 | tf_op jit(solution)/shard_map/dot_general | solution.py:46
  32.5 1.2 %fusion.66 = f32[8,4,128,128]{3,2,1,0:T(8,128)S(1)} fusion(f32[8,4,128,128]{3,2,1,0:T(8,128)S(1)} %add_multiply_fusion, f32[1,2,128,128]{3,2,1,0:T(8,128)S(1)} %get-tuple-element.20), kind=kOutput, calls=%fused_computation.90 | convolution fusion | flops 402653184 | bytes 4259840 | tf_op jit(solution)/shard_map/dot_general | solution.py:46
  33.7 1.3 %fusion.12 = f32[8,4,128,256]{3,2,1,0:T(8,128)S(1)} fusion(f32[8,4,128,128]{3,2,1,0:T(8,128)S(1)} %fusion.63, f32[8,4,128,128]{3,2,1,0:T(8,128)S(1)} %fusion.66, s32[256]{0:T(256)S(1)} %get-tuple-element.24), kind=kOutput, calls=%fused_computation.14 | convolution fusion | flops 805863424 | bytes 8389632 | tf_op jit(solution)/shard_map/dot_general | solution.py:46
  35.0 2.0 %add_reduce_fusion = (f32[8,4,256]{2,1,0:T(4,128)S(1)}, f32[8,4,256]{2,1,0:T(4,128)S(1)}) fusion(f32[8,4,128,256]{3,2,1,0:T(8,128)S(1)} %fusion.12, f32[128,256]{1,0:T(8,128)S(1)} %get-tuple-element.27, f32[128,256]{1,0:T(8,128)S(1)} %get-tuple-element.26, s32[256]{0:T(256)S(1)} %get-tuple-element.24, f32[8,4,128,128]{3,2,1,0:T(8,128)S(1)} %fusion.62, ...), kind=kOutput, calls=%fused_computation.3 | convolution fusion | flops 814235648 | bytes 8717312 | tf_op jit(solution)/shard_map/dot_general | solution.py:46
  37.0 0.1 stack.65
  37.1 0.1 stack.64
  37.2 0.1 copy.64
  37.3 0.1 broadcast_in_dim.2
  37.4 1.1 %reshape.246 = f32[32,1,2048]{2,1,0:T(1,128)} reshape(f32[32,4,2,8,32]{4,3,2,1,0:T(8,128)S(1)} %bitcast.104) | data formatting | bytes 524288
  38.6 2.6 %all-to-all-start.1 = ((f32[32,1,2048]{2,1,0:T(1,128)}), f32[32,1,2048]{2,1,0:T(1,128)S(1)}, u32[]{:S(2)}, u32[]{:S(2)}) async-start(f32[32,1,2048]{2,1,0:T(1,128)} %reshape.246), calls=%async_computation.1 | async-start | bytes 524288 | tf_op jit(solution)/shard_map/all_to_all | solution.py:117
  41.1 10.6 %all-to-all-done.1 = f32[32,1,2048]{2,1,0:T(1,128)S(1)} async-done(((f32[32,1,2048]{2,1,0:T(1,128)}), f32[32,1,2048]{2,1,0:T(1,128)S(1)}, u32[]{:S(2)}, u32[]{:S(2)}) %all-to-all-start.1) | async-done | bytes 262176 | tf_op jit(solution)/shard_map/all_to_all | solution.py:117
  51.7 1.3 %reduce.2 = f32[32,2048]{1,0:T(8,128)S(1)} reduce(f32[32,1,2048]{2,1,0:T(1,128)S(1)} %all-to-all-done.1, f32[]{:T(128)} %broadcast.385), dimensions={1}, to_apply=%all_to_all.10.reduce_sub_computation | reduce | bytes 524292 | tf_op jit(solution)/shard_map/all_to_all | solution.py:117
  53.0 0.3 reshape.247
  53.4 1.1 %convolution_bitcast_fusion = f32[8,32,2,128]{3,1,2,0:T(8,128)S(1)} fusion(f32[128,2,8,32,1]{3,2,1,0,4:T(8,128)S(1)} %bitcast.103, f32[1,2,128,128]{3,2,1,0:T(8,128)S(1)} %get-tuple-element.19, f32[1,2,128,128]{3,2,1,0:T(8,128)S(1)} %get-tuple-element.18), kind=kOutput, calls=%fused_computation.26 | convolution fusion | flops 100728832 | bytes 786432 | tf_op jit(solution)/shard_map/dckz,zcbs->dbsk/dot_general | solution.py:119
  54.5 4.5 %fusion.22 = f32[2,8,1,256]{3,1,0,2:T(8,128)S(1)} fusion(bf16[2,256,32,128]{3,2,1,0:T(8,128)(2,1)} %param.5, bf16[2,16,32,128]{3,2,0,1:T(8,128)(2,1)S(1)} %maximum_maximum_fusion), kind=kOutput, calls=%fused_computation.28 | convolution fusion | flops 67108864 | bytes 4472832 | tf_op jit(solution)/shard_map/dot_general | solution.py:76
  59.0 0.6 copy.68
  59.6 3.3 %all-to-all-start.2 = ((f32[2,8,1,256]{3,0,2,1:T(2,128)}), f32[2,8,1,256]{3,0,2,1:T(2,128)S(1)}, u32[]{:S(2)}, u32[]{:S(2)}) async-start(f32[2,8,1,256]{3,0,2,1:T(2,128)} %copy.68), calls=%async_computation.2 | async-start | bytes 32768 | tf_op jit(solution)/shard_map/all_to_all | solution.py:80
  62.9 0.6 copy.69
  63.6 5.9 %all-to-all-done.2 = f32[2,8,1,256]{3,0,2,1:T(2,128)S(1)} async-done(((f32[2,8,1,256]{3,0,2,1:T(2,128)}), f32[2,8,1,256]{3,0,2,1:T(2,128)S(1)}, u32[]{:S(2)}, u32[]{:S(2)}) %all-to-all-start.2) | async-done | bytes 16416 | tf_op jit(solution)/shard_map/all_to_all | solution.py:80
  69.4 0.6 reduce_sum.32
  (16 shorter events, 0.3 us)
Async XLA Ops:
  2.3 9.9 %copy-start = (s32[256]{0:T(256)S(1)}, s32[256]{0:T(256)}, u32[]{:S(2)}) copy-start(s32[256]{0:T(256)} %param.7) | copy-start | bytes 3076
  4.9 15.5 %all-to-all-start = ((f32[32,1,1024]{2,1,0:T(1,128)}), f32[32,1,1024]{2,1,0:T(1,128)S(1)}, u32[]{:S(2)}, u32[]{:S(2)}) async-start(f32[32,1,1024]{2,1,0:T(1,128)} %reshape.244), calls=%async_computation | async-start | bytes 262144 | tf_op jit(solution)/shard_map/all_to_all | solution.py:105
  38.6 13.2 %all-to-all-start.1 = ((f32[32,1,2048]{2,1,0:T(1,128)}), f32[32,1,2048]{2,1,0:T(1,128)S(1)}, u32[]{:S(2)}, u32[]{:S(2)}) async-start(f32[32,1,2048]{2,1,0:T(1,128)} %reshape.246), calls=%async_computation.1 | async-start | bytes 524288 | tf_op jit(solution)/shard_map/all_to_all | solution.py:117
  59.6 9.8 %all-to-all-start.2 = ((f32[2,8,1,256]{3,0,2,1:T(2,128)}), f32[2,8,1,256]{3,0,2,1:T(2,128)S(1)}, u32[]{:S(2)}, u32[]{:S(2)}) async-start(f32[2,8,1,256]{3,0,2,1:T(2,128)} %copy.68), calls=%async_computation.2 | async-start | bytes 32768 | tf_op jit(solution)/shard_map/all_to_all | solution.py:80

commit v4 on v3

--- a/solution.py
+++ b/solution.py
@@ -1,6 +1,7 @@
 import math
 
 import jax
+import numpy as np
 import jax.numpy as jnp
 from jax import lax
 from jax.sharding import PartitionSpec as P
@@ -19,12 +20,13 @@
 
 
 def dft_table(grid_size, sign):
-    indices = jnp.arange(grid_size, dtype=jnp.int32)
+    indices = np.arange(grid_size)
     products = indices[:, None] * indices[None, :] % grid_size
-    angles = 2.0 * math.pi / grid_size * products.astype(jnp.float32)
-    cosine = jnp.cos(angles)
-    sine = sign * jnp.sin(angles)
-    return jnp.stack([jnp.stack([cosine, -sine]), jnp.stack([sine, cosine])])
+    angles = 2.0 * np.pi / grid_size * products
+    cosine = np.cos(angles)
+    sine = sign * np.sin(angles)
+    table = np.stack([np.stack([cosine, -sine]), np.stack([sine, cosine])])
+    return jnp.asarray(table.astype(np.float32))
 
 
 def plane_tables(stick_col, grid_size):
@@ -72,54 +74,14 @@
 def intersect(lowered, psi_all, pw_count):
     turned = jnp.stack([-lowered[1], lowered[0]])
     both = jnp.concatenate([lowered, turned], axis=1)
-    dims = (((0, 2, 3), (0, 2, 3)), ((), ()))
+    dims = (((2, 3), (2, 3)), ((0,), (0,)))
     partial_value = lax.dot_general(both, psi_all, dims, preferred_element_type=jnp.float32)
+    partial_value = jnp.sum(partial_value, axis=0)
     partial_value = partial_value.reshape(2, lowered.shape[1], partial_value.shape[-1])
     rows_dev = partial_value.shape[1] // pw_count
     pieces = partial_value.reshape(2, pw_count, rows_dev, partial_value.shape[-1])
     pieces = lax.all_to_all(pieces, "pw", split_axis=1, concat_axis=1, tiled=True)
     return jnp.sum(pieces, axis=1)
-
-
-def per_device_spread(psi_block, psi_all, potential, stick_col):
-    local_bands = psi_block.shape[1]
-    sticks_dev = psi_block.shape[2]
-    grid_size = psi_block.shape[3]
-    fast = lax.Precision.HIGH
-    rank = lax.axis_index("pw")
-    band_rank = lax.axis_index("band")
-    pw_count = lax.axis_size("pw")
-    band_count = lax.axis_size("band")
-    planes = potential.shape[0] // band_count
-    all_bands = local_bands * band_count
-    groups = pw_count * band_count
-    my_columns = lax.dynamic_slice_in_dim(stick_col, rank * sticks_dev, sticks_dev)
-    kinetic = kinetic_table(my_columns, grid_size)
-    inverse = dft_table(grid_size, 1.0)
-    forward = dft_table(grid_size, -1.0)
-    tables = plane_tables(stick_col, grid_size)
-    kin_part = kinetic[None, None] * psi_block / float(grid_size)
-    sources = jnp.concatenate([psi_block, kin_part], axis=1)
-    z_lines = jnp.einsum("dczk,cbsk->zdbs", inverse, sources, precision=fast)
-    z_lines = z_lines.reshape((groups, planes) + z_lines.shape[1:])
-    received = lax.all_to_all(z_lines, ("pw", "band"), split_axis=0, concat_axis=0, tiled=True)
-    received = received.reshape(pw_count, band_count, planes, 2, 2, local_bands, sticks_dev)
-    received = jnp.transpose(received, (4, 3, 1, 5, 2, 0, 6)).reshape(
-        2, 2, all_bands, planes, pw_count * sticks_dev
-    )
-    pot = lax.dynamic_slice_in_dim(potential, band_rank * planes, planes)
-    picked = plane_phase(received[0], pot, tables, grid_size) + received[1]
-    outgoing = picked.reshape(2, all_bands, planes, pw_count, sticks_dev)
-    outgoing = jnp.transpose(outgoing, (3, 2, 0, 1, 4))
-    outgoing = jnp.broadcast_to(
-        outgoing[:, None], (pw_count, band_count) + outgoing.shape[1:]
-    ).reshape((groups,) + outgoing.shape[1:])
-    gathered = lax.all_to_all(outgoing, ("pw", "band"), split_axis=0, concat_axis=0, tiled=True)
-    gathered = gathered.reshape((groups * planes,) + gathered.shape[2:])
-    hpsi = jnp.einsum("dckz,zcbs->dbsk", forward, gathered, precision=fast)
-    applied = lax.dynamic_slice_in_dim(hpsi, band_rank * local_bands, local_bands, 1)
-    intersection = intersect(hpsi.astype(jnp.bfloat16), psi_all, pw_count)
-    return (intersection, applied)
 
 
 def per_device_rows(psi_block, psi_all, potential, stick_col):
@@ -154,9 +116,6 @@
 
 
 def per_device(psi_block, psi_all, potential, stick_col):
-    band_count = lax.axis_size("band")
-    if potential.shape[0] % band_count == 0:
-        return per_device_spread(psi_block, psi_all, potential, stick_col)
     return per_device_rows(psi_block, psi_all, potential, stick_col)
 
 

time: 70.5 us -> 68.4 us (0.970)
  blocking collectives: 0 us -> 5.43 us
  waiting for transfers between devices: 23.1 us -> 18.1 us
  other arithmetic: 6.39 us -> 3.13 us
    all_gather x0 -> x1, blocking collectives: none -> 5.43 us  [per_device_rows(): gathered = lax.all_gather(lowered, 'band', axis=1, tiled=True)]
    all_to_all x2, waiting for transfers between devices: 17.3 us -> 12.2 us  [the longest x1 6.77 us: per_device_rows(): lax.all_to_all(outgoing, 'pw', split_axis=0, concat_axis=0, tiled=True)]
    div x1, other arithmetic: 0.97 us -> 0.08 us  [plane_phase(): scaled_pot = (pot / float(grid_size ** 3))[None]]
    unnamed x1 -> x0, other arithmetic: 0.86 us -> none
    all_to_all x2, starting transfers between devices: 9.88 us -> 10.6 us  [the longest x1 7.28 us: per_device_rows(): lax.all_to_all(z_lines, 'pw', split_axis=0, concat_axis=0, tiled=True)]
    unnamed x7 -> x17, local copies, waits for them, and re-layouts: 3.37 us -> 2.96 us
where the time goes in v4:
time: 68.4 us; the launch traced here: 67.9 us
  matrix products  20.6 us (30%)
  waiting for transfers between devices  18.1 us (26%)
  starting transfers between devices  13.9 us (20%)
  local copies, waits for them, and re-layouts  5.7 us (8%)
  blocking collectives  5.43 us (8%)
  other arithmetic  3.13 us (5%)
  between operations  0.99 us (1%)
    dot_general x12, matrix products, mult(): jnp.dot(left, right, precision=lax.Precision.HIGH, preferred_element_type...  14.4 us
    all_to_all x1, starting transfers between devices, per_device_rows(): lax.all_to_all(z_lines, 'pw', split_axis=0, concat_axis=0, tiled=True)  7.28 us
    all_to_all x1, waiting for transfers between devices, per_device_rows(): lax.all_to_all(outgoing, 'pw', split_axis=0, concat_axis=0, tiled=True)  6.77 us
    all_to_all x1, waiting for transfers between devices, intersect(): lax.all_to_all(pieces, 'pw', split_axis=1, concat_axis=1, tiled=True)  5.88 us
    all_to_all x1, waiting for transfers between devices, per_device_rows(): lax.all_to_all(z_lines, 'pw', split_axis=0, concat_axis=0, tiled=True)  5.47 us
    all_gather x1, blocking collectives, per_device_rows(): gathered = lax.all_gather(lowered, 'band', axis=1, tiled=True)  5.43 us
    dot_general x1, matrix products, intersect(): lax.dot_general(both, psi_all, dims, preferred_element_type=jnp.float32)  4.53 us
    all_to_all x1, starting transfers between devices, per_device_rows(): lax.all_to_all(outgoing, 'pw', split_axis=0, concat_axis=0, tiled=True)  3.35 us
  transfers between devices with their start and end apart: 3, of which 3 were waited for; matrix products, arithmetic and copies ran while one was open for 3% of the time, Pallas kernels for 0%

profile of v4, /device:TPU:0, one launch (start us, length us, event | category | flops | bytes accessed | tf_op | source)
XLA Modules:
  0.0 67.9 jit_solution(1184896225335423957)
XLA Ops:
  0.6 0.0 copy-start.5
  0.6 0.0 copy-start.2
  0.7 1.3 %convolution_bitcast_fusion = f32[128,2,2,32]{0,3,2,1:T(8,128)S(1)} fusion(f32[2,2,128,128,1]{3,2,1,4,0:T(8,128)} %constant.96, f32[2,2,32,128]{3,2,1,0:T(8,128)} %param.7), kind=kOutput, calls=%fused_computation.26 | convolution fusion | flops 25165824 | bytes 393216 | tf_op jit(solution)/shard_map/dczk,cbsk->zdbs/dot_general | solution.py:99
  2.0 0.2 copy.26
  2.2 0.9 %reshape.130 = f32[8,1,2048]{2,1,0:T(1,128)} reshape(f32[128,2,2,32]{3,2,1,0:T(2,128)S(1)} %copy.26) | data formatting | bytes 131072
  3.1 7.3 %all-to-all-start = ((f32[8,1,2048]{2,1,0:T(1,128)}), f32[8,1,2048]{2,1,0:T(1,128)S(1)}, u32[]{:S(2)}, u32[]{:S(2)}) async-start(f32[8,1,2048]{2,1,0:T(1,128)} %reshape.130), calls=%async_computation | async-start | bytes 131072 | tf_op jit(solution)/shard_map/all_to_all | solution.py:100
  10.4 0.7 %and_select_fusion = (s32[256]{0:T(256)S(1)}, s32[256]{0:T(256)S(1)}) fusion(s32[256]{0:T(256)} %param.10), kind=kLoop, calls=%fused_computation.64 | loop fusion | flops 4864 | bytes 3072 | tf_op jit(solution)/shard_map/jit(remainder)/select_n | solution.py:35
  11.0 0.5 fusion.50
  11.6 0.0 copy-done.2
  11.6 0.1 broadcast_multiply_fusion
  11.7 0.0 copy-done.5
  11.7 0.1 fusion.54
  11.8 5.5 %all-to-all-done = f32[8,1,2048]{2,1,0:T(1,128)S(1)} async-done(((f32[8,1,2048]{2,1,0:T(1,128)}), f32[8,1,2048]{2,1,0:T(1,128)S(1)}, u32[]{:S(2)}, u32[]{:S(2)}) %all-to-all-start) | async-done | bytes 65568 | tf_op jit(solution)/shard_map/all_to_all | solution.py:100
  17.3 0.5 broadcast.179
  17.8 0.8 %reduce.1 = f32[8,2048]{1,0:T(8,128)S(1)} reduce(f32[8,1,2048]{2,1,0:T(1,128)S(1)} %all-to-all-done, f32[]{:T(128)} %broadcast.179), dimensions={1}, to_apply=%all_to_all.9.reduce_sub_computation | reduce | bytes 131076 | tf_op jit(solution)/shard_map/all_to_all | solution.py:100
  18.6 0.2 reshape.131
  18.9 0.1 mul.155
  19.1 0.1 mul.164
  19.2 1.3 %fusion.6 = f32[2,16,128,128]{3,2,1,0:T(8,128)S(1)} fusion(f32[128,256]{1,0:T(8,128)S(1)} %get-tuple-element.17, f32[2,16,256]{2,1,0:T(8,128)S(1)} %mul.164, f32[128,256]{1,0:T(8,128)S(1)} %get-tuple-element.16, f32[2,16,256]{2,1,0:T(8,128)S(1)} %mul.155, s32[256]{0:T(256)S(1)} %get-tuple-element.14), kind=kOutput, calls=%fused_computation.8 | convolution fusion | flops 808484864 | bytes 2425856 | tf_op jit(solution)/shard_map/dot_general | solution.py:48
  20.5 0.0 copy-start
  20.5 1.3 %fusion.2 = f32[2,16,128,128]{3,2,1,0:T(8,128)S(1)} fusion(f32[128,256]{1,0:T(8,128)S(1)} %get-tuple-element.17, f32[2,16,256]{2,1,0:T(8,128)S(1)} %mul.164, f32[128,256]{1,0:T(8,128)S(1)} %get-tuple-element.16, f32[2,16,256]{2,1,0:T(8,128)S(1)} %mul.155, s32[256]{0:T(256)S(1)} %get-tuple-element.14), kind=kOutput, calls=%fused_computation.4 | convolution fusion | flops 808484864 | bytes 2425856 | tf_op jit(solution)/shard_map/dot_general | solution.py:48
  21.9 0.0 copy-done
  21.9 0.0 copy-start.1
  21.9 1.0 %fusion.64 = f32[2,16,128,128]{3,2,1,0:T(8,128)S(1)} fusion(f32[2,16,128,128]{3,2,1,0:T(8,128)S(1)} %fusion.6, f32[128,128,1,1]{1,0,3,2:T(8,128)S(1)} %copy-done), kind=kOutput, calls=%fused_computation.90 | convolution fusion | flops 402653184 | bytes 4259840 | tf_op jit(solution)/shard_map/dot_general | solution.py:48
  22.9 0.0 copy-done.1
  22.9 1.0 %fusion.62 = f32[2,16,128,128]{3,2,1,0:T(8,128)S(1)} fusion(f32[2,16,128,128]{3,2,1,0:T(8,128)S(1)} %fusion.6, f32[128,128,1,1]{1,0,3,2:T(8,128)S(1)} %copy-done.1), kind=kOutput, calls=%fused_computation.88 | convolution fusion | flops 402653184 | bytes 4259840 | tf_op jit(solution)/shard_map/dot_general | solution.py:48
  23.9 1.1 %add_multiply_fusion = f32[2,16,128,128]{3,2,1,0:T(8,128)S(1)} fusion(f32[2,16,128,128]{3,2,1,0:T(8,128)S(1)} %fusion.64, f32[2,16,128,128]{3,2,1,0:T(8,128)S(1)} %fusion.2, f32[128,128,1,1]{1,0,3,2:T(8,128)S(1)} %copy-done.1, f32[16,128,128]{2,1,0:T(8,128)S(1)} %broadcast_multiply_fusion), kind=kOutput, calls=%fused_computation.16 | convolution fusion | flops 403701760 | bytes 7405568 | tf_op jit(solution)/shard_map/dot_general | solution.py:48
  25.0 1.0 %fusion.65 = f32[2,16,128,128]{3,2,1,0:T(8,128)S(1)} fusion(f32[2,16,128,128]{3,2,1,0:T(8,128)S(1)} %add_multiply_fusion, f32[128,128,1,1]{1,0,3,2:T(8,128)S(1)} %copy-done), kind=kOutput, calls=%fused_computation.91 | convolution fusion | flops 402653184 | bytes 4259840 | tf_op jit(solution)/shard_map/dot_general | solution.py:48
  26.0 1.0 %fusion.66 = f32[2,16,128,128]{3,2,1,0:T(8,128)S(1)} fusion(f32[2,16,128,128]{3,2,1,0:T(8,128)S(1)} %add_multiply_fusion, f32[128,128,1,1]{1,0,3,2:T(8,128)S(1)} %copy-done.1), kind=kOutput, calls=%fused_computation.92 | convolution fusion | flops 402653184 | bytes 4259840 | tf_op jit(solution)/shard_map/dot_general | solution.py:48
  27.0 1.1 %subtract_multiply_fusion = f32[2,16,128,128]{3,2,1,0:T(8,128)S(1)} fusion(f32[2,16,128,128]{3,2,1,0:T(8,128)S(1)} %fusion.62, f32[2,16,128,128]{3,2,1,0:T(8,128)S(1)} %fusion.2, f32[128,128,1,1]{1,0,3,2:T(8,128)S(1)} %copy-done, f32[16,128,128]{2,1,0:T(8,128)S(1)} %broadcast_multiply_fusion), kind=kOutput, calls=%fused_computation.17 | convolution fusion | flops 403701760 | bytes 7405568 | tf_op jit(solution)/shard_map/dot_general | solution.py:48
  28.1 1.0 %fusion.63 = f32[2,16,128,128]{3,2,1,0:T(8,128)S(1)} fusion(f32[2,16,128,128]{3,2,1,0:T(8,128)S(1)} %subtract_multiply_fusion, f32[128,128,1,1]{1,0,3,2:T(8,128)S(1)} %copy-done.1), kind=kOutput, calls=%fused_computation.89 | convolution fusion | flops 402653184 | bytes 4259840 | tf_op jit(solution)/shard_map/dot_general | solution.py:48
  29.1 1.0 %fusion.67 = f32[2,16,128,128]{3,2,1,0:T(8,128)S(1)} fusion(f32[2,16,128,128]{3,2,1,0:T(8,128)S(1)} %subtract_multiply_fusion, f32[128,128,1,1]{1,0,3,2:T(8,128)S(1)} %copy-done), kind=kOutput, calls=%fused_computation.93 | convolution fusion | flops 402653184 | bytes 4259840 | tf_op jit(solution)/shard_map/dot_general | solution.py:48
  30.1 1.5 %fusion.12 = f32[2,16,128,256]{3,2,1,0:T(8,128)S(1)} fusion(f32[2,16,128,128]{3,2,1,0:T(8,128)S(1)} %fusion.63, f32[2,16,128,128]{3,2,1,0:T(8,128)S(1)} %fusion.65, s32[256]{0:T(256)S(1)} %get-tuple-element.14), kind=kOutput, calls=%fused_computation.14 | convolution fusion | flops 805863424 | bytes 8389632 | tf_op jit(solution)/shard_map/dot_general | solution.py:48
  31.6 2.2 %add_reduce_fusion = (f32[2,16,256]{2,1,0:T(8,128)S(1)}, f32[2,16,256]{2,1,0:T(8,128)S(1)}) fusion(f32[2,16,128,256]{3,2,1,0:T(8,128)S(1)} %fusion.12, f32[128,256]{1,0:T(8,128)S(1)} %get-tuple-element.17, f32[128,256]{1,0:T(8,128)S(1)} %get-tuple-element.16, s32[256]{0:T(256)S(1)} %get-tuple-element.14, f32[2,16,128,128]{3,2,1,0:T(8,128)S(1)} %fusion.66, ...), kind=kOutput, calls=%fused_computation.3 | convolution fusion | flops 814235648 | bytes 8717312 | tf_op jit(solution)/shard_map/dot_general | solution.py:48
  33.7 0.0 copy-start.3
  33.8 0.0 copy-start.4
  33.8 0.1 stack.13
  33.9 0.1 stack.14
  34.0 0.2 copy.64
  34.2 0.9 %reshape.132 = f32[8,1,2048]{2,1,0:T(1,128)} reshape(f32[128,2,2,32]{3,2,1,0:T(2,128)S(1)} %bitcast.80) | data formatting | bytes 131072
  35.2 3.4 %all-to-all-start.1 = ((f32[8,1,2048]{2,1,0:T(1,128)}), f32[8,1,2048]{2,1,0:T(1,128)S(1)}, u32[]{:S(2)}, u32[]{:S(2)}) async-start(f32[8,1,2048]{2,1,0:T(1,128)} %reshape.132), calls=%async_computation.1 | async-start | bytes 131072 | tf_op jit(solution)/shard_map/all_to_all | solution.py:109
  38.5 0.1 add_multiply_fusion.1
  38.6 6.8 %all-to-all-done.1 = f32[8,1,2048]{2,1,0:T(1,128)S(1)} async-done(((f32[8,1,2048]{2,1,0:T(1,128)}), f32[8,1,2048]{2,1,0:T(1,128)S(1)}, u32[]{:S(2)}, u32[]{:S(2)}) %all-to-all-start.1) | async-done | bytes 65568 | tf_op jit(solution)/shard_map/all_to_all | solution.py:109
  45.4 0.8 %reduce.2 = f32[8,2048]{1,0:T(8,128)S(1)} reduce(f32[8,1,2048]{2,1,0:T(1,128)S(1)} %all-to-all-done.1, f32[]{:T(128)} %broadcast.179), dimensions={1}, to_apply=%all_to_all.10.reduce_sub_computation | reduce | bytes 131076 | tf_op jit(solution)/shard_map/all_to_all | solution.py:109
  46.2 0.2 reshape.133
  46.4 0.0 copy-done.3
  46.4 0.0 copy-done.4
  46.5 0.4 fusion.61
  46.8 5.4 %all_gather.3 = bf16[2,8,32,128]{3,2,0,1:T(8,128)(2,1)S(1)} all-gather(bf16[2,2,32,128]{3,2,0,1:T(8,128)(2,1)S(1)} %get-tuple-element.18), channel_id=1, replica_groups=mesh['pw'=8,'band'=4] {'band'}, dimensions={1}, use_global_device_ids=true | all-gather | bytes 163840 | tf_op jit(solution)/shard_map/all_gather | solution.py:113
  52.2 0.1 copy.35
  52.4 4.5 %fusion.23 = f32[2,8,1,256]{3,1,0,2:T(8,128)S(1)} fusion(bf16[2,256,32,128]{3,2,1,0:T(8,128)(2,1)} %param.8, bf16[1,8,32,128]{3,1,0,2:T(8,128)(2,1)S(1)} %get-tuple-element.13, bf16[1,8,32,128]{3,1,0,2:T(8,128)(2,1)S(1)} %get-tuple-element.12, bf16[2,8,32,128]{3,1,0,2:T(8,128)(2,1)S(1)} %copy.35), kind=kOutput, calls=%fused_computation.29 | convolution fusion | flops 67895296 | bytes 4472832 | tf_op jit(solution)/shard_map/dot_general | solution.py:78
  56.9 0.6 copy.37
  57.5 3.3 %all-to-all-start.2 = ((f32[2,8,1,256]{3,0,2,1:T(2,128)}), f32[2,8,1,256]{3,0,2,1:T(2,128)S(1)}, u32[]{:S(2)}, u32[]{:S(2)}) async-start(f32[2,8,1,256]{3,0,2,1:T(2,128)} %copy.37), calls=%async_computation.2 | async-start | bytes 32768 | tf_op jit(solution)/shard_map/all_to_all | solution.py:83
  60.8 0.6 copy.38
  61.5 5.9 %all-to-all-done.2 = f32[2,8,1,256]{3,0,2,1:T(2,128)S(1)} async-done(((f32[2,8,1,256]{3,0,2,1:T(2,128)}), f32[2,8,1,256]{3,0,2,1:T(2,128)S(1)}, u32[]{:S(2)}, u32[]{:S(2)}) %all-to-all-start.2) | async-done | bytes 16416 | tf_op jit(solution)/shard_map/all_to_all | solution.py:83
  67.4 0.6 reduce_sum.36
  (10 shorter events, 0.3 us)
Async XLA Ops:
  0.6 11.1 %copy-start.5 = (s32[256]{0:T(256)S(1)}, s32[256]{0:T(256)}, u32[]{:S(2)}) copy-start(s32[256]{0:T(256)} %param.10) | copy-start | bytes 3076
  0.6 10.9 %copy-start.2 = (f32[16,128,128]{2,1,0:T(8,128)S(1)}, f32[16,128,128]{2,1,0:T(8,128)}, u32[]{:S(2)}) copy-start(f32[16,128,128]{2,1,0:T(8,128)} %param.9) | copy-start | bytes 3145732
  3.1 14.2 %all-to-all-start = ((f32[8,1,2048]{2,1,0:T(1,128)}), f32[8,1,2048]{2,1,0:T(1,128)S(1)}, u32[]{:S(2)}, u32[]{:S(2)}) async-start(f32[8,1,2048]{2,1,0:T(1,128)} %reshape.130), calls=%async_computation | async-start | bytes 131072 | tf_op jit(solution)/shard_map/all_to_all | solution.py:100
  20.5 1.4 %copy-start = (f32[128,128,1,1]{1,0,3,2:T(8,128)S(1)}, f32[128,128,1,1]{1,0,3,2:T(8,128)}, u32[]{:S(2)}) copy-start(f32[128,128,1,1]{1,0,3,2:T(8,128)} %constant.98) | copy-start | bytes 196612
  21.9 1.0 %copy-start.1 = (f32[128,128,1,1]{1,0,3,2:T(8,128)S(1)}, f32[128,128,1,1]{1,0,3,2:T(8,128)}, u32[]{:S(2)}) copy-start(f32[128,128,1,1]{1,0,3,2:T(8,128)} %constant.97) | copy-start | bytes 196612
  33.7 12.7 %copy-start.3 = (f32[2,2,128,128,1]{3,2,1,0,4:T(8,128)S(1)}, f32[2,2,128,128,1]{3,2,1,0,4:T(8,128)}, u32[]{:S(2)}) copy-start(f32[2,2,128,128,1]{3,2,1,0,4:T(8,128)} %constant.99) | copy-start | bytes 786436
  33.8 12.7 %copy-start.4 = (f32[2,2,32,128]{3,2,1,0:T(8,128)S(1)}, f32[2,2,32,128]{3,2,1,0:T(8,128)}, u32[]{:S(2)}) copy-start(f32[2,2,32,128]{3,2,1,0:T(8,128)} %param.7) | copy-start | bytes 196612
  35.2 10.2 %all-to-all-start.1 = ((f32[8,1,2048]{2,1,0:T(1,128)}), f32[8,1,2048]{2,1,0:T(1,128)S(1)}, u32[]{:S(2)}, u32[]{:S(2)}) async-start(f32[8,1,2048]{2,1,0:T(1,128)} %reshape.132), calls=%async_computation.1 | async-start | bytes 131072 | tf_op jit(solution)/shard_map/all_to_all | solution.py:109
  57.5 9.8 %all-to-all-start.2 = ((f32[2,8,1,256]{3,0,2,1:T(2,128)}), f32[2,8,1,256]{3,0,2,1:T(2,128)S(1)}, u32[]{:S(2)}, u32[]{:S(2)}) async-start(f32[2,8,1,256]{3,0,2,1:T(2,128)} %copy.37), calls=%async_computation.2 | async-start | bytes 32768 | tf_op jit(solution)/shard_map/all_to_all | solution.py:83

commit v5 on v4

--- a/solution.py
+++ b/solution.py
@@ -5,6 +5,8 @@
 import jax.numpy as jnp
 from jax import lax
 from jax.sharding import PartitionSpec as P
+from jax.experimental import pallas as pl
+from jax.experimental.pallas import tpu as pltpu
 
 
 def frequency(index, size):
@@ -71,6 +73,90 @@
     return jnp.stack([picked_re, picked_im])
 
 
+def split_bf16(value):
+    high = value.astype(jnp.bfloat16)
+    low = (value - high.astype(jnp.float32)).astype(jnp.bfloat16)
+    return high, low
+
+
+def dot_f32(left, right):
+    return jnp.dot(left, right, preferred_element_type=jnp.float32)
+
+
+def exact_select(value, table):
+    high, low = split_bf16(value)
+    return dot_f32(high, table) + dot_f32(low, table)
+
+
+def split_product(value, table_high, table_low):
+    high, low = split_bf16(value)
+    return dot_f32(high, table_high) + dot_f32(high, table_low) + dot_f32(low, table_high)
+
+
+def plane_kernel(amp_ref, pot_ref, pcos_ref, psin_ref, place_ref, pick_ref, thigh_ref, tlow_ref, out_ref):
+    count = amp_ref.shape[1]
+    planes = pot_ref.shape[0]
+    half = pcos_ref.shape[0]
+
+    def body(i, carry):
+        a_re = amp_ref[0, pl.ds(i, 1), :]
+        a_im = amp_ref[1, pl.ds(i, 1), :]
+        pc = pcos_ref[...]
+        ps = psin_ref[...]
+        spread = jnp.concatenate([a_re * pc - a_im * ps, a_re * ps + a_im * pc], axis=0)
+        rows = exact_select(spread, place_ref[...])
+        thigh = thigh_ref[...]
+        tlow = tlow_ref[...]
+        prod = split_product(rows, thigh, tlow)
+        pot = pot_ref[i % planes]
+        w_re = (prod[:half, :half] - prod[half:, half:]) * pot
+        w_im = (prod[:half, half:] + prod[half:, :half]) * pot
+        prod = split_product(jnp.concatenate([w_re, w_im], axis=0), thigh, tlow)
+        b_re = prod[:half, :half] + prod[half:, half:]
+        b_im = prod[half:, :half] - prod[:half, half:]
+        sel = exact_select(jnp.concatenate([b_re, b_im], axis=0), pick_ref[...])
+        s_re = sel[:half]
+        s_im = sel[half:]
+        out_ref[0, pl.ds(i, 1), :] = jnp.sum(s_re * pc + s_im * ps, axis=0, keepdims=True)
+        out_ref[1, pl.ds(i, 1), :] = jnp.sum(s_im * pc - s_re * ps, axis=0, keepdims=True)
+        return carry
+
+    lax.fori_loop(0, count, body, 0)
+
+
+def plane_phase_kernel(amp, pot, stick_col, grid_size):
+    bands, planes, sticks = amp.shape[1:]
+    phase_cos, phase_sin, place_cols, pick_cols = plane_tables(stick_col, grid_size)
+    inverse = dft_table(grid_size, 1.0)
+    table = jnp.concatenate([inverse[0, 0], inverse[1, 0]], axis=1)
+    t_high, t_low = split_bf16(table)
+    scaled_pot = pot / float(grid_size**3)
+    flat = amp.reshape(2, bands * planes, sticks)
+    vmem = pl.BlockSpec(memory_space=pltpu.VMEM)
+    per_plane = 2 * (2 * 2 * grid_size * sticks * grid_size) + 2 * (3 * 2 * 2 * grid_size * grid_size * 2 * grid_size)
+    out = pl.pallas_call(
+        plane_kernel,
+        out_shape=jax.ShapeDtypeStruct(flat.shape, jnp.float32),
+        in_specs=[vmem] * 8,
+        out_specs=vmem,
+        cost_estimate=pl.CostEstimate(
+            flops=per_plane * bands * planes,
+            transcendentals=0,
+            bytes_accessed=4 * (2 * flat.size + scaled_pot.size + 4 * grid_size * sticks),
+        ),
+    )(
+        flat,
+        scaled_pot,
+        phase_cos,
+        phase_sin,
+        place_cols.astype(jnp.bfloat16),
+        pick_cols.astype(jnp.bfloat16),
+        t_high,
+        t_low,
+    )
+    return out.reshape(2, bands, planes, sticks)
+
+
 def intersect(lowered, psi_all, pw_count):
     turned = jnp.stack([-lowered[1], lowered[0]])
     both = jnp.concatenate([lowered, turned], axis=1)
@@ -95,7 +181,6 @@
     kinetic = kinetic_table(my_columns, grid_size)
     inverse = dft_table(grid_size, 1.0)
     forward = dft_table(grid_size, -1.0)
-    tables = plane_tables(stick_col, grid_size)
     z_lines = jnp.einsum("dczk,cbsk->zdbs", inverse, psi_block, precision=fast)
     received = lax.all_to_all(z_lines, "pw", split_axis=0, concat_axis=0, tiled=True)
     lanes = received.shape[1:]
@@ -103,7 +188,7 @@
     amp = jnp.transpose(received, (2, 3, 1, 0, 4)).reshape(
         lanes[0], lanes[1], planes, pw_count * sticks_dev
     )
-    picked = plane_phase(amp, potential, tables, grid_size)
+    picked = plane_phase_kernel(amp, potential, stick_col, grid_size)
     outgoing = picked.reshape(lanes[0], lanes[1], planes, pw_count, sticks_dev)
     outgoing = jnp.transpose(outgoing, (3, 2, 0, 1, 4)).reshape((pw_count * planes,) + lanes)
     sticks_back = lax.all_to_all(outgoing, "pw", split_axis=0, concat_axis=0, tiled=True)

time: 68.4 us -> 92.8 us (1.36)
  Pallas kernels: 0 us -> 35.6 us
  matrix products: 20.6 us -> 6.11 us
  other arithmetic: 3.13 us -> 8.05 us
  waiting for transfers between devices: 18.1 us -> 13.3 us
  starting transfers between devices: 13.9 us -> 16 us
  local copies, waits for them, and re-layouts: 5.7 us -> 7 us
    pallas_call x0 -> x1, Pallas kernels: none -> 35.6 us  [plane_phase_kernel(): pl.pallas_call(plane_kernel, out_shape=jax.ShapeDtypeStruct(flat.shape, j...]
    dot_general x12 -> x0, matrix products: 14.4 us -> none  [mult(): jnp.dot(left, right, precision=lax.Precision.HIGH, preferred_element_type...]
    all_to_all x1, waiting for transfers between devices: 5.47 us -> 0.57 us  [per_device_rows(): lax.all_to_all(z_lines, 'pw', split_axis=0, concat_axis=0, tiled=True)]
    div x1, other arithmetic: 0.08 us -> 2.29 us  [plane_phase_kernel(): scaled_pot = pot / float(grid_size ** 3)]
    all_to_all x1, starting transfers between devices: 3.35 us -> 5.43 us  [per_device_rows(): lax.all_to_all(outgoing, 'pw', split_axis=0, concat_axis=0, tiled=True)]
    another operation x2 -> x3, local copies, waits for them, and re-layouts: 0.17 us -> 1.75 us  [the longest x2 1 us: per_device_rows(): outgoing = picked.reshape(lanes[0], lanes[1], planes, pw_count, sticks_dev)]
    convert_element_type x0 -> x2, other arithmetic: none -> 1.36 us  [the longest x1 0.72 us: plane_phase_kernel(): place_cols.astype(jnp.bfloat16)]
    sin x0 -> x1, other arithmetic: none -> 1.23 us  [plane_tables(): return (jnp.cos(phase_angles), jnp.sin(phase_angles), place_cols, pick_cols)]
  transfers between devices with their start and end apart: 3 -> 3, of which waited for: 3 -> 3; matrix products, arithmetic and copies ran while one was open for 3% -> 8% of each run, Pallas kernels for 0% -> 0%
where the time goes in v5:
time: 92.8 us; the launch traced here: 92.3 us
  Pallas kernels  35.6 us (38%)
  starting transfers between devices  16 us (17%)
  waiting for transfers between devices  13.3 us (14%)
  other arithmetic  8.05 us (9%)
  local copies, waits for them, and re-layouts  7 us (8%)
  matrix products  6.11 us (7%)
  blocking collectives  5.43 us (6%)
    pallas_call x1, Pallas kernels, plane_phase_kernel(): pl.pallas_call(plane_kernel, out_shape=jax.ShapeDtypeStruct(flat.shape, j...  35.6 us
    all_to_all x1, starting transfers between devices, per_device_rows(): lax.all_to_all(z_lines, 'pw', split_axis=0, concat_axis=0, tiled=True)  7.28 us
    all_to_all x1, waiting for transfers between devices, per_device_rows(): lax.all_to_all(outgoing, 'pw', split_axis=0, concat_axis=0, tiled=True)  6.83 us
    all_to_all x1, waiting for transfers between devices, intersect(): lax.all_to_all(pieces, 'pw', split_axis=1, concat_axis=1, tiled=True)  5.88 us
    all_to_all x1, starting transfers between devices, per_device_rows(): lax.all_to_all(outgoing, 'pw', split_axis=0, concat_axis=0, tiled=True)  5.43 us
    all_gather x1, blocking collectives, per_device_rows(): gathered = lax.all_gather(lowered, 'band', axis=1, tiled=True)  5.43 us
    dot_general x1, matrix products, intersect(): lax.dot_general(both, psi_all, dims, preferred_element_type=jnp.float32)  4.53 us
    all_to_all x1, starting transfers between devices, intersect(): lax.all_to_all(pieces, 'pw', split_axis=1, concat_axis=1, tiled=True)  3.31 us
  transfers between devices with their start and end apart: 3, of which 3 were waited for; matrix products, arithmetic and copies ran while one was open for 8% of the time, Pallas kernels for 0%

profile of v5, /device:TPU:0, one launch (start us, length us, event | category | flops | bytes accessed | tf_op | source)
XLA Modules:
  0.0 92.3 jit_solution(16144662996904270139)
XLA Ops:
  0.6 1.2 %convolution_bitcast_fusion = f32[128,2,2,32]{0,3,2,1:T(8,128)S(1)} fusion(f32[2,2,128,128,1]{3,2,1,4,0:T(8,128)} %constant.101, f32[2,2,32,128]{3,2,1,0:T(8,128)} %param.7), kind=kOutput, calls=%fused_computation.2 | convolution fusion | flops 25165824 | bytes 393216 | tf_op jit(solution)/shard_map/dczk,cbsk->zdbs/dot_general | solution.py:184
  1.9 0.2 copy.27
  2.1 0.9 reshape.61
  3.0 7.3 %all-to-all-start = ((f32[8,1,2048]{2,1,0:T(1,128)}), f32[8,1,2048]{2,1,0:T(1,128)S(1)}, u32[]{:S(2)}, u32[]{:S(2)}) async-start(f32[8,1,2048]{2,1,0:T(1,128)} %reshape.61), calls=%async_computation | async-start | bytes 131072 | tf_op jit(solution)/shard_map/all_to_all | solution.py:185
  10.2 0.7 and_select_fusion
  10.9 0.6 convert_convert_fusion.pick_ref
  11.6 0.7 convert_convert_fusion.1.place_ref
  12.3 1.2 %fusion.19 = (f32[128,256]{1,0:T(8,128)}, f32[128,256]{1,0:T(8,128)}) fusion(s32[256]{0:T(256)S(1)} %get-tuple-element.11), kind=kLoop, calls=%fused_computation.28 | loop fusion | flops 458752 | bytes 263168 | tf_op jit(solution)/shard_map/sin | solution.py:46
  13.5 2.3 %broadcast_multiply_fusion.pot_ref = f32[16,128,128]{2,1,0:T(8,128)} fusion(f32[16,128,128]{2,1,0:T(8,128)} %param.9), kind=kLoop, calls=%fused_computation.6 | loop fusion | flops 262144 | bytes 2097152 | tf_op jit(solution)/shard_map/div | solution.py:133
  15.8 0.8 fusion.24
  16.6 0.6 all-to-all-done
  17.1 0.5 broadcast.112
  17.7 0.8 reduce.1
  18.5 0.2 reshape.62
  18.7 0.1 copy.29
  18.8 0.8 reshape_reshape.9.amp_ref
  19.6 0.0 copy-start
  19.6 0.0 copy-start.1
  19.6 35.6 %shard_map.86 = f32[2,32,256]{2,1,0:T(8,128)} custom-call(f32[2,32,256]{2,1,0:T(8,128)} %reshape_reshape.9.amp_ref, f32[16,128,128]{2,1,0:T(8,128)} %broadcast_multiply_fusion.pot_ref, f32[128,256]{1,0:T(8,128)} %get-tuple-element.13.pcos_ref, f32[128,256]{1,0:T(8,128)} %get-tuple-element.12.psin_ref, bf16[256,128]{1,0:T(8,128)(2,1)} %convert_convert_fusion.1.place_ref, ...), custom_call_target="tpu_custom_call" | custom-call | flops 4294967296 | bytes 1703936 | tf_op jit(solution)/shard_map/pallas_call | solution.py:137
  55.2 0.9 %reshape_reshape.10 = f32[2,2,16,8,32]{4,3,2,1,0:T(8,128)S(1)} reshape(f32[2,32,256]{2,1,0:T(8,128)} %shard_map.86) | data formatting | bytes 131072 | tf_op jit(solution)/shard_map/reshape;reshape | solution.py:192
  56.2 0.2 copy.60
  56.4 0.9 reshape.63
  57.4 5.4 %all-to-all-start.1 = ((f32[8,1,2048]{2,1,0:T(1,128)}), f32[8,1,2048]{2,1,0:T(1,128)S(1)}, u32[]{:S(2)}, u32[]{:S(2)}) async-start(f32[8,1,2048]{2,1,0:T(1,128)} %reshape.63), calls=%async_computation.1 | async-start | bytes 131072 | tf_op jit(solution)/shard_map/all_to_all | solution.py:194
  62.8 0.1 add_multiply_fusion
  62.9 6.8 %all-to-all-done.1 = f32[8,1,2048]{2,1,0:T(1,128)S(1)} async-done(((f32[8,1,2048]{2,1,0:T(1,128)}), f32[8,1,2048]{2,1,0:T(1,128)S(1)}, u32[]{:S(2)}, u32[]{:S(2)}) %all-to-all-start.1) | async-done | bytes 65568 | tf_op jit(solution)/shard_map/all_to_all | solution.py:194
  69.7 0.8 reduce.2
  70.5 0.2 reshape.64
  70.8 0.0 copy-done
  70.8 0.0 copy-done.1
  70.8 0.4 fusion.30
  71.2 5.4 %all_gather.3 = bf16[2,8,32,128]{3,2,0,1:T(8,128)(2,1)S(1)} all-gather(bf16[2,2,32,128]{3,2,0,1:T(8,128)(2,1)S(1)} %get-tuple-element.14), channel_id=1, replica_groups=mesh['pw'=8,'band'=4] {'band'}, dimensions={1}, use_global_device_ids=true | all-gather | bytes 163840 | tf_op jit(solution)/shard_map/all_gather | solution.py:198
  76.6 0.1 copy.35
  76.7 4.5 %fusion.3 = f32[2,8,1,256]{3,1,0,2:T(8,128)S(1)} fusion(bf16[2,256,32,128]{3,2,1,0:T(8,128)(2,1)} %param.8, bf16[1,8,32,128]{3,1,0,2:T(8,128)(2,1)S(1)} %get-tuple-element.9, bf16[1,8,32,128]{3,1,0,2:T(8,128)(2,1)S(1)} %get-tuple-element.8, bf16[2,8,32,128]{3,1,0,2:T(8,128)(2,1)S(1)} %copy.35), kind=kOutput, calls=%fused_computation.5 | convolution fusion | flops 67895296 | bytes 4472832 | tf_op jit(solution)/shard_map/dot_general | solution.py:164
  81.2 0.6 copy.37
  81.8 3.3 %all-to-all-start.2 = ((f32[2,8,1,256]{3,0,2,1:T(2,128)}), f32[2,8,1,256]{3,0,2,1:T(2,128)S(1)}, u32[]{:S(2)}, u32[]{:S(2)}) async-start(f32[2,8,1,256]{3,0,2,1:T(2,128)} %copy.37), calls=%async_computation.2 | async-start | bytes 32768 | tf_op jit(solution)/shard_map/all_to_all | solution.py:169
  85.2 0.6 copy.38
  85.8 5.9 %all-to-all-done.2 = f32[2,8,1,256]{3,0,2,1:T(2,128)S(1)} async-done(((f32[2,8,1,256]{3,0,2,1:T(2,128)}), f32[2,8,1,256]{3,0,2,1:T(2,128)S(1)}, u32[]{:S(2)}, u32[]{:S(2)}) %all-to-all-start.2) | async-done | bytes 16416 | tf_op jit(solution)/shard_map/all_to_all | solution.py:169
  91.7 0.6 reduce_sum.16
  (6 shorter events, 0.1 us)
Async XLA Ops:
  3.0 14.2 %all-to-all-start = ((f32[8,1,2048]{2,1,0:T(1,128)}), f32[8,1,2048]{2,1,0:T(1,128)S(1)}, u32[]{:S(2)}, u32[]{:S(2)}) async-start(f32[8,1,2048]{2,1,0:T(1,128)} %reshape.61), calls=%async_computation | async-start | bytes 131072 | tf_op jit(solution)/shard_map/all_to_all | solution.py:185
  19.6 51.2 %copy-start = (f32[2,2,128,128,1]{3,2,1,0,4:T(8,128)S(1)}, f32[2,2,128,128,1]{3,2,1,0,4:T(8,128)}, u32[]{:S(2)}) copy-start(f32[2,2,128,128,1]{3,2,1,0,4:T(8,128)} %constant.102) | copy-start | bytes 786436
  19.6 51.2 %copy-start.1 = (f32[2,2,32,128]{3,2,1,0:T(8,128)S(1)}, f32[2,2,32,128]{3,2,1,0:T(8,128)}, u32[]{:S(2)}) copy-start(f32[2,2,32,128]{3,2,1,0:T(8,128)} %param.7) | copy-start | bytes 196612
  57.4 12.3 %all-to-all-start.1 = ((f32[8,1,2048]{2,1,0:T(1,128)}), f32[8,1,2048]{2,1,0:T(1,128)S(1)}, u32[]{:S(2)}, u32[]{:S(2)}) async-start(f32[8,1,2048]{2,1,0:T(1,128)} %reshape.63), calls=%async_computation.1 | async-start | bytes 131072 | tf_op jit(solution)/shard_map/all_to_all | solution.py:194
  81.8 9.8 %all-to-all-start.2 = ((f32[2,8,1,256]{3,0,2,1:T(2,128)}), f32[2,8,1,256]{3,0,2,1:T(2,128)S(1)}, u32[]{:S(2)}, u32[]{:S(2)}) async-start(f32[2,8,1,256]{3,0,2,1:T(2,128)} %copy.37), calls=%async_computation.2 | async-start | bytes 32768 | tf_op jit(solution)/shard_map/all_to_all | solution.py:169

commit v6 on v4

--- a/solution.py
+++ b/solution.py
@@ -60,10 +60,12 @@
     spread_im = val_re * phase_sin + val_im * phase_cos
     rows_re = mult(spread_re, place_cols)
     rows_im = mult(spread_im, place_cols)
-    wave_re = (mult(rows_re, cosine) - mult(rows_im, sine)) * scaled_pot
-    wave_im = (mult(rows_re, sine) + mult(rows_im, cosine)) * scaled_pot
-    back_re = mult(wave_re, cosine) + mult(wave_im, sine)
-    back_im = mult(wave_im, cosine) - mult(wave_re, sine)
+    shared = mult(rows_re + rows_im, cosine)
+    wave_re = (shared - mult(rows_im, cosine + sine)) * scaled_pot
+    wave_im = (shared + mult(rows_re, sine - cosine)) * scaled_pot
+    shared = mult(wave_re + wave_im, cosine)
+    back_re = shared - mult(wave_im, cosine - sine)
+    back_im = shared - mult(wave_re, sine + cosine)
     sel_re = mult(back_re, pick_cols)
     sel_im = mult(back_im, pick_cols)
     picked_re = jnp.sum(sel_re * phase_cos + sel_im * phase_sin, axis=2)

time: 68.4 us -> 66.5 us (0.972)
  matrix products: 20.6 us -> 18.7 us
    dot_general x12 -> x10, matrix products: 14.4 us -> 12.5 us  [mult(): jnp.dot(left, right, precision=lax.Precision.HIGH, preferred_element_type...]
    unnamed x17 -> x21, local copies, waits for them, and re-layouts: 2.96 us -> 2.98 us
where the time goes in v6:
time: 66.5 us; the launch traced here: 66 us
  matrix products  18.7 us (28%)
  waiting for transfers between devices  18.1 us (27%)
  starting transfers between devices  14 us (21%)
  local copies, waits for them, and re-layouts  5.72 us (9%)
  blocking collectives  5.43 us (8%)
  other arithmetic  3.13 us (5%)
  between operations  1.01 us (2%)
    dot_general x10, matrix products, mult(): jnp.dot(left, right, precision=lax.Precision.HIGH, preferred_element_type...  12.5 us
    all_to_all x1, starting transfers between devices, per_device_rows(): lax.all_to_all(z_lines, 'pw', split_axis=0, concat_axis=0, tiled=True)  7.28 us
    all_to_all x1, waiting for transfers between devices, per_device_rows(): lax.all_to_all(outgoing, 'pw', split_axis=0, concat_axis=0, tiled=True)  6.77 us
    all_to_all x1, waiting for transfers between devices, intersect(): lax.all_to_all(pieces, 'pw', split_axis=1, concat_axis=1, tiled=True)  5.88 us
    all_to_all x1, waiting for transfers between devices, per_device_rows(): lax.all_to_all(z_lines, 'pw', split_axis=0, concat_axis=0, tiled=True)  5.47 us
    all_gather x1, blocking collectives, per_device_rows(): gathered = lax.all_gather(lowered, 'band', axis=1, tiled=True)  5.43 us
    dot_general x1, matrix products, intersect(): lax.dot_general(both, psi_all, dims, preferred_element_type=jnp.float32)  4.5 us
    all_to_all x1, starting transfers between devices, per_device_rows(): lax.all_to_all(outgoing, 'pw', split_axis=0, concat_axis=0, tiled=True)  3.35 us
  transfers between devices with their start and end apart: 3, of which 3 were waited for; matrix products, arithmetic and copies ran while one was open for 3% of the time, Pallas kernels for 0%

profile of v6, /device:TPU:0, one launch (start us, length us, event | category | flops | bytes accessed | tf_op | source)
XLA Modules:
  0.0 66.0 jit_solution(8240100198775211149)
XLA Ops:
  0.6 0.0 copy-start.7
  0.6 0.0 copy-start
  0.7 1.3 %convolution_bitcast_fusion = f32[128,2,2,32]{0,3,2,1:T(8,128)S(1)} fusion(f32[2,2,128,128,1]{3,2,1,4,0:T(8,128)} %constant.99, f32[2,2,32,128]{3,2,1,0:T(8,128)} %param.7), kind=kOutput, calls=%fused_computation.30 | convolution fusion | flops 25165824 | bytes 393216 | tf_op jit(solution)/shard_map/dczk,cbsk->zdbs/dot_general | solution.py:101
  2.0 0.2 copy.26
  2.2 0.9 %reshape.132 = f32[8,1,2048]{2,1,0:T(1,128)} reshape(f32[128,2,2,32]{3,2,1,0:T(2,128)S(1)} %copy.26) | data formatting | bytes 131072
  3.1 7.3 %all-to-all-start = ((f32[8,1,2048]{2,1,0:T(1,128)}), f32[8,1,2048]{2,1,0:T(1,128)S(1)}, u32[]{:S(2)}, u32[]{:S(2)}) async-start(f32[8,1,2048]{2,1,0:T(1,128)} %reshape.132), calls=%async_computation | async-start | bytes 131072 | tf_op jit(solution)/shard_map/all_to_all | solution.py:102
  10.4 0.7 %and_select_fusion = (s32[256]{0:T(256)S(1)}, s32[256]{0:T(256)S(1)}) fusion(s32[256]{0:T(256)} %param.10), kind=kLoop, calls=%fused_computation.68 | loop fusion | flops 4864 | bytes 3072 | tf_op jit(solution)/shard_map/jit(remainder)/select_n | solution.py:35
  11.0 0.5 fusion.54
  11.6 0.0 copy-done
  11.6 0.1 broadcast_multiply_fusion
  11.7 0.0 copy-done.7
  11.7 0.1 fusion.58
  11.8 5.5 %all-to-all-done = f32[8,1,2048]{2,1,0:T(1,128)S(1)} async-done(((f32[8,1,2048]{2,1,0:T(1,128)}), f32[8,1,2048]{2,1,0:T(1,128)S(1)}, u32[]{:S(2)}, u32[]{:S(2)}) %all-to-all-start) | async-done | bytes 65568 | tf_op jit(solution)/shard_map/all_to_all | solution.py:102
  17.3 0.5 broadcast.179
  17.8 0.8 %reduce.1 = f32[8,2048]{1,0:T(8,128)S(1)} reduce(f32[8,1,2048]{2,1,0:T(1,128)S(1)} %all-to-all-done, f32[]{:T(128)} %broadcast.179), dimensions={1}, to_apply=%all_to_all.9.reduce_sub_computation | reduce | bytes 131076 | tf_op jit(solution)/shard_map/all_to_all | solution.py:102
  18.6 0.2 reshape.133
  18.9 0.1 mul.155
  19.1 0.1 mul.164
  19.2 1.3 %fusion.2 = f32[2,16,128,128]{3,2,1,0:T(8,128)S(1)} fusion(f32[128,256]{1,0:T(8,128)S(1)} %get-tuple-element.17, f32[2,16,256]{2,1,0:T(8,128)S(1)} %mul.164, f32[128,256]{1,0:T(8,128)S(1)} %get-tuple-element.16, f32[2,16,256]{2,1,0:T(8,128)S(1)} %mul.155, s32[256]{0:T(256)S(1)} %get-tuple-element.14), kind=kOutput, calls=%fused_computation.4 | convolution fusion | flops 808484864 | bytes 2425856 | tf_op jit(solution)/shard_map/dot_general | solution.py:48
  20.5 0.0 copy-start.1
  20.5 1.3 %fusion.6 = f32[2,16,128,128]{3,2,1,0:T(8,128)S(1)} fusion(f32[128,256]{1,0:T(8,128)S(1)} %get-tuple-element.17, f32[2,16,256]{2,1,0:T(8,128)S(1)} %mul.164, f32[128,256]{1,0:T(8,128)S(1)} %get-tuple-element.16, f32[2,16,256]{2,1,0:T(8,128)S(1)} %mul.155, s32[256]{0:T(256)S(1)} %get-tuple-element.14), kind=kOutput, calls=%fused_computation.8 | convolution fusion | flops 808484864 | bytes 2425856 | tf_op jit(solution)/shard_map/dot_general | solution.py:48
  21.9 0.0 copy-done.1
  21.9 0.0 copy-start.6
  21.9 1.0 %fusion.16 = f32[2,16,128,128]{3,2,1,0:T(8,128)S(1)} fusion(f32[128,128,1,1]{1,0,3,2:T(8,128)S(1)} %copy-done.1, f32[2,16,128,128]{3,2,1,0:T(8,128)S(1)} %fusion.6, f32[2,16,128,128]{3,2,1,0:T(8,128)S(1)} %fusion.2), kind=kOutput, calls=%fused_computation.20 | convolution fusion | flops 403177472 | bytes 6356992 | tf_op jit(solution)/shard_map/dot_general | solution.py:48
  22.9 0.0 copy-done.6
  22.9 0.0 copy-start.2
  22.9 1.1 %add_multiply_fusion = f32[2,16,128,128]{3,2,1,0:T(8,128)S(1)} fusion(f32[2,16,128,128]{3,2,1,0:T(8,128)S(1)} %fusion.16, f32[2,16,128,128]{3,2,1,0:T(8,128)S(1)} %fusion.6, f32[128,128,1,1]{1,0,3,2:T(8,128)S(1)} %copy-done.6, f32[16,128,128]{2,1,0:T(8,128)S(1)} %broadcast_multiply_fusion), kind=kOutput, calls=%fused_computation.18 | convolution fusion | flops 403701760 | bytes 7405568 | tf_op jit(solution)/shard_map/dot_general | solution.py:48
  24.0 0.0 copy-done.2
  24.0 1.1 %subtract_multiply_fusion = f32[2,16,128,128]{3,2,1,0:T(8,128)S(1)} fusion(f32[2,16,128,128]{3,2,1,0:T(8,128)S(1)} %fusion.16, f32[2,16,128,128]{3,2,1,0:T(8,128)S(1)} %fusion.2, f32[128,128,1,1]{1,0,3,2:T(8,128)S(1)} %copy-done.2, f32[16,128,128]{2,1,0:T(8,128)S(1)} %broadcast_multiply_fusion), kind=kOutput, calls=%fused_computation.19 | convolution fusion | flops 403701760 | bytes 7405568 | tf_op jit(solution)/shard_map/dot_general | solution.py:48
  25.1 1.0 %fusion.67 = f32[2,16,128,128]{3,2,1,0:T(8,128)S(1)} fusion(f32[2,16,128,128]{3,2,1,0:T(8,128)S(1)} %subtract_multiply_fusion, f32[128,128,1,1]{1,0,3,2:T(8,128)S(1)} %copy-done.2), kind=kOutput, calls=%fused_computation.93 | convolution fusion | flops 402653184 | bytes 4259840 | tf_op jit(solution)/shard_map/dot_general | solution.py:48
  26.1 0.0 copy-start.5
  26.1 1.0 %fusion.14 = f32[2,16,128,128]{3,2,1,0:T(8,128)S(1)} fusion(f32[128,128,1,1]{1,0,3,2:T(8,128)S(1)} %copy-done.1, f32[2,16,128,128]{3,2,1,0:T(8,128)S(1)} %subtract_multiply_fusion, f32[2,16,128,128]{3,2,1,0:T(8,128)S(1)} %add_multiply_fusion), kind=kOutput, calls=%fused_computation.16 | convolution fusion | flops 403177472 | bytes 6356992 | tf_op jit(solution)/shard_map/dot_general | solution.py:48
  27.1 0.0 copy-done.5
  27.1 1.0 %fusion.66 = f32[2,16,128,128]{3,2,1,0:T(8,128)S(1)} fusion(f32[2,16,128,128]{3,2,1,0:T(8,128)S(1)} %add_multiply_fusion, f32[128,128,1,1]{1,0,3,2:T(8,128)S(1)} %copy-done.5), kind=kOutput, calls=%fused_computation.92 | convolution fusion | flops 402653184 | bytes 4259840 | tf_op jit(solution)/shard_map/dot_general | solution.py:48
  28.2 1.3 %fusion.12 = f32[2,16,128,256]{3,2,1,0:T(8,128)S(1)} fusion(f32[2,16,128,128]{3,2,1,0:T(8,128)S(1)} %fusion.14, f32[2,16,128,128]{3,2,1,0:T(8,128)S(1)} %fusion.66, s32[256]{0:T(256)S(1)} %get-tuple-element.14), kind=kOutput, calls=%fused_computation.14 | convolution fusion | flops 805863424 | bytes 8389632 | tf_op jit(solution)/shard_map/dot_general | solution.py:48
  29.4 2.4 %add_reduce_fusion = (f32[2,16,256]{2,1,0:T(8,128)S(1)}, f32[2,16,256]{2,1,0:T(8,128)S(1)}) fusion(f32[2,16,128,256]{3,2,1,0:T(8,128)S(1)} %fusion.12, f32[128,256]{1,0:T(8,128)S(1)} %get-tuple-element.17, f32[128,256]{1,0:T(8,128)S(1)} %get-tuple-element.16, s32[256]{0:T(256)S(1)} %get-tuple-element.14, f32[2,16,128,128]{3,2,1,0:T(8,128)S(1)} %fusion.14, ...), kind=kOutput, calls=%fused_computation.3 | convolution fusion | flops 814235648 | bytes 8717312 | tf_op jit(solution)/shard_map/dot_general | solution.py:48
  31.8 0.0 copy-start.3
  31.8 0.0 copy-start.4
  31.9 0.1 stack.13
  31.9 0.1 stack.14
  32.1 0.2 copy.66
  32.3 0.9 %reshape.134 = f32[8,1,2048]{2,1,0:T(1,128)} reshape(f32[128,2,2,32]{3,2,1,0:T(2,128)S(1)} %bitcast.80) | data formatting | bytes 131072
  33.2 3.4 %all-to-all-start.1 = ((f32[8,1,2048]{2,1,0:T(1,128)}), f32[8,1,2048]{2,1,0:T(1,128)S(1)}, u32[]{:S(2)}, u32[]{:S(2)}) async-start(f32[8,1,2048]{2,1,0:T(1,128)} %reshape.134), calls=%async_computation.1 | async-start | bytes 131072 | tf_op jit(solution)/shard_map/all_to_all | solution.py:111
  36.6 0.1 add_multiply_fusion.1
  36.7 6.8 %all-to-all-done.1 = f32[8,1,2048]{2,1,0:T(1,128)S(1)} async-done(((f32[8,1,2048]{2,1,0:T(1,128)}), f32[8,1,2048]{2,1,0:T(1,128)S(1)}, u32[]{:S(2)}, u32[]{:S(2)}) %all-to-all-start.1) | async-done | bytes 65568 | tf_op jit(solution)/shard_map/all_to_all | solution.py:111
  43.4 0.8 %reduce.2 = f32[8,2048]{1,0:T(8,128)S(1)} reduce(f32[8,1,2048]{2,1,0:T(1,128)S(1)} %all-to-all-done.1, f32[]{:T(128)} %broadcast.179), dimensions={1}, to_apply=%all_to_all.10.reduce_sub_computation | reduce | bytes 131076 | tf_op jit(solution)/shard_map/all_to_all | solution.py:111
  44.3 0.2 reshape.135
  44.5 0.0 copy-done.3
  44.5 0.0 copy-done.4
  44.5 0.4 fusion.65
  44.9 5.4 %all_gather.3 = bf16[2,8,32,128]{3,2,0,1:T(8,128)(2,1)S(1)} all-gather(bf16[2,2,32,128]{3,2,0,1:T(8,128)(2,1)S(1)} %get-tuple-element.18), channel_id=1, replica_groups=mesh['pw'=8,'band'=4] {'band'}, dimensions={1}, use_global_device_ids=true | all-gather | bytes 163840 | tf_op jit(solution)/shard_map/all_gather | solution.py:115
  50.3 0.1 copy.35
  50.5 4.5 %fusion.27 = f32[2,8,1,256]{3,1,0,2:T(8,128)S(1)} fusion(bf16[2,256,32,128]{3,2,1,0:T(8,128)(2,1)} %param.8, bf16[1,8,32,128]{3,1,0,2:T(8,128)(2,1)S(1)} %get-tuple-element.13, bf16[1,8,32,128]{3,1,0,2:T(8,128)(2,1)S(1)} %get-tuple-element.12, bf16[2,8,32,128]{3,1,0,2:T(8,128)(2,1)S(1)} %copy.35), kind=kOutput, calls=%fused_computation.33 | convolution fusion | flops 67895296 | bytes 4472832 | tf_op jit(solution)/shard_map/dot_general | solution.py:80
  55.0 0.6 copy.37
  55.6 3.3 %all-to-all-start.2 = ((f32[2,8,1,256]{3,0,2,1:T(2,128)}), f32[2,8,1,256]{3,0,2,1:T(2,128)S(1)}, u32[]{:S(2)}, u32[]{:S(2)}) async-start(f32[2,8,1,256]{3,0,2,1:T(2,128)} %copy.37), calls=%async_computation.2 | async-start | bytes 32768 | tf_op jit(solution)/shard_map/all_to_all | solution.py:85
  58.9 0.6 copy.38
  59.5 5.9 %all-to-all-done.2 = f32[2,8,1,256]{3,0,2,1:T(2,128)S(1)} async-done(((f32[2,8,1,256]{3,0,2,1:T(2,128)}), f32[2,8,1,256]{3,0,2,1:T(2,128)S(1)}, u32[]{:S(2)}, u32[]{:S(2)}) %all-to-all-start.2) | async-done | bytes 16416 | tf_op jit(solution)/shard_map/all_to_all | solution.py:85
  65.4 0.6 reduce_sum.36
  (10 shorter events, 0.3 us)
Async XLA Ops:
  0.6 11.1 %copy-start.7 = (s32[256]{0:T(256)S(1)}, s32[256]{0:T(256)}, u32[]{:S(2)}) copy-start(s32[256]{0:T(256)} %param.10) | copy-start | bytes 3076
  0.6 10.9 %copy-start = (f32[16,128,128]{2,1,0:T(8,128)S(1)}, f32[16,128,128]{2,1,0:T(8,128)}, u32[]{:S(2)}) copy-start(f32[16,128,128]{2,1,0:T(8,128)} %param.9) | copy-start | bytes 3145732
  3.1 14.2 %all-to-all-start = ((f32[8,1,2048]{2,1,0:T(1,128)}), f32[8,1,2048]{2,1,0:T(1,128)S(1)}, u32[]{:S(2)}, u32[]{:S(2)}) async-start(f32[8,1,2048]{2,1,0:T(1,128)} %reshape.132), calls=%async_computation | async-start | bytes 131072 | tf_op jit(solution)/shard_map/all_to_all | solution.py:102
  20.5 1.4 %copy-start.1 = (f32[128,128,1,1]{1,0,3,2:T(8,128)S(1)}, f32[128,128,1,1]{1,0,3,2:T(8,128)}, u32[]{:S(2)}) copy-start(f32[128,128,1,1]{1,0,3,2:T(8,128)} %constant.100) | copy-start | bytes 196612
  21.9 1.0 %copy-start.6 = (f32[128,128,1,1]{1,0,3,2:T(8,128)S(1)}, f32[128,128,1,1]{1,0,3,2:T(8,128)}, u32[]{:S(2)}) copy-start(f32[128,128,1,1]{1,0,3,2:T(8,128)} %constant.102) | copy-start | bytes 196612
  22.9 1.1 %copy-start.2 = (f32[128,128,1,1]{1,0,3,2:T(8,128)S(1)}, f32[128,128,1,1]{1,0,3,2:T(8,128)}, u32[]{:S(2)}) copy-start(f32[128,128,1,1]{1,0,3,2:T(8,128)} %constant.101) | copy-start | bytes 196612
  26.1 1.0 %copy-start.5 = (f32[128,128,1,1]{1,0,3,2:T(8,128)S(1)}, f32[128,128,1,1]{1,0,3,2:T(8,128)}, u32[]{:S(2)}) copy-start(f32[128,128,1,1]{1,0,3,2:T(8,128)} %constant.103) | copy-start | bytes 196612
  31.8 12.7 %copy-start.3 = (f32[2,2,128,128,1]{3,2,1,0,4:T(8,128)S(1)}, f32[2,2,128,128,1]{3,2,1,0,4:T(8,128)}, u32[]{:S(2)}) copy-start(f32[2,2,128,128,1]{3,2,1,0,4:T(8,128)} %constant.104) | copy-start | bytes 786436
  31.8 12.7 %copy-start.4 = (f32[2,2,32,128]{3,2,1,0:T(8,128)S(1)}, f32[2,2,32,128]{3,2,1,0:T(8,128)}, u32[]{:S(2)}) copy-start(f32[2,2,32,128]{3,2,1,0:T(8,128)} %param.7) | copy-start | bytes 196612
  33.2 10.2 %all-to-all-start.1 = ((f32[8,1,2048]{2,1,0:T(1,128)}), f32[8,1,2048]{2,1,0:T(1,128)S(1)}, u32[]{:S(2)}, u32[]{:S(2)}) async-start(f32[8,1,2048]{2,1,0:T(1,128)} %reshape.134), calls=%async_computation.1 | async-start | bytes 131072 | tf_op jit(solution)/shard_map/all_to_all | solution.py:111
  55.6 9.9 %all-to-all-start.2 = ((f32[2,8,1,256]{3,0,2,1:T(2,128)}), f32[2,8,1,256]{3,0,2,1:T(2,128)S(1)}, u32[]{:S(2)}, u32[]{:S(2)}) async-start(f32[2,8,1,256]{3,0,2,1:T(2,128)} %copy.37), calls=%async_computation.2 | async-start | bytes 32768 | tf_op jit(solution)/shard_map/all_to_all | solution.py:85

commit v7 on v6

--- a/solution.py
+++ b/solution.py
@@ -77,8 +77,22 @@
     turned = jnp.stack([-lowered[1], lowered[0]])
     both = jnp.concatenate([lowered, turned], axis=1)
     dims = (((2, 3), (2, 3)), ((0,), (0,)))
-    partial_value = lax.dot_general(both, psi_all, dims, preferred_element_type=jnp.float32)
-    partial_value = jnp.sum(partial_value, axis=0)
+    width = psi_all.shape[1] // 4
+    partial_value = jnp.concatenate(
+        [
+            jnp.sum(
+                lax.dot_general(
+                    both,
+                    psi_all[:, k * width : (k + 1) * width],
+                    dims,
+                    preferred_element_type=jnp.float32,
+                ),
+                axis=0,
+            )
+            for k in range(4)
+        ],
+        axis=-1,
+    )
     partial_value = partial_value.reshape(2, lowered.shape[1], partial_value.shape[-1])
     rows_dev = partial_value.shape[1] // pw_count
     pieces = partial_value.reshape(2, pw_count, rows_dev, partial_value.shape[-1])

time: 66.5 us -> 66 us (level)
  local copies, waits for them, and re-layouts: 5.72 us -> 10.1 us
  waiting for transfers between devices: 18.1 us -> 14 us
  matrix products: 18.7 us -> 16.5 us
  starting transfers between devices: 14 us -> 15.3 us
    slice x0 -> x1, local copies, waits for them, and re-layouts: none -> 4.13 us  [intersect(): psi_all[:, k * width:(k + 1) * width]]
    all_to_all x1, waiting for transfers between devices: 5.47 us -> 1.34 us  [per_device_rows(): lax.all_to_all(z_lines, 'pw', split_axis=0, concat_axis=0, tiled=True)]
    dot_general x1 -> x4, matrix products: 4.5 us -> 1.72 us  [intersect(): lax.dot_general(both, psi_all[:, k * width:(k + 1) * width], dims, prefer...]
    all_to_all x1, starting transfers between devices: 3.35 us -> 4.67 us  [per_device_rows(): lax.all_to_all(outgoing, 'pw', split_axis=0, concat_axis=0, tiled=True)]
    dot_general x1, matrix products: 0.36 us -> 1.31 us  [per_device_rows(): vpsi = jnp.einsum('dckz,zcbs->dbsk', forward, sticks_back, precision=fast)]
    unnamed x21 -> x25, local copies, waits for them, and re-layouts: 2.98 us -> 3.2 us
  transfers between devices with their start and end apart: 3 -> 3, of which waited for: 3 -> 3; matrix products, arithmetic and copies ran while one was open for 3% -> 10% of each run, Pallas kernels for 0% -> 0%
where the time goes in v7:
time: 66 us; the launch traced here: 65.5 us
  matrix products  16.5 us (25%)
  starting transfers between devices  15.3 us (23%)
  waiting for transfers between devices  14 us (21%)
  local copies, waits for them, and re-layouts  10.1 us (15%)
  blocking collectives  5.43 us (8%)
  other arithmetic  3.21 us (5%)
  between operations  1 us (2%)
    dot_general x10, matrix products, mult(): jnp.dot(left, right, precision=lax.Precision.HIGH, preferred_element_type...  12.1 us
    all_to_all x1, starting transfers between devices, per_device_rows(): lax.all_to_all(z_lines, 'pw', split_axis=0, concat_axis=0, tiled=True)  7.28 us
    all_to_all x1, waiting for transfers between devices, per_device_rows(): lax.all_to_all(outgoing, 'pw', split_axis=0, concat_axis=0, tiled=True)  6.83 us
    all_to_all x1, waiting for transfers between devices, intersect(): lax.all_to_all(pieces, 'pw', split_axis=1, concat_axis=1, tiled=True)  5.88 us
    all_gather x1, blocking collectives, per_device_rows(): gathered = lax.all_gather(lowered, 'band', axis=1, tiled=True)  5.43 us
    all_to_all x1, starting transfers between devices, per_device_rows(): lax.all_to_all(outgoing, 'pw', split_axis=0, concat_axis=0, tiled=True)  4.67 us
    slice x1, local copies, waits for them, and re-layouts, intersect(): psi_all[:, k * width:(k + 1) * width]  4.13 us
    all_to_all x1, starting transfers between devices, intersect(): lax.all_to_all(pieces, 'pw', split_axis=1, concat_axis=1, tiled=True)  3.34 us
  transfers between devices with their start and end apart: 3, of which 3 were waited for; matrix products, arithmetic and copies ran while one was open for 10% of the time, Pallas kernels for 0%

profile of v7, /device:TPU:0, one launch (start us, length us, event | category | flops | bytes accessed | tf_op | source)
XLA Modules:
  0.0 65.5 jit_solution(15762398272243328260)
XLA Ops:
  0.6 0.0 copy-start
  0.6 1.3 %convolution_bitcast_fusion = f32[128,2,2,32]{0,3,2,1:T(8,128)S(1)} fusion(f32[2,2,128,128,1]{3,2,1,4,0:T(8,128)} %constant.99, f32[2,2,32,128]{3,2,1,0:T(8,128)} %param.7), kind=kOutput, calls=%fused_computation.28 | convolution fusion | flops 25165824 | bytes 393216 | tf_op jit(solution)/shard_map/dczk,cbsk->zdbs/dot_general | solution.py:115
  2.0 0.2 copy.38
  2.2 0.9 %reshape.135 = f32[8,1,2048]{2,1,0:T(1,128)} reshape(f32[128,2,2,32]{3,2,1,0:T(2,128)S(1)} %copy.38) | data formatting | bytes 131072
  3.1 7.3 %all-to-all-start = ((f32[8,1,2048]{2,1,0:T(1,128)}), f32[8,1,2048]{2,1,0:T(1,128)S(1)}, u32[]{:S(2)}, u32[]{:S(2)}) async-start(f32[8,1,2048]{2,1,0:T(1,128)} %reshape.135), calls=%async_computation | async-start | bytes 131072 | tf_op jit(solution)/shard_map/all_to_all | solution.py:116
  10.3 0.7 %and_select_fusion = (s32[256]{0:T(256)S(1)}, s32[256]{0:T(256)S(1)}) fusion(s32[256]{0:T(256)} %param.10), kind=kLoop, calls=%fused_computation.70 | loop fusion | flops 4864 | bytes 3072 | tf_op jit(solution)/shard_map/jit(remainder)/select_n | solution.py:35
  11.0 0.5 fusion.48
  11.6 0.0 copy-done
  11.6 0.1 broadcast_multiply_fusion
  11.7 0.0 copy-start.9
  11.7 4.1 %fusion.57 = (bf16[2,64,32,128]{3,2,1,0:T(8,128)(2,1)}, bf16[2,64,32,128]{3,2,1,0:T(8,128)(2,1)}, bf16[2,64,32,128]{3,2,1,0:T(8,128)(2,1)}, bf16[2,64,32,128]{3,2,1,0:T(8,128)(2,1)S(1)}) fusion(bf16[2,256,32,128]{3,2,1,0:T(8,128)(2,1)} %param.8), kind=kLoop, calls=%fused_computation.89 | loop fusion | bytes 8388608 | tf_op jit(solution)/shard_map/slice | solution.py:86
  15.8 0.0 copy-done.9
  15.8 0.1 fusion.52
  15.9 1.3 %all-to-all-done = f32[8,1,2048]{2,1,0:T(1,128)S(1)} async-done(((f32[8,1,2048]{2,1,0:T(1,128)}), f32[8,1,2048]{2,1,0:T(1,128)S(1)}, u32[]{:S(2)}, u32[]{:S(2)}) %all-to-all-start) | async-done | bytes 65568 | tf_op jit(solution)/shard_map/all_to_all | solution.py:116
  17.2 0.5 broadcast.179
  17.8 0.8 %reduce.1 = f32[8,2048]{1,0:T(8,128)S(1)} reduce(f32[8,1,2048]{2,1,0:T(1,128)S(1)} %all-to-all-done, f32[]{:T(128)} %broadcast.179), dimensions={1}, to_apply=%all_to_all.9.reduce_sub_computation | reduce | bytes 131076 | tf_op jit(solution)/shard_map/all_to_all | solution.py:116
  18.6 0.2 reshape.136
  18.9 0.1 mul.155
  19.1 0.1 mul.164
  19.2 1.3 %fusion = f32[2,16,128,128]{3,2,1,0:T(8,128)S(1)} fusion(f32[128,256]{1,0:T(8,128)S(1)} %get-tuple-element.21, f32[2,16,256]{2,1,0:T(8,128)S(1)} %mul.164, f32[128,256]{1,0:T(8,128)S(1)} %get-tuple-element.20, f32[2,16,256]{2,1,0:T(8,128)S(1)} %mul.155, s32[256]{0:T(256)S(1)} %get-tuple-element.18), kind=kOutput, calls=%fused_computation.2 | convolution fusion | flops 808484864 | bytes 2425856 | tf_op jit(solution)/shard_map/dot_general | solution.py:48
  20.5 0.0 copy-start.4
  20.5 1.3 %fusion.4 = f32[2,16,128,128]{3,2,1,0:T(8,128)S(1)} fusion(f32[128,256]{1,0:T(8,128)S(1)} %get-tuple-element.21, f32[2,16,256]{2,1,0:T(8,128)S(1)} %mul.164, f32[128,256]{1,0:T(8,128)S(1)} %get-tuple-element.20, f32[2,16,256]{2,1,0:T(8,128)S(1)} %mul.155, s32[256]{0:T(256)S(1)} %get-tuple-element.18), kind=kOutput, calls=%fused_computation.6 | convolution fusion | flops 808484864 | bytes 2425856 | tf_op jit(solution)/shard_map/dot_general | solution.py:48
  21.9 0.0 copy-done.4
  21.9 0.0 copy-start.8
  21.9 1.0 %fusion.14 = f32[2,16,128,128]{3,2,1,0:T(8,128)S(1)} fusion(f32[128,128,1,1]{1,0,3,2:T(8,128)S(1)} %copy-done.4, f32[2,16,128,128]{3,2,1,0:T(8,128)S(1)} %fusion.4, f32[2,16,128,128]{3,2,1,0:T(8,128)S(1)} %fusion), kind=kOutput, calls=%fused_computation.18 | convolution fusion | flops 403177472 | bytes 6356992 | tf_op jit(solution)/shard_map/dot_general | solution.py:48
  22.9 0.0 copy-done.8
  22.9 0.0 copy-start.5
  22.9 1.0 %add_multiply_fusion = f32[2,16,128,128]{3,2,1,0:T(8,128)S(1)} fusion(f32[2,16,128,128]{3,2,1,0:T(8,128)S(1)} %fusion.14, f32[2,16,128,128]{3,2,1,0:T(8,128)S(1)} %fusion.4, f32[128,128,1,1]{1,0,3,2:T(8,128)S(1)} %copy-done.8, f32[16,128,128]{2,1,0:T(8,128)S(1)} %broadcast_multiply_fusion), kind=kOutput, calls=%fused_computation.16 | convolution fusion | flops 403701760 | bytes 7405568 | tf_op jit(solution)/shard_map/dot_general | solution.py:48
  23.9 0.0 copy-done.5
  23.9 1.1 %subtract_multiply_fusion = f32[2,16,128,128]{3,2,1,0:T(8,128)S(1)} fusion(f32[2,16,128,128]{3,2,1,0:T(8,128)S(1)} %fusion.14, f32[2,16,128,128]{3,2,1,0:T(8,128)S(1)} %fusion, f32[128,128,1,1]{1,0,3,2:T(8,128)S(1)} %copy-done.5, f32[16,128,128]{2,1,0:T(8,128)S(1)} %broadcast_multiply_fusion), kind=kOutput, calls=%fused_computation.17 | convolution fusion | flops 403701760 | bytes 7405568 | tf_op jit(solution)/shard_map/dot_general | solution.py:48
  25.0 1.0 %fusion.61 = f32[2,16,128,128]{3,2,1,0:T(8,128)S(1)} fusion(f32[2,16,128,128]{3,2,1,0:T(8,128)S(1)} %subtract_multiply_fusion, f32[128,128,1,1]{1,0,3,2:T(8,128)S(1)} %copy-done.5), kind=kOutput, calls=%fused_computation.95 | convolution fusion | flops 402653184 | bytes 4259840 | tf_op jit(solution)/shard_map/dot_general | solution.py:48
  26.0 0.0 copy-start.7
  26.0 1.0 %fusion.12 = f32[2,16,128,128]{3,2,1,0:T(8,128)S(1)} fusion(f32[128,128,1,1]{1,0,3,2:T(8,128)S(1)} %copy-done.4, f32[2,16,128,128]{3,2,1,0:T(8,128)S(1)} %subtract_multiply_fusion, f32[2,16,128,128]{3,2,1,0:T(8,128)S(1)} %add_multiply_fusion), kind=kOutput, calls=%fused_computation.14 | convolution fusion | flops 403177472 | bytes 6356992 | tf_op jit(solution)/shard_map/dot_general | solution.py:48
  27.0 0.0 copy-done.7
  27.1 1.0 %fusion.60 = f32[2,16,128,128]{3,2,1,0:T(8,128)S(1)} fusion(f32[2,16,128,128]{3,2,1,0:T(8,128)S(1)} %add_multiply_fusion, f32[128,128,1,1]{1,0,3,2:T(8,128)S(1)} %copy-done.7), kind=kOutput, calls=%fused_computation.94 | convolution fusion | flops 402653184 | bytes 4259840 | tf_op jit(solution)/shard_map/dot_general | solution.py:48
  28.1 1.3 %fusion.10 = f32[2,16,128,256]{3,2,1,0:T(8,128)S(1)} fusion(f32[2,16,128,128]{3,2,1,0:T(8,128)S(1)} %fusion.12, f32[2,16,128,128]{3,2,1,0:T(8,128)S(1)} %fusion.60, s32[256]{0:T(256)S(1)} %get-tuple-element.18), kind=kOutput, calls=%fused_computation.12 | convolution fusion | flops 805863424 | bytes 8389632 | tf_op jit(solution)/shard_map/dot_general | solution.py:48
  29.3 2.1 %add_reduce_fusion = (f32[2,16,256]{2,1,0:T(8,128)S(1)}, f32[2,16,256]{2,1,0:T(8,128)S(1)}) fusion(f32[2,16,128,256]{3,2,1,0:T(8,128)S(1)} %fusion.10, f32[128,256]{1,0:T(8,128)S(1)} %get-tuple-element.21, f32[128,256]{1,0:T(8,128)S(1)} %get-tuple-element.20, s32[256]{0:T(256)S(1)} %get-tuple-element.18, f32[2,16,128,128]{3,2,1,0:T(8,128)S(1)} %fusion.12, ...), kind=kOutput, calls=%fused_computation.1 | convolution fusion | flops 814235648 | bytes 8717312 | tf_op jit(solution)/shard_map/dot_general | solution.py:48
  31.5 0.0 copy-start.6
  31.5 0.1 stack.13
  31.6 0.1 stack.14
  31.6 0.0 copy-start.3
  31.7 0.2 copy.92
  32.0 0.9 %reshape.137 = f32[8,1,2048]{2,1,0:T(1,128)} reshape(f32[128,2,2,32]{3,2,1,0:T(2,128)S(1)} %bitcast.92) | data formatting | bytes 131072
  32.9 4.7 %all-to-all-start.1 = ((f32[8,1,2048]{2,1,0:T(1,128)}), f32[8,1,2048]{2,1,0:T(1,128)S(1)}, u32[]{:S(2)}, u32[]{:S(2)}) async-start(f32[8,1,2048]{2,1,0:T(1,128)} %reshape.137), calls=%async_computation.1 | async-start | bytes 131072 | tf_op jit(solution)/shard_map/all_to_all | solution.py:125
  37.5 0.1 add_multiply_fusion.1
  37.6 6.8 %all-to-all-done.1 = f32[8,1,2048]{2,1,0:T(1,128)S(1)} async-done(((f32[8,1,2048]{2,1,0:T(1,128)}), f32[8,1,2048]{2,1,0:T(1,128)S(1)}, u32[]{:S(2)}, u32[]{:S(2)}) %all-to-all-start.1) | async-done | bytes 65568 | tf_op jit(solution)/shard_map/all_to_all | solution.py:125
  44.4 0.8 %reduce.2 = f32[8,2048]{1,0:T(8,128)S(1)} reduce(f32[8,1,2048]{2,1,0:T(1,128)S(1)} %all-to-all-done.1, f32[]{:T(128)} %broadcast.179), dimensions={1}, to_apply=%all_to_all.10.reduce_sub_computation | reduce | bytes 131076 | tf_op jit(solution)/shard_map/all_to_all | solution.py:125
  45.2 0.2 reshape.138
  45.5 0.0 copy-done.6
  45.5 1.3 %fusion.59 = (bf16[2,2,32,128]{3,2,0,1:T(8,128)(2,1)S(1)}, f32[2,2,32,128]{3,2,0,1:T(8,128)S(1)}) fusion(f32[2,2,128,128,1]{3,2,1,0,4:T(8,128)} %constant.104, f32[128,2,2,32,1]{3,1,2,0,4:T(2,128)S(1)} %bitcast_bitcast_fusion, f32[2,2,32,128]{3,2,1,0:T(8,128)S(1)} %copy-done.6, f32[32,128]{1,0:T(8,128)S(1)} %add_multiply_fusion.1), kind=kOutput, calls=%fused_computation.91 | convolution fusion | flops 25214976 | bytes 507904 | tf_op jit(solution)/shard_map/dckz,zcbs->dbsk/dot_general | solution.py:126
  46.8 5.4 %all_gather.3 = bf16[2,8,32,128]{3,2,0,1:T(8,128)(2,1)S(1)} all-gather(bf16[2,2,32,128]{3,2,0,1:T(8,128)(2,1)S(1)} %get-tuple-element.22), channel_id=1, replica_groups=mesh['pw'=8,'band'=4] {'band'}, dimensions={1}, use_global_device_ids=true | all-gather | bytes 163840 | tf_op jit(solution)/shard_map/all_gather | solution.py:129
  52.3 0.1 copy.47
  52.4 0.0 copy-done.3
  52.4 0.4 convolution_bitcast_fusion.5
  52.8 0.4 convolution_bitcast_fusion.4
  53.3 0.2 copy-done.1
  53.5 0.4 convolution_bitcast_fusion.3
  53.9 0.4 convolution_bitcast_fusion.2
  54.4 0.1 maximum_bitcast_fusion.1
  54.4 0.6 copy.52
  55.1 3.3 %all-to-all-start.2 = ((f32[2,8,1,256]{3,0,2,1:T(2,128)}), f32[2,8,1,256]{3,0,2,1:T(2,128)S(1)}, u32[]{:S(2)}, u32[]{:S(2)}) async-start(f32[2,8,1,256]{3,0,2,1:T(2,128)} %copy.52), calls=%async_computation.2 | async-start | bytes 32768 | tf_op jit(solution)/shard_map/all_to_all | solution.py:99
  58.4 0.6 copy.53
  59.0 5.9 %all-to-all-done.2 = f32[2,8,1,256]{3,0,2,1:T(2,128)S(1)} async-done(((f32[2,8,1,256]{3,0,2,1:T(2,128)}), f32[2,8,1,256]{3,0,2,1:T(2,128)S(1)}, u32[]{:S(2)}, u32[]{:S(2)}) %all-to-all-start.2) | async-done | bytes 16416 | tf_op jit(solution)/shard_map/all_to_all | solution.py:99
  64.9 0.6 reduce_sum.35
  (13 shorter events, 0.3 us)
Async XLA Ops:
  0.6 10.9 %copy-start = (f32[16,128,128]{2,1,0:T(8,128)S(1)}, f32[16,128,128]{2,1,0:T(8,128)}, u32[]{:S(2)}) copy-start(f32[16,128,128]{2,1,0:T(8,128)} %param.9) | copy-start | bytes 3145732
  3.1 14.2 %all-to-all-start = ((f32[8,1,2048]{2,1,0:T(1,128)}), f32[8,1,2048]{2,1,0:T(1,128)S(1)}, u32[]{:S(2)}, u32[]{:S(2)}) async-start(f32[8,1,2048]{2,1,0:T(1,128)} %reshape.135), calls=%async_computation | async-start | bytes 131072 | tf_op jit(solution)/shard_map/all_to_all | solution.py:116
  11.7 4.2 %copy-start.9 = (s32[256]{0:T(256)S(1)}, s32[256]{0:T(256)}, u32[]{:S(2)}) copy-start(s32[256]{0:T(256)} %param.10) | copy-start | bytes 3076
  20.5 1.4 %copy-start.4 = (f32[128,128,1,1]{1,0,3,2:T(8,128)S(1)}, f32[128,128,1,1]{1,0,3,2:T(8,128)}, u32[]{:S(2)}) copy-start(f32[128,128,1,1]{1,0,3,2:T(8,128)} %constant.100) | copy-start | bytes 196612
  21.9 1.0 %copy-start.8 = (f32[128,128,1,1]{1,0,3,2:T(8,128)S(1)}, f32[128,128,1,1]{1,0,3,2:T(8,128)}, u32[]{:S(2)}) copy-start(f32[128,128,1,1]{1,0,3,2:T(8,128)} %constant.102) | copy-start | bytes 196612
  22.9 1.1 %copy-start.5 = (f32[128,128,1,1]{1,0,3,2:T(8,128)S(1)}, f32[128,128,1,1]{1,0,3,2:T(8,128)}, u32[]{:S(2)}) copy-start(f32[128,128,1,1]{1,0,3,2:T(8,128)} %constant.101) | copy-start | bytes 196612
  26.0 1.0 %copy-start.7 = (f32[128,128,1,1]{1,0,3,2:T(8,128)S(1)}, f32[128,128,1,1]{1,0,3,2:T(8,128)}, u32[]{:S(2)}) copy-start(f32[128,128,1,1]{1,0,3,2:T(8,128)} %constant.103) | copy-start | bytes 196612
  31.5 14.1 %copy-start.6 = (f32[2,2,32,128]{3,2,1,0:T(8,128)S(1)}, f32[2,2,32,128]{3,2,1,0:T(8,128)}, u32[]{:S(2)}) copy-start(f32[2,2,32,128]{3,2,1,0:T(8,128)} %param.7) | copy-start | bytes 196612
  31.6 20.7 %copy-start.3 = (bf16[2,64,32,128]{3,2,1,0:T(8,128)(2,1)S(1)}, bf16[2,64,32,128]{3,2,1,0:T(8,128)(2,1)}, u32[]{:S(2)}) copy-start(bf16[2,64,32,128]{3,2,1,0:T(8,128)(2,1)} %get-tuple-element.10) | copy-start | bytes 3145732
  32.9 11.6 %all-to-all-start.1 = ((f32[8,1,2048]{2,1,0:T(1,128)}), f32[8,1,2048]{2,1,0:T(1,128)S(1)}, u32[]{:S(2)}, u32[]{:S(2)}) async-start(f32[8,1,2048]{2,1,0:T(1,128)} %reshape.137), calls=%async_computation.1 | async-start | bytes 131072 | tf_op jit(solution)/shard_map/all_to_all | solution.py:125
  37.5 15.3 %copy-start.2 = (bf16[2,64,32,128]{3,2,1,0:T(8,128)(2,1)S(1)}, bf16[2,64,32,128]{3,2,1,0:T(8,128)(2,1)}, u32[]{:S(2)}) copy-start(bf16[2,64,32,128]{3,2,1,0:T(8,128)(2,1)} %get-tuple-element.12) | copy-start | bytes 3145732
  52.3 1.2 %copy-start.1 = (bf16[2,64,32,128]{3,2,1,0:T(8,128)(2,1)S(1)}, bf16[2,64,32,128]{3,2,1,0:T(8,128)(2,1)}, u32[]{:S(2)}) copy-start(bf16[2,64,32,128]{3,2,1,0:T(8,128)(2,1)} %get-tuple-element.11) | copy-start | bytes 3145732
  55.1 9.9 %all-to-all-start.2 = ((f32[2,8,1,256]{3,0,2,1:T(2,128)}), f32[2,8,1,256]{3,0,2,1:T(2,128)S(1)}, u32[]{:S(2)}, u32[]{:S(2)}) async-start(f32[2,8,1,256]{3,0,2,1:T(2,128)} %copy.52), calls=%async_computation.2 | async-start | bytes 32768 | tf_op jit(solution)/shard_map/all_to_all | solution.py:99

commit v8 on v7

--- a/solution.py
+++ b/solution.py
@@ -60,12 +60,17 @@
     spread_im = val_re * phase_sin + val_im * phase_cos
     rows_re = mult(spread_re, place_cols)
     rows_im = mult(spread_im, place_cols)
-    shared = mult(rows_re + rows_im, cosine)
-    wave_re = (shared - mult(rows_im, cosine + sine)) * scaled_pot
-    wave_im = (shared + mult(rows_re, sine - cosine)) * scaled_pot
-    shared = mult(wave_re + wave_im, cosine)
-    back_re = shared - mult(wave_im, cosine - sine)
-    back_im = shared - mult(wave_re, sine + cosine)
+    into_real = jnp.concatenate(
+        [jnp.concatenate([cosine, sine], axis=1), jnp.concatenate([-sine, cosine], axis=1)], axis=0
+    )
+    into_spec = jnp.concatenate(
+        [jnp.concatenate([cosine, -sine], axis=1), jnp.concatenate([sine, cosine], axis=1)], axis=0
+    )
+    wave = mult(jnp.concatenate([rows_re, rows_im], axis=-1), into_real)
+    wave = (wave.reshape(wave.shape[:-1] + (2, grid_size)) * scaled_pot[..., None, :]).reshape(wave.shape)
+    back = mult(wave, into_spec)
+    back_re = back[..., :grid_size]
+    back_im = back[..., grid_size:]
     sel_re = mult(back_re, pick_cols)
     sel_im = mult(back_im, pick_cols)
     picked_re = jnp.sum(sel_re * phase_cos + sel_im * phase_sin, axis=2)

time: 66 us -> 78.8 us (1.19)
  local copies, waits for them, and re-layouts: 10.1 us -> 16.4 us
  other arithmetic: 3.21 us -> 6.91 us
  matrix products: 16.5 us -> 19.8 us
  waiting for transfers between devices: 14 us -> 12 us
  starting transfers between devices: 15.3 us -> 16.6 us
    mul x0 -> x2, local copies, waits for them, and re-layouts: none -> 5.2 us  [plane_phase(): wave.reshape(wave.shape[:-1] + (2, grid_size)) * scaled_pot[..., None, :]]
    dot_general x10 -> x6, matrix products: 12.1 us -> 14.3 us  [mult(): jnp.dot(left, right, precision=lax.Precision.HIGH, preferred_element_type...]
    all_to_all x1, waiting for transfers between devices: 1.34 us -> 0.01 us  [per_device_rows(): lax.all_to_all(z_lines, 'pw', split_axis=0, concat_axis=0, tiled=True)]
    all_to_all x1, starting transfers between devices: 4.67 us -> 6 us  [per_device_rows(): lax.all_to_all(outgoing, 'pw', split_axis=0, concat_axis=0, tiled=True)]
    dot_general x4, matrix products: 1.72 us -> 2.96 us  [intersect(): lax.dot_general(both, psi_all[:, k * width:(k + 1) * width], dims, prefer...]
    mul x2, local copies, waits for them, and re-layouts: 0.19 us -> 1.42 us  [plane_phase(): spread_re = val_re * phase_cos - val_im * phase_sin]
    div x1, other arithmetic: 0.08 us -> 1.3 us  [plane_phase(): scaled_pot = (pot / float(grid_size ** 3))[None]]
    unnamed x25 -> x21, local copies, waits for them, and re-layouts: 3.2 us -> 2.96 us
  transfers between devices with their start and end apart: 3 -> 3, of which waited for: 3 -> 2; matrix products, arithmetic and copies ran while one was open for 10% -> 20% of each run, Pallas kernels for 0% -> 0%
where the time goes in v8:
time: 78.8 us; the launch traced here: 78.2 us
  matrix products  19.8 us (25%)
  starting transfers between devices  16.6 us (21%)
  local copies, waits for them, and re-layouts  16.4 us (21%)
  waiting for transfers between devices  12 us (15%)
  other arithmetic  6.91 us (9%)
  blocking collectives  5.43 us (7%)
  between operations  0.95 us (1%)
    dot_general x6, matrix products, mult(): jnp.dot(left, right, precision=lax.Precision.HIGH, preferred_element_type...  14.3 us
    all_to_all x1, starting transfers between devices, per_device_rows(): lax.all_to_all(z_lines, 'pw', split_axis=0, concat_axis=0, tiled=True)  7.28 us
    all_to_all x1, waiting for transfers between devices, per_device_rows(): lax.all_to_all(outgoing, 'pw', split_axis=0, concat_axis=0, tiled=True)  6.16 us
    all_to_all x1, starting transfers between devices, per_device_rows(): lax.all_to_all(outgoing, 'pw', split_axis=0, concat_axis=0, tiled=True)  6 us
    all_to_all x1, waiting for transfers between devices, intersect(): lax.all_to_all(pieces, 'pw', split_axis=1, concat_axis=1, tiled=True)  5.88 us
    all_gather x1, blocking collectives, per_device_rows(): gathered = lax.all_gather(lowered, 'band', axis=1, tiled=True)  5.43 us
    mul x2, local copies, waits for them, and re-layouts, plane_phase(): wave.reshape(wave.shape[:-1] + (2, grid_size)) * scaled_pot[..., None, :]  5.2 us
    slice x1, local copies, waits for them, and re-layouts, intersect(): psi_all[:, k * width:(k + 1) * width]  4.26 us
  transfers between devices with their start and end apart: 3, of which 2 were waited for; matrix products, arithmetic and copies ran while one was open for 20% of the time, Pallas kernels for 0%

profile of v8, /device:TPU:0, one launch (start us, length us, event | category | flops | bytes accessed | tf_op | source)
XLA Modules:
  0.0 78.2 jit_solution(10520428119069100383)
XLA Ops:
  0.6 1.2 %convolution_bitcast_fusion = f32[128,2,2,32]{0,3,2,1:T(8,128)S(1)} fusion(f32[2,2,128,128,1]{3,2,1,4,0:T(8,128)} %constant.103, f32[2,2,32,128]{3,2,1,0:T(8,128)} %param.7), kind=kOutput, calls=%fused_computation.29 | convolution fusion | flops 25165824 | bytes 393216 | tf_op jit(solution)/shard_map/dczk,cbsk->zdbs/dot_general | solution.py:120
  1.9 0.2 copy.38
  2.1 0.9 %reshape.136 = f32[8,1,2048]{2,1,0:T(1,128)} reshape(f32[128,2,2,32]{3,2,1,0:T(2,128)S(1)} %copy.38) | data formatting | bytes 131072
  3.0 7.3 %all-to-all-start = ((f32[8,1,2048]{2,1,0:T(1,128)}), f32[8,1,2048]{2,1,0:T(1,128)S(1)}, u32[]{:S(2)}, u32[]{:S(2)}) async-start(f32[8,1,2048]{2,1,0:T(1,128)} %reshape.136), calls=%async_computation | async-start | bytes 131072 | tf_op jit(solution)/shard_map/all_to_all | solution.py:121
  10.2 0.7 and_select_fusion
  10.9 1.2 %fusion.51 = (f32[128,256]{1,0:T(8,128)}, f32[128,256]{1,0:T(8,128)}) fusion(s32[256]{0:T(256)S(1)} %get-tuple-element.19), kind=kLoop, calls=%fused_computation.64 | loop fusion | flops 458752 | bytes 263168 | tf_op jit(solution)/shard_map/cos | solution.py:44
  12.2 1.3 %broadcast_multiply_fusion = f32[16,128,128]{2,1,0:T(8,128)S(1)} fusion(f32[16,128,128]{2,1,0:T(8,128)} %param.9), kind=kLoop, calls=%fused_computation.40 | loop fusion | flops 262144 | bytes 2097152 | tf_op jit(solution)/shard_map/div | solution.py:56
  13.5 4.3 %fusion.61 = (bf16[2,64,32,128]{3,2,1,0:T(8,128)(2,1)}, bf16[2,64,32,128]{3,2,1,0:T(8,128)(2,1)}, bf16[2,64,32,128]{3,2,1,0:T(8,128)(2,1)}, bf16[2,64,32,128]{3,2,1,0:T(8,128)(2,1)S(1)}) fusion(bf16[2,256,32,128]{3,2,1,0:T(8,128)(2,1)} %param.8), kind=kLoop, calls=%fused_computation.91 | loop fusion | bytes 8388608 | tf_op jit(solution)/shard_map/slice | solution.py:91
  17.7 0.0 copy-start.7
  17.8 0.5 fusion.59
  18.3 2.1 %mul.169 = f32[16,128,2,128]{3,2,1,0:T(2,128)} broadcast(f32[16,128,128]{2,1,0:T(8,128)S(1)} %broadcast_multiply_fusion), dimensions={0,1,3} | broadcast | bytes 3145728 | tf_op jit(solution)/shard_map/mul | solution.py:70
  20.4 3.1 %mul.170 = f32[16,128,256]{2,1,0:T(8,128)S(1)} reshape(f32[16,128,2,128]{3,2,1,0:T(2,128)} %mul.169) | data formatting | bytes 4194304 | tf_op jit(solution)/shard_map/mul | solution.py:70
  23.5 0.0 copy-done.7
  23.5 0.7 fusion.55
  24.2 0.0 all-to-all-done
  24.2 0.5 broadcast.181
  24.7 0.8 %reduce.1 = f32[8,2048]{1,0:T(8,128)S(1)} reduce(f32[8,1,2048]{2,1,0:T(1,128)S(1)} %all-to-all-done, f32[]{:T(128)} %broadcast.181), dimensions={1}, to_apply=%all_to_all.9.reduce_sub_computation | reduce | bytes 131076 | tf_op jit(solution)/shard_map/all_to_all | solution.py:121
  25.5 0.2 reshape.137
  25.8 0.7 mul.154
  26.6 0.0 copy-start.3
  26.6 0.7 mul.163
  27.3 2.8 %fusion.10 = f32[2,16,128,128]{2,3,1,0:T(8,128)S(1)} fusion(f32[128,256]{1,0:T(8,128)} %get-tuple-element.21, f32[2,16,256]{2,1,0:T(8,128)} %mul.163, f32[128,256]{1,0:T(8,128)} %get-tuple-element.20, f32[2,16,256]{2,1,0:T(8,128)} %mul.154, s32[256]{0:T(256)S(1)} %get-tuple-element.18), kind=kOutput, calls=%fused_computation.12 | convolution fusion | flops 808484864 | bytes 2425856 | tf_op jit(solution)/shard_map/dot_general | solution.py:48
  30.1 2.8 %fusion.6 = f32[2,16,128,128]{2,3,1,0:T(8,128)S(1)} fusion(f32[128,256]{1,0:T(8,128)} %get-tuple-element.21, f32[2,16,256]{2,1,0:T(8,128)} %mul.163, f32[128,256]{1,0:T(8,128)} %get-tuple-element.20, f32[2,16,256]{2,1,0:T(8,128)} %mul.154, s32[256]{0:T(256)S(1)} %get-tuple-element.18), kind=kOutput, calls=%fused_computation.8 | convolution fusion | flops 808484864 | bytes 2425856 | tf_op jit(solution)/shard_map/dot_general | solution.py:48
  32.9 0.0 copy-done.3
  32.9 0.0 copy-start.2
  32.9 3.6 %fusion = f32[2,16,128,256]{3,2,1,0:T(8,128)S(1)} fusion(f32[256,256,1,1]{1,0,3,2:T(8,128)S(1)} %copy-done.3, f32[2,16,128,128]{2,3,1,0:T(8,128)S(1)} %fusion.6, f32[2,16,128,128]{2,3,1,0:T(8,128)S(1)} %fusion.10), kind=kOutput, calls=%fused_computation | convolution fusion | flops 1611661312 | bytes 8650752 | tf_op jit(solution)/shard_map/dot_general | solution.py:48
  36.5 0.0 copy-done.2
  36.5 1.8 %fusion.4 = f32[2,16,128,256]{3,2,1,0:T(8,128)S(1)} fusion(f32[256,256,1,1]{1,0,3,2:T(8,128)S(1)} %copy-done.2, f32[2,16,128,256]{3,2,1,0:T(8,128)S(1)} %fusion, f32[16,128,256]{2,1,0:T(8,128)S(1)} %mul.170), kind=kOutput, calls=%fused_computation.6 | convolution fusion | flops 1611661312 | bytes 10747904 | tf_op jit(solution)/shard_map/dot_general | solution.py:48
  38.4 0.0 copy-start.5
  38.4 0.0 copy-start.6
  38.4 1.2 %fusion.16 = f32[2,16,128,256]{3,2,1,0:T(8,128)S(1)} fusion(f32[2,16,128,256]{3,2,1,0:T(8,128)S(1)} %fusion.4, s32[256]{0:T(256)S(1)} %get-tuple-element.18), kind=kOutput, calls=%fused_computation.18 | convolution fusion | flops 805339136 | bytes 6292480 | tf_op jit(solution)/shard_map/dot_general | solution.py:48
  39.6 0.0 copy-done.5
  39.6 0.0 copy-done.6
  39.6 0.0 copy-start.4
  39.7 2.1 %add_reduce_fusion = (f32[2,16,256]{2,1,0:T(8,128)S(1)}, f32[2,16,256]{2,1,0:T(8,128)S(1)}) fusion(f32[2,16,128,256]{3,2,1,0:T(8,128)S(1)} %fusion.16, f32[128,256]{1,0:T(8,128)S(1)} %copy-done.6, f32[128,256]{1,0:T(8,128)S(1)} %copy-done.5, s32[256]{0:T(256)S(1)} %get-tuple-element.18, f32[2,16,128,256]{3,2,1,0:T(8,128)S(1)} %fusion.4), kind=kOutput, calls=%fused_computation.5 | convolution fusion | flops 813711360 | bytes 6620160 | tf_op jit(solution)/shard_map/dot_general | solution.py:48
  41.8 0.0 copy-start.1
  41.8 0.0 copy-start
  41.8 0.1 stack.13
  41.9 0.1 stack.14
  42.1 0.2 copy.92
  42.3 0.9 %reshape.138 = f32[8,1,2048]{2,1,0:T(1,128)} reshape(f32[128,2,2,32]{3,2,1,0:T(2,128)S(1)} %bitcast.78) | data formatting | bytes 131072
  43.2 6.0 %all-to-all-start.1 = ((f32[8,1,2048]{2,1,0:T(1,128)}), f32[8,1,2048]{2,1,0:T(1,128)S(1)}, u32[]{:S(2)}, u32[]{:S(2)}) async-start(f32[8,1,2048]{2,1,0:T(1,128)} %reshape.138), calls=%async_computation.1 | async-start | bytes 131072 | tf_op jit(solution)/shard_map/all_to_all | solution.py:130
  49.2 0.7 add_multiply_fusion
  49.9 6.2 %all-to-all-done.1 = f32[8,1,2048]{2,1,0:T(1,128)S(1)} async-done(((f32[8,1,2048]{2,1,0:T(1,128)}), f32[8,1,2048]{2,1,0:T(1,128)S(1)}, u32[]{:S(2)}, u32[]{:S(2)}) %all-to-all-start.1) | async-done | bytes 65568 | tf_op jit(solution)/shard_map/all_to_all | solution.py:130
  56.1 0.8 %reduce.2 = f32[8,2048]{1,0:T(8,128)S(1)} reduce(f32[8,1,2048]{2,1,0:T(1,128)S(1)} %all-to-all-done.1, f32[]{:T(128)} %broadcast.181), dimensions={1}, to_apply=%all_to_all.10.reduce_sub_computation | reduce | bytes 131076 | tf_op jit(solution)/shard_map/all_to_all | solution.py:130
  56.9 0.2 reshape.139
  57.2 0.0 copy-done.4
  57.2 1.3 %fusion.63 = (bf16[2,2,32,128]{3,2,0,1:T(8,128)(2,1)S(1)}, f32[2,2,32,128]{3,2,0,1:T(8,128)S(1)}) fusion(f32[2,2,128,128,1]{3,2,1,0,4:T(8,128)} %constant.106, f32[128,2,2,32,1]{3,1,2,0,4:T(2,128)S(1)} %bitcast_bitcast_fusion, f32[2,2,32,128]{3,2,1,0:T(8,128)S(1)} %copy-done.4, f32[32,128]{1,0:T(8,128)S(1)} %add_multiply_fusion), kind=kOutput, calls=%fused_computation.93 | convolution fusion | flops 25214976 | bytes 507904 | tf_op jit(solution)/shard_map/dckz,zcbs->dbsk/dot_general | solution.py:131
  58.5 5.4 %all_gather.3 = bf16[2,8,32,128]{3,2,0,1:T(8,128)(2,1)S(1)} all-gather(bf16[2,2,32,128]{3,2,0,1:T(8,128)(2,1)S(1)} %get-tuple-element.22), channel_id=1, replica_groups=mesh['pw'=8,'band'=4] {'band'}, dimensions={1}, use_global_device_ids=true | all-gather | bytes 163840 | tf_op jit(solution)/shard_map/all_gather | solution.py:134
  63.9 0.1 copy.48
  64.0 1.7 %convolution_bitcast_fusion.5 = f32[16,64]{1,0:T(8,128)S(1)} fusion(bf16[2,64,32,128]{3,2,1,0:T(8,128)(2,1)} %get-tuple-element.10, bf16[1,8,32,128]{3,1,0,2:T(8,128)(2,1)S(1)} %get-tuple-element.17, bf16[1,8,32,128]{3,1,0,2:T(8,128)(2,1)S(1)} %get-tuple-element.16, bf16[2,8,32,128]{3,1,0,2:T(8,128)(2,1)S(1)} %copy.48), kind=kOutput, calls=%fused_computation.35 | convolution fusion | flops 17563648 | bytes 1314816 | tf_op jit(solution)/shard_map/dot_general | solution.py:89
  65.7 0.0 copy-done.1
  65.7 0.4 convolution_bitcast_fusion.4
  66.1 0.0 copy-done
  66.1 0.4 convolution_bitcast_fusion.3
  66.6 0.4 convolution_bitcast_fusion.2
  67.0 0.1 maximum_bitcast_fusion.1
  67.1 0.6 copy.53
  67.7 3.3 %all-to-all-start.2 = ((f32[2,8,1,256]{3,0,2,1:T(2,128)}), f32[2,8,1,256]{3,0,2,1:T(2,128)S(1)}, u32[]{:S(2)}, u32[]{:S(2)}) async-start(f32[2,8,1,256]{3,0,2,1:T(2,128)} %copy.53), calls=%async_computation.2 | async-start | bytes 32768 | tf_op jit(solution)/shard_map/all_to_all | solution.py:104
  71.1 0.6 copy.54
  71.7 5.9 %all-to-all-done.2 = f32[2,8,1,256]{3,0,2,1:T(2,128)S(1)} async-done(((f32[2,8,1,256]{3,0,2,1:T(2,128)}), f32[2,8,1,256]{3,0,2,1:T(2,128)S(1)}, u32[]{:S(2)}, u32[]{:S(2)}) %all-to-all-start.2) | async-done | bytes 16416 | tf_op jit(solution)/shard_map/all_to_all | solution.py:104
  77.6 0.6 reduce_sum.35
  (9 shorter events, 0.3 us)
Async XLA Ops:
  3.0 21.2 %all-to-all-start = ((f32[8,1,2048]{2,1,0:T(1,128)}), f32[8,1,2048]{2,1,0:T(1,128)S(1)}, u32[]{:S(2)}, u32[]{:S(2)}) async-start(f32[8,1,2048]{2,1,0:T(1,128)} %reshape.136), calls=%async_computation | async-start | bytes 131072 | tf_op jit(solution)/shard_map/all_to_all | solution.py:121
  17.7 5.7 %copy-start.7 = (s32[256]{0:T(256)S(1)}, s32[256]{0:T(256)}, u32[]{:S(2)}) copy-start(s32[256]{0:T(256)} %param.10) | copy-start | bytes 3076
  26.6 6.3 %copy-start.3 = (f32[256,256,1,1]{1,0,3,2:T(8,128)S(1)}, f32[256,256,1,1]{1,0,3,2:T(8,128)}, u32[]{:S(2)}) copy-start(f32[256,256,1,1]{1,0,3,2:T(8,128)} %constant.104) | copy-start | bytes 786436
  32.9 3.6 %copy-start.2 = (f32[256,256,1,1]{1,0,3,2:T(8,128)S(1)}, f32[256,256,1,1]{1,0,3,2:T(8,128)}, u32[]{:S(2)}) copy-start(f32[256,256,1,1]{1,0,3,2:T(8,128)} %constant.105) | copy-start | bytes 786436
  38.4 1.3 %copy-start.5 = (f32[128,256]{1,0:T(8,128)S(1)}, f32[128,256]{1,0:T(8,128)}, u32[]{:S(2)}) copy-start(f32[128,256]{1,0:T(8,128)} %get-tuple-element.20) | copy-start | bytes 393220
  38.4 1.3 %copy-start.6 = (f32[128,256]{1,0:T(8,128)S(1)}, f32[128,256]{1,0:T(8,128)}, u32[]{:S(2)}) copy-start(f32[128,256]{1,0:T(8,128)} %get-tuple-element.21) | copy-start | bytes 393220
  39.6 17.5 %copy-start.4 = (f32[2,2,32,128]{3,2,1,0:T(8,128)S(1)}, f32[2,2,32,128]{3,2,1,0:T(8,128)}, u32[]{:S(2)}) copy-start(f32[2,2,32,128]{3,2,1,0:T(8,128)} %param.7) | copy-start | bytes 196612
  41.8 23.9 %copy-start.1 = (bf16[2,64,32,128]{3,2,1,0:T(8,128)(2,1)S(1)}, bf16[2,64,32,128]{3,2,1,0:T(8,128)(2,1)}, u32[]{:S(2)}) copy-start(bf16[2,64,32,128]{3,2,1,0:T(8,128)(2,1)} %get-tuple-element.12) | copy-start | bytes 3145732
  41.8 24.3 %copy-start = (bf16[2,64,32,128]{3,2,1,0:T(8,128)(2,1)S(1)}, bf16[2,64,32,128]{3,2,1,0:T(8,128)(2,1)}, u32[]{:S(2)}) copy-start(bf16[2,64,32,128]{3,2,1,0:T(8,128)(2,1)} %get-tuple-element.11) | copy-start | bytes 3145732
  43.2 12.9 %all-to-all-start.1 = ((f32[8,1,2048]{2,1,0:T(1,128)}), f32[8,1,2048]{2,1,0:T(1,128)S(1)}, u32[]{:S(2)}, u32[]{:S(2)}) async-start(f32[8,1,2048]{2,1,0:T(1,128)} %reshape.138), calls=%async_computation.1 | async-start | bytes 131072 | tf_op jit(solution)/shard_map/all_to_all | solution.py:130
  67.7 9.9 %all-to-all-start.2 = ((f32[2,8,1,256]{3,0,2,1:T(2,128)}), f32[2,8,1,256]{3,0,2,1:T(2,128)S(1)}, u32[]{:S(2)}, u32[]{:S(2)}) async-start(f32[2,8,1,256]{3,0,2,1:T(2,128)} %copy.53), calls=%async_computation.2 | async-start | bytes 32768 | tf_op jit(solution)/shard_map/all_to_all | solution.py:104

commit v9 on v6

--- a/solution.py
+++ b/solution.py
@@ -76,9 +76,11 @@
 def intersect(lowered, psi_all, pw_count):
     turned = jnp.stack([-lowered[1], lowered[0]])
     both = jnp.concatenate([lowered, turned], axis=1)
-    dims = (((2, 3), (2, 3)), ((0,), (0,)))
-    partial_value = lax.dot_general(both, psi_all, dims, preferred_element_type=jnp.float32)
-    partial_value = jnp.sum(partial_value, axis=0)
+    dims = (((1, 2), (1, 2)), ((), ()))
+    partial_value = sum(
+        lax.dot_general(both[part], psi_all[part], dims, preferred_element_type=jnp.float32)
+        for part in range(psi_all.shape[0])
+    )
     partial_value = partial_value.reshape(2, lowered.shape[1], partial_value.shape[-1])
     rows_dev = partial_value.shape[1] // pw_count
     pieces = partial_value.reshape(2, pw_count, rows_dev, partial_value.shape[-1])

time: 66.5 us -> 70 us (1.053)
  local copies, waits for them, and re-layouts: 5.72 us -> 14.4 us
  waiting for transfers between devices: 18.1 us -> 13.9 us
  matrix products: 18.7 us -> 16 us
  starting transfers between devices: 14 us -> 15.4 us
    all_to_all x1, waiting for transfers between devices: 5.47 us -> 1.18 us  [per_device_rows(): lax.all_to_all(z_lines, 'pw', split_axis=0, concat_axis=0, tiled=True)]
    slice x0 -> x1, local copies, waits for them, and re-layouts: none -> 4.29 us  [intersect(): psi_all[part]]
    dot_general x1 -> x2, matrix products: 4.5 us -> 1.35 us  [intersect(): lax.dot_general(both[part], psi_all[part], dims, preferred_element_type=j...]
    all_to_all x1, starting transfers between devices: 3.35 us -> 4.83 us  [per_device_rows(): lax.all_to_all(outgoing, 'pw', split_axis=0, concat_axis=0, tiled=True)]
    mul x2, local copies, waits for them, and re-layouts: 0.19 us -> 1.42 us  [plane_phase(): spread_re = val_re * phase_cos - val_im * phase_sin]
    all_to_all x2, local copies, waits for them, and re-layouts: 0.53 us -> 1.48 us  [per_device_rows(): lax.all_to_all(z_lines, 'pw', split_axis=0, concat_axis=0, tiled=True)]
    slice x1, local copies, waits for them, and re-layouts: 0.04 us -> 0.95 us  [plane_phase(): val_im = amp[1][:, :, None, :]]
    unnamed x21 -> x27, local copies, waits for them, and re-layouts: 2.98 us -> 3.68 us
  transfers between devices with their start and end apart: 3 -> 3, of which waited for: 3 -> 3; matrix products, arithmetic and copies ran while one was open for 3% -> 9% of each run, Pallas kernels for 0% -> 0%
where the time goes in v9:
time: 70 us; the launch traced here: 69.5 us
  matrix products  16 us (23%)
  starting transfers between devices  15.4 us (22%)
  local copies, waits for them, and re-layouts  14.4 us (21%)
  waiting for transfers between devices  13.9 us (20%)
  blocking collectives  5.56 us (8%)
  other arithmetic  3.17 us (5%)
  between operations  1 us (1%)
    dot_general x10, matrix products, mult(): jnp.dot(left, right, precision=lax.Precision.HIGH, preferred_element_type...  13 us
    all_to_all x1, starting transfers between devices, per_device_rows(): lax.all_to_all(z_lines, 'pw', split_axis=0, concat_axis=0, tiled=True)  7.28 us
    all_to_all x1, waiting for transfers between devices, per_device_rows(): lax.all_to_all(outgoing, 'pw', split_axis=0, concat_axis=0, tiled=True)  6.83 us
    all_to_all x1, waiting for transfers between devices, intersect(): lax.all_to_all(pieces, 'pw', split_axis=1, concat_axis=1, tiled=True)  5.88 us
    all_gather x1, blocking collectives, per_device_rows(): gathered = lax.all_gather(lowered, 'band', axis=1, tiled=True)  5.56 us
    all_to_all x1, starting transfers between devices, per_device_rows(): lax.all_to_all(outgoing, 'pw', split_axis=0, concat_axis=0, tiled=True)  4.83 us
    slice x1, local copies, waits for them, and re-layouts, intersect(): psi_all[part]  4.29 us
    unnamed x27, local copies, waits for them, and re-layouts  3.68 us
  transfers between devices with their start and end apart: 3, of which 3 were waited for; matrix products, arithmetic and copies ran while one was open for 9% of the time, Pallas kernels for 0%

profile of v9, /device:TPU:0, one launch (start us, length us, event | category | flops | bytes accessed | tf_op | source)
XLA Modules:
  0.0 69.5 jit_solution(4873803156114571183)
XLA Ops:
  0.6 0.0 copy-start.1
  0.6 1.3 %convolution_bitcast_fusion = f32[128,2,2,32]{0,3,2,1:T(8,128)S(1)} fusion(f32[2,2,128,128,1]{3,2,1,4,0:T(8,128)} %constant.99, f32[2,2,32,128]{3,2,1,0:T(8,128)} %param.7), kind=kOutput, calls=%fused_computation.32 | convolution fusion | flops 25165824 | bytes 393216 | tf_op jit(solution)/shard_map/dczk,cbsk->zdbs/dot_general | solution.py:103
  2.0 0.2 copy.30
  2.2 0.9 %reshape.133 = f32[8,1,2048]{2,1,0:T(1,128)} reshape(f32[128,2,2,32]{3,2,1,0:T(2,128)S(1)} %copy.30) | data formatting | bytes 131072
  3.1 7.3 %all-to-all-start = ((f32[8,1,2048]{2,1,0:T(1,128)}), f32[8,1,2048]{2,1,0:T(1,128)S(1)}, u32[]{:S(2)}, u32[]{:S(2)}) async-start(f32[8,1,2048]{2,1,0:T(1,128)} %reshape.133), calls=%async_computation | async-start | bytes 131072 | tf_op jit(solution)/shard_map/all_to_all | solution.py:104
  10.3 0.7 and_select_fusion
  11.0 0.5 fusion.50
  11.6 0.0 copy-done.1
  11.6 0.1 broadcast_multiply_fusion
  11.7 0.0 copy-start.10
  11.7 4.3 %fusion.59 = (bf16[1,256,32,128]{3,2,1,0:T(8,128)(2,1)S(1)}, bf16[1,256,32,128]{3,2,1,0:T(8,128)(2,1)}) fusion(bf16[2,256,32,128]{3,2,1,0:T(8,128)(2,1)} %param.8), kind=kLoop, calls=%fused_computation.90 | loop fusion | bytes 8388608 | tf_op jit(solution)/shard_map/slice | solution.py:81
  16.0 0.0 copy-done.10
  16.0 0.1 fusion.54
  16.1 1.2 %all-to-all-done = f32[8,1,2048]{2,1,0:T(1,128)S(1)} async-done(((f32[8,1,2048]{2,1,0:T(1,128)}), f32[8,1,2048]{2,1,0:T(1,128)S(1)}, u32[]{:S(2)}, u32[]{:S(2)}) %all-to-all-start) | async-done | bytes 65568 | tf_op jit(solution)/shard_map/all_to_all | solution.py:104
  17.2 0.5 broadcast.179
  17.8 0.8 %reduce.1 = f32[8,2048]{1,0:T(8,128)S(1)} reduce(f32[8,1,2048]{2,1,0:T(1,128)S(1)} %all-to-all-done, f32[]{:T(128)} %broadcast.179), dimensions={1}, to_apply=%all_to_all.9.reduce_sub_computation | reduce | bytes 131076 | tf_op jit(solution)/shard_map/all_to_all | solution.py:104
  18.6 0.9 %reshape.134 = f32[128,2,2,32]{3,2,1,0:T(2,128)} reshape(f32[8,2048]{1,0:T(8,128)S(1)} %reduce.1) | data formatting | bytes 131072
  19.5 1.0 %copy.31 = f32[128,2,2,32]{3,0,2,1:T(8,128)S(1)} copy(f32[128,2,2,32]{3,2,1,0:T(2,128)} %reshape.134) | data formatting | bytes 131072 | tf_op jit(solution)/shard_map/all_to_all | solution.py:104
  20.5 0.7 fusion.60
  21.2 0.7 %mul.155 = f32[2,16,256]{2,1,0:T(8,128)} reshape(f32[1,2,16,8,32]{4,3,2,1,0:T(8,128)S(1)} %copy.32) | data formatting | bytes 65536 | tf_op jit(solution)/shard_map/mul | solution.py:59
  21.9 0.9 %copy.33 = f32[1,2,16,8,32]{4,3,2,1,0:T(8,128)S(1)} copy(f32[1,2,16,8,32]{4,2,3,1,0:T(8,128)} %get-tuple-element.13) | data formatting | bytes 65536 | tf_op jit(solution)/shard_map/slice | solution.py:58
  22.8 0.7 %mul.164 = f32[2,16,256]{2,1,0:T(8,128)} reshape(f32[1,2,16,8,32]{4,3,2,1,0:T(8,128)S(1)} %copy.33) | data formatting | bytes 65536 | tf_op jit(solution)/shard_map/mul | solution.py:59
  23.6 2.2 %fusion = f32[2,16,128,128]{3,2,1,0:T(8,128)S(1)} fusion(f32[128,256]{1,0:T(8,128)S(1)} %get-tuple-element.19, f32[2,16,256]{2,1,0:T(8,128)} %mul.164, f32[128,256]{1,0:T(8,128)S(1)} %get-tuple-element.18, f32[2,16,256]{2,1,0:T(8,128)} %mul.155, s32[256]{0:T(256)S(1)} %get-tuple-element.16), kind=kOutput, calls=%fused_computation.2 | convolution fusion | flops 808484864 | bytes 2425856 | tf_op jit(solution)/shard_map/dot_general | solution.py:48
  25.7 0.0 copy-done.8
  25.7 0.0 copy-done.9
  25.8 0.0 copy-start.2
  25.8 1.3 %fusion.4 = f32[2,16,128,128]{3,2,1,0:T(8,128)S(1)} fusion(f32[128,256]{1,0:T(8,128)S(1)} %get-tuple-element.19, f32[2,16,256]{2,1,0:T(8,128)S(1)} %copy-done.9, f32[128,256]{1,0:T(8,128)S(1)} %get-tuple-element.18, f32[2,16,256]{2,1,0:T(8,128)S(1)} %copy-done.8, s32[256]{0:T(256)S(1)} %get-tuple-element.16), kind=kOutput, calls=%fused_computation.6 | convolution fusion | flops 808484864 | bytes 2425856 | tf_op jit(solution)/shard_map/dot_general | solution.py:48
  27.1 0.0 copy-done.2
  27.1 0.0 copy-start.7
  27.1 1.0 %fusion.16 = f32[2,16,128,128]{3,2,1,0:T(8,128)S(1)} fusion(f32[128,128,1,1]{1,0,3,2:T(8,128)S(1)} %copy-done.2, f32[2,16,128,128]{3,2,1,0:T(8,128)S(1)} %fusion.4, f32[2,16,128,128]{3,2,1,0:T(8,128)S(1)} %fusion), kind=kOutput, calls=%fused_computation.22 | convolution fusion | flops 403177472 | bytes 6356992 | tf_op jit(solution)/shard_map/dot_general | solution.py:48
  28.1 0.0 copy-done.7
  28.1 0.0 copy-start.3
  28.1 1.0 %add_multiply_fusion = f32[2,16,128,128]{3,2,1,0:T(8,128)S(1)} fusion(f32[2,16,128,128]{3,2,1,0:T(8,128)S(1)} %fusion.16, f32[2,16,128,128]{3,2,1,0:T(8,128)S(1)} %fusion.4, f32[128,128,1,1]{1,0,3,2:T(8,128)S(1)} %copy-done.7, f32[16,128,128]{2,1,0:T(8,128)S(1)} %broadcast_multiply_fusion), kind=kOutput, calls=%fused_computation.20 | convolution fusion | flops 403701760 | bytes 7405568 | tf_op jit(solution)/shard_map/dot_general | solution.py:48
  29.2 0.0 copy-done.3
  29.2 1.1 %subtract_multiply_fusion = f32[2,16,128,128]{3,2,1,0:T(8,128)S(1)} fusion(f32[2,16,128,128]{3,2,1,0:T(8,128)S(1)} %fusion.16, f32[2,16,128,128]{3,2,1,0:T(8,128)S(1)} %fusion, f32[128,128,1,1]{1,0,3,2:T(8,128)S(1)} %copy-done.3, f32[16,128,128]{2,1,0:T(8,128)S(1)} %broadcast_multiply_fusion), kind=kOutput, calls=%fused_computation.21 | convolution fusion | flops 403701760 | bytes 7405568 | tf_op jit(solution)/shard_map/dot_general | solution.py:48
  30.3 1.0 %fusion.63 = f32[2,16,128,128]{3,2,1,0:T(8,128)S(1)} fusion(f32[2,16,128,128]{3,2,1,0:T(8,128)S(1)} %subtract_multiply_fusion, f32[128,128,1,1]{1,0,3,2:T(8,128)S(1)} %copy-done.3), kind=kOutput, calls=%fused_computation.96 | convolution fusion | flops 402653184 | bytes 4259840 | tf_op jit(solution)/shard_map/dot_general | solution.py:48
  31.3 0.0 copy-start.6
  31.3 1.0 %fusion.14 = f32[2,16,128,128]{3,2,1,0:T(8,128)S(1)} fusion(f32[128,128,1,1]{1,0,3,2:T(8,128)S(1)} %copy-done.2, f32[2,16,128,128]{3,2,1,0:T(8,128)S(1)} %subtract_multiply_fusion, f32[2,16,128,128]{3,2,1,0:T(8,128)S(1)} %add_multiply_fusion), kind=kOutput, calls=%fused_computation.18 | convolution fusion | flops 403177472 | bytes 6356992 | tf_op jit(solution)/shard_map/dot_general | solution.py:48
  32.3 0.0 copy-done.6
  32.3 1.0 %fusion.62 = f32[2,16,128,128]{3,2,1,0:T(8,128)S(1)} fusion(f32[2,16,128,128]{3,2,1,0:T(8,128)S(1)} %add_multiply_fusion, f32[128,128,1,1]{1,0,3,2:T(8,128)S(1)} %copy-done.6), kind=kOutput, calls=%fused_computation.95 | convolution fusion | flops 402653184 | bytes 4259840 | tf_op jit(solution)/shard_map/dot_general | solution.py:48
  33.3 1.3 %fusion.12 = f32[2,16,128,256]{3,2,1,0:T(8,128)S(1)} fusion(f32[2,16,128,128]{3,2,1,0:T(8,128)S(1)} %fusion.14, f32[2,16,128,128]{3,2,1,0:T(8,128)S(1)} %fusion.62, s32[256]{0:T(256)S(1)} %get-tuple-element.16), kind=kOutput, calls=%fused_computation.16 | convolution fusion | flops 805863424 | bytes 8389632 | tf_op jit(solution)/shard_map/dot_general | solution.py:48
  34.6 2.1 %add_reduce_fusion = (f32[2,16,256]{2,1,0:T(8,128)S(1)}, f32[2,16,256]{2,1,0:T(8,128)S(1)}) fusion(f32[2,16,128,256]{3,2,1,0:T(8,128)S(1)} %fusion.12, f32[128,256]{1,0:T(8,128)S(1)} %get-tuple-element.19, f32[128,256]{1,0:T(8,128)S(1)} %get-tuple-element.18, s32[256]{0:T(256)S(1)} %get-tuple-element.16, f32[2,16,128,128]{3,2,1,0:T(8,128)S(1)} %fusion.14, ...), kind=kOutput, calls=%fused_computation.1 | convolution fusion | flops 814235648 | bytes 8717312 | tf_op jit(solution)/shard_map/dot_general | solution.py:48
  36.7 0.0 copy-start.4
  36.7 0.0 copy-start.5
  36.7 0.1 stack.13
  36.8 0.1 stack.14
  37.0 0.2 copy.80
  37.2 0.9 %reshape.135 = f32[8,1,2048]{2,1,0:T(1,128)} reshape(f32[128,2,2,32]{3,2,1,0:T(2,128)S(1)} %bitcast.104) | data formatting | bytes 131072
  38.1 4.8 %all-to-all-start.1 = ((f32[8,1,2048]{2,1,0:T(1,128)}), f32[8,1,2048]{2,1,0:T(1,128)S(1)}, u32[]{:S(2)}, u32[]{:S(2)}) async-start(f32[8,1,2048]{2,1,0:T(1,128)} %reshape.135), calls=%async_computation.1 | async-start | bytes 131072 | tf_op jit(solution)/shard_map/all_to_all | solution.py:113
  43.0 0.1 add_multiply_fusion.1
  43.0 6.8 %all-to-all-done.1 = f32[8,1,2048]{2,1,0:T(1,128)S(1)} async-done(((f32[8,1,2048]{2,1,0:T(1,128)}), f32[8,1,2048]{2,1,0:T(1,128)S(1)}, u32[]{:S(2)}, u32[]{:S(2)}) %all-to-all-start.1) | async-done | bytes 65568 | tf_op jit(solution)/shard_map/all_to_all | solution.py:113
  49.9 0.8 %reduce.2 = f32[8,2048]{1,0:T(8,128)S(1)} reduce(f32[8,1,2048]{2,1,0:T(1,128)S(1)} %all-to-all-done.1, f32[]{:T(128)} %broadcast.179), dimensions={1}, to_apply=%all_to_all.10.reduce_sub_computation | reduce | bytes 131076 | tf_op jit(solution)/shard_map/all_to_all | solution.py:113
  50.7 0.2 reshape.136
  50.9 0.0 copy-start
  51.0 0.4 fusion.61
  51.3 5.6 %all_gather.3 = bf16[2,8,32,128]{3,2,0,1:T(8,128)(2,1)S(1)} all-gather(bf16[2,2,32,128]{3,2,0,1:T(8,128)(2,1)S(1)} %get-tuple-element.20), channel_id=1, replica_groups=mesh['pw'=8,'band'=4] {'band'}, dimensions={1}, use_global_device_ids=true | all-gather | bytes 163840 | tf_op jit(solution)/shard_map/all_gather | solution.py:117
  56.9 0.1 copy.39
  57.1 0.7 fusion.27
  57.8 0.7 fusion.30
  58.4 0.6 copy.42
  59.0 3.3 %all-to-all-start.2 = ((f32[2,8,1,256]{3,0,2,1:T(2,128)}), f32[2,8,1,256]{3,0,2,1:T(2,128)S(1)}, u32[]{:S(2)}, u32[]{:S(2)}) async-start(f32[2,8,1,256]{3,0,2,1:T(2,128)} %copy.42), calls=%async_computation.2 | async-start | bytes 32768 | tf_op jit(solution)/shard_map/all_to_all | solution.py:87
  62.4 0.6 copy.43
  63.0 5.9 %all-to-all-done.2 = f32[2,8,1,256]{3,0,2,1:T(2,128)S(1)} async-done(((f32[2,8,1,256]{3,0,2,1:T(2,128)}), f32[2,8,1,256]{3,0,2,1:T(2,128)S(1)}, u32[]{:S(2)}, u32[]{:S(2)}) %all-to-all-start.2) | async-done | bytes 16416 | tf_op jit(solution)/shard_map/all_to_all | solution.py:87
  68.9 0.6 reduce_sum.32
  (13 shorter events, 0.2 us)
Async XLA Ops:
  0.6 10.9 %copy-start.1 = (f32[16,128,128]{2,1,0:T(8,128)S(1)}, f32[16,128,128]{2,1,0:T(8,128)}, u32[]{:S(2)}) copy-start(f32[16,128,128]{2,1,0:T(8,128)} %param.9) | copy-start | bytes 3145732
  3.1 14.2 %all-to-all-start = ((f32[8,1,2048]{2,1,0:T(1,128)}), f32[8,1,2048]{2,1,0:T(1,128)S(1)}, u32[]{:S(2)}, u32[]{:S(2)}) async-start(f32[8,1,2048]{2,1,0:T(1,128)} %reshape.133), calls=%async_computation | async-start | bytes 131072 | tf_op jit(solution)/shard_map/all_to_all | solution.py:104
  11.7 4.3 %copy-start.10 = (s32[256]{0:T(256)S(1)}, s32[256]{0:T(256)}, u32[]{:S(2)}) copy-start(s32[256]{0:T(256)} %param.10) | copy-start | bytes 3076
  23.6 2.2 %copy-start.8 = (f32[2,16,256]{2,1,0:T(8,128)S(1)}, f32[2,16,256]{2,1,0:T(8,128)}, u32[]{:S(2)}) copy-start(f32[2,16,256]{2,1,0:T(8,128)} %mul.155) | copy-start | bytes 98308
  23.6 2.2 %copy-start.9 = (f32[2,16,256]{2,1,0:T(8,128)S(1)}, f32[2,16,256]{2,1,0:T(8,128)}, u32[]{:S(2)}) copy-start(f32[2,16,256]{2,1,0:T(8,128)} %mul.164) | copy-start | bytes 98308
  25.8 1.4 %copy-start.2 = (f32[128,128,1,1]{1,0,3,2:T(8,128)S(1)}, f32[128,128,1,1]{1,0,3,2:T(8,128)}, u32[]{:S(2)}) copy-start(f32[128,128,1,1]{1,0,3,2:T(8,128)} %constant.100) | copy-start | bytes 196612
  27.1 1.0 %copy-start.7 = (f32[128,128,1,1]{1,0,3,2:T(8,128)S(1)}, f32[128,128,1,1]{1,0,3,2:T(8,128)}, u32[]{:S(2)}) copy-start(f32[128,128,1,1]{1,0,3,2:T(8,128)} %constant.102) | copy-start | bytes 196612
  28.1 1.1 %copy-start.3 = (f32[128,128,1,1]{1,0,3,2:T(8,128)S(1)}, f32[128,128,1,1]{1,0,3,2:T(8,128)}, u32[]{:S(2)}) copy-start(f32[128,128,1,1]{1,0,3,2:T(8,128)} %constant.101) | copy-start | bytes 196612
  31.3 1.0 %copy-start.6 = (f32[128,128,1,1]{1,0,3,2:T(8,128)S(1)}, f32[128,128,1,1]{1,0,3,2:T(8,128)}, u32[]{:S(2)}) copy-start(f32[128,128,1,1]{1,0,3,2:T(8,128)} %constant.103) | copy-start | bytes 196612
  36.7 14.2 %copy-start.4 = (f32[2,2,128,128,1]{3,2,1,0,4:T(8,128)S(1)}, f32[2,2,128,128,1]{3,2,1,0,4:T(8,128)}, u32[]{:S(2)}) copy-start(f32[2,2,128,128,1]{3,2,1,0,4:T(8,128)} %constant.104) | copy-start | bytes 786436
  36.7 14.2 %copy-start.5 = (f32[2,2,32,128]{3,2,1,0:T(8,128)S(1)}, f32[2,2,32,128]{3,2,1,0:T(8,128)}, u32[]{:S(2)}) copy-start(f32[2,2,32,128]{3,2,1,0:T(8,128)} %param.7) | copy-start | bytes 196612
  38.1 11.7 %all-to-all-start.1 = ((f32[8,1,2048]{2,1,0:T(1,128)}), f32[8,1,2048]{2,1,0:T(1,128)S(1)}, u32[]{:S(2)}, u32[]{:S(2)}) async-start(f32[8,1,2048]{2,1,0:T(1,128)} %reshape.135), calls=%async_computation.1 | async-start | bytes 131072 | tf_op jit(solution)/shard_map/all_to_all | solution.py:113
  50.9 6.2 %copy-start = (bf16[1,256,32,128]{3,2,1,0:T(8,128)(2,1)S(1)}, bf16[1,256,32,128]{3,2,1,0:T(8,128)(2,1)}, u32[]{:S(2)}) copy-start(bf16[1,256,32,128]{3,2,1,0:T(8,128)(2,1)} %get-tuple-element.11) | copy-start | bytes 6291460
  59.0 9.8 %all-to-all-start.2 = ((f32[2,8,1,256]{3,0,2,1:T(2,128)}), f32[2,8,1,256]{3,0,2,1:T(2,128)S(1)}, u32[]{:S(2)}, u32[]{:S(2)}) async-start(f32[2,8,1,256]{3,0,2,1:T(2,128)} %copy.42), calls=%async_computation.2 | async-start | bytes 32768 | tf_op jit(solution)/shard_map/all_to_all | solution.py:87

commit v10 on v7

--- a/solution.py
+++ b/solution.py
@@ -127,6 +127,7 @@
     applied = kinetic[None, None] * psi_block + vpsi
     lowered = applied.astype(jnp.bfloat16)
     gathered = lax.all_gather(lowered, "band", axis=1, tiled=True)
+    psi_all, _ = lax.optimization_barrier((psi_all, outgoing))
     intersection = intersect(gathered, psi_all, pw_count)
     return (intersection, applied)
 

time: 66 us -> 67.6 us (1.024)
  waiting for transfers between devices: 14 us -> 12.4 us
  local copies, waits for them, and re-layouts: 10.1 us -> 11.5 us
  matrix products: 16.5 us -> 17.8 us
    all_to_all x1, waiting for transfers between devices: 6.83 us -> 0.96 us  [per_device_rows(): lax.all_to_all(outgoing, 'pw', split_axis=0, concat_axis=0, tiled=True)]
    optimization_barrier x0 -> x1, local copies, waits for them, and re-layouts: none -> 5.8 us  [per_device_rows(): psi_all, _ = lax.optimization_barrier((psi_all, outgoing))]
    slice x1 -> x0, local copies, waits for them, and re-layouts: 4.13 us -> none  [intersect(): psi_all[:, k * width:(k + 1) * width]]
    all_to_all x1, waiting for transfers between devices: 1.34 us -> 5.46 us  [per_device_rows(): lax.all_to_all(z_lines, 'pw', split_axis=0, concat_axis=0, tiled=True)]
    dot_general x4, matrix products: 1.72 us -> 4 us  [intersect(): lax.dot_general(both, psi_all[:, k * width:(k + 1) * width], dims, prefer...]
    all_to_all x1, starting transfers between devices: 3.34 us -> 4.97 us  [intersect(): lax.all_to_all(pieces, 'pw', split_axis=1, concat_axis=1, tiled=True)]
    all_to_all x1, starting transfers between devices: 4.67 us -> 3.35 us  [per_device_rows(): lax.all_to_all(outgoing, 'pw', split_axis=0, concat_axis=0, tiled=True)]
    dot_general x1, matrix products: 1.31 us -> 0.36 us  [per_device_rows(): vpsi = jnp.einsum('dckz,zcbs->dbsk', forward, sticks_back, precision=fast)]
  transfers between devices with their start and end apart: 3 -> 3, of which waited for: 3 -> 3; matrix products, arithmetic and copies ran while one was open for 10% -> 12% of each run, Pallas kernels for 0% -> 0%
where the time goes in v10:
time: 67.6 us; the launch traced here: 67.1 us
  matrix products  17.8 us (26%)
  starting transfers between devices  15.6 us (23%)
  waiting for transfers between devices  12.4 us (18%)
  local copies, waits for them, and re-layouts  11.5 us (17%)
  blocking collectives  5.56 us (8%)
  other arithmetic  3.22 us (5%)
  between operations  1 us (1%)
    dot_general x10, matrix products, mult(): jnp.dot(left, right, precision=lax.Precision.HIGH, preferred_element_type...  12.1 us
    all_to_all x1, starting transfers between devices, per_device_rows(): lax.all_to_all(z_lines, 'pw', split_axis=0, concat_axis=0, tiled=True)  7.28 us
    all_to_all x1, waiting for transfers between devices, intersect(): lax.all_to_all(pieces, 'pw', split_axis=1, concat_axis=1, tiled=True)  5.94 us
    optimization_barrier x1, local copies, waits for them, and re-layouts, per_device_rows(): psi_all, _ = lax.optimization_barrier((psi_all, outgoing))  5.8 us
    all_gather x1, blocking collectives, per_device_rows(): gathered = lax.all_gather(lowered, 'band', axis=1, tiled=True)  5.56 us
    all_to_all x1, waiting for transfers between devices, per_device_rows(): lax.all_to_all(z_lines, 'pw', split_axis=0, concat_axis=0, tiled=True)  5.46 us
    all_to_all x1, starting transfers between devices, intersect(): lax.all_to_all(pieces, 'pw', split_axis=1, concat_axis=1, tiled=True)  4.97 us
    dot_general x4, matrix products, intersect(): lax.dot_general(both, psi_all[:, k * width:(k + 1) * width], dims, prefer...  4 us
  transfers between devices with their start and end apart: 3, of which 3 were waited for; matrix products, arithmetic and copies ran while one was open for 12% of the time, Pallas kernels for 0%

profile of v10, /device:TPU:0, one launch (start us, length us, event | category | flops | bytes accessed | tf_op | source)
XLA Modules:
  0.0 67.1 jit_solution(14808370204689774023)
XLA Ops:
  0.6 0.0 copy-start.8
  0.6 0.0 copy-start.1
  0.7 1.3 %convolution_bitcast_fusion = f32[128,2,2,32]{0,3,2,1:T(8,128)S(1)} fusion(f32[2,2,128,128,1]{3,2,1,4,0:T(8,128)} %constant.99, f32[2,2,32,128]{3,2,1,0:T(8,128)} %param.7), kind=kOutput, calls=%fused_computation.28 | convolution fusion | flops 25165824 | bytes 393216 | tf_op jit(solution)/shard_map/dczk,cbsk->zdbs/dot_general | solution.py:115
  2.0 0.2 copy.38
  2.2 0.9 %reshape.135 = f32[8,1,2048]{2,1,0:T(1,128)} reshape(f32[128,2,2,32]{3,2,1,0:T(2,128)S(1)} %copy.38) | data formatting | bytes 131072
  3.1 7.3 %all-to-all-start = ((f32[8,1,2048]{2,1,0:T(1,128)}), f32[8,1,2048]{2,1,0:T(1,128)S(1)}, u32[]{:S(2)}, u32[]{:S(2)}) async-start(f32[8,1,2048]{2,1,0:T(1,128)} %reshape.135), calls=%async_computation | async-start | bytes 131072 | tf_op jit(solution)/shard_map/all_to_all | solution.py:116
  10.4 0.7 %and_select_fusion = (s32[256]{0:T(256)S(1)}, s32[256]{0:T(256)S(1)}) fusion(s32[256]{0:T(256)} %param.10), kind=kLoop, calls=%fused_computation.70 | loop fusion | flops 4864 | bytes 3072 | tf_op jit(solution)/shard_map/jit(remainder)/select_n | solution.py:35
  11.0 0.5 fusion.48
  11.6 0.0 copy-done.1
  11.6 0.1 broadcast_multiply_fusion
  11.7 0.0 copy-done.8
  11.7 0.1 fusion.52
  11.8 5.5 %all-to-all-done = f32[8,1,2048]{2,1,0:T(1,128)S(1)} async-done(((f32[8,1,2048]{2,1,0:T(1,128)}), f32[8,1,2048]{2,1,0:T(1,128)S(1)}, u32[]{:S(2)}, u32[]{:S(2)}) %all-to-all-start) | async-done | bytes 65568 | tf_op jit(solution)/shard_map/all_to_all | solution.py:116
  17.3 0.5 broadcast.179
  17.8 0.8 %reduce.1 = f32[8,2048]{1,0:T(8,128)S(1)} reduce(f32[8,1,2048]{2,1,0:T(1,128)S(1)} %all-to-all-done, f32[]{:T(128)} %broadcast.179), dimensions={1}, to_apply=%all_to_all.9.reduce_sub_computation | reduce | bytes 131076 | tf_op jit(solution)/shard_map/all_to_all | solution.py:116
  18.6 0.2 reshape.136
  18.9 0.1 mul.155
  19.1 0.1 mul.164
  19.2 1.3 %fusion = f32[2,16,128,128]{3,2,1,0:T(8,128)S(1)} fusion(f32[128,256]{1,0:T(8,128)S(1)} %get-tuple-element.19, f32[2,16,256]{2,1,0:T(8,128)S(1)} %mul.164, f32[128,256]{1,0:T(8,128)S(1)} %get-tuple-element.18, f32[2,16,256]{2,1,0:T(8,128)S(1)} %mul.155, s32[256]{0:T(256)S(1)} %get-tuple-element.16), kind=kOutput, calls=%fused_computation.2 | convolution fusion | flops 808484864 | bytes 2425856 | tf_op jit(solution)/shard_map/dot_general | solution.py:48
  20.5 0.0 copy-start.2
  20.5 1.3 %fusion.4 = f32[2,16,128,128]{3,2,1,0:T(8,128)S(1)} fusion(f32[128,256]{1,0:T(8,128)S(1)} %get-tuple-element.19, f32[2,16,256]{2,1,0:T(8,128)S(1)} %mul.164, f32[128,256]{1,0:T(8,128)S(1)} %get-tuple-element.18, f32[2,16,256]{2,1,0:T(8,128)S(1)} %mul.155, s32[256]{0:T(256)S(1)} %get-tuple-element.16), kind=kOutput, calls=%fused_computation.6 | convolution fusion | flops 808484864 | bytes 2425856 | tf_op jit(solution)/shard_map/dot_general | solution.py:48
  21.9 0.0 copy-done.2
  21.9 0.0 copy-start.7
  21.9 1.0 %fusion.14 = f32[2,16,128,128]{3,2,1,0:T(8,128)S(1)} fusion(f32[128,128,1,1]{1,0,3,2:T(8,128)S(1)} %copy-done.2, f32[2,16,128,128]{3,2,1,0:T(8,128)S(1)} %fusion.4, f32[2,16,128,128]{3,2,1,0:T(8,128)S(1)} %fusion), kind=kOutput, calls=%fused_computation.18 | convolution fusion | flops 403177472 | bytes 6356992 | tf_op jit(solution)/shard_map/dot_general | solution.py:48
  22.9 0.0 copy-done.7
  22.9 0.0 copy-start.3
  22.9 1.0 %add_multiply_fusion = f32[2,16,128,128]{3,2,1,0:T(8,128)S(1)} fusion(f32[2,16,128,128]{3,2,1,0:T(8,128)S(1)} %fusion.14, f32[2,16,128,128]{3,2,1,0:T(8,128)S(1)} %fusion.4, f32[128,128,1,1]{1,0,3,2:T(8,128)S(1)} %copy-done.7, f32[16,128,128]{2,1,0:T(8,128)S(1)} %broadcast_multiply_fusion), kind=kOutput, calls=%fused_computation.16 | convolution fusion | flops 403701760 | bytes 7405568 | tf_op jit(solution)/shard_map/dot_general | solution.py:48
  24.0 0.0 copy-done.3
  24.0 1.1 %subtract_multiply_fusion = f32[2,16,128,128]{3,2,1,0:T(8,128)S(1)} fusion(f32[2,16,128,128]{3,2,1,0:T(8,128)S(1)} %fusion.14, f32[2,16,128,128]{3,2,1,0:T(8,128)S(1)} %fusion, f32[128,128,1,1]{1,0,3,2:T(8,128)S(1)} %copy-done.3, f32[16,128,128]{2,1,0:T(8,128)S(1)} %broadcast_multiply_fusion), kind=kOutput, calls=%fused_computation.17 | convolution fusion | flops 403701760 | bytes 7405568 | tf_op jit(solution)/shard_map/dot_general | solution.py:48
  25.1 1.0 %fusion.60 = f32[2,16,128,128]{3,2,1,0:T(8,128)S(1)} fusion(f32[2,16,128,128]{3,2,1,0:T(8,128)S(1)} %subtract_multiply_fusion, f32[128,128,1,1]{1,0,3,2:T(8,128)S(1)} %copy-done.3), kind=kOutput, calls=%fused_computation.94 | convolution fusion | flops 402653184 | bytes 4259840 | tf_op jit(solution)/shard_map/dot_general | solution.py:48
  26.0 0.0 copy-start.6
  26.1 1.0 %fusion.12 = f32[2,16,128,128]{3,2,1,0:T(8,128)S(1)} fusion(f32[128,128,1,1]{1,0,3,2:T(8,128)S(1)} %copy-done.2, f32[2,16,128,128]{3,2,1,0:T(8,128)S(1)} %subtract_multiply_fusion, f32[2,16,128,128]{3,2,1,0:T(8,128)S(1)} %add_multiply_fusion), kind=kOutput, calls=%fused_computation.14 | convolution fusion | flops 403177472 | bytes 6356992 | tf_op jit(solution)/shard_map/dot_general | solution.py:48
  27.1 0.0 copy-done.6
  27.1 1.0 %fusion.59 = f32[2,16,128,128]{3,2,1,0:T(8,128)S(1)} fusion(f32[2,16,128,128]{3,2,1,0:T(8,128)S(1)} %add_multiply_fusion, f32[128,128,1,1]{1,0,3,2:T(8,128)S(1)} %copy-done.6), kind=kOutput, calls=%fused_computation.93 | convolution fusion | flops 402653184 | bytes 4259840 | tf_op jit(solution)/shard_map/dot_general | solution.py:48
  28.1 1.3 %fusion.10 = f32[2,16,128,256]{3,2,1,0:T(8,128)S(1)} fusion(f32[2,16,128,128]{3,2,1,0:T(8,128)S(1)} %fusion.12, f32[2,16,128,128]{3,2,1,0:T(8,128)S(1)} %fusion.59, s32[256]{0:T(256)S(1)} %get-tuple-element.16), kind=kOutput, calls=%fused_computation.12 | convolution fusion | flops 805863424 | bytes 8389632 | tf_op jit(solution)/shard_map/dot_general | solution.py:48
  29.3 2.1 %add_reduce_fusion = (f32[2,16,256]{2,1,0:T(8,128)S(1)}, f32[2,16,256]{2,1,0:T(8,128)S(1)}) fusion(f32[2,16,128,256]{3,2,1,0:T(8,128)S(1)} %fusion.10, f32[128,256]{1,0:T(8,128)S(1)} %get-tuple-element.19, f32[128,256]{1,0:T(8,128)S(1)} %get-tuple-element.18, s32[256]{0:T(256)S(1)} %get-tuple-element.16, f32[2,16,128,128]{3,2,1,0:T(8,128)S(1)} %fusion.12, ...), kind=kOutput, calls=%fused_computation.1 | convolution fusion | flops 814235648 | bytes 8717312 | tf_op jit(solution)/shard_map/dot_general | solution.py:48
  31.5 0.1 stack.13
  31.6 0.1 stack.14
  31.7 0.2 copy.80
  32.0 0.9 %reshape.137 = f32[8,1,2048]{2,1,0:T(1,128)} reshape(f32[128,2,2,32]{3,2,1,0:T(2,128)S(1)} %bitcast.92) | data formatting | bytes 131072
  32.9 3.4 %all-to-all-start.1 = ((f32[8,1,2048]{2,1,0:T(1,128)}), f32[8,1,2048]{2,1,0:T(1,128)S(1)}, u32[]{:S(2)}, u32[]{:S(2)}) async-start(f32[8,1,2048]{2,1,0:T(1,128)} %reshape.137), calls=%async_computation.1 | async-start | bytes 131072 | tf_op jit(solution)/shard_map/all_to_all | solution.py:125
  36.2 0.1 add_multiply_fusion.1
  36.3 0.0 copy-start.4
  36.3 5.8 %copy.48 = bf16[2,256,32,128]{3,1,0,2:T(8,128)(2,1)} copy(bf16[2,256,32,128]{3,2,1,0:T(8,128)(2,1)} %param.8) | data formatting | bytes 8388608 | tf_op jit(solution)/shard_map/optimization_barrier | solution.py:130
  42.1 1.0 %all-to-all-done.1 = f32[8,1,2048]{2,1,0:T(1,128)S(1)} async-done(((f32[8,1,2048]{2,1,0:T(1,128)}), f32[8,1,2048]{2,1,0:T(1,128)S(1)}, u32[]{:S(2)}, u32[]{:S(2)}) %all-to-all-start.1) | async-done | bytes 65568 | tf_op jit(solution)/shard_map/all_to_all | solution.py:125
  43.1 0.8 %reduce.2 = f32[8,2048]{1,0:T(8,128)S(1)} reduce(f32[8,1,2048]{2,1,0:T(1,128)S(1)} %all-to-all-done.1, f32[]{:T(128)} %broadcast.179), dimensions={1}, to_apply=%all_to_all.10.reduce_sub_computation | reduce | bytes 131076 | tf_op jit(solution)/shard_map/all_to_all | solution.py:125
  43.9 0.2 reshape.138
  44.1 0.0 copy-done.4
  44.1 0.0 copy-done.5
  44.2 0.4 fusion.58
  44.5 0.0 copy-start
  44.5 5.6 %all_gather.3 = bf16[2,8,32,128]{3,2,0,1:T(8,128)(2,1)S(1)} all-gather(bf16[2,2,32,128]{3,2,0,1:T(8,128)(2,1)S(1)} %get-tuple-element.20), channel_id=1, replica_groups=mesh['pw'=8,'band'=4] {'band'}, dimensions={1}, use_global_device_ids=true | all-gather | bytes 163840 | tf_op jit(solution)/shard_map/all_gather | solution.py:129
  50.1 0.1 copy.47
  50.2 1.6 %convolution_bitcast_fusion.5 = f32[16,64]{1,0:T(8,128)S(1)} fusion(bf16[2,256,32,128]{3,1,0,2:T(8,128)(2,1)} %copy.48, bf16[1,8,32,128]{3,1,0,2:T(8,128)(2,1)S(1)} %get-tuple-element.15, bf16[1,8,32,128]{3,1,0,2:T(8,128)(2,1)S(1)} %get-tuple-element.14, bf16[2,8,32,128]{3,1,0,2:T(8,128)(2,1)S(1)} %copy.47), kind=kOutput, calls=%fused_computation.34 | convolution fusion | flops 17563648 | bytes 1314816 | tf_op jit(solution)/shard_map/dot_general | solution.py:84
  51.8 1.6 %convolution_bitcast_fusion.4 = f32[16,64]{1,0:T(8,128)S(1)} fusion(bf16[2,256,32,128]{3,1,0,2:T(8,128)(2,1)} %copy.48, bf16[1,8,32,128]{3,1,0,2:T(8,128)(2,1)S(1)} %get-tuple-element.15, bf16[1,8,32,128]{3,1,0,2:T(8,128)(2,1)S(1)} %get-tuple-element.14, bf16[2,8,32,128]{3,1,0,2:T(8,128)(2,1)S(1)} %copy.47), kind=kOutput, calls=%fused_computation.33 | convolution fusion | flops 17563648 | bytes 1314816 | tf_op jit(solution)/shard_map/dot_general | solution.py:84
  53.4 0.0 copy-done
  53.4 0.4 convolution_bitcast_fusion.3
  53.8 0.4 convolution_bitcast_fusion.2
  54.2 0.1 maximum_bitcast_fusion.1
  54.3 0.6 copy.52
  54.9 5.0 %all-to-all-start.2 = ((f32[2,8,1,256]{3,0,2,1:T(2,128)}), f32[2,8,1,256]{3,0,2,1:T(2,128)S(1)}, u32[]{:S(2)}, u32[]{:S(2)}) async-start(f32[2,8,1,256]{3,0,2,1:T(2,128)} %copy.52), calls=%async_computation.2 | async-start | bytes 32768 | tf_op jit(solution)/shard_map/all_to_all | solution.py:99
  59.9 0.6 copy.53
  60.5 5.9 %all-to-all-done.2 = f32[2,8,1,256]{3,0,2,1:T(2,128)S(1)} async-done(((f32[2,8,1,256]{3,0,2,1:T(2,128)}), f32[2,8,1,256]{3,0,2,1:T(2,128)S(1)}, u32[]{:S(2)}, u32[]{:S(2)}) %all-to-all-start.2) | async-done | bytes 16416 | tf_op jit(solution)/shard_map/all_to_all | solution.py:99
  66.5 0.6 reduce_sum.35
  (11 shorter events, 0.3 us)
Async XLA Ops:
  0.6 11.1 %copy-start.8 = (s32[256]{0:T(256)S(1)}, s32[256]{0:T(256)}, u32[]{:S(2)}) copy-start(s32[256]{0:T(256)} %param.10) | copy-start | bytes 3076
  0.6 10.9 %copy-start.1 = (f32[16,128,128]{2,1,0:T(8,128)S(1)}, f32[16,128,128]{2,1,0:T(8,128)}, u32[]{:S(2)}) copy-start(f32[16,128,128]{2,1,0:T(8,128)} %param.9) | copy-start | bytes 3145732
  3.1 14.2 %all-to-all-start = ((f32[8,1,2048]{2,1,0:T(1,128)}), f32[8,1,2048]{2,1,0:T(1,128)S(1)}, u32[]{:S(2)}, u32[]{:S(2)}) async-start(f32[8,1,2048]{2,1,0:T(1,128)} %reshape.135), calls=%async_computation | async-start | bytes 131072 | tf_op jit(solution)/shard_map/all_to_all | solution.py:116
  20.5 1.4 %copy-start.2 = (f32[128,128,1,1]{1,0,3,2:T(8,128)S(1)}, f32[128,128,1,1]{1,0,3,2:T(8,128)}, u32[]{:S(2)}) copy-start(f32[128,128,1,1]{1,0,3,2:T(8,128)} %constant.100) | copy-start | bytes 196612
  21.9 1.0 %copy-start.7 = (f32[128,128,1,1]{1,0,3,2:T(8,128)S(1)}, f32[128,128,1,1]{1,0,3,2:T(8,128)}, u32[]{:S(2)}) copy-start(f32[128,128,1,1]{1,0,3,2:T(8,128)} %constant.102) | copy-start | bytes 196612
  22.9 1.1 %copy-start.3 = (f32[128,128,1,1]{1,0,3,2:T(8,128)S(1)}, f32[128,128,1,1]{1,0,3,2:T(8,128)}, u32[]{:S(2)}) copy-start(f32[128,128,1,1]{1,0,3,2:T(8,128)} %constant.101) | copy-start | bytes 196612
  26.0 1.0 %copy-start.6 = (f32[128,128,1,1]{1,0,3,2:T(8,128)S(1)}, f32[128,128,1,1]{1,0,3,2:T(8,128)}, u32[]{:S(2)}) copy-start(f32[128,128,1,1]{1,0,3,2:T(8,128)} %constant.103) | copy-start | bytes 196612
  32.9 10.2 %all-to-all-start.1 = ((f32[8,1,2048]{2,1,0:T(1,128)}), f32[8,1,2048]{2,1,0:T(1,128)S(1)}, u32[]{:S(2)}, u32[]{:S(2)}) async-start(f32[8,1,2048]{2,1,0:T(1,128)} %reshape.137), calls=%async_computation.1 | async-start | bytes 131072 | tf_op jit(solution)/shard_map/all_to_all | solution.py:125
  36.3 7.8 %copy-start.4 = (f32[2,2,128,128,1]{3,2,1,0,4:T(8,128)S(1)}, f32[2,2,128,128,1]{3,2,1,0,4:T(8,128)}, u32[]{:S(2)}) copy-start(f32[2,2,128,128,1]{3,2,1,0,4:T(8,128)} %constant.104) | copy-start | bytes 786436
  36.3 7.9 %copy-start.5 = (f32[2,2,32,128]{3,2,1,0:T(8,128)S(1)}, f32[2,2,32,128]{3,2,1,0:T(8,128)}, u32[]{:S(2)}) copy-start(f32[2,2,32,128]{3,2,1,0:T(8,128)} %param.7) | copy-start | bytes 196612
  44.5 8.9 %copy-start = (bf16[2,256,32,128]{3,1,0,2:T(8,128)(2,1)S(1)}, bf16[2,256,32,128]{3,1,0,2:T(8,128)(2,1)}, u32[]{:S(2)}) copy-start(bf16[2,256,32,128]{3,1,0,2:T(8,128)(2,1)} %copy.48) | copy-start | bytes 12582916
  54.9 11.5 %all-to-all-start.2 = ((f32[2,8,1,256]{3,0,2,1:T(2,128)}), f32[2,8,1,256]{3,0,2,1:T(2,128)S(1)}, u32[]{:S(2)}, u32[]{:S(2)}) async-start(f32[2,8,1,256]{3,0,2,1:T(2,128)} %copy.52), calls=%async_computation.2 | async-start | bytes 32768 | tf_op jit(solution)/shard_map/all_to_all | solution.py:99

commit v11 on v7

--- a/solution.py
+++ b/solution.py
@@ -113,7 +113,9 @@
     forward = dft_table(grid_size, -1.0)
     tables = plane_tables(stick_col, grid_size)
     z_lines = jnp.einsum("dczk,cbsk->zdbs", inverse, psi_block, precision=fast)
-    received = lax.all_to_all(z_lines, "pw", split_axis=0, concat_axis=0, tiled=True)
+    received = lax.all_to_all(
+        z_lines.astype(jnp.bfloat16), "pw", split_axis=0, concat_axis=0, tiled=True
+    ).astype(jnp.float32)
     lanes = received.shape[1:]
     received = received.reshape((pw_count, planes) + lanes)
     amp = jnp.transpose(received, (2, 3, 1, 0, 4)).reshape(
@@ -122,7 +124,9 @@
     picked = plane_phase(amp, potential, tables, grid_size)
     outgoing = picked.reshape(lanes[0], lanes[1], planes, pw_count, sticks_dev)
     outgoing = jnp.transpose(outgoing, (3, 2, 0, 1, 4)).reshape((pw_count * planes,) + lanes)
-    sticks_back = lax.all_to_all(outgoing, "pw", split_axis=0, concat_axis=0, tiled=True)
+    sticks_back = lax.all_to_all(
+        outgoing.astype(jnp.bfloat16), "pw", split_axis=0, concat_axis=0, tiled=True
+    ).astype(jnp.float32)
     vpsi = jnp.einsum("dckz,zcbs->dbsk", forward, sticks_back, precision=fast)
     applied = kinetic[None, None] * psi_block + vpsi
     lowered = applied.astype(jnp.bfloat16)

time: 66 us -> 71.8 us (1.088)
  local copies, waits for them, and re-layouts: 10.1 us -> 13.3 us
  waiting for transfers between devices: 14 us -> 11.9 us
  matrix products: 16.5 us -> 18.2 us
  other arithmetic: 3.21 us -> 4.6 us
  starting transfers between devices: 15.3 us -> 16.6 us
    all_to_all x2, waiting for transfers between devices: 8.17 us -> 6.05 us  [the longest x1 6.05 us: per_device_rows(): lax.all_to_all(outgoing.astype(jnp.bfloat16), 'pw', split_axis=0, concat_...]
    all_to_all x2 -> x0, other arithmetic: 1.6 us -> none  [the longest x1 0.8 us: per_device_rows(): lax.all_to_all(outgoing, 'pw', split_axis=0, concat_axis=0, tiled=True)]
    all_to_all x2, starting transfers between devices: 11.9 us -> 13.3 us  [the longest x1 7.28 us: per_device_rows(): lax.all_to_all(z_lines.astype(jnp.bfloat16), 'pw', split_axis=0, concat_a...]
    dot_general x4, matrix products: 1.72 us -> 2.96 us  [intersect(): lax.dot_general(both, psi_all[:, k * width:(k + 1) * width], dims, prefer...]
    div x1, other arithmetic: 0.08 us -> 1.31 us  [plane_phase(): scaled_pot = (pot / float(grid_size ** 3))[None]]
    mul x2, local copies, waits for them, and re-layouts: 0.19 us -> 1.41 us  [plane_phase(): spread_re = val_re * phase_cos - val_im * phase_sin]
    slice x1, local copies, waits for them, and re-layouts: 0.04 us -> 0.95 us  [plane_phase(): val_im = amp[1][:, :, None, :]]
    dot_general x10, matrix products: 12.1 us -> 13 us  [mult(): jnp.dot(left, right, precision=lax.Precision.HIGH, preferred_element_type...]
  transfers between devices with their start and end apart: 3 -> 3, of which waited for: 3 -> 2; matrix products, arithmetic and copies ran while one was open for 10% -> 13% of each run, Pallas kernels for 0% -> 0%
where the time goes in v11:
time: 71.8 us; the launch traced here: 71 us
  matrix products  18.2 us (25%)
  starting transfers between devices  16.6 us (23%)
  local copies, waits for them, and re-layouts  13.3 us (19%)
  waiting for transfers between devices  11.9 us (17%)
  blocking collectives  5.43 us (8%)
  other arithmetic  4.6 us (6%)
  between operations  0.95 us (1%)
    dot_general x10, matrix products, mult(): jnp.dot(left, right, precision=lax.Precision.HIGH, preferred_element_type...  13 us
    all_to_all x1, starting transfers between devices, per_device_rows(): lax.all_to_all(z_lines.astype(jnp.bfloat16), 'pw', split_axis=0, concat_a...  7.28 us
    all_to_all x1, waiting for transfers between devices, per_device_rows(): lax.all_to_all(outgoing.astype(jnp.bfloat16), 'pw', split_axis=0, concat_...  6.05 us
    all_to_all x1, starting transfers between devices, per_device_rows(): lax.all_to_all(outgoing.astype(jnp.bfloat16), 'pw', split_axis=0, concat_...  6.01 us
    all_to_all x1, waiting for transfers between devices, intersect(): lax.all_to_all(pieces, 'pw', split_axis=1, concat_axis=1, tiled=True)  5.88 us
    all_gather x1, blocking collectives, per_device_rows(): gathered = lax.all_gather(lowered, 'band', axis=1, tiled=True)  5.43 us
    slice x1, local copies, waits for them, and re-layouts, intersect(): psi_all[:, k * width:(k + 1) * width]  4.28 us
    unnamed x23, local copies, waits for them, and re-layouts  4.05 us
  transfers between devices with their start and end apart: 3, of which 2 were waited for; matrix products, arithmetic and copies ran while one was open for 13% of the time, Pallas kernels for 0%

profile of v11, /device:TPU:0, one launch (start us, length us, event | category | flops | bytes accessed | tf_op | source)
XLA Modules:
  0.0 71.0 jit_solution(6232123622699708583)
XLA Ops:
  0.6 1.2 %fusion.26 = bf16[128,2,2,32]{0,3,2,1:T(8,128)(2,1)S(1)} fusion(f32[2,2,128,128,1]{3,2,1,4,0:T(8,128)} %constant.99, f32[2,2,32,128]{3,2,1,0:T(8,128)} %param.7), kind=kOutput, calls=%fused_computation.32 | convolution fusion | flops 25182208 | bytes 360448 | tf_op jit(solution)/shard_map/dczk,cbsk->zdbs/dot_general | solution.py:115
  1.9 0.1 copy.38
  2.0 0.8 %reshape.137 = bf16[8,2,1024]{2,1,0:T(2,128)(2,1)} reshape(bf16[128,2,2,32]{3,2,1,0:T(2,128)(2,1)S(1)} %copy.38) | data formatting | bytes 65536
  2.8 7.3 %all-to-all-start = ((bf16[8,2,1024]{2,1,0:T(2,128)(2,1)}), bf16[8,2,1024]{2,1,0:T(2,128)(2,1)}, u32[]{:S(2)}, u32[]{:S(2)}) async-start(bf16[8,2,1024]{2,1,0:T(2,128)(2,1)} %reshape.137), calls=%async_computation | async-start | bytes 65536 | tf_op jit(solution)/shard_map/all_to_all | solution.py:116
  10.1 0.5 fusion.58
  10.6 0.7 and_select_fusion
  11.3 0.5 fusion.50
  11.8 1.3 %broadcast_multiply_fusion = f32[16,128,128]{2,1,0:T(8,128)S(1)} fusion(f32[16,128,128]{2,1,0:T(8,128)} %param.9), kind=kLoop, calls=%fused_computation.41 | loop fusion | flops 262144 | bytes 2097152 | tf_op jit(solution)/shard_map/div | solution.py:56
  13.1 0.0 copy-start.8
  13.1 4.3 %fusion.59 = (bf16[2,64,32,128]{3,2,1,0:T(8,128)(2,1)}, bf16[2,64,32,128]{3,2,1,0:T(8,128)(2,1)S(1)}, bf16[2,64,32,128]{3,2,1,0:T(8,128)(2,1)}, bf16[2,64,32,128]{3,2,1,0:T(8,128)(2,1)S(1)}) fusion(bf16[2,256,32,128]{3,2,1,0:T(8,128)(2,1)} %param.8), kind=kLoop, calls=%fused_computation.92 | loop fusion | bytes 8388608 | tf_op jit(solution)/shard_map/slice | solution.py:86
  17.4 0.0 copy-done.8
  17.4 0.6 fusion.54
  18.0 0.0 all-to-all-done
  18.1 0.9 %reshape.138 = bf16[128,2,2,32]{3,2,1,0:T(2,128)(2,1)S(1)} reshape(bf16[8,2,1024]{2,1,0:T(2,128)(2,1)} %all-to-all-done) | data formatting | bytes 65536
  19.0 0.7 fusion.60
  19.7 0.7 mul.155
  20.4 0.9 %copy.41 = f32[1,2,16,8,32]{4,3,2,1,0:T(8,128)S(1)} copy(f32[1,2,16,8,32]{4,2,3,1,0:T(8,128)} %get-tuple-element.15) | data formatting | bytes 65536 | tf_op jit(solution)/shard_map/slice | solution.py:58
  21.4 0.7 %mul.164 = f32[2,16,256]{2,1,0:T(8,128)} reshape(f32[1,2,16,8,32]{4,3,2,1,0:T(8,128)S(1)} %copy.41) | data formatting | bytes 65536 | tf_op jit(solution)/shard_map/mul | solution.py:59
  22.1 2.2 %fusion = f32[2,16,128,128]{3,2,1,0:T(8,128)S(1)} fusion(f32[128,256]{1,0:T(8,128)S(1)} %get-tuple-element.21, f32[2,16,256]{2,1,0:T(8,128)} %mul.164, f32[128,256]{1,0:T(8,128)S(1)} %get-tuple-element.20, f32[2,16,256]{2,1,0:T(8,128)} %mul.155, s32[256]{0:T(256)S(1)} %get-tuple-element.18), kind=kOutput, calls=%fused_computation.2 | convolution fusion | flops 808484864 | bytes 2425856 | tf_op jit(solution)/shard_map/dot_general | solution.py:48
  24.3 0.0 copy-done.6
  24.3 0.0 copy-done.7
  24.3 0.0 copy-start.1
  24.3 1.3 %fusion.4 = f32[2,16,128,128]{3,2,1,0:T(8,128)S(1)} fusion(f32[128,256]{1,0:T(8,128)S(1)} %get-tuple-element.21, f32[2,16,256]{2,1,0:T(8,128)S(1)} %copy-done.7, f32[128,256]{1,0:T(8,128)S(1)} %get-tuple-element.20, f32[2,16,256]{2,1,0:T(8,128)S(1)} %copy-done.6, s32[256]{0:T(256)S(1)} %get-tuple-element.18), kind=kOutput, calls=%fused_computation.6 | convolution fusion | flops 808484864 | bytes 2425856 | tf_op jit(solution)/shard_map/dot_general | solution.py:48
  25.6 0.0 copy-done.1
  25.6 0.0 copy-start.5
  25.7 1.0 %fusion.14 = f32[2,16,128,128]{3,2,1,0:T(8,128)S(1)} fusion(f32[128,128,1,1]{1,0,3,2:T(8,128)S(1)} %copy-done.1, f32[2,16,128,128]{3,2,1,0:T(8,128)S(1)} %fusion.4, f32[2,16,128,128]{3,2,1,0:T(8,128)S(1)} %fusion), kind=kOutput, calls=%fused_computation.18 | convolution fusion | flops 403177472 | bytes 6356992 | tf_op jit(solution)/shard_map/dot_general | solution.py:48
  26.6 0.0 copy-done.5
  26.6 0.0 copy-start.2
  26.7 1.0 %add_multiply_fusion = f32[2,16,128,128]{3,2,1,0:T(8,128)S(1)} fusion(f32[2,16,128,128]{3,2,1,0:T(8,128)S(1)} %fusion.14, f32[2,16,128,128]{3,2,1,0:T(8,128)S(1)} %fusion.4, f32[128,128,1,1]{1,0,3,2:T(8,128)S(1)} %copy-done.5, f32[16,128,128]{2,1,0:T(8,128)S(1)} %broadcast_multiply_fusion), kind=kOutput, calls=%fused_computation.16 | convolution fusion | flops 403701760 | bytes 7405568 | tf_op jit(solution)/shard_map/dot_general | solution.py:48
  27.7 0.0 copy-done.2
  27.7 1.1 %subtract_multiply_fusion = f32[2,16,128,128]{3,2,1,0:T(8,128)S(1)} fusion(f32[2,16,128,128]{3,2,1,0:T(8,128)S(1)} %fusion.14, f32[2,16,128,128]{3,2,1,0:T(8,128)S(1)} %fusion, f32[128,128,1,1]{1,0,3,2:T(8,128)S(1)} %copy-done.2, f32[16,128,128]{2,1,0:T(8,128)S(1)} %broadcast_multiply_fusion), kind=kOutput, calls=%fused_computation.17 | convolution fusion | flops 403701760 | bytes 7405568 | tf_op jit(solution)/shard_map/dot_general | solution.py:48
  28.8 1.0 %fusion.63 = f32[2,16,128,128]{3,2,1,0:T(8,128)S(1)} fusion(f32[2,16,128,128]{3,2,1,0:T(8,128)S(1)} %subtract_multiply_fusion, f32[128,128,1,1]{1,0,3,2:T(8,128)S(1)} %copy-done.2), kind=kOutput, calls=%fused_computation.98 | convolution fusion | flops 402653184 | bytes 4259840 | tf_op jit(solution)/shard_map/dot_general | solution.py:48
  29.8 0.0 copy-start.4
  29.8 1.0 %fusion.12 = f32[2,16,128,128]{3,2,1,0:T(8,128)S(1)} fusion(f32[128,128,1,1]{1,0,3,2:T(8,128)S(1)} %copy-done.1, f32[2,16,128,128]{3,2,1,0:T(8,128)S(1)} %subtract_multiply_fusion, f32[2,16,128,128]{3,2,1,0:T(8,128)S(1)} %add_multiply_fusion), kind=kOutput, calls=%fused_computation.14 | convolution fusion | flops 403177472 | bytes 6356992 | tf_op jit(solution)/shard_map/dot_general | solution.py:48
  30.8 0.0 copy-done.4
  30.8 1.0 %fusion.62 = f32[2,16,128,128]{3,2,1,0:T(8,128)S(1)} fusion(f32[2,16,128,128]{3,2,1,0:T(8,128)S(1)} %add_multiply_fusion, f32[128,128,1,1]{1,0,3,2:T(8,128)S(1)} %copy-done.4), kind=kOutput, calls=%fused_computation.97 | convolution fusion | flops 402653184 | bytes 4259840 | tf_op jit(solution)/shard_map/dot_general | solution.py:48
  31.8 1.3 %fusion.10 = f32[2,16,128,256]{3,2,1,0:T(8,128)S(1)} fusion(f32[2,16,128,128]{3,2,1,0:T(8,128)S(1)} %fusion.12, f32[2,16,128,128]{3,2,1,0:T(8,128)S(1)} %fusion.62, s32[256]{0:T(256)S(1)} %get-tuple-element.18), kind=kOutput, calls=%fused_computation.12 | convolution fusion | flops 805863424 | bytes 8389632 | tf_op jit(solution)/shard_map/dot_general | solution.py:48
  33.1 0.0 copy-start.3
  33.1 2.1 %add_reduce_fusion = (bf16[2,16,256]{2,1,0:T(8,128)(2,1)S(1)}, bf16[2,16,256]{2,1,0:T(8,128)(2,1)S(1)}) fusion(f32[2,16,128,256]{3,2,1,0:T(8,128)S(1)} %fusion.10, f32[128,256]{1,0:T(8,128)S(1)} %get-tuple-element.21, f32[128,256]{1,0:T(8,128)S(1)} %get-tuple-element.20, s32[256]{0:T(256)S(1)} %get-tuple-element.18, f32[2,16,128,128]{3,2,1,0:T(8,128)S(1)} %fusion.12, ...), kind=kOutput, calls=%fused_computation.1 | convolution fusion | flops 814235648 | bytes 8684544 | tf_op jit(solution)/shard_map/dot_general | solution.py:48
  35.3 0.1 stack.13
  35.4 0.1 stack.14
  35.5 0.0 copy-start
  35.6 0.1 copy.92
  35.7 0.8 %reshape.139 = bf16[8,2,1024]{2,1,0:T(2,128)(2,1)} reshape(bf16[128,2,2,32]{3,2,1,0:T(2,128)(2,1)S(1)} %bitcast.98) | data formatting | bytes 65536
  36.5 6.0 %all-to-all-start.1 = ((bf16[8,2,1024]{2,1,0:T(2,128)(2,1)}), bf16[8,2,1024]{2,1,0:T(2,128)(2,1)}, u32[]{:S(2)}, u32[]{:S(2)}) async-start(bf16[8,2,1024]{2,1,0:T(2,128)(2,1)} %reshape.139), calls=%async_computation.1 | async-start | bytes 65536 | tf_op jit(solution)/shard_map/all_to_all | solution.py:127
  42.5 0.7 %add_multiply_fusion.1 = f32[32,128]{1,0:T(8,128)S(1)} fusion(f32[128]{0:T(128)} %fusion.58, f32[32]{0:T(128)} %fusion.54), kind=kLoop, calls=%fused_computation.69 | loop fusion | flops 8192 | bytes 17024 | tf_op jit(solution)/shard_map/div | solution.py:19
  43.2 6.0 %all-to-all-done.1 = bf16[8,2,1024]{2,1,0:T(2,128)(2,1)} async-done(((bf16[8,2,1024]{2,1,0:T(2,128)(2,1)}), bf16[8,2,1024]{2,1,0:T(2,128)(2,1)}, u32[]{:S(2)}, u32[]{:S(2)}) %all-to-all-start.1) | async-done | bytes 32800 | tf_op jit(solution)/shard_map/all_to_all | solution.py:127
  49.3 0.9 %reshape.140 = bf16[128,2,2,32]{3,2,1,0:T(2,128)(2,1)S(1)} reshape(bf16[8,2,1024]{2,1,0:T(2,128)(2,1)} %all-to-all-done.1) | data formatting | bytes 65536
  50.2 0.1 bitcast_bitcast_fusion
  50.3 0.0 copy-done.3
  50.3 1.1 %fusion.61 = (bf16[2,2,32,128]{3,2,0,1:T(8,128)(2,1)S(1)}, f32[2,2,32,128]{3,2,0,1:T(8,128)S(1)}) fusion(f32[2,2,128,128,1]{3,2,1,0,4:T(8,128)S(1)} %copy-done.3, bf16[128,2,2,32,1]{3,1,2,0,4:T(2,128)(2,1)S(1)} %bitcast_bitcast_fusion, f32[2,2,32,128]{3,2,1,0:T(8,128)} %param.7, f32[32,128]{1,0:T(8,128)S(1)} %add_multiply_fusion.1), kind=kOutput, calls=%fused_computation.94 | convolution fusion | flops 25214976 | bytes 475136 | tf_op jit(solution)/shard_map/dckz,zcbs->dbsk/dot_general | solution.py:130
  51.4 5.4 %all_gather.3 = bf16[2,8,32,128]{3,2,0,1:T(8,128)(2,1)S(1)} all-gather(bf16[2,2,32,128]{3,2,0,1:T(8,128)(2,1)S(1)} %get-tuple-element.22), channel_id=1, replica_groups=mesh['pw'=8,'band'=4] {'band'}, dimensions={1}, use_global_device_ids=true | all-gather | bytes 163840 | tf_op jit(solution)/shard_map/all_gather | solution.py:133
  56.8 0.1 copy.47
  56.9 1.7 %convolution_bitcast_fusion.5 = f32[16,64]{1,0:T(8,128)S(1)} fusion(bf16[2,64,32,128]{3,2,1,0:T(8,128)(2,1)} %get-tuple-element.10, bf16[1,8,32,128]{3,1,0,2:T(8,128)(2,1)S(1)} %get-tuple-element.17, bf16[1,8,32,128]{3,1,0,2:T(8,128)(2,1)S(1)} %get-tuple-element.16, bf16[2,8,32,128]{3,1,0,2:T(8,128)(2,1)S(1)} %copy.47), kind=kOutput, calls=%fused_computation.36 | convolution fusion | flops 17563648 | bytes 1314816 | tf_op jit(solution)/shard_map/dot_general | solution.py:84
  58.6 0.0 copy-done
  58.6 0.4 convolution_bitcast_fusion.4
  59.0 0.4 convolution_bitcast_fusion.3
  59.5 0.4 convolution_bitcast_fusion.2
  59.9 0.1 maximum_bitcast_fusion.1
  60.0 0.6 copy.52
  60.6 3.3 %all-to-all-start.2 = ((f32[2,8,1,256]{3,0,2,1:T(2,128)}), f32[2,8,1,256]{3,0,2,1:T(2,128)S(1)}, u32[]{:S(2)}, u32[]{:S(2)}) async-start(f32[2,8,1,256]{3,0,2,1:T(2,128)} %copy.52), calls=%async_computation.2 | async-start | bytes 32768 | tf_op jit(solution)/shard_map/all_to_all | solution.py:99
  63.9 0.6 copy.53
  64.6 5.9 %all-to-all-done.2 = f32[2,8,1,256]{3,0,2,1:T(2,128)S(1)} async-done(((f32[2,8,1,256]{3,0,2,1:T(2,128)}), f32[2,8,1,256]{3,0,2,1:T(2,128)S(1)}, u32[]{:S(2)}, u32[]{:S(2)}) %all-to-all-start.2) | async-done | bytes 16416 | tf_op jit(solution)/shard_map/all_to_all | solution.py:99
  70.5 0.6 reduce_sum.35
  (9 shorter events, 0.2 us)
Async XLA Ops:
  2.8 15.3 %all-to-all-start = ((bf16[8,2,1024]{2,1,0:T(2,128)(2,1)}), bf16[8,2,1024]{2,1,0:T(2,128)(2,1)}, u32[]{:S(2)}, u32[]{:S(2)}) async-start(bf16[8,2,1024]{2,1,0:T(2,128)(2,1)} %reshape.137), calls=%async_computation | async-start | bytes 65536 | tf_op jit(solution)/shard_map/all_to_all | solution.py:116
  13.1 4.3 %copy-start.8 = (s32[256]{0:T(256)S(1)}, s32[256]{0:T(256)}, u32[]{:S(2)}) copy-start(s32[256]{0:T(256)} %param.10) | copy-start | bytes 3076
  22.1 2.2 %copy-start.6 = (f32[2,16,256]{2,1,0:T(8,128)S(1)}, f32[2,16,256]{2,1,0:T(8,128)}, u32[]{:S(2)}) copy-start(f32[2,16,256]{2,1,0:T(8,128)} %mul.155) | copy-start | bytes 98308
  22.1 2.2 %copy-start.7 = (f32[2,16,256]{2,1,0:T(8,128)S(1)}, f32[2,16,256]{2,1,0:T(8,128)}, u32[]{:S(2)}) copy-start(f32[2,16,256]{2,1,0:T(8,128)} %mul.164) | copy-start | bytes 98308
  24.3 1.4 %copy-start.1 = (f32[128,128,1,1]{1,0,3,2:T(8,128)S(1)}, f32[128,128,1,1]{1,0,3,2:T(8,128)}, u32[]{:S(2)}) copy-start(f32[128,128,1,1]{1,0,3,2:T(8,128)} %constant.100) | copy-start | bytes 196612
  25.6 1.0 %copy-start.5 = (f32[128,128,1,1]{1,0,3,2:T(8,128)S(1)}, f32[128,128,1,1]{1,0,3,2:T(8,128)}, u32[]{:S(2)}) copy-start(f32[128,128,1,1]{1,0,3,2:T(8,128)} %constant.102) | copy-start | bytes 196612
  26.6 1.1 %copy-start.2 = (f32[128,128,1,1]{1,0,3,2:T(8,128)S(1)}, f32[128,128,1,1]{1,0,3,2:T(8,128)}, u32[]{:S(2)}) copy-start(f32[128,128,1,1]{1,0,3,2:T(8,128)} %constant.101) | copy-start | bytes 196612
  29.8 1.0 %copy-start.4 = (f32[128,128,1,1]{1,0,3,2:T(8,128)S(1)}, f32[128,128,1,1]{1,0,3,2:T(8,128)}, u32[]{:S(2)}) copy-start(f32[128,128,1,1]{1,0,3,2:T(8,128)} %constant.103) | copy-start | bytes 196612
  33.1 17.2 %copy-start.3 = (f32[2,2,128,128,1]{3,2,1,0,4:T(8,128)S(1)}, f32[2,2,128,128,1]{3,2,1,0,4:T(8,128)}, u32[]{:S(2)}) copy-start(f32[2,2,128,128,1]{3,2,1,0,4:T(8,128)} %constant.104) | copy-start | bytes 786436
  35.5 23.1 %copy-start = (bf16[2,64,32,128]{3,2,1,0:T(8,128)(2,1)S(1)}, bf16[2,64,32,128]{3,2,1,0:T(8,128)(2,1)}, u32[]{:S(2)}) copy-start(bf16[2,64,32,128]{3,2,1,0:T(8,128)(2,1)} %get-tuple-element.12) | copy-start | bytes 3145732
  36.5 12.8 %all-to-all-start.1 = ((bf16[8,2,1024]{2,1,0:T(2,128)(2,1)}), bf16[8,2,1024]{2,1,0:T(2,128)(2,1)}, u32[]{:S(2)}, u32[]{:S(2)}) async-start(bf16[8,2,1024]{2,1,0:T(2,128)(2,1)} %reshape.139), calls=%async_computation.1 | async-start | bytes 65536 | tf_op jit(solution)/shard_map/all_to_all | solution.py:127
  60.6 9.8 %all-to-all-start.2 = ((f32[2,8,1,256]{3,0,2,1:T(2,128)}), f32[2,8,1,256]{3,0,2,1:T(2,128)S(1)}, u32[]{:S(2)}, u32[]{:S(2)}) async-start(f32[2,8,1,256]{3,0,2,1:T(2,128)} %copy.52), calls=%async_computation.2 | async-start | bytes 32768 | tf_op jit(solution)/shard_map/all_to_all | solution.py:99

commit v12 on v7

--- a/solution.py
+++ b/solution.py
@@ -112,18 +112,22 @@
     inverse = dft_table(grid_size, 1.0)
     forward = dft_table(grid_size, -1.0)
     tables = plane_tables(stick_col, grid_size)
-    z_lines = jnp.einsum("dczk,cbsk->zdbs", inverse, psi_block, precision=fast)
-    received = lax.all_to_all(z_lines, "pw", split_axis=0, concat_axis=0, tiled=True)
-    lanes = received.shape[1:]
-    received = received.reshape((pw_count, planes) + lanes)
-    amp = jnp.transpose(received, (2, 3, 1, 0, 4)).reshape(
-        lanes[0], lanes[1], planes, pw_count * sticks_dev
-    )
-    picked = plane_phase(amp, potential, tables, grid_size)
-    outgoing = picked.reshape(lanes[0], lanes[1], planes, pw_count, sticks_dev)
-    outgoing = jnp.transpose(outgoing, (3, 2, 0, 1, 4)).reshape((pw_count * planes,) + lanes)
-    sticks_back = lax.all_to_all(outgoing, "pw", split_axis=0, concat_axis=0, tiled=True)
-    vpsi = jnp.einsum("dckz,zcbs->dbsk", forward, sticks_back, precision=fast)
+    parts = []
+    for band in range(psi_block.shape[1]):
+        coeffs = psi_block[:, band : band + 1]
+        z_lines = jnp.einsum("dczk,cbsk->zdbs", inverse, coeffs, precision=fast)
+        received = lax.all_to_all(z_lines, "pw", split_axis=0, concat_axis=0, tiled=True)
+        lanes = received.shape[1:]
+        received = received.reshape((pw_count, planes) + lanes)
+        amp = jnp.transpose(received, (2, 3, 1, 0, 4)).reshape(
+            lanes[0], lanes[1], planes, pw_count * sticks_dev
+        )
+        picked = plane_phase(amp, potential, tables, grid_size)
+        outgoing = picked.reshape(lanes[0], lanes[1], planes, pw_count, sticks_dev)
+        outgoing = jnp.transpose(outgoing, (3, 2, 0, 1, 4)).reshape((pw_count * planes,) + lanes)
+        sticks_back = lax.all_to_all(outgoing, "pw", split_axis=0, concat_axis=0, tiled=True)
+        parts.append(jnp.einsum("dckz,zcbs->dbsk", forward, sticks_back, precision=fast))
+    vpsi = jnp.concatenate(parts, axis=1)
     applied = kinetic[None, None] * psi_block + vpsi
     lowered = applied.astype(jnp.bfloat16)
     gathered = lax.all_gather(lowered, "band", axis=1, tiled=True)

time: 66 us -> 95.2 us (1.44)
  starting transfers between devices: 15.3 us -> 23.9 us
  local copies, waits for them, and re-layouts: 10.1 us -> 15.8 us
  matrix products: 16.5 us -> 22 us
  waiting for transfers between devices: 14 us -> 18.4 us
  other arithmetic: 3.21 us -> 7.35 us
    all_to_all x1 -> x2, starting transfers between devices: 7.28 us -> 13.3 us  [per_device_rows(): lax.all_to_all(z_lines, 'pw', split_axis=0, concat_axis=0, tiled=True)]
    unnamed x25 -> x33, local copies, waits for them, and re-layouts: 3.2 us -> 7.24 us
    dot_general x10 -> x20, matrix products: 12.1 us -> 15.8 us  [mult(): jnp.dot(left, right, precision=lax.Precision.HIGH, preferred_element_type...]
    all_to_all x1 -> x2, other arithmetic: 0.8 us -> 3.5 us  [per_device_rows(): lax.all_to_all(outgoing, 'pw', split_axis=0, concat_axis=0, tiled=True)]
    all_to_all x1 -> x2, starting transfers between devices: 4.67 us -> 7.3 us  [per_device_rows(): lax.all_to_all(outgoing, 'pw', split_axis=0, concat_axis=0, tiled=True)]
    all_to_all x1 -> x2, waiting for transfers between devices: 6.83 us -> 9.14 us  [per_device_rows(): lax.all_to_all(outgoing, 'pw', split_axis=0, concat_axis=0, tiled=True)]
    all_to_all x1 -> x2, waiting for transfers between devices: 1.34 us -> 3.41 us  [per_device_rows(): lax.all_to_all(z_lines, 'pw', split_axis=0, concat_axis=0, tiled=True)]
    dot_general x2 -> x4, matrix products: 2.62 us -> 4.46 us  [the longest x2 2.42 us: per_device_rows(): z_lines = jnp.einsum('dczk,cbsk->zdbs', inverse, coeffs, precision=fast)]
  transfers between devices with their start and end apart: 3 -> 5, of which waited for: 3 -> 4; matrix products, arithmetic and copies ran while one was open for 10% -> 17% of each run, Pallas kernels for 0% -> 0%
where the time goes in v12:
time: 95.2 us; the launch traced here: 94 us
  starting transfers between devices  23.9 us (25%)
  matrix products  22 us (23%)
  waiting for transfers between devices  18.4 us (19%)
  local copies, waits for them, and re-layouts  15.8 us (17%)
  other arithmetic  7.35 us (8%)
  blocking collectives  5.43 us (6%)
  between operations  1.15 us (1%)
    dot_general x20, matrix products, mult(): jnp.dot(left, right, precision=lax.Precision.HIGH, preferred_element_type...  15.8 us
    all_to_all x2, starting transfers between devices, per_device_rows(): lax.all_to_all(z_lines, 'pw', split_axis=0, concat_axis=0, tiled=True)  13.3 us
    all_to_all x2, waiting for transfers between devices, per_device_rows(): lax.all_to_all(outgoing, 'pw', split_axis=0, concat_axis=0, tiled=True)  9.14 us
    all_to_all x2, starting transfers between devices, per_device_rows(): lax.all_to_all(outgoing, 'pw', split_axis=0, concat_axis=0, tiled=True)  7.3 us
    unnamed x33, local copies, waits for them, and re-layouts  7.24 us
    all_to_all x1, waiting for transfers between devices, intersect(): lax.all_to_all(pieces, 'pw', split_axis=1, concat_axis=1, tiled=True)  5.88 us
    all_gather x1, blocking collectives, per_device_rows(): gathered = lax.all_gather(lowered, 'band', axis=1, tiled=True)  5.43 us
    slice x1, local copies, waits for them, and re-layouts, intersect(): psi_all[:, k * width:(k + 1) * width]  4.12 us
  transfers between devices with their start and end apart: 5, of which 4 were waited for; matrix products, arithmetic and copies ran while one was open for 17% of the time, Pallas kernels for 0%

profile of v12, /device:TPU:0, one launch (start us, length us, event | category | flops | bytes accessed | tf_op | source)
XLA Modules:
  0.0 94.0 jit_solution(17449898297534052666)
XLA Ops:
  0.6 1.2 %convolution_bitcast_fusion.1 = f32[128,2,1,32]{0,3,1,2:T(8,128)S(1)} fusion(f32[2,2,128,128]{3,2,1,0:T(8,128)} %constant.89.clone, f32[2,2,32,128]{3,2,1,0:T(8,128)} %param.8), kind=kOutput, calls=%fused_computation.33 | convolution fusion | flops 12582912 | bytes 327680 | tf_op jit(solution)/shard_map/dczk,cbsk->zdbs/dot_general | solution.py:118
  2.0 0.8 reshape.302
  2.7 7.3 %all-to-all-start.2 = ((f32[8,1,1024]{2,1,0:T(1,128)}), f32[8,1,1024]{2,1,0:T(1,128)S(1)}, u32[]{:S(2)}, u32[]{:S(2)}) async-start(f32[8,1,1024]{2,1,0:T(1,128)} %reshape.302), calls=%async_computation.2 | async-start | bytes 65536 | tf_op jit(solution)/shard_map/all_to_all | solution.py:119
  10.0 1.2 %convolution_bitcast_fusion.3 = f32[128,2,1,32]{0,3,1,2:T(8,128)S(1)} fusion(f32[2,2,128,128]{3,2,1,0:T(8,128)} %constant.89.clone, f32[2,2,32,128]{3,2,1,0:T(8,128)} %param.8), kind=kOutput, calls=%fused_computation.35 | convolution fusion | flops 12582912 | bytes 327680 | tf_op jit(solution)/shard_map/dczk,cbsk->zdbs/dot_general | solution.py:118
  11.2 0.7 and_select_fusion
  11.9 0.5 fusion.77
  12.6 0.8 reshape.300
  13.4 4.1 %fusion.88 = (bf16[2,64,32,128]{3,2,1,0:T(8,128)(2,1)}, bf16[2,64,32,128]{3,2,1,0:T(8,128)(2,1)}, bf16[2,64,32,128]{3,2,1,0:T(8,128)(2,1)}, bf16[2,64,32,128]{3,2,1,0:T(8,128)(2,1)S(1)}) fusion(bf16[2,256,32,128]{3,2,1,0:T(8,128)(2,1)} %param.9), kind=kLoop, calls=%fused_computation.129 | loop fusion | bytes 8388608 | tf_op jit(solution)/shard_map/slice | solution.py:86
  17.6 6.0 %all-to-all-start = ((f32[8,1,1024]{2,1,0:T(1,128)}), f32[8,1,1024]{2,1,0:T(1,128)S(1)}, u32[]{:S(2)}, u32[]{:S(2)}) async-start(f32[8,1,1024]{2,1,0:T(1,128)} %reshape.300), calls=%async_computation | async-start | bytes 65536 | tf_op jit(solution)/shard_map/all_to_all | solution.py:119
  23.6 0.5 broadcast.248
  24.1 0.7 reduce.10
  24.8 0.2 reshape.303
  25.3 0.8 fusion
  26.1 0.8 fusion.4
  26.9 3.4 %all-to-all-done = f32[8,1,1024]{2,1,0:T(1,128)S(1)} async-done(((f32[8,1,1024]{2,1,0:T(1,128)}), f32[8,1,1024]{2,1,0:T(1,128)S(1)}, u32[]{:S(2)}, u32[]{:S(2)}) %all-to-all-start) | async-done | bytes 32800 | tf_op jit(solution)/shard_map/all_to_all | solution.py:119
  30.3 0.7 reduce.9
  31.0 0.2 reshape.301
  31.5 1.7 %fusion.12 = f32[16,128,128]{2,1,0:T(8,128)S(1)} fusion(f32[128,256]{1,0:T(8,128)} %copy-done.9, f32[16,256]{1,0:T(8,128)S(1)} %mul.266, f32[128,256]{1,0:T(8,128)S(1)} %get-tuple-element.30, f32[16,256]{1,0:T(8,128)S(1)} %mul.257, s32[256]{0:T(256)S(1)} %get-tuple-element.28), kind=kOutput, calls=%fused_computation.16 | convolution fusion | flops 404258816 | bytes 1344512 | tf_op jit(solution)/shard_map/dot_general | solution.py:48
  33.2 1.7 %fusion.8 = f32[16,128,128]{2,1,0:T(8,128)S(1)} fusion(f32[128,256]{1,0:T(8,128)} %copy-done.9, f32[16,256]{1,0:T(8,128)S(1)} %mul.266, f32[128,256]{1,0:T(8,128)S(1)} %get-tuple-element.30, f32[16,256]{1,0:T(8,128)S(1)} %mul.257, s32[256]{0:T(256)S(1)} %get-tuple-element.28), kind=kOutput, calls=%fused_computation.12 | convolution fusion | flops 404258816 | bytes 1344512 | tf_op jit(solution)/shard_map/dot_general | solution.py:48
  34.9 0.6 fusion.26
  35.5 0.6 copy-done
  36.1 0.6 fusion.16
  36.7 0.3 copy-done.1
  36.9 0.6 fusion.17
  37.5 0.6 fusion.34
  38.1 0.6 fusion.18
  38.7 0.6 fusion.19
  39.2 0.6 fusion.24
  39.8 0.6 convolution_subtract_fusion
  40.4 0.2 copy-done.8
  40.7 0.6 convolution_subtract_fusion.1
  41.2 0.6 fusion.32
  41.8 0.6 convolution_subtract_fusion.3
  42.4 0.6 convolution_subtract_fusion.4
  43.0 0.7 fusion.60
  43.7 0.7 fusion.62
  44.4 0.9 fusion.66
  45.3 1.7 %add_reduce_fusion.1 = (f32[16,256]{1,0:T(8,128)S(1)}, f32[16,256]{1,0:T(8,128)S(1)}, f32[16,256]{1,0:T(8,128)S(1)}, f32[16,256]{1,0:T(8,128)S(1)}) fusion(f32[16,128,256]{2,1,0:T(8,128)S(1)} %fusion.66, f32[128,256]{1,0:T(8,128)S(1)} %copy-done.10, f32[128,256]{1,0:T(8,128)S(1)} %get-tuple-element.30, f32[16,128,256]{2,1,0:T(8,128)S(1)} %fusion.62, ...), kind=kOutput, calls=%fused_computation.11 | convolution fusion | flops 411058176 | bytes 7668736 | tf_op jit(solution)/shard_map/dot_general | solution.py:48
  47.3 0.8 reshape.306
  48.1 3.3 %all-to-all-start.1 = ((f32[8,1,1024]{2,1,0:T(1,128)}), f32[8,1,1024]{2,1,0:T(1,128)S(1)}, u32[]{:S(2)}, u32[]{:S(2)}) async-start(f32[8,1,1024]{2,1,0:T(1,128)} %reshape.306), calls=%async_computation.1 | async-start | bytes 65536 | tf_op jit(solution)/shard_map/all_to_all | solution.py:128
  51.8 0.8 reshape.304
  52.5 5.5 %all-to-all-done.1 = f32[8,1,1024]{2,1,0:T(1,128)S(1)} async-done(((f32[8,1,1024]{2,1,0:T(1,128)}), f32[8,1,1024]{2,1,0:T(1,128)S(1)}, u32[]{:S(2)}, u32[]{:S(2)}) %all-to-all-start.1) | async-done | bytes 32800 | tf_op jit(solution)/shard_map/all_to_all | solution.py:128
  58.1 4.0 %all-to-all-start.3 = ((f32[8,1,1024]{2,1,0:T(1,128)}), f32[8,1,1024]{2,1,0:T(1,128)}, u32[]{:S(2)}, u32[]{:S(2)}) async-start(f32[8,1,1024]{2,1,0:T(1,128)} %reshape.304), calls=%async_computation.3 | async-start | bytes 65536 | tf_op jit(solution)/shard_map/all_to_all | solution.py:128
  62.1 1.4 %reduce.12 = f32[8,1024]{1,0:T(8,128)} reduce(f32[8,1,1024]{2,1,0:T(1,128)S(1)} %all-to-all-done.1, f32[]{:T(128)} %broadcast.248), dimensions={1}, to_apply=%all_to_all.16.reduce_sub_computation | reduce | bytes 65540 | tf_op jit(solution)/shard_map/all_to_all | solution.py:128
  63.5 0.9 reshape.307
  64.4 0.7 copy.74
  65.1 3.6 %all-to-all-done.3 = f32[8,1,1024]{2,1,0:T(1,128)} async-done(((f32[8,1,1024]{2,1,0:T(1,128)}), f32[8,1,1024]{2,1,0:T(1,128)}, u32[]{:S(2)}, u32[]{:S(2)}) %all-to-all-start.3) | async-done | bytes 32800 | tf_op jit(solution)/shard_map/all_to_all | solution.py:128
  68.7 2.1 %reduce.11 = f32[8,1024]{1,0:T(8,128)} reduce(f32[8,1,1024]{2,1,0:T(1,128)} %all-to-all-done.3, f32[]{:T(128)} %broadcast.248), dimensions={1}, to_apply=%all_to_all.18.reduce_sub_computation | reduce | bytes 65540 | tf_op jit(solution)/shard_map/all_to_all | solution.py:128
  70.8 0.9 reshape.305
  71.8 0.7 copy.82
  72.5 1.0 %convolution_bitcast_fusion.2 = f32[2,1,32,128]{3,2,0,1:T(8,128)S(1)} fusion(f32[2,2,128,128]{3,2,1,0:T(8,128)S(1)} %copy-done.3, f32[128,2,1,32]{0,3,1,2:T(8,128)} %copy.74), kind=kOutput, calls=%fused_computation.34 | convolution fusion | flops 12582912 | bytes 327680 | tf_op jit(solution)/shard_map/dckz,zcbs->dbsk/dot_general | solution.py:129
  73.5 1.0 %convolution_bitcast_fusion = f32[2,1,32,128]{3,2,0,1:T(8,128)S(1)} fusion(f32[2,2,128,128]{3,2,1,0:T(8,128)S(1)} %copy-done.3, f32[128,2,1,32]{0,3,1,2:T(8,128)} %copy.82), kind=kOutput, calls=%fused_computation.32 | convolution fusion | flops 12582912 | bytes 327680 | tf_op jit(solution)/shard_map/dckz,zcbs->dbsk/dot_general | solution.py:129
  74.5 0.9 fusion.87
  75.4 5.4 %all_gather.3 = bf16[2,8,32,128]{3,2,0,1:T(8,128)(2,1)S(1)} all-gather(bf16[2,2,32,128]{3,2,0,1:T(8,128)(2,1)S(1)} %get-tuple-element.16), channel_id=1, replica_groups=mesh['pw'=8,'band'=4] {'band'}, dimensions={1}, use_global_device_ids=true | all-gather | bytes 163840 | tf_op jit(solution)/shard_map/all_gather | solution.py:133
  80.9 0.4 convolution_bitcast_fusion.7
  81.4 0.4 convolution_bitcast_fusion.6
  81.8 0.2 copy-done.4
  82.0 0.4 convolution_bitcast_fusion.5
  82.4 0.4 convolution_bitcast_fusion.4
  83.0 0.6 copy.90
  83.6 3.3 %all-to-all-start.4 = ((f32[2,8,1,256]{3,0,2,1:T(2,128)}), f32[2,8,1,256]{3,0,2,1:T(2,128)S(1)}, u32[]{:S(2)}, u32[]{:S(2)}) async-start(f32[2,8,1,256]{3,0,2,1:T(2,128)} %copy.90), calls=%async_computation.4 | async-start | bytes 32768 | tf_op jit(solution)/shard_map/all_to_all | solution.py:99
  86.9 0.6 copy.91
  87.5 5.9 %all-to-all-done.4 = f32[2,8,1,256]{3,0,2,1:T(2,128)S(1)} async-done(((f32[2,8,1,256]{3,0,2,1:T(2,128)}), f32[2,8,1,256]{3,0,2,1:T(2,128)S(1)}, u32[]{:S(2)}, u32[]{:S(2)}) %all-to-all-start.4) | async-done | bytes 16416 | tf_op jit(solution)/shard_map/all_to_all | solution.py:99
  93.4 0.6 reduce_sum.56
  (52 shorter events, 1.7 us)
Async XLA Ops:
  2.7 14.9 %all-to-all-start.2 = ((f32[8,1,1024]{2,1,0:T(1,128)}), f32[8,1,1024]{2,1,0:T(1,128)S(1)}, u32[]{:S(2)}, u32[]{:S(2)}) async-start(f32[8,1,1024]{2,1,0:T(1,128)} %reshape.302), calls=%async_computation.2 | async-start | bytes 65536 | tf_op jit(solution)/shard_map/all_to_all | solution.py:119
  12.5 13.6 %copy-start.9 = (f32[128,256]{1,0:T(8,128)}, f32[128,256]{1,0:T(8,128)S(1)}, u32[]{:S(2)}) copy-start(f32[128,256]{1,0:T(8,128)S(1)} %get-tuple-element.31) | copy-start | bytes 393220
  13.4 4.1 %copy-start.11 = (s32[256]{0:T(256)S(1)}, s32[256]{0:T(256)}, u32[]{:S(2)}) copy-start(s32[256]{0:T(256)} %param.11) | copy-start | bytes 3076
  17.6 12.7 %all-to-all-start = ((f32[8,1,1024]{2,1,0:T(1,128)}), f32[8,1,1024]{2,1,0:T(1,128)S(1)}, u32[]{:S(2)}, u32[]{:S(2)}) async-start(f32[8,1,1024]{2,1,0:T(1,128)} %reshape.300), calls=%async_computation | async-start | bytes 65536 | tf_op jit(solution)/shard_map/all_to_all | solution.py:119
  31.3 3.5 %copy-start.2 = (f32[128,128,1]{1,0,2:T(8,128)S(1)}, f32[128,128,1]{1,0,2:T(8,128)}, u32[]{:S(2)}) copy-start(f32[128,128,1]{1,0,2:T(8,128)} %constant.101) | copy-start | bytes 196612
  34.9 1.2 %copy-start = (f32[16,128,128]{2,1,0:T(8,128)S(1)}, f32[16,128,128]{2,1,0:T(8,128)}, u32[]{:S(2)}) copy-start(f32[16,128,128]{2,1,0:T(8,128)} %param.10) | copy-start | bytes 3145732
  34.9 1.2 %copy-start.7 = (f32[128,128,1]{1,0,2:T(8,128)S(1)}, f32[128,128,1]{1,0,2:T(8,128)}, u32[]{:S(2)}) copy-start(f32[128,128,1]{1,0,2:T(8,128)} %constant.103) | copy-start | bytes 196612
  36.1 0.8 copy-start.1
  39.8 0.8 copy-start.8
  44.4 0.9 copy-start.10
  47.0 25.4 %copy-start.3 = (f32[2,2,128,128]{3,2,1,0:T(8,128)S(1)}, f32[2,2,128,128]{3,2,1,0:T(8,128)}, u32[]{:S(2)}) copy-start(f32[2,2,128,128]{3,2,1,0:T(8,128)} %constant.90.clone) | copy-start | bytes 786436
  47.2 33.7 %copy-start.6 = (bf16[2,64,32,128]{3,2,1,0:T(8,128)(2,1)S(1)}, bf16[2,64,32,128]{3,2,1,0:T(8,128)(2,1)}, u32[]{:S(2)}) copy-start(bf16[2,64,32,128]{3,2,1,0:T(8,128)(2,1)} %get-tuple-element.18) | copy-start | bytes 3145732
  48.1 10.0 %all-to-all-start.1 = ((f32[8,1,1024]{2,1,0:T(1,128)}), f32[8,1,1024]{2,1,0:T(1,128)S(1)}, u32[]{:S(2)}, u32[]{:S(2)}) async-start(f32[8,1,1024]{2,1,0:T(1,128)} %reshape.306), calls=%async_computation.1 | async-start | bytes 65536 | tf_op jit(solution)/shard_map/all_to_all | solution.py:128
  58.1 10.7 %all-to-all-start.3 = ((f32[8,1,1024]{2,1,0:T(1,128)}), f32[8,1,1024]{2,1,0:T(1,128)}, u32[]{:S(2)}, u32[]{:S(2)}) async-start(f32[8,1,1024]{2,1,0:T(1,128)} %reshape.304), calls=%async_computation.3 | async-start | bytes 65536 | tf_op jit(solution)/shard_map/all_to_all | solution.py:128
  62.1 19.2 %copy-start.5 = (bf16[2,64,32,128]{3,2,1,0:T(8,128)(2,1)S(1)}, bf16[2,64,32,128]{3,2,1,0:T(8,128)(2,1)}, u32[]{:S(2)}) copy-start(bf16[2,64,32,128]{3,2,1,0:T(8,128)(2,1)} %get-tuple-element.20) | copy-start | bytes 3145732
  80.8 1.2 %copy-start.4 = (bf16[2,64,32,128]{3,2,1,0:T(8,128)(2,1)S(1)}, bf16[2,64,32,128]{3,2,1,0:T(8,128)(2,1)}, u32[]{:S(2)}) copy-start(bf16[2,64,32,128]{3,2,1,0:T(8,128)(2,1)} %get-tuple-element.19) | copy-start | bytes 3145732
  83.6 9.8 %all-to-all-start.4 = ((f32[2,8,1,256]{3,0,2,1:T(2,128)}), f32[2,8,1,256]{3,0,2,1:T(2,128)S(1)}, u32[]{:S(2)}, u32[]{:S(2)}) async-start(f32[2,8,1,256]{3,0,2,1:T(2,128)} %copy.90), calls=%async_computation.4 | async-start | bytes 32768 | tf_op jit(solution)/shard_map/all_to_all | solution.py:99

commit v13 on v7

--- a/solution.py
+++ b/solution.py
@@ -75,7 +75,9 @@
 
 def intersect(lowered, psi_all, pw_count):
     turned = jnp.stack([-lowered[1], lowered[0]])
-    both = jnp.concatenate([lowered, turned], axis=1)
+    both = jnp.stack([lowered, turned], axis=2).reshape(
+        (lowered.shape[0], 2 * lowered.shape[1]) + lowered.shape[2:]
+    )
     dims = (((2, 3), (2, 3)), ((0,), (0,)))
     width = psi_all.shape[1] // 4
     partial_value = jnp.concatenate(
@@ -93,11 +95,11 @@
         ],
         axis=-1,
     )
-    partial_value = partial_value.reshape(2, lowered.shape[1], partial_value.shape[-1])
-    rows_dev = partial_value.shape[1] // pw_count
-    pieces = partial_value.reshape(2, pw_count, rows_dev, partial_value.shape[-1])
-    pieces = lax.all_to_all(pieces, "pw", split_axis=1, concat_axis=1, tiled=True)
-    return jnp.sum(pieces, axis=1)
+    rows_dev = lowered.shape[1] // pw_count
+    pieces = partial_value.reshape(pw_count, rows_dev * 2 * partial_value.shape[-1])
+    pieces = lax.all_to_all(pieces, "pw", split_axis=0, concat_axis=0, tiled=True)
+    summed = jnp.sum(pieces, axis=0).reshape(rows_dev, 2, partial_value.shape[-1])
+    return jnp.transpose(summed, (1, 0, 2))
 
 
 def per_device_rows(psi_block, psi_all, potential, stick_col):

time: 66 us -> 65.1 us (0.986)
  matrix products: 16.5 us -> 15.7 us
  local copies, waits for them, and re-layouts: 10.1 us -> 9.38 us
    dot_general x1, matrix products: 1.31 us -> 0.36 us  [per_device_rows(): vpsi = jnp.einsum('dckz,zcbs->dbsk', forward, sticks_back, precision=fast)]
    unnamed x25 -> x27, local copies, waits for them, and re-layouts: 3.2 us -> 3.16 us
where the time goes in v13:
time: 65.1 us; the launch traced here: 64.7 us
  matrix products  15.7 us (24%)
  starting transfers between devices  15.2 us (23%)
  waiting for transfers between devices  14.1 us (22%)
  local copies, waits for them, and re-layouts  9.38 us (14%)
  blocking collectives  5.43 us (8%)
  other arithmetic  3.83 us (6%)
  between operations  1.03 us (2%)
    dot_general x10, matrix products, mult(): jnp.dot(left, right, precision=lax.Precision.HIGH, preferred_element_type...  12.1 us
    all_to_all x1, starting transfers between devices, per_device_rows(): lax.all_to_all(z_lines, 'pw', split_axis=0, concat_axis=0, tiled=True)  7.28 us
    all_to_all x1, waiting for transfers between devices, per_device_rows(): lax.all_to_all(outgoing, 'pw', split_axis=0, concat_axis=0, tiled=True)  6.83 us
    all_to_all x1, waiting for transfers between devices, intersect(): lax.all_to_all(pieces, 'pw', split_axis=0, concat_axis=0, tiled=True)  5.88 us
    all_gather x1, blocking collectives, per_device_rows(): gathered = lax.all_gather(lowered, 'band', axis=1, tiled=True)  5.43 us
    all_to_all x1, starting transfers between devices, per_device_rows(): lax.all_to_all(outgoing, 'pw', split_axis=0, concat_axis=0, tiled=True)  4.65 us
    slice x1, local copies, waits for them, and re-layouts, intersect(): psi_all[:, k * width:(k + 1) * width]  4.12 us
    all_to_all x1, starting transfers between devices, intersect(): lax.all_to_all(pieces, 'pw', split_axis=0, concat_axis=0, tiled=True)  3.31 us
  transfers between devices with their start and end apart: 3, of which 3 were waited for; matrix products, arithmetic and copies ran while one was open for 10% of the time, Pallas kernels for 0%

profile of v13, /device:TPU:0, one launch (start us, length us, event | category | flops | bytes accessed | tf_op | source)
XLA Modules:
  0.0 64.7 jit_solution(17253178013780530339)
XLA Ops:
  0.6 0.0 copy-start
  0.6 1.3 %convolution_bitcast_fusion = f32[128,2,2,32]{0,3,2,1:T(8,128)S(1)} fusion(f32[2,2,128,128,1]{3,2,1,4,0:T(8,128)} %constant.99, f32[2,2,32,128]{3,2,1,0:T(8,128)} %param.7), kind=kOutput, calls=%fused_computation.28 | convolution fusion | flops 25165824 | bytes 393216 | tf_op jit(solution)/shard_map/dczk,cbsk->zdbs/dot_general | solution.py:117
  2.0 0.2 copy.35
  2.2 0.9 %reshape.142 = f32[8,1,2048]{2,1,0:T(1,128)} reshape(f32[128,2,2,32]{3,2,1,0:T(2,128)S(1)} %copy.35) | data formatting | bytes 131072
  3.1 7.3 %all-to-all-start = ((f32[8,1,2048]{2,1,0:T(1,128)}), f32[8,1,2048]{2,1,0:T(1,128)S(1)}, u32[]{:S(2)}, u32[]{:S(2)}) async-start(f32[8,1,2048]{2,1,0:T(1,128)} %reshape.142), calls=%async_computation | async-start | bytes 131072 | tf_op jit(solution)/shard_map/all_to_all | solution.py:118
  10.3 0.7 %and_select_fusion = (s32[256]{0:T(256)S(1)}, s32[256]{0:T(256)S(1)}) fusion(s32[256]{0:T(256)} %param.10), kind=kLoop, calls=%fused_computation.75 | loop fusion | flops 4864 | bytes 3072 | tf_op jit(solution)/shard_map/jit(remainder)/select_n | solution.py:35
  11.0 0.5 fusion.52
  11.6 0.0 copy-done
  11.6 0.1 broadcast_multiply_fusion
  11.7 0.0 copy-start.10
  11.7 4.1 %fusion.61 = (bf16[2,64,32,128]{3,2,1,0:T(8,128)(2,1)}, bf16[2,64,32,128]{3,2,1,0:T(8,128)(2,1)}, bf16[2,64,32,128]{3,2,1,0:T(8,128)(2,1)}, bf16[2,64,32,128]{3,2,1,0:T(8,128)(2,1)S(1)}) fusion(bf16[2,256,32,128]{3,2,1,0:T(8,128)(2,1)} %param.8), kind=kLoop, calls=%fused_computation.95 | loop fusion | bytes 8388608 | tf_op jit(solution)/shard_map/slice | solution.py:88
  15.8 0.0 copy-done.10
  15.8 0.1 fusion.56
  15.9 1.4 %all-to-all-done = f32[8,1,2048]{2,1,0:T(1,128)S(1)} async-done(((f32[8,1,2048]{2,1,0:T(1,128)}), f32[8,1,2048]{2,1,0:T(1,128)S(1)}, u32[]{:S(2)}, u32[]{:S(2)}) %all-to-all-start) | async-done | bytes 65568 | tf_op jit(solution)/shard_map/all_to_all | solution.py:118
  17.2 0.5 broadcast.179
  17.8 0.8 %reduce.1 = f32[8,2048]{1,0:T(8,128)S(1)} reduce(f32[8,1,2048]{2,1,0:T(1,128)S(1)} %all-to-all-done, f32[]{:T(128)} %broadcast.179), dimensions={1}, to_apply=%all_to_all.12.reduce_sub_computation | reduce | bytes 131076 | tf_op jit(solution)/shard_map/all_to_all | solution.py:118
  18.6 0.2 reshape.143
  18.9 0.1 mul.155
  19.1 0.1 mul.164
  19.2 1.3 %fusion = f32[2,16,128,128]{3,2,1,0:T(8,128)S(1)} fusion(f32[128,256]{1,0:T(8,128)S(1)} %get-tuple-element.23, f32[2,16,256]{2,1,0:T(8,128)S(1)} %mul.164, f32[128,256]{1,0:T(8,128)S(1)} %get-tuple-element.22, f32[2,16,256]{2,1,0:T(8,128)S(1)} %mul.155, s32[256]{0:T(256)S(1)} %get-tuple-element.20), kind=kOutput, calls=%fused_computation.2 | convolution fusion | flops 808484864 | bytes 2425856 | tf_op jit(solution)/shard_map/dot_general | solution.py:48
  20.5 0.0 copy-start.4
  20.5 1.3 %fusion.4 = f32[2,16,128,128]{3,2,1,0:T(8,128)S(1)} fusion(f32[128,256]{1,0:T(8,128)S(1)} %get-tuple-element.23, f32[2,16,256]{2,1,0:T(8,128)S(1)} %mul.164, f32[128,256]{1,0:T(8,128)S(1)} %get-tuple-element.22, f32[2,16,256]{2,1,0:T(8,128)S(1)} %mul.155, s32[256]{0:T(256)S(1)} %get-tuple-element.20), kind=kOutput, calls=%fused_computation.6 | convolution fusion | flops 808484864 | bytes 2425856 | tf_op jit(solution)/shard_map/dot_general | solution.py:48
  21.9 0.0 copy-done.4
  21.9 0.0 copy-start.9
  21.9 1.0 %fusion.14 = f32[2,16,128,128]{3,2,1,0:T(8,128)S(1)} fusion(f32[128,128,1,1]{1,0,3,2:T(8,128)S(1)} %copy-done.4, f32[2,16,128,128]{3,2,1,0:T(8,128)S(1)} %fusion.4, f32[2,16,128,128]{3,2,1,0:T(8,128)S(1)} %fusion), kind=kOutput, calls=%fused_computation.18 | convolution fusion | flops 403177472 | bytes 6356992 | tf_op jit(solution)/shard_map/dot_general | solution.py:48
  22.9 0.0 copy-done.9
  22.9 0.0 copy-start.5
  22.9 1.0 %add_multiply_fusion = f32[2,16,128,128]{3,2,1,0:T(8,128)S(1)} fusion(f32[2,16,128,128]{3,2,1,0:T(8,128)S(1)} %fusion.14, f32[2,16,128,128]{3,2,1,0:T(8,128)S(1)} %fusion.4, f32[128,128,1,1]{1,0,3,2:T(8,128)S(1)} %copy-done.9, f32[16,128,128]{2,1,0:T(8,128)S(1)} %broadcast_multiply_fusion), kind=kOutput, calls=%fused_computation.16 | convolution fusion | flops 403701760 | bytes 7405568 | tf_op jit(solution)/shard_map/dot_general | solution.py:48
  23.9 0.0 copy-done.5
  23.9 1.1 %subtract_multiply_fusion = f32[2,16,128,128]{3,2,1,0:T(8,128)S(1)} fusion(f32[2,16,128,128]{3,2,1,0:T(8,128)S(1)} %fusion.14, f32[2,16,128,128]{3,2,1,0:T(8,128)S(1)} %fusion, f32[128,128,1,1]{1,0,3,2:T(8,128)S(1)} %copy-done.5, f32[16,128,128]{2,1,0:T(8,128)S(1)} %broadcast_multiply_fusion), kind=kOutput, calls=%fused_computation.17 | convolution fusion | flops 403701760 | bytes 7405568 | tf_op jit(solution)/shard_map/dot_general | solution.py:48
  25.0 1.0 %fusion.65 = f32[2,16,128,128]{3,2,1,0:T(8,128)S(1)} fusion(f32[2,16,128,128]{3,2,1,0:T(8,128)S(1)} %subtract_multiply_fusion, f32[128,128,1,1]{1,0,3,2:T(8,128)S(1)} %copy-done.5), kind=kOutput, calls=%fused_computation.101 | convolution fusion | flops 402653184 | bytes 4259840 | tf_op jit(solution)/shard_map/dot_general | solution.py:48
  26.0 0.0 copy-start.8
  26.0 1.0 %fusion.12 = f32[2,16,128,128]{3,2,1,0:T(8,128)S(1)} fusion(f32[128,128,1,1]{1,0,3,2:T(8,128)S(1)} %copy-done.4, f32[2,16,128,128]{3,2,1,0:T(8,128)S(1)} %subtract_multiply_fusion, f32[2,16,128,128]{3,2,1,0:T(8,128)S(1)} %add_multiply_fusion), kind=kOutput, calls=%fused_computation.14 | convolution fusion | flops 403177472 | bytes 6356992 | tf_op jit(solution)/shard_map/dot_general | solution.py:48
  27.1 0.0 copy-done.8
  27.1 1.0 %fusion.64 = f32[2,16,128,128]{3,2,1,0:T(8,128)S(1)} fusion(f32[2,16,128,128]{3,2,1,0:T(8,128)S(1)} %add_multiply_fusion, f32[128,128,1,1]{1,0,3,2:T(8,128)S(1)} %copy-done.8), kind=kOutput, calls=%fused_computation.100 | convolution fusion | flops 402653184 | bytes 4259840 | tf_op jit(solution)/shard_map/dot_general | solution.py:48
  28.1 1.3 %fusion.10 = f32[2,16,128,256]{3,2,1,0:T(8,128)S(1)} fusion(f32[2,16,128,128]{3,2,1,0:T(8,128)S(1)} %fusion.12, f32[2,16,128,128]{3,2,1,0:T(8,128)S(1)} %fusion.64, s32[256]{0:T(256)S(1)} %get-tuple-element.20), kind=kOutput, calls=%fused_computation.12 | convolution fusion | flops 805863424 | bytes 8389632 | tf_op jit(solution)/shard_map/dot_general | solution.py:48
  29.3 2.1 %add_reduce_fusion = (f32[2,16,256]{2,1,0:T(8,128)S(1)}, f32[2,16,256]{2,1,0:T(8,128)S(1)}) fusion(f32[2,16,128,256]{3,2,1,0:T(8,128)S(1)} %fusion.10, f32[128,256]{1,0:T(8,128)S(1)} %get-tuple-element.23, f32[128,256]{1,0:T(8,128)S(1)} %get-tuple-element.22, s32[256]{0:T(256)S(1)} %get-tuple-element.20, f32[2,16,128,128]{3,2,1,0:T(8,128)S(1)} %fusion.12, ...), kind=kOutput, calls=%fused_computation.1 | convolution fusion | flops 814235648 | bytes 8717312 | tf_op jit(solution)/shard_map/dot_general | solution.py:48
  31.5 0.0 copy-start.6
  31.5 0.0 copy-start.7
  31.5 0.1 stack.22
  31.6 0.1 stack.23
  31.8 0.2 copy.104
  32.0 0.9 %reshape.144 = f32[8,1,2048]{2,1,0:T(1,128)} reshape(f32[128,2,2,32]{3,2,1,0:T(2,128)S(1)} %bitcast.98) | data formatting | bytes 131072
  32.9 4.7 %all-to-all-start.1 = ((f32[8,1,2048]{2,1,0:T(1,128)}), f32[8,1,2048]{2,1,0:T(1,128)S(1)}, u32[]{:S(2)}, u32[]{:S(2)}) async-start(f32[8,1,2048]{2,1,0:T(1,128)} %reshape.144), calls=%async_computation.1 | async-start | bytes 131072 | tf_op jit(solution)/shard_map/all_to_all | solution.py:127
  37.5 0.1 add_multiply_fusion.1
  37.6 6.8 %all-to-all-done.1 = f32[8,1,2048]{2,1,0:T(1,128)S(1)} async-done(((f32[8,1,2048]{2,1,0:T(1,128)}), f32[8,1,2048]{2,1,0:T(1,128)S(1)}, u32[]{:S(2)}, u32[]{:S(2)}) %all-to-all-start.1) | async-done | bytes 65568 | tf_op jit(solution)/shard_map/all_to_all | solution.py:127
  44.4 0.8 %reduce.2 = f32[8,2048]{1,0:T(8,128)S(1)} reduce(f32[8,1,2048]{2,1,0:T(1,128)S(1)} %all-to-all-done.1, f32[]{:T(128)} %broadcast.179), dimensions={1}, to_apply=%all_to_all.13.reduce_sub_computation | reduce | bytes 131076 | tf_op jit(solution)/shard_map/all_to_all | solution.py:127
  45.2 0.2 reshape.145
  45.5 0.0 copy-start.2
  45.5 0.0 copy-done.6
  45.5 0.0 copy-done.7
  45.5 0.4 fusion.63
  45.9 5.4 %all_gather.3 = bf16[2,8,32,128]{3,2,0,1:T(8,128)(2,1)S(1)} all-gather(bf16[2,2,32,128]{3,2,0,1:T(8,128)(2,1)S(1)} %get-tuple-element.24), channel_id=1, replica_groups=mesh['pw'=8,'band'=4] {'band'}, dimensions={1}, use_global_device_ids=true | all-gather | bytes 163840 | tf_op jit(solution)/shard_map/all_gather | solution.py:131
  51.4 0.5 convolution_bitcast_fusion.5
  51.9 0.5 convolution_bitcast_fusion.4
  52.4 0.2 copy-done.1
  52.6 0.5 convolution_bitcast_fusion.3
  53.0 0.5 convolution_bitcast_fusion.2
  53.5 0.1 pad_maximum_fusion.1
  53.6 0.6 all_to_all.16
  54.2 3.3 %all-to-all-start.2 = ((f32[8,1,512]{2,1,0:T(1,128)}), f32[8,1,512]{2,1,0:T(1,128)S(1)}, u32[]{:S(2)}, u32[]{:S(2)}) async-start(f32[8,1,512]{2,1,0:T(1,128)} %all_to_all.16), calls=%async_computation.2 | async-start | bytes 32768 | tf_op jit(solution)/shard_map/all_to_all | solution.py:100
  57.5 0.6 copy.54
  58.2 5.9 %all-to-all-done.2 = f32[8,1,512]{2,1,0:T(1,128)S(1)} async-done(((f32[8,1,512]{2,1,0:T(1,128)}), f32[8,1,512]{2,1,0:T(1,128)S(1)}, u32[]{:S(2)}, u32[]{:S(2)}) %all-to-all-start.2) | async-done | bytes 16416 | tf_op jit(solution)/shard_map/all_to_all | solution.py:100
  64.0 0.6 reduce_sum.29
  (16 shorter events, 0.3 us)
Async XLA Ops:
  0.6 10.9 %copy-start = (f32[16,128,128]{2,1,0:T(8,128)S(1)}, f32[16,128,128]{2,1,0:T(8,128)}, u32[]{:S(2)}) copy-start(f32[16,128,128]{2,1,0:T(8,128)} %param.9) | copy-start | bytes 3145732
  3.1 14.2 %all-to-all-start = ((f32[8,1,2048]{2,1,0:T(1,128)}), f32[8,1,2048]{2,1,0:T(1,128)S(1)}, u32[]{:S(2)}, u32[]{:S(2)}) async-start(f32[8,1,2048]{2,1,0:T(1,128)} %reshape.142), calls=%async_computation | async-start | bytes 131072 | tf_op jit(solution)/shard_map/all_to_all | solution.py:118
  11.7 4.1 %copy-start.10 = (s32[256]{0:T(256)S(1)}, s32[256]{0:T(256)}, u32[]{:S(2)}) copy-start(s32[256]{0:T(256)} %param.10) | copy-start | bytes 3076
  20.5 1.4 %copy-start.4 = (f32[128,128,1,1]{1,0,3,2:T(8,128)S(1)}, f32[128,128,1,1]{1,0,3,2:T(8,128)}, u32[]{:S(2)}) copy-start(f32[128,128,1,1]{1,0,3,2:T(8,128)} %constant.100) | copy-start | bytes 196612
  21.9 1.0 %copy-start.9 = (f32[128,128,1,1]{1,0,3,2:T(8,128)S(1)}, f32[128,128,1,1]{1,0,3,2:T(8,128)}, u32[]{:S(2)}) copy-start(f32[128,128,1,1]{1,0,3,2:T(8,128)} %constant.102) | copy-start | bytes 196612
  22.9 1.1 %copy-start.5 = (f32[128,128,1,1]{1,0,3,2:T(8,128)S(1)}, f32[128,128,1,1]{1,0,3,2:T(8,128)}, u32[]{:S(2)}) copy-start(f32[128,128,1,1]{1,0,3,2:T(8,128)} %constant.101) | copy-start | bytes 196612
  26.0 1.0 %copy-start.8 = (f32[128,128,1,1]{1,0,3,2:T(8,128)S(1)}, f32[128,128,1,1]{1,0,3,2:T(8,128)}, u32[]{:S(2)}) copy-start(f32[128,128,1,1]{1,0,3,2:T(8,128)} %constant.103) | copy-start | bytes 196612
  31.5 14.1 %copy-start.6 = (f32[2,2,128,128,1]{3,2,1,0,4:T(8,128)S(1)}, f32[2,2,128,128,1]{3,2,1,0,4:T(8,128)}, u32[]{:S(2)}) copy-start(f32[2,2,128,128,1]{3,2,1,0,4:T(8,128)} %constant.104) | copy-start | bytes 786436
  31.5 14.1 %copy-start.7 = (f32[2,2,32,128]{3,2,1,0:T(8,128)S(1)}, f32[2,2,32,128]{3,2,1,0:T(8,128)}, u32[]{:S(2)}) copy-start(f32[2,2,32,128]{3,2,1,0:T(8,128)} %param.7) | copy-start | bytes 196612
  31.8 19.7 %copy-start.3 = (bf16[2,64,32,128]{3,2,1,0:T(8,128)(2,1)S(1)}, bf16[2,64,32,128]{3,2,1,0:T(8,128)(2,1)}, u32[]{:S(2)}) copy-start(bf16[2,64,32,128]{3,2,1,0:T(8,128)(2,1)} %get-tuple-element.10) | copy-start | bytes 3145732
  32.9 11.6 %all-to-all-start.1 = ((f32[8,1,2048]{2,1,0:T(1,128)}), f32[8,1,2048]{2,1,0:T(1,128)S(1)}, u32[]{:S(2)}, u32[]{:S(2)}) async-start(f32[8,1,2048]{2,1,0:T(1,128)} %reshape.144), calls=%async_computation.1 | async-start | bytes 131072 | tf_op jit(solution)/shard_map/all_to_all | solution.py:127
  45.5 6.4 %copy-start.2 = (bf16[2,64,32,128]{3,2,1,0:T(8,128)(2,1)S(1)}, bf16[2,64,32,128]{3,2,1,0:T(8,128)(2,1)}, u32[]{:S(2)}) copy-start(bf16[2,64,32,128]{3,2,1,0:T(8,128)(2,1)} %get-tuple-element.12) | copy-start | bytes 3145732
  51.3 1.2 %copy-start.1 = (bf16[2,64,32,128]{3,2,1,0:T(8,128)(2,1)S(1)}, bf16[2,64,32,128]{3,2,1,0:T(8,128)(2,1)}, u32[]{:S(2)}) copy-start(bf16[2,64,32,128]{3,2,1,0:T(8,128)(2,1)} %get-tuple-element.11) | copy-start | bytes 3145732
  54.2 9.8 %all-to-all-start.2 = ((f32[8,1,512]{2,1,0:T(1,128)}), f32[8,1,512]{2,1,0:T(1,128)S(1)}, u32[]{:S(2)}, u32[]{:S(2)}) async-start(f32[8,1,512]{2,1,0:T(1,128)} %all_to_all.16), calls=%async_computation.2 | async-start | bytes 32768 | tf_op jit(solution)/shard_map/all_to_all | solution.py:100

commit v14 on v13

--- a/solution.py
+++ b/solution.py
@@ -115,16 +115,19 @@
     forward = dft_table(grid_size, -1.0)
     tables = plane_tables(stick_col, grid_size)
     z_lines = jnp.einsum("dczk,cbsk->zdbs", inverse, psi_block, precision=fast)
-    received = lax.all_to_all(z_lines, "pw", split_axis=0, concat_axis=0, tiled=True)
-    lanes = received.shape[1:]
+    lanes = z_lines.shape[1:]
+    received = lax.all_to_all(
+        z_lines.reshape(pw_count, -1), "pw", split_axis=0, concat_axis=0, tiled=True
+    )
     received = received.reshape((pw_count, planes) + lanes)
     amp = jnp.transpose(received, (2, 3, 1, 0, 4)).reshape(
         lanes[0], lanes[1], planes, pw_count * sticks_dev
     )
     picked = plane_phase(amp, potential, tables, grid_size)
     outgoing = picked.reshape(lanes[0], lanes[1], planes, pw_count, sticks_dev)
-    outgoing = jnp.transpose(outgoing, (3, 2, 0, 1, 4)).reshape((pw_count * planes,) + lanes)
+    outgoing = jnp.transpose(outgoing, (3, 2, 0, 1, 4)).reshape(pw_count, -1)
     sticks_back = lax.all_to_all(outgoing, "pw", split_axis=0, concat_axis=0, tiled=True)
+    sticks_back = sticks_back.reshape((pw_count * planes,) + lanes)
     vpsi = jnp.einsum("dckz,zcbs->dbsk", forward, sticks_back, precision=fast)
     applied = kinetic[None, None] * psi_block + vpsi
     lowered = applied.astype(jnp.bfloat16)

time: 65.1 us -> 64.4 us (0.989)
  other arithmetic: 3.83 us -> 2.54 us
  matrix products: 15.7 us -> 16.6 us
    unnamed x27 -> x21, local copies, waits for them, and re-layouts: 3.16 us -> 0.87 us
    dot_general x1, matrix products: 0.36 us -> 1.31 us  [per_device_rows(): vpsi = jnp.einsum('dckz,zcbs->dbsk', forward, sticks_back, precision=fast)]
    all_to_all x1, local copies, waits for them, and re-layouts: 0.02 us -> 0.91 us  [per_device_rows(): lax.all_to_all(outgoing, 'pw', split_axis=0, concat_axis=0, tiled=True)]
where the time goes in v14:
time: 64.4 us; the launch traced here: 64 us
  matrix products  16.6 us (26%)
  starting transfers between devices  15.4 us (24%)
  waiting for transfers between devices  14.1 us (22%)
  local copies, waits for them, and re-layouts  8.93 us (14%)
  blocking collectives  5.43 us (8%)
  other arithmetic  2.54 us (4%)
  between operations  0.97 us (2%)
    dot_general x10, matrix products, mult(): jnp.dot(left, right, precision=lax.Precision.HIGH, preferred_element_type...  12.1 us
    all_to_all x1, starting transfers between devices, per_device_rows(): lax.all_to_all(z_lines.reshape(pw_count, -1), 'pw', split_axis=0, concat_...  7.28 us
    all_to_all x1, waiting for transfers between devices, per_device_rows(): lax.all_to_all(outgoing, 'pw', split_axis=0, concat_axis=0, tiled=True)  6.83 us
    all_to_all x1, waiting for transfers between devices, intersect(): lax.all_to_all(pieces, 'pw', split_axis=0, concat_axis=0, tiled=True)  5.88 us
    all_gather x1, blocking collectives, per_device_rows(): gathered = lax.all_gather(lowered, 'band', axis=1, tiled=True)  5.43 us
    all_to_all x1, starting transfers between devices, per_device_rows(): lax.all_to_all(outgoing, 'pw', split_axis=0, concat_axis=0, tiled=True)  4.8 us
    slice x1, local copies, waits for them, and re-layouts, intersect(): psi_all[:, k * width:(k + 1) * width]  4.13 us
    all_to_all x1, starting transfers between devices, intersect(): lax.all_to_all(pieces, 'pw', split_axis=0, concat_axis=0, tiled=True)  3.34 us
  transfers between devices with their start and end apart: 3, of which 3 were waited for; matrix products, arithmetic and copies ran while one was open for 10% of the time, Pallas kernels for 0%

profile of v14, /device:TPU:0, one launch (start us, length us, event | category | flops | bytes accessed | tf_op | source)
XLA Modules:
  0.0 64.0 jit_solution(13527227845371263649)
XLA Ops:
  0.6 0.0 copy-start
  0.6 1.3 %convolution_bitcast_fusion = f32[128,2,2,32]{0,3,2,1:T(8,128)S(1)} fusion(f32[2,2,128,128,1]{3,2,1,4,0:T(8,128)} %constant.99, f32[2,2,32,128]{3,2,1,0:T(8,128)} %param.7), kind=kOutput, calls=%fused_computation.28 | convolution fusion | flops 25165824 | bytes 393216 | tf_op jit(solution)/shard_map/dczk,cbsk->zdbs/dot_general | solution.py:117
  2.0 0.2 copy.49
  2.2 0.9 %all_to_all.24 = f32[8,1,2048]{2,1,0:T(1,128)} reshape(f32[128,2,2,32]{3,2,1,0:T(2,128)S(1)} %copy.49) | data formatting | bytes 131072 | tf_op jit(solution)/shard_map/all_to_all | solution.py:119
  3.1 7.3 %all-to-all-start = ((f32[8,1,2048]{2,1,0:T(1,128)}), f32[8,1,2048]{2,1,0:T(1,128)S(1)}, u32[]{:S(2)}, u32[]{:S(2)}) async-start(f32[8,1,2048]{2,1,0:T(1,128)} %all_to_all.24), calls=%async_computation | async-start | bytes 131072 | tf_op jit(solution)/shard_map/all_to_all | solution.py:119
  10.3 0.7 %and_select_fusion = (s32[256]{0:T(256)S(1)}, s32[256]{0:T(256)S(1)}) fusion(s32[256]{0:T(256)} %param.10), kind=kLoop, calls=%fused_computation.75 | loop fusion | flops 4864 | bytes 3072 | tf_op jit(solution)/shard_map/jit(remainder)/select_n | solution.py:35
  11.0 0.5 fusion.52
  11.6 0.0 copy-done
  11.6 0.1 broadcast_multiply_fusion
  11.7 0.0 copy-start.9
  11.7 4.1 %fusion.61 = (bf16[2,64,32,128]{3,2,1,0:T(8,128)(2,1)}, bf16[2,64,32,128]{3,2,1,0:T(8,128)(2,1)}, bf16[2,64,32,128]{3,2,1,0:T(8,128)(2,1)}, bf16[2,64,32,128]{3,2,1,0:T(8,128)(2,1)S(1)}) fusion(bf16[2,256,32,128]{3,2,1,0:T(8,128)(2,1)} %param.8), kind=kLoop, calls=%fused_computation.95 | loop fusion | bytes 8388608 | tf_op jit(solution)/shard_map/slice | solution.py:88
  15.8 0.0 copy-done.9
  15.8 0.1 fusion.56
  15.9 1.3 %all-to-all-done = f32[8,1,2048]{2,1,0:T(1,128)S(1)} async-done(((f32[8,1,2048]{2,1,0:T(1,128)}), f32[8,1,2048]{2,1,0:T(1,128)S(1)}, u32[]{:S(2)}, u32[]{:S(2)}) %all-to-all-start) | async-done | bytes 65568 | tf_op jit(solution)/shard_map/all_to_all | solution.py:119
  17.2 0.2 reduce.1
  17.4 0.2 reshape.133
  17.6 0.1 fusion.62
  17.7 0.1 copy.51
  17.8 0.1 mul.155
  17.9 0.1 copy.52
  18.0 0.1 mul.164
  18.1 1.3 %fusion = f32[2,16,128,128]{3,2,1,0:T(8,128)S(1)} fusion(f32[128,256]{1,0:T(8,128)S(1)} %get-tuple-element.25, f32[2,16,256]{2,1,0:T(8,128)S(1)} %mul.164, f32[128,256]{1,0:T(8,128)S(1)} %get-tuple-element.24, f32[2,16,256]{2,1,0:T(8,128)S(1)} %mul.155, s32[256]{0:T(256)S(1)} %get-tuple-element.22), kind=kOutput, calls=%fused_computation.2 | convolution fusion | flops 808484864 | bytes 2425856 | tf_op jit(solution)/shard_map/dot_general | solution.py:48
  19.5 0.0 copy-start.4
  19.5 1.3 %fusion.4 = f32[2,16,128,128]{3,2,1,0:T(8,128)S(1)} fusion(f32[128,256]{1,0:T(8,128)S(1)} %get-tuple-element.25, f32[2,16,256]{2,1,0:T(8,128)S(1)} %mul.164, f32[128,256]{1,0:T(8,128)S(1)} %get-tuple-element.24, f32[2,16,256]{2,1,0:T(8,128)S(1)} %mul.155, s32[256]{0:T(256)S(1)} %get-tuple-element.22), kind=kOutput, calls=%fused_computation.6 | convolution fusion | flops 808484864 | bytes 2425856 | tf_op jit(solution)/shard_map/dot_general | solution.py:48
  20.8 0.0 copy-done.4
  20.8 0.0 copy-start.8
  20.8 1.0 %fusion.14 = f32[2,16,128,128]{3,2,1,0:T(8,128)S(1)} fusion(f32[128,128,1,1]{1,0,3,2:T(8,128)S(1)} %copy-done.4, f32[2,16,128,128]{3,2,1,0:T(8,128)S(1)} %fusion.4, f32[2,16,128,128]{3,2,1,0:T(8,128)S(1)} %fusion), kind=kOutput, calls=%fused_computation.18 | convolution fusion | flops 403177472 | bytes 6356992 | tf_op jit(solution)/shard_map/dot_general | solution.py:48
  21.8 0.0 copy-done.8
  21.8 0.0 copy-start.5
  21.8 1.0 %add_multiply_fusion = f32[2,16,128,128]{3,2,1,0:T(8,128)S(1)} fusion(f32[2,16,128,128]{3,2,1,0:T(8,128)S(1)} %fusion.14, f32[2,16,128,128]{3,2,1,0:T(8,128)S(1)} %fusion.4, f32[128,128,1,1]{1,0,3,2:T(8,128)S(1)} %copy-done.8, f32[16,128,128]{2,1,0:T(8,128)S(1)} %broadcast_multiply_fusion), kind=kOutput, calls=%fused_computation.16 | convolution fusion | flops 403701760 | bytes 7405568 | tf_op jit(solution)/shard_map/dot_general | solution.py:48
  22.9 0.0 copy-done.5
  22.9 1.1 %subtract_multiply_fusion = f32[2,16,128,128]{3,2,1,0:T(8,128)S(1)} fusion(f32[2,16,128,128]{3,2,1,0:T(8,128)S(1)} %fusion.14, f32[2,16,128,128]{3,2,1,0:T(8,128)S(1)} %fusion, f32[128,128,1,1]{1,0,3,2:T(8,128)S(1)} %copy-done.5, f32[16,128,128]{2,1,0:T(8,128)S(1)} %broadcast_multiply_fusion), kind=kOutput, calls=%fused_computation.17 | convolution fusion | flops 403701760 | bytes 7405568 | tf_op jit(solution)/shard_map/dot_general | solution.py:48
  24.0 1.0 %fusion.65 = f32[2,16,128,128]{3,2,1,0:T(8,128)S(1)} fusion(f32[2,16,128,128]{3,2,1,0:T(8,128)S(1)} %subtract_multiply_fusion, f32[128,128,1,1]{1,0,3,2:T(8,128)S(1)} %copy-done.5), kind=kOutput, calls=%fused_computation.99 | convolution fusion | flops 402653184 | bytes 4259840 | tf_op jit(solution)/shard_map/dot_general | solution.py:48
  25.0 0.0 copy-start.7
  25.0 1.0 %fusion.12 = f32[2,16,128,128]{3,2,1,0:T(8,128)S(1)} fusion(f32[128,128,1,1]{1,0,3,2:T(8,128)S(1)} %copy-done.4, f32[2,16,128,128]{3,2,1,0:T(8,128)S(1)} %subtract_multiply_fusion, f32[2,16,128,128]{3,2,1,0:T(8,128)S(1)} %add_multiply_fusion), kind=kOutput, calls=%fused_computation.14 | convolution fusion | flops 403177472 | bytes 6356992 | tf_op jit(solution)/shard_map/dot_general | solution.py:48
  26.0 0.0 copy-done.7
  26.0 1.0 %fusion.64 = f32[2,16,128,128]{3,2,1,0:T(8,128)S(1)} fusion(f32[2,16,128,128]{3,2,1,0:T(8,128)S(1)} %add_multiply_fusion, f32[128,128,1,1]{1,0,3,2:T(8,128)S(1)} %copy-done.7), kind=kOutput, calls=%fused_computation.98 | convolution fusion | flops 402653184 | bytes 4259840 | tf_op jit(solution)/shard_map/dot_general | solution.py:48
  27.0 1.3 %fusion.10 = f32[2,16,128,256]{3,2,1,0:T(8,128)S(1)} fusion(f32[2,16,128,128]{3,2,1,0:T(8,128)S(1)} %fusion.12, f32[2,16,128,128]{3,2,1,0:T(8,128)S(1)} %fusion.64, s32[256]{0:T(256)S(1)} %get-tuple-element.22), kind=kOutput, calls=%fused_computation.12 | convolution fusion | flops 805863424 | bytes 8389632 | tf_op jit(solution)/shard_map/dot_general | solution.py:48
  28.3 2.1 %add_reduce_fusion = (f32[2,16,256]{2,1,0:T(8,128)S(1)}, f32[2,16,256]{2,1,0:T(8,128)S(1)}) fusion(f32[2,16,128,256]{3,2,1,0:T(8,128)S(1)} %fusion.10, f32[128,256]{1,0:T(8,128)S(1)} %get-tuple-element.25, f32[128,256]{1,0:T(8,128)S(1)} %get-tuple-element.24, s32[256]{0:T(256)S(1)} %get-tuple-element.22, f32[2,16,128,128]{3,2,1,0:T(8,128)S(1)} %fusion.12, ...), kind=kOutput, calls=%fused_computation.1 | convolution fusion | flops 814235648 | bytes 8717312 | tf_op jit(solution)/shard_map/dot_general | solution.py:48
  30.4 0.0 copy-start.6
  30.4 0.1 stack.22
  30.5 0.1 stack.23
  30.6 0.0 copy-start.3
  30.6 0.2 copy.53
  30.9 0.9 %all_to_all.25 = f32[8,1,2048]{2,1,0:T(1,128)} reshape(f32[8,16,2,2,32]{4,3,2,1,0:T(2,128)S(1)} %copy.53) | data formatting | bytes 131072 | tf_op jit(solution)/shard_map/all_to_all | solution.py:129
  31.8 4.8 %all-to-all-start.1 = ((f32[8,1,2048]{2,1,0:T(1,128)}), f32[8,1,2048]{2,1,0:T(1,128)S(1)}, u32[]{:S(2)}, u32[]{:S(2)}) async-start(f32[8,1,2048]{2,1,0:T(1,128)} %all_to_all.25), calls=%async_computation.1 | async-start | bytes 131072 | tf_op jit(solution)/shard_map/all_to_all | solution.py:129
  36.6 0.1 add_multiply_fusion.1
  36.6 6.8 %all-to-all-done.1 = f32[8,1,2048]{2,1,0:T(1,128)S(1)} async-done(((f32[8,1,2048]{2,1,0:T(1,128)}), f32[8,1,2048]{2,1,0:T(1,128)S(1)}, u32[]{:S(2)}, u32[]{:S(2)}) %all-to-all-start.1) | async-done | bytes 65568 | tf_op jit(solution)/shard_map/all_to_all | solution.py:129
  43.5 0.2 reduce.2
  43.6 0.2 reshape.134
  43.9 0.0 copy-done.6
  43.9 1.3 %fusion.63 = (bf16[2,2,32,128]{3,2,0,1:T(8,128)(2,1)S(1)}, f32[2,2,32,128]{3,2,0,1:T(8,128)S(1)}) fusion(f32[2,2,128,128,1]{3,2,1,0,4:T(8,128)} %constant.104, f32[128,2,2,32,1]{3,2,1,0,4:T(2,128)S(1)} %bitcast.90, f32[2,2,32,128]{3,2,1,0:T(8,128)S(1)} %copy-done.6, f32[32,128]{1,0:T(8,128)S(1)} %add_multiply_fusion.1), kind=kOutput, calls=%fused_computation.97 | convolution fusion | flops 25214976 | bytes 507904 | tf_op jit(solution)/shard_map/dckz,zcbs->dbsk/dot_general | solution.py:131
  45.2 5.4 %all_gather.3 = bf16[2,8,32,128]{3,2,0,1:T(8,128)(2,1)S(1)} all-gather(bf16[2,2,32,128]{3,2,0,1:T(8,128)(2,1)S(1)} %get-tuple-element.26), channel_id=1, replica_groups=mesh['pw'=8,'band'=4] {'band'}, dimensions={1}, use_global_device_ids=true | all-gather | bytes 163840 | tf_op jit(solution)/shard_map/all_gather | solution.py:134
  50.7 0.5 convolution_bitcast_fusion.5
  51.2 0.5 convolution_bitcast_fusion.4
  51.7 0.2 copy-done.1
  51.9 0.5 convolution_bitcast_fusion.3
  52.3 0.5 convolution_bitcast_fusion.2
  52.8 0.1 pad_maximum_fusion.1
  52.9 0.6 all_to_all.26
  53.5 3.3 %all-to-all-start.2 = ((f32[8,1,512]{2,1,0:T(1,128)}), f32[8,1,512]{2,1,0:T(1,128)S(1)}, u32[]{:S(2)}, u32[]{:S(2)}) async-start(f32[8,1,512]{2,1,0:T(1,128)} %all_to_all.26), calls=%async_computation.2 | async-start | bytes 32768 | tf_op jit(solution)/shard_map/all_to_all | solution.py:100
  56.8 0.6 copy.68
  57.5 5.9 %all-to-all-done.2 = f32[8,1,512]{2,1,0:T(1,128)S(1)} async-done(((f32[8,1,512]{2,1,0:T(1,128)}), f32[8,1,512]{2,1,0:T(1,128)S(1)}, u32[]{:S(2)}, u32[]{:S(2)}) %all-to-all-start.2) | async-done | bytes 16416 | tf_op jit(solution)/shard_map/all_to_all | solution.py:100
  63.4 0.6 reduce_sum.29
  (10 shorter events, 0.1 us)
Async XLA Ops:
  0.6 10.9 %copy-start = (f32[16,128,128]{2,1,0:T(8,128)S(1)}, f32[16,128,128]{2,1,0:T(8,128)}, u32[]{:S(2)}) copy-start(f32[16,128,128]{2,1,0:T(8,128)} %param.9) | copy-start | bytes 3145732
  3.1 14.2 %all-to-all-start = ((f32[8,1,2048]{2,1,0:T(1,128)}), f32[8,1,2048]{2,1,0:T(1,128)S(1)}, u32[]{:S(2)}, u32[]{:S(2)}) async-start(f32[8,1,2048]{2,1,0:T(1,128)} %all_to_all.24), calls=%async_computation | async-start | bytes 131072 | tf_op jit(solution)/shard_map/all_to_all | solution.py:119
  11.7 4.2 %copy-start.9 = (s32[256]{0:T(256)S(1)}, s32[256]{0:T(256)}, u32[]{:S(2)}) copy-start(s32[256]{0:T(256)} %param.10) | copy-start | bytes 3076
  19.5 1.4 %copy-start.4 = (f32[128,128,1,1]{1,0,3,2:T(8,128)S(1)}, f32[128,128,1,1]{1,0,3,2:T(8,128)}, u32[]{:S(2)}) copy-start(f32[128,128,1,1]{1,0,3,2:T(8,128)} %constant.100) | copy-start | bytes 196612
  20.8 1.0 %copy-start.8 = (f32[128,128,1,1]{1,0,3,2:T(8,128)S(1)}, f32[128,128,1,1]{1,0,3,2:T(8,128)}, u32[]{:S(2)}) copy-start(f32[128,128,1,1]{1,0,3,2:T(8,128)} %constant.102) | copy-start | bytes 196612
  21.8 1.1 %copy-start.5 = (f32[128,128,1,1]{1,0,3,2:T(8,128)S(1)}, f32[128,128,1,1]{1,0,3,2:T(8,128)}, u32[]{:S(2)}) copy-start(f32[128,128,1,1]{1,0,3,2:T(8,128)} %constant.101) | copy-start | bytes 196612
  25.0 1.0 %copy-start.7 = (f32[128,128,1,1]{1,0,3,2:T(8,128)S(1)}, f32[128,128,1,1]{1,0,3,2:T(8,128)}, u32[]{:S(2)}) copy-start(f32[128,128,1,1]{1,0,3,2:T(8,128)} %constant.103) | copy-start | bytes 196612
  30.4 13.5 %copy-start.6 = (f32[2,2,32,128]{3,2,1,0:T(8,128)S(1)}, f32[2,2,32,128]{3,2,1,0:T(8,128)}, u32[]{:S(2)}) copy-start(f32[2,2,32,128]{3,2,1,0:T(8,128)} %param.7) | copy-start | bytes 196612
  30.6 20.1 %copy-start.3 = (bf16[2,64,32,128]{3,2,1,0:T(8,128)(2,1)S(1)}, bf16[2,64,32,128]{3,2,1,0:T(8,128)(2,1)}, u32[]{:S(2)}) copy-start(bf16[2,64,32,128]{3,2,1,0:T(8,128)(2,1)} %get-tuple-element.12) | copy-start | bytes 3145732
  31.8 19.4 %copy-start.2 = (bf16[2,64,32,128]{3,2,1,0:T(8,128)(2,1)S(1)}, bf16[2,64,32,128]{3,2,1,0:T(8,128)(2,1)}, u32[]{:S(2)}) copy-start(bf16[2,64,32,128]{3,2,1,0:T(8,128)(2,1)} %get-tuple-element.14) | copy-start | bytes 3145732
  31.8 11.7 %all-to-all-start.1 = ((f32[8,1,2048]{2,1,0:T(1,128)}), f32[8,1,2048]{2,1,0:T(1,128)S(1)}, u32[]{:S(2)}, u32[]{:S(2)}) async-start(f32[8,1,2048]{2,1,0:T(1,128)} %all_to_all.25), calls=%async_computation.1 | async-start | bytes 131072 | tf_op jit(solution)/shard_map/all_to_all | solution.py:129
  50.6 1.2 %copy-start.1 = (bf16[2,64,32,128]{3,2,1,0:T(8,128)(2,1)S(1)}, bf16[2,64,32,128]{3,2,1,0:T(8,128)(2,1)}, u32[]{:S(2)}) copy-start(bf16[2,64,32,128]{3,2,1,0:T(8,128)(2,1)} %get-tuple-element.13) | copy-start | bytes 3145732
  53.5 9.9 %all-to-all-start.2 = ((f32[8,1,512]{2,1,0:T(1,128)}), f32[8,1,512]{2,1,0:T(1,128)S(1)}, u32[]{:S(2)}, u32[]{:S(2)}) async-start(f32[8,1,512]{2,1,0:T(1,128)} %all_to_all.26), calls=%async_computation.2 | async-start | bytes 32768 | tf_op jit(solution)/shard_map/all_to_all | solution.py:100

commit v15 on v14

--- a/solution.py
+++ b/solution.py
@@ -114,20 +114,21 @@
     inverse = dft_table(grid_size, 1.0)
     forward = dft_table(grid_size, -1.0)
     tables = plane_tables(stick_col, grid_size)
-    z_lines = jnp.einsum("dczk,cbsk->zdbs", inverse, psi_block, precision=fast)
-    lanes = z_lines.shape[1:]
+    inverse_split = inverse.reshape(2, 2, pw_count, planes, grid_size)
+    z_lines = jnp.einsum("dcpzk,cbsk->pdbzs", inverse_split, psi_block, precision=fast)
+    lanes = z_lines.shape[1:3]
     received = lax.all_to_all(
         z_lines.reshape(pw_count, -1), "pw", split_axis=0, concat_axis=0, tiled=True
     )
-    received = received.reshape((pw_count, planes) + lanes)
-    amp = jnp.transpose(received, (2, 3, 1, 0, 4)).reshape(
+    received = received.reshape((pw_count,) + lanes + (planes, sticks_dev))
+    amp = jnp.transpose(received, (1, 2, 3, 0, 4)).reshape(
         lanes[0], lanes[1], planes, pw_count * sticks_dev
     )
     picked = plane_phase(amp, potential, tables, grid_size)
     outgoing = picked.reshape(lanes[0], lanes[1], planes, pw_count, sticks_dev)
     outgoing = jnp.transpose(outgoing, (3, 2, 0, 1, 4)).reshape(pw_count, -1)
     sticks_back = lax.all_to_all(outgoing, "pw", split_axis=0, concat_axis=0, tiled=True)
-    sticks_back = sticks_back.reshape((pw_count * planes,) + lanes)
+    sticks_back = sticks_back.reshape((pw_count * planes,) + lanes + (sticks_dev,))
     vpsi = jnp.einsum("dckz,zcbs->dbsk", forward, sticks_back, precision=fast)
     applied = kinetic[None, None] * psi_block + vpsi
     lowered = applied.astype(jnp.bfloat16)

time: 64.4 us -> 64 us (level)
  no operation moved by 1% of the time
where the time goes in v15:
time: 64 us; the launch traced here: 63.5 us
  matrix products  16.6 us (26%)
  starting transfers between devices  15.4 us (24%)
  waiting for transfers between devices  14.1 us (22%)
  local copies, waits for them, and re-layouts  8.45 us (13%)
  blocking collectives  5.43 us (8%)
  other arithmetic  2.54 us (4%)
  between operations  0.97 us (2%)
    dot_general x10, matrix products, mult(): jnp.dot(left, right, precision=lax.Precision.HIGH, preferred_element_type...  12.1 us
    all_to_all x1, starting transfers between devices, per_device_rows(): lax.all_to_all(z_lines.reshape(pw_count, -1), 'pw', split_axis=0, concat_...  7.28 us
    all_to_all x1, waiting for transfers between devices, per_device_rows(): lax.all_to_all(outgoing, 'pw', split_axis=0, concat_axis=0, tiled=True)  6.83 us
    all_to_all x1, waiting for transfers between devices, intersect(): lax.all_to_all(pieces, 'pw', split_axis=0, concat_axis=0, tiled=True)  5.88 us
    all_gather x1, blocking collectives, per_device_rows(): gathered = lax.all_gather(lowered, 'band', axis=1, tiled=True)  5.43 us
    all_to_all x1, starting transfers between devices, per_device_rows(): lax.all_to_all(outgoing, 'pw', split_axis=0, concat_axis=0, tiled=True)  4.8 us
    slice x1, local copies, waits for them, and re-layouts, intersect(): psi_all[:, k * width:(k + 1) * width]  4.13 us
    all_to_all x1, starting transfers between devices, intersect(): lax.all_to_all(pieces, 'pw', split_axis=0, concat_axis=0, tiled=True)  3.34 us
  transfers between devices with their start and end apart: 3, of which 3 were waited for; matrix products, arithmetic and copies ran while one was open for 10% of the time, Pallas kernels for 0%

profile of v15, /device:TPU:0, one launch (start us, length us, event | category | flops | bytes accessed | tf_op | source)
XLA Modules:
  0.0 63.5 jit_solution(11168831397349537302)
XLA Ops:
  0.6 0.0 copy-start
  0.6 1.3 %convolution_bitcast_fusion = f32[8,2,2,16,32]{4,3,2,0,1:T(8,128)S(1)} fusion(f32[2,2,8,16,128,1]{4,3,1,5,2,0:T(8,128)} %constant.100, f32[2,2,32,128]{3,2,1,0:T(8,128)} %param.7), kind=kOutput, calls=%fused_computation.28 | convolution fusion | flops 25165824 | bytes 393216 | tf_op jit(solution)/shard_map/dcpzk,cbsk->pdbzs/dot_general | solution.py:118
  2.0 0.8 %all_to_all.24 = f32[8,1,2048]{2,1,0:T(1,128)} reshape(f32[8,2,2,16,32]{4,3,2,1,0:T(8,128)S(1)} %copy.49) | data formatting | bytes 131072 | tf_op jit(solution)/shard_map/all_to_all | solution.py:120
  2.8 7.3 %all-to-all-start = ((f32[8,1,2048]{2,1,0:T(1,128)}), f32[8,1,2048]{2,1,0:T(1,128)S(1)}, u32[]{:S(2)}, u32[]{:S(2)}) async-start(f32[8,1,2048]{2,1,0:T(1,128)} %all_to_all.24), calls=%async_computation | async-start | bytes 131072 | tf_op jit(solution)/shard_map/all_to_all | solution.py:120
  10.1 0.7 %and_select_fusion = (s32[256]{0:T(256)S(1)}, s32[256]{0:T(256)S(1)}) fusion(s32[256]{0:T(256)} %param.10), kind=kLoop, calls=%fused_computation.76 | loop fusion | flops 4864 | bytes 3072 | tf_op jit(solution)/shard_map/jit(remainder)/select_n | solution.py:35
  10.8 0.5 fusion.53
  11.3 0.0 copy-done
  11.3 0.1 broadcast_multiply_fusion
  11.4 0.0 copy-start.9
  11.4 4.1 %fusion.61 = (bf16[2,64,32,128]{3,2,1,0:T(8,128)(2,1)}, bf16[2,64,32,128]{3,2,1,0:T(8,128)(2,1)}, bf16[2,64,32,128]{3,2,1,0:T(8,128)(2,1)}, bf16[2,64,32,128]{3,2,1,0:T(8,128)(2,1)S(1)}) fusion(bf16[2,256,32,128]{3,2,1,0:T(8,128)(2,1)} %param.8), kind=kLoop, calls=%fused_computation.96 | loop fusion | bytes 8388608 | tf_op jit(solution)/shard_map/slice | solution.py:88
  15.5 0.0 copy-done.9
  15.5 0.1 fusion.56
  15.6 1.3 %all-to-all-done = f32[8,1,2048]{2,1,0:T(1,128)S(1)} async-done(((f32[8,1,2048]{2,1,0:T(1,128)}), f32[8,1,2048]{2,1,0:T(1,128)S(1)}, u32[]{:S(2)}, u32[]{:S(2)}) %all-to-all-start) | async-done | bytes 65568 | tf_op jit(solution)/shard_map/all_to_all | solution.py:120
  17.0 0.2 reduce.1
  17.1 0.1 reshape.137
  17.3 0.1 copy.51
  17.4 0.1 mul.155
  17.5 0.1 copy.52
  17.6 0.1 mul.164
  17.6 1.3 %fusion = f32[2,16,128,128]{3,2,1,0:T(8,128)S(1)} fusion(f32[128,256]{1,0:T(8,128)S(1)} %get-tuple-element.25, f32[2,16,256]{2,1,0:T(8,128)S(1)} %mul.164, f32[128,256]{1,0:T(8,128)S(1)} %get-tuple-element.24, f32[2,16,256]{2,1,0:T(8,128)S(1)} %mul.155, s32[256]{0:T(256)S(1)} %get-tuple-element.22), kind=kOutput, calls=%fused_computation.2 | convolution fusion | flops 808484864 | bytes 2425856 | tf_op jit(solution)/shard_map/dot_general | solution.py:48
  19.0 0.0 copy-start.4
  19.0 1.3 %fusion.4 = f32[2,16,128,128]{3,2,1,0:T(8,128)S(1)} fusion(f32[128,256]{1,0:T(8,128)S(1)} %get-tuple-element.25, f32[2,16,256]{2,1,0:T(8,128)S(1)} %mul.164, f32[128,256]{1,0:T(8,128)S(1)} %get-tuple-element.24, f32[2,16,256]{2,1,0:T(8,128)S(1)} %mul.155, s32[256]{0:T(256)S(1)} %get-tuple-element.22), kind=kOutput, calls=%fused_computation.6 | convolution fusion | flops 808484864 | bytes 2425856 | tf_op jit(solution)/shard_map/dot_general | solution.py:48
  20.3 0.0 copy-done.4
  20.4 0.0 copy-start.8
  20.4 1.0 %fusion.14 = f32[2,16,128,128]{3,2,1,0:T(8,128)S(1)} fusion(f32[128,128,1,1]{1,0,3,2:T(8,128)S(1)} %copy-done.4, f32[2,16,128,128]{3,2,1,0:T(8,128)S(1)} %fusion.4, f32[2,16,128,128]{3,2,1,0:T(8,128)S(1)} %fusion), kind=kOutput, calls=%fused_computation.18 | convolution fusion | flops 403177472 | bytes 6356992 | tf_op jit(solution)/shard_map/dot_general | solution.py:48
  21.3 0.0 copy-done.8
  21.4 0.0 copy-start.5
  21.4 1.0 %add_multiply_fusion = f32[2,16,128,128]{3,2,1,0:T(8,128)S(1)} fusion(f32[2,16,128,128]{3,2,1,0:T(8,128)S(1)} %fusion.14, f32[2,16,128,128]{3,2,1,0:T(8,128)S(1)} %fusion.4, f32[128,128,1,1]{1,0,3,2:T(8,128)S(1)} %copy-done.8, f32[16,128,128]{2,1,0:T(8,128)S(1)} %broadcast_multiply_fusion), kind=kOutput, calls=%fused_computation.16 | convolution fusion | flops 403701760 | bytes 7405568 | tf_op jit(solution)/shard_map/dot_general | solution.py:48
  22.4 0.0 copy-done.5
  22.4 1.1 %subtract_multiply_fusion = f32[2,16,128,128]{3,2,1,0:T(8,128)S(1)} fusion(f32[2,16,128,128]{3,2,1,0:T(8,128)S(1)} %fusion.14, f32[2,16,128,128]{3,2,1,0:T(8,128)S(1)} %fusion, f32[128,128,1,1]{1,0,3,2:T(8,128)S(1)} %copy-done.5, f32[16,128,128]{2,1,0:T(8,128)S(1)} %broadcast_multiply_fusion), kind=kOutput, calls=%fused_computation.17 | convolution fusion | flops 403701760 | bytes 7405568 | tf_op jit(solution)/shard_map/dot_general | solution.py:48
  23.5 1.0 %fusion.65 = f32[2,16,128,128]{3,2,1,0:T(8,128)S(1)} fusion(f32[2,16,128,128]{3,2,1,0:T(8,128)S(1)} %subtract_multiply_fusion, f32[128,128,1,1]{1,0,3,2:T(8,128)S(1)} %copy-done.5), kind=kOutput, calls=%fused_computation.100 | convolution fusion | flops 402653184 | bytes 4259840 | tf_op jit(solution)/shard_map/dot_general | solution.py:48
  24.5 0.0 copy-start.7
  24.5 1.0 %fusion.12 = f32[2,16,128,128]{3,2,1,0:T(8,128)S(1)} fusion(f32[128,128,1,1]{1,0,3,2:T(8,128)S(1)} %copy-done.4, f32[2,16,128,128]{3,2,1,0:T(8,128)S(1)} %subtract_multiply_fusion, f32[2,16,128,128]{3,2,1,0:T(8,128)S(1)} %add_multiply_fusion), kind=kOutput, calls=%fused_computation.14 | convolution fusion | flops 403177472 | bytes 6356992 | tf_op jit(solution)/shard_map/dot_general | solution.py:48
  25.5 0.0 copy-done.7
  25.6 1.0 %fusion.64 = f32[2,16,128,128]{3,2,1,0:T(8,128)S(1)} fusion(f32[2,16,128,128]{3,2,1,0:T(8,128)S(1)} %add_multiply_fusion, f32[128,128,1,1]{1,0,3,2:T(8,128)S(1)} %copy-done.7), kind=kOutput, calls=%fused_computation.99 | convolution fusion | flops 402653184 | bytes 4259840 | tf_op jit(solution)/shard_map/dot_general | solution.py:48
  26.6 1.3 %fusion.10 = f32[2,16,128,256]{3,2,1,0:T(8,128)S(1)} fusion(f32[2,16,128,128]{3,2,1,0:T(8,128)S(1)} %fusion.12, f32[2,16,128,128]{3,2,1,0:T(8,128)S(1)} %fusion.64, s32[256]{0:T(256)S(1)} %get-tuple-element.22), kind=kOutput, calls=%fused_computation.12 | convolution fusion | flops 805863424 | bytes 8389632 | tf_op jit(solution)/shard_map/dot_general | solution.py:48
  27.8 2.1 %add_reduce_fusion = (f32[2,16,256]{2,1,0:T(8,128)S(1)}, f32[2,16,256]{2,1,0:T(8,128)S(1)}) fusion(f32[2,16,128,256]{3,2,1,0:T(8,128)S(1)} %fusion.10, f32[128,256]{1,0:T(8,128)S(1)} %get-tuple-element.25, f32[128,256]{1,0:T(8,128)S(1)} %get-tuple-element.24, s32[256]{0:T(256)S(1)} %get-tuple-element.22, f32[2,16,128,128]{3,2,1,0:T(8,128)S(1)} %fusion.12, ...), kind=kOutput, calls=%fused_computation.1 | convolution fusion | flops 814235648 | bytes 8717312 | tf_op jit(solution)/shard_map/dot_general | solution.py:48
  29.9 0.0 copy-start.6
  30.0 0.1 stack.22
  30.0 0.1 stack.23
  30.1 0.0 copy-start.3
  30.2 0.2 copy.53
  30.4 0.9 %all_to_all.25 = f32[8,1,2048]{2,1,0:T(1,128)} reshape(f32[8,16,2,2,32]{4,3,2,1,0:T(2,128)S(1)} %copy.53) | data formatting | bytes 131072 | tf_op jit(solution)/shard_map/all_to_all | solution.py:130
  31.3 4.8 %all-to-all-start.1 = ((f32[8,1,2048]{2,1,0:T(1,128)}), f32[8,1,2048]{2,1,0:T(1,128)S(1)}, u32[]{:S(2)}, u32[]{:S(2)}) async-start(f32[8,1,2048]{2,1,0:T(1,128)} %all_to_all.25), calls=%async_computation.1 | async-start | bytes 131072 | tf_op jit(solution)/shard_map/all_to_all | solution.py:130
  36.1 0.1 add_multiply_fusion.1
  36.2 6.8 %all-to-all-done.1 = f32[8,1,2048]{2,1,0:T(1,128)S(1)} async-done(((f32[8,1,2048]{2,1,0:T(1,128)}), f32[8,1,2048]{2,1,0:T(1,128)S(1)}, u32[]{:S(2)}, u32[]{:S(2)}) %all-to-all-start.1) | async-done | bytes 65568 | tf_op jit(solution)/shard_map/all_to_all | solution.py:130
  43.0 0.2 reduce.2
  43.2 0.2 reshape.138
  43.4 0.0 copy-done.6
  43.4 1.3 %fusion.63 = (bf16[2,2,32,128]{3,2,0,1:T(8,128)(2,1)S(1)}, f32[2,2,32,128]{3,2,0,1:T(8,128)S(1)}) fusion(f32[2,2,128,128,1]{3,2,1,0,4:T(8,128)} %constant.105, f32[128,2,2,32,1]{3,2,1,0,4:T(2,128)S(1)} %bitcast.96, f32[2,2,32,128]{3,2,1,0:T(8,128)S(1)} %copy-done.6, f32[32,128]{1,0:T(8,128)S(1)} %add_multiply_fusion.1), kind=kOutput, calls=%fused_computation.98 | convolution fusion | flops 25214976 | bytes 507904 | tf_op jit(solution)/shard_map/dckz,zcbs->dbsk/dot_general | solution.py:132
  44.7 5.4 %all_gather.3 = bf16[2,8,32,128]{3,2,0,1:T(8,128)(2,1)S(1)} all-gather(bf16[2,2,32,128]{3,2,0,1:T(8,128)(2,1)S(1)} %get-tuple-element.26), channel_id=1, replica_groups=mesh['pw'=8,'band'=4] {'band'}, dimensions={1}, use_global_device_ids=true | all-gather | bytes 163840 | tf_op jit(solution)/shard_map/all_gather | solution.py:135
  50.3 0.0 copy-done.3
  50.3 0.5 convolution_bitcast_fusion.5
  50.7 0.0 copy-done.2
  50.7 0.5 convolution_bitcast_fusion.4
  51.2 0.2 copy-done.1
  51.4 0.5 convolution_bitcast_fusion.3
  51.9 0.5 convolution_bitcast_fusion.2
  52.3 0.1 pad_maximum_fusion.1
  52.4 0.6 all_to_all.26
  53.0 3.3 %all-to-all-start.2 = ((f32[8,1,512]{2,1,0:T(1,128)}), f32[8,1,512]{2,1,0:T(1,128)S(1)}, u32[]{:S(2)}, u32[]{:S(2)}) async-start(f32[8,1,512]{2,1,0:T(1,128)} %all_to_all.26), calls=%async_computation.2 | async-start | bytes 32768 | tf_op jit(solution)/shard_map/all_to_all | solution.py:100
  56.4 0.6 copy.68
  57.0 5.9 %all-to-all-done.2 = f32[8,1,512]{2,1,0:T(1,128)S(1)} async-done(((f32[8,1,512]{2,1,0:T(1,128)}), f32[8,1,512]{2,1,0:T(1,128)S(1)}, u32[]{:S(2)}, u32[]{:S(2)}) %all-to-all-start.2) | async-done | bytes 16416 | tf_op jit(solution)/shard_map/all_to_all | solution.py:100
  62.9 0.6 reduce_sum.29
  (10 shorter events, 0.1 us)
Async XLA Ops:
  0.6 10.7 %copy-start = (f32[16,128,128]{2,1,0:T(8,128)S(1)}, f32[16,128,128]{2,1,0:T(8,128)}, u32[]{:S(2)}) copy-start(f32[16,128,128]{2,1,0:T(8,128)} %param.9) | copy-start | bytes 3145732
  2.8 14.2 %all-to-all-start = ((f32[8,1,2048]{2,1,0:T(1,128)}), f32[8,1,2048]{2,1,0:T(1,128)S(1)}, u32[]{:S(2)}, u32[]{:S(2)}) async-start(f32[8,1,2048]{2,1,0:T(1,128)} %all_to_all.24), calls=%async_computation | async-start | bytes 131072 | tf_op jit(solution)/shard_map/all_to_all | solution.py:120
  11.4 4.2 %copy-start.9 = (s32[256]{0:T(256)S(1)}, s32[256]{0:T(256)}, u32[]{:S(2)}) copy-start(s32[256]{0:T(256)} %param.10) | copy-start | bytes 3076
  19.0 1.4 %copy-start.4 = (f32[128,128,1,1]{1,0,3,2:T(8,128)S(1)}, f32[128,128,1,1]{1,0,3,2:T(8,128)}, u32[]{:S(2)}) copy-start(f32[128,128,1,1]{1,0,3,2:T(8,128)} %constant.101) | copy-start | bytes 196612
  20.4 1.0 %copy-start.8 = (f32[128,128,1,1]{1,0,3,2:T(8,128)S(1)}, f32[128,128,1,1]{1,0,3,2:T(8,128)}, u32[]{:S(2)}) copy-start(f32[128,128,1,1]{1,0,3,2:T(8,128)} %constant.103) | copy-start | bytes 196612
  21.4 1.1 %copy-start.5 = (f32[128,128,1,1]{1,0,3,2:T(8,128)S(1)}, f32[128,128,1,1]{1,0,3,2:T(8,128)}, u32[]{:S(2)}) copy-start(f32[128,128,1,1]{1,0,3,2:T(8,128)} %constant.102) | copy-start | bytes 196612
  24.5 1.0 %copy-start.7 = (f32[128,128,1,1]{1,0,3,2:T(8,128)S(1)}, f32[128,128,1,1]{1,0,3,2:T(8,128)}, u32[]{:S(2)}) copy-start(f32[128,128,1,1]{1,0,3,2:T(8,128)} %constant.104) | copy-start | bytes 196612
  29.9 13.5 %copy-start.6 = (f32[2,2,32,128]{3,2,1,0:T(8,128)S(1)}, f32[2,2,32,128]{3,2,1,0:T(8,128)}, u32[]{:S(2)}) copy-start(f32[2,2,32,128]{3,2,1,0:T(8,128)} %param.7) | copy-start | bytes 196612
  30.1 20.1 %copy-start.3 = (bf16[2,64,32,128]{3,2,1,0:T(8,128)(2,1)S(1)}, bf16[2,64,32,128]{3,2,1,0:T(8,128)(2,1)}, u32[]{:S(2)}) copy-start(bf16[2,64,32,128]{3,2,1,0:T(8,128)(2,1)} %get-tuple-element.12) | copy-start | bytes 3145732
  31.3 19.4 %copy-start.2 = (bf16[2,64,32,128]{3,2,1,0:T(8,128)(2,1)S(1)}, bf16[2,64,32,128]{3,2,1,0:T(8,128)(2,1)}, u32[]{:S(2)}) copy-start(bf16[2,64,32,128]{3,2,1,0:T(8,128)(2,1)} %get-tuple-element.14) | copy-start | bytes 3145732
  31.3 11.7 %all-to-all-start.1 = ((f32[8,1,2048]{2,1,0:T(1,128)}), f32[8,1,2048]{2,1,0:T(1,128)S(1)}, u32[]{:S(2)}, u32[]{:S(2)}) async-start(f32[8,1,2048]{2,1,0:T(1,128)} %all_to_all.25), calls=%async_computation.1 | async-start | bytes 131072 | tf_op jit(solution)/shard_map/all_to_all | solution.py:130
  50.2 1.2 %copy-start.1 = (bf16[2,64,32,128]{3,2,1,0:T(8,128)(2,1)S(1)}, bf16[2,64,32,128]{3,2,1,0:T(8,128)(2,1)}, u32[]{:S(2)}) copy-start(bf16[2,64,32,128]{3,2,1,0:T(8,128)(2,1)} %get-tuple-element.13) | copy-start | bytes 3145732
  53.0 9.9 %all-to-all-start.2 = ((f32[8,1,512]{2,1,0:T(1,128)}), f32[8,1,512]{2,1,0:T(1,128)S(1)}, u32[]{:S(2)}, u32[]{:S(2)}) async-start(f32[8,1,512]{2,1,0:T(1,128)} %all_to_all.26), calls=%async_computation.2 | async-start | bytes 32768 | tf_op jit(solution)/shard_map/all_to_all | solution.py:100

commit v16 on v15

--- a/solution.py
+++ b/solution.py
@@ -126,10 +126,11 @@
     )
     picked = plane_phase(amp, potential, tables, grid_size)
     outgoing = picked.reshape(lanes[0], lanes[1], planes, pw_count, sticks_dev)
-    outgoing = jnp.transpose(outgoing, (3, 2, 0, 1, 4)).reshape(pw_count, -1)
+    outgoing = jnp.transpose(outgoing, (3, 0, 1, 2, 4)).reshape(pw_count, -1)
     sticks_back = lax.all_to_all(outgoing, "pw", split_axis=0, concat_axis=0, tiled=True)
-    sticks_back = sticks_back.reshape((pw_count * planes,) + lanes + (sticks_dev,))
-    vpsi = jnp.einsum("dckz,zcbs->dbsk", forward, sticks_back, precision=fast)
+    sticks_back = sticks_back.reshape((pw_count,) + lanes + (planes, sticks_dev))
+    forward_split = forward.reshape(2, 2, grid_size, pw_count, planes)
+    vpsi = jnp.einsum("dckpz,pcbzs->dbsk", forward_split, sticks_back, precision=fast)
     applied = kinetic[None, None] * psi_block + vpsi
     lowered = applied.astype(jnp.bfloat16)
     gathered = lax.all_gather(lowered, "band", axis=1, tiled=True)

time: 64 us -> 62.6 us (0.978)
  blocking collectives: 5.43 us -> 14.4 us
  waiting for transfers between devices: 14.1 us -> 8.17 us
  starting transfers between devices: 15.4 us -> 12 us
  local copies, waits for them, and re-layouts: 8.45 us -> 6.83 us
  other arithmetic: 2.54 us -> 3.19 us
    all_to_all x0 -> x1, blocking collectives: none -> 8.94 us  [intersect(): lax.all_to_all(pieces, 'pw', split_axis=0, concat_axis=0, tiled=True)]
    all_to_all x1 -> x0, waiting for transfers between devices: 5.88 us -> none  [intersect(): lax.all_to_all(pieces, 'pw', split_axis=0, concat_axis=0, tiled=True)]
    all_to_all x1 -> x0, starting transfers between devices: 3.34 us -> none  [intersect(): lax.all_to_all(pieces, 'pw', split_axis=0, concat_axis=0, tiled=True)]
    convert_element_type x0 -> x1, other arithmetic: none -> 0.64 us  [per_device_rows(): lowered = applied.astype(jnp.bfloat16)]
  transfers between devices with their start and end apart: 3 -> 2, of which waited for: 3 -> 2; matrix products, arithmetic and copies ran while one was open for 10% -> 9% of each run, Pallas kernels for 0% -> 0%
where the time goes in v16:
time: 62.6 us; the launch traced here: 62.2 us
  matrix products  16.7 us (27%)
  blocking collectives  14.4 us (23%)
  starting transfers between devices  12 us (19%)
  waiting for transfers between devices  8.17 us (13%)
  local copies, waits for them, and re-layouts  6.83 us (11%)
  other arithmetic  3.19 us (5%)
  between operations  0.96 us (2%)
    dot_general x10, matrix products, mult(): jnp.dot(left, right, precision=lax.Precision.HIGH, preferred_element_type...  12.1 us
    all_to_all x1, blocking collectives, intersect(): lax.all_to_all(pieces, 'pw', split_axis=0, concat_axis=0, tiled=True)  8.94 us
    all_to_all x1, starting transfers between devices, per_device_rows(): lax.all_to_all(z_lines.reshape(pw_count, -1), 'pw', split_axis=0, concat_...  7.28 us
    all_to_all x1, waiting for transfers between devices, per_device_rows(): lax.all_to_all(outgoing, 'pw', split_axis=0, concat_axis=0, tiled=True)  6.83 us
    all_gather x1, blocking collectives, per_device_rows(): gathered = lax.all_gather(lowered, 'band', axis=1, tiled=True)  5.41 us
    all_to_all x1, starting transfers between devices, per_device_rows(): lax.all_to_all(outgoing, 'pw', split_axis=0, concat_axis=0, tiled=True)  4.67 us
    slice x1, local copies, waits for them, and re-layouts, intersect(): psi_all[:, k * width:(k + 1) * width]  4.13 us
    dot_general x4, matrix products, intersect(): lax.dot_general(both, psi_all[:, k * width:(k + 1) * width], dims, prefer...  1.87 us
  transfers between devices with their start and end apart: 2, of which 2 were waited for; matrix products, arithmetic and copies ran while one was open for 9% of the time, Pallas kernels for 0%

profile of v16, /device:TPU:0, one launch (start us, length us, event | category | flops | bytes accessed | tf_op | source)
XLA Modules:
  0.0 62.2 jit_solution(7023874745931645327)
XLA Ops:
  0.6 0.0 copy-start
  0.6 1.3 %convolution_bitcast_fusion = f32[8,2,2,16,32]{4,3,2,0,1:T(8,128)S(1)} fusion(f32[2,2,8,16,128,1]{4,3,1,5,2,0:T(8,128)} %constant.101, f32[2,2,32,128]{3,2,1,0:T(8,128)} %param.7), kind=kOutput, calls=%fused_computation.28 | convolution fusion | flops 25165824 | bytes 393216 | tf_op jit(solution)/shard_map/dcpzk,cbsk->pdbzs/dot_general | solution.py:118
  2.0 0.8 %all_to_all.24 = f32[8,1,2048]{2,1,0:T(1,128)} reshape(f32[8,2,2,16,32]{4,3,2,1,0:T(8,128)S(1)} %copy.66) | data formatting | bytes 131072 | tf_op jit(solution)/shard_map/all_to_all | solution.py:120
  2.8 7.3 %all-to-all-start = ((f32[8,1,2048]{2,1,0:T(1,128)}), f32[8,1,2048]{2,1,0:T(1,128)S(1)}, u32[]{:S(2)}, u32[]{:S(2)}) async-start(f32[8,1,2048]{2,1,0:T(1,128)} %all_to_all.24), calls=%async_computation | async-start | bytes 131072 | tf_op jit(solution)/shard_map/all_to_all | solution.py:120
  10.1 0.7 %and_select_fusion = (s32[256]{0:T(256)S(1)}, s32[256]{0:T(256)S(1)}) fusion(s32[256]{0:T(256)} %param.10), kind=kLoop, calls=%fused_computation.75 | loop fusion | flops 4864 | bytes 3072 | tf_op jit(solution)/shard_map/jit(remainder)/select_n | solution.py:35
  10.8 0.5 fusion.53
  11.3 0.0 copy-done
  11.3 0.1 broadcast_multiply_fusion
  11.4 0.0 copy-start.9
  11.4 4.1 %fusion.62 = (bf16[2,64,32,128]{3,2,1,0:T(8,128)(2,1)}, bf16[2,64,32,128]{3,2,1,0:T(8,128)(2,1)}, bf16[2,64,32,128]{3,2,1,0:T(8,128)(2,1)}, bf16[2,64,32,128]{3,2,1,0:T(8,128)(2,1)S(1)}) fusion(bf16[2,256,32,128]{3,2,1,0:T(8,128)(2,1)} %param.8), kind=kLoop, calls=%fused_computation.96 | loop fusion | bytes 8388608 | tf_op jit(solution)/shard_map/slice | solution.py:88
  15.5 0.0 copy-done.9
  15.5 0.1 fusion.56
  15.6 1.3 %all-to-all-done = f32[8,1,2048]{2,1,0:T(1,128)S(1)} async-done(((f32[8,1,2048]{2,1,0:T(1,128)}), f32[8,1,2048]{2,1,0:T(1,128)S(1)}, u32[]{:S(2)}, u32[]{:S(2)}) %all-to-all-start) | async-done | bytes 65568 | tf_op jit(solution)/shard_map/all_to_all | solution.py:120
  17.0 0.2 reduce.1
  17.1 0.1 reshape.140
  17.3 0.1 copy.68
  17.4 0.1 mul.155
  17.5 0.1 copy.69
  17.6 0.1 mul.164
  17.6 1.3 %fusion = f32[2,16,128,128]{3,2,1,0:T(8,128)S(1)} fusion(f32[128,256]{1,0:T(8,128)S(1)} %get-tuple-element.25, f32[2,16,256]{2,1,0:T(8,128)S(1)} %mul.164, f32[128,256]{1,0:T(8,128)S(1)} %get-tuple-element.24, f32[2,16,256]{2,1,0:T(8,128)S(1)} %mul.155, s32[256]{0:T(256)S(1)} %get-tuple-element.22), kind=kOutput, calls=%fused_computation.2 | convolution fusion | flops 808484864 | bytes 2425856 | tf_op jit(solution)/shard_map/dot_general | solution.py:48
  19.0 0.0 copy-start.4
  19.0 1.3 %fusion.4 = f32[2,16,128,128]{3,2,1,0:T(8,128)S(1)} fusion(f32[128,256]{1,0:T(8,128)S(1)} %get-tuple-element.25, f32[2,16,256]{2,1,0:T(8,128)S(1)} %mul.164, f32[128,256]{1,0:T(8,128)S(1)} %get-tuple-element.24, f32[2,16,256]{2,1,0:T(8,128)S(1)} %mul.155, s32[256]{0:T(256)S(1)} %get-tuple-element.22), kind=kOutput, calls=%fused_computation.6 | convolution fusion | flops 808484864 | bytes 2425856 | tf_op jit(solution)/shard_map/dot_general | solution.py:48
  20.3 0.0 copy-done.4
  20.4 0.0 copy-start.8
  20.4 1.0 %fusion.14 = f32[2,16,128,128]{3,2,1,0:T(8,128)S(1)} fusion(f32[128,128,1,1]{1,0,3,2:T(8,128)S(1)} %copy-done.4, f32[2,16,128,128]{3,2,1,0:T(8,128)S(1)} %fusion.4, f32[2,16,128,128]{3,2,1,0:T(8,128)S(1)} %fusion), kind=kOutput, calls=%fused_computation.18 | convolution fusion | flops 403177472 | bytes 6356992 | tf_op jit(solution)/shard_map/dot_general | solution.py:48
  21.3 0.0 copy-done.8
  21.4 0.0 copy-start.5
  21.4 1.0 %add_multiply_fusion = f32[2,16,128,128]{3,2,1,0:T(8,128)S(1)} fusion(f32[2,16,128,128]{3,2,1,0:T(8,128)S(1)} %fusion.14, f32[2,16,128,128]{3,2,1,0:T(8,128)S(1)} %fusion.4, f32[128,128,1,1]{1,0,3,2:T(8,128)S(1)} %copy-done.8, f32[16,128,128]{2,1,0:T(8,128)S(1)} %broadcast_multiply_fusion), kind=kOutput, calls=%fused_computation.16 | convolution fusion | flops 403701760 | bytes 7405568 | tf_op jit(solution)/shard_map/dot_general | solution.py:48
  22.4 0.0 copy-done.5
  22.4 1.1 %subtract_multiply_fusion = f32[2,16,128,128]{3,2,1,0:T(8,128)S(1)} fusion(f32[2,16,128,128]{3,2,1,0:T(8,128)S(1)} %fusion.14, f32[2,16,128,128]{3,2,1,0:T(8,128)S(1)} %fusion, f32[128,128,1,1]{1,0,3,2:T(8,128)S(1)} %copy-done.5, f32[16,128,128]{2,1,0:T(8,128)S(1)} %broadcast_multiply_fusion), kind=kOutput, calls=%fused_computation.17 | convolution fusion | flops 403701760 | bytes 7405568 | tf_op jit(solution)/shard_map/dot_general | solution.py:48
  23.5 1.0 %fusion.65 = f32[2,16,128,128]{3,2,1,0:T(8,128)S(1)} fusion(f32[2,16,128,128]{3,2,1,0:T(8,128)S(1)} %subtract_multiply_fusion, f32[128,128,1,1]{1,0,3,2:T(8,128)S(1)} %copy-done.5), kind=kOutput, calls=%fused_computation.99 | convolution fusion | flops 402653184 | bytes 4259840 | tf_op jit(solution)/shard_map/dot_general | solution.py:48
  24.5 0.0 copy-start.7
  24.5 1.0 %fusion.12 = f32[2,16,128,128]{3,2,1,0:T(8,128)S(1)} fusion(f32[128,128,1,1]{1,0,3,2:T(8,128)S(1)} %copy-done.4, f32[2,16,128,128]{3,2,1,0:T(8,128)S(1)} %subtract_multiply_fusion, f32[2,16,128,128]{3,2,1,0:T(8,128)S(1)} %add_multiply_fusion), kind=kOutput, calls=%fused_computation.14 | convolution fusion | flops 403177472 | bytes 6356992 | tf_op jit(solution)/shard_map/dot_general | solution.py:48
  25.5 0.0 copy-done.7
  25.6 1.0 %fusion.64 = f32[2,16,128,128]{3,2,1,0:T(8,128)S(1)} fusion(f32[2,16,128,128]{3,2,1,0:T(8,128)S(1)} %add_multiply_fusion, f32[128,128,1,1]{1,0,3,2:T(8,128)S(1)} %copy-done.7), kind=kOutput, calls=%fused_computation.98 | convolution fusion | flops 402653184 | bytes 4259840 | tf_op jit(solution)/shard_map/dot_general | solution.py:48
  26.6 1.3 %fusion.10 = f32[2,16,128,256]{3,2,1,0:T(8,128)S(1)} fusion(f32[2,16,128,128]{3,2,1,0:T(8,128)S(1)} %fusion.12, f32[2,16,128,128]{3,2,1,0:T(8,128)S(1)} %fusion.64, s32[256]{0:T(256)S(1)} %get-tuple-element.22), kind=kOutput, calls=%fused_computation.12 | convolution fusion | flops 805863424 | bytes 8389632 | tf_op jit(solution)/shard_map/dot_general | solution.py:48
  27.8 2.1 %add_reduce_fusion = (f32[2,16,256]{2,1,0:T(8,128)S(1)}, f32[2,16,256]{2,1,0:T(8,128)S(1)}) fusion(f32[2,16,128,256]{3,2,1,0:T(8,128)S(1)} %fusion.10, f32[128,256]{1,0:T(8,128)S(1)} %get-tuple-element.25, f32[128,256]{1,0:T(8,128)S(1)} %get-tuple-element.24, s32[256]{0:T(256)S(1)} %get-tuple-element.22, f32[2,16,128,128]{3,2,1,0:T(8,128)S(1)} %fusion.12, ...), kind=kOutput, calls=%fused_computation.1 | convolution fusion | flops 814235648 | bytes 8717312 | tf_op jit(solution)/shard_map/dot_general | solution.py:48
  29.9 0.0 copy-start.6
  30.0 0.1 stack.22
  30.0 0.1 stack.23
  30.1 0.0 copy-start.3
  30.2 0.1 copy.70
  30.2 0.8 %all_to_all.25 = f32[8,1,2048]{2,1,0:T(1,128)} reshape(f32[8,2,2,16,32]{4,3,2,1,0:T(8,128)S(1)} %copy.70) | data formatting | bytes 131072 | tf_op jit(solution)/shard_map/all_to_all | solution.py:130
  31.0 4.7 %all-to-all-start.1 = ((f32[8,1,2048]{2,1,0:T(1,128)}), f32[8,1,2048]{2,1,0:T(1,128)S(1)}, u32[]{:S(2)}, u32[]{:S(2)}) async-start(f32[8,1,2048]{2,1,0:T(1,128)} %all_to_all.25), calls=%async_computation.1 | async-start | bytes 131072 | tf_op jit(solution)/shard_map/all_to_all | solution.py:130
  35.7 0.1 add_multiply_fusion.1
  35.8 6.8 %all-to-all-done.1 = f32[8,1,2048]{2,1,0:T(1,128)S(1)} async-done(((f32[8,1,2048]{2,1,0:T(1,128)}), f32[8,1,2048]{2,1,0:T(1,128)S(1)}, u32[]{:S(2)}, u32[]{:S(2)}) %all-to-all-start.1) | async-done | bytes 65568 | tf_op jit(solution)/shard_map/all_to_all | solution.py:130
  42.6 0.2 reduce.2
  42.8 0.0 copy-start.2
  42.8 0.1 reshape.141
  42.9 1.4 %fusion.29 = f32[2,32,2,128,1,1]{3,1,4,2,0,5:T(8,128)S(1)} fusion(f32[2,2,128,8,16,1]{2,4,1,0,5,3:T(8,128)} %constant.106, f32[8,2,2,16,32]{4,3,2,1,0:T(8,128)S(1)} %reshape.141), kind=kOutput, calls=%fused_computation.41 | convolution fusion | flops 25165824 | bytes 393216 | tf_op jit(solution)/shard_map/dckpz,pcbzs->dbsk/dot_general | solution.py:133
  44.3 0.0 copy-done.6
  44.3 0.6 %fusion.61 = (bf16[2,2,32,128]{3,2,1,0:T(8,128)(2,1)S(1)}, f32[2,2,32,128]{3,2,1,0:T(8,128)}) fusion(f32[2,32,2,128,1,1]{3,1,4,2,0,5:T(8,128)S(1)} %fusion.29, f32[2,2,32,128]{3,2,1,0:T(8,128)S(1)} %copy-done.6, f32[32,128]{1,0:T(8,128)S(1)} %add_multiply_fusion.1), kind=kLoop, calls=%fused_computation.95 | loop fusion | flops 49152 | bytes 245760 | tf_op jit(solution)/shard_map/convert_element_type | solution.py:135
  44.9 5.4 %all_gather.3 = bf16[2,8,32,128]{3,2,0,1:T(8,128)(2,1)S(1)} all-gather(bf16[2,2,32,128]{3,2,0,1:T(8,128)(2,1)S(1)} %copy.73), channel_id=1, replica_groups=mesh['pw'=8,'band'=4] {'band'}, dimensions={1}, use_global_device_ids=true | all-gather | bytes 163840 | tf_op jit(solution)/shard_map/all_gather | solution.py:136
  50.3 0.0 copy-start.1
  50.4 0.0 copy-done.3
  50.4 0.5 convolution_bitcast_fusion.4
  50.9 0.0 copy-done.2
  50.9 0.5 convolution_bitcast_fusion.3
  51.4 0.2 copy-done.1
  51.6 0.5 convolution_bitcast_fusion.2
  52.0 0.5 convolution_bitcast_fusion.1
  52.5 0.1 pad_maximum_fusion.1
  52.6 8.9 %all_to_all.30 = f32[8,1,512]{2,1,0:T(1,128)S(1)} all-to-all(f32[8,1,512]{2,1,0:T(1,128)S(1)} %all_to_all.26), channel_id=1, replica_groups=mesh['pw'=8,'band'=4] {'pw'}, dimensions={0} | all-to-all | bytes 32768 | tf_op jit(solution)/shard_map/all_to_all | solution.py:100
  61.6 0.6 reduce_sum.29
  (10 shorter events, 0.2 us)
Async XLA Ops:
  0.6 10.7 %copy-start = (f32[16,128,128]{2,1,0:T(8,128)S(1)}, f32[16,128,128]{2,1,0:T(8,128)}, u32[]{:S(2)}) copy-start(f32[16,128,128]{2,1,0:T(8,128)} %param.9) | copy-start | bytes 3145732
  2.8 14.2 %all-to-all-start = ((f32[8,1,2048]{2,1,0:T(1,128)}), f32[8,1,2048]{2,1,0:T(1,128)S(1)}, u32[]{:S(2)}, u32[]{:S(2)}) async-start(f32[8,1,2048]{2,1,0:T(1,128)} %all_to_all.24), calls=%async_computation | async-start | bytes 131072 | tf_op jit(solution)/shard_map/all_to_all | solution.py:120
  11.4 4.2 %copy-start.9 = (s32[256]{0:T(256)S(1)}, s32[256]{0:T(256)}, u32[]{:S(2)}) copy-start(s32[256]{0:T(256)} %param.10) | copy-start | bytes 3076
  19.0 1.4 %copy-start.4 = (f32[128,128,1,1]{1,0,3,2:T(8,128)S(1)}, f32[128,128,1,1]{1,0,3,2:T(8,128)}, u32[]{:S(2)}) copy-start(f32[128,128,1,1]{1,0,3,2:T(8,128)} %constant.102) | copy-start | bytes 196612
  20.4 1.0 %copy-start.8 = (f32[128,128,1,1]{1,0,3,2:T(8,128)S(1)}, f32[128,128,1,1]{1,0,3,2:T(8,128)}, u32[]{:S(2)}) copy-start(f32[128,128,1,1]{1,0,3,2:T(8,128)} %constant.104) | copy-start | bytes 196612
  21.4 1.1 %copy-start.5 = (f32[128,128,1,1]{1,0,3,2:T(8,128)S(1)}, f32[128,128,1,1]{1,0,3,2:T(8,128)}, u32[]{:S(2)}) copy-start(f32[128,128,1,1]{1,0,3,2:T(8,128)} %constant.103) | copy-start | bytes 196612
  24.5 1.0 %copy-start.7 = (f32[128,128,1,1]{1,0,3,2:T(8,128)S(1)}, f32[128,128,1,1]{1,0,3,2:T(8,128)}, u32[]{:S(2)}) copy-start(f32[128,128,1,1]{1,0,3,2:T(8,128)} %constant.105) | copy-start | bytes 196612
  29.9 14.3 %copy-start.6 = (f32[2,2,32,128]{3,2,1,0:T(8,128)S(1)}, f32[2,2,32,128]{3,2,1,0:T(8,128)}, u32[]{:S(2)}) copy-start(f32[2,2,32,128]{3,2,1,0:T(8,128)} %param.7) | copy-start | bytes 196612
  30.1 20.3 %copy-start.3 = (bf16[2,64,32,128]{3,2,1,0:T(8,128)(2,1)S(1)}, bf16[2,64,32,128]{3,2,1,0:T(8,128)(2,1)}, u32[]{:S(2)}) copy-start(bf16[2,64,32,128]{3,2,1,0:T(8,128)(2,1)} %get-tuple-element.12) | copy-start | bytes 3145732
  31.0 11.6 %all-to-all-start.1 = ((f32[8,1,2048]{2,1,0:T(1,128)}), f32[8,1,2048]{2,1,0:T(1,128)S(1)}, u32[]{:S(2)}, u32[]{:S(2)}) async-start(f32[8,1,2048]{2,1,0:T(1,128)} %all_to_all.25), calls=%async_computation.1 | async-start | bytes 131072 | tf_op jit(solution)/shard_map/all_to_all | solution.py:130
  42.8 8.1 %copy-start.2 = (bf16[2,64,32,128]{3,2,1,0:T(8,128)(2,1)S(1)}, bf16[2,64,32,128]{3,2,1,0:T(8,128)(2,1)}, u32[]{:S(2)}) copy-start(bf16[2,64,32,128]{3,2,1,0:T(8,128)(2,1)} %get-tuple-element.14) | copy-start | bytes 3145732
  50.3 1.2 %copy-start.1 = (bf16[2,64,32,128]{3,2,1,0:T(8,128)(2,1)S(1)}, bf16[2,64,32,128]{3,2,1,0:T(8,128)(2,1)}, u32[]{:S(2)}) copy-start(bf16[2,64,32,128]{3,2,1,0:T(8,128)(2,1)} %get-tuple-element.13) | copy-start | bytes 3145732
